TPU v7x, 32 devices: a whole 2x2x4 slice. The times are simulated.
32 devices in a mesh: groups: 2 (over y), leaf: 4 (over x, core), sub: 4 (over z).
Axes of the slice: x: 2, y: 2, z: 4, core: 2. Of those that a mesh axis runs over, the one named last changes fastest.
Arguments:
- embeddings: bfloat16 [128, 32768], P(None, ('groups', 'leaf', 'sub')), parts along dimension 1
- directions: float32 [32, 32768], P(None, ('groups', 'leaf', 'sub')), parts along dimension 1, may hold values from -6 to 6
- level_basis: bfloat16 [5, 64, 32768], P(None, None, ('groups', 'leaf', 'sub')), parts along dimension 2, may hold values from -6 to 6
- neighbours: int32 [64, 8], P(('groups', 'leaf', 'sub')), parts along dimension 0, may hold values from 0 to 31, as said below
- counts: int32 [64], P(('groups', 'leaf', 'sub')), parts along dimension 0, may hold values from 2 to 8
Outputs:
- kernel_image: float32 [32, 32768], P(None, ('groups', 'leaf', 'sub')), parts along dimension 1
There are 2 independent parts, one for each index of `groups`. A program takes and returns all parts, laid end to end along the dimension named above; each array names one. Nothing has to cross between parts.
Inputs may be any that keep to these rules, and one draw needn't show every extreme that they name: `neighbours`: every entry names the leaf just before or just after its own row's leaf; slot 0 names the leaf just before and slot 1 the leaf just after (for the first and the last leaf, both name the one adjacent leaf).
All inputs are finite; a program needn't handle non-finite values.
Results may differ from a plain program's by a relative error of at most 0.0039.
Values may be sent and summed in bfloat16 or wider, within the bound.
No kernel may reach another device: no remote copies, remote signals or barrier semaphores. Data moves between devices by JAX's collectives and lax.ppermute only.
A program may use at most 64 MiB of HBM per device.

v0:
```python
import math

import jax
import jax.numpy as jnp
from jax import lax
from jax.sharding import PartitionSpec as P

LEAF = 512


AMPLITUDE = 0.5
DISTANCE_SCALE = 0.125
RIDGE = 0.5


def padded(x, sides, width):
    for axis, dim in sides:
        count, length = (lax.axis_size(axis), x.shape[dim])
        up = [(i, (i + 1) % count) for i in range(count - 1)]
        down = [(j, i) for i, j in up]
        last = lax.slice_in_dim(x, length - width, length, axis=dim)
        leading = lax.slice_in_dim(x, 0, width, axis=dim)
        before = lax.ppermute(last, axis, up)
        after = lax.ppermute(leading, axis, down)
        x = jnp.concatenate([before, x, after], axis=dim)
    return x


def from_partner(value, axis, distance):
    mask = 2**distance
    pairs = [(source, source ^ mask) for source in range(lax.axis_size(axis))]
    return lax.ppermute(value, axis, pairs)


def kernel_apply(target_points, source_points, source_values):
    inner = lax.dot_general(
        target_points, source_points, (((0,), (0,)), ((), ())), preferred_element_type=jnp.float32
    )
    target_float = target_points.astype(jnp.float32)
    source_float = source_points.astype(jnp.float32)
    target_norms = jnp.sum(target_float * target_float, axis=0)
    source_norms = jnp.sum(source_float * source_float, axis=0)
    distance = target_norms[:, None] + source_norms[None, :] - 2.0 * inner
    weights = (AMPLITUDE * jnp.exp(-DISTANCE_SCALE * distance)).astype(jnp.bfloat16)
    return lax.dot_general(
        source_values, weights, (((1,), (1,)), ((), ())), preferred_element_type=jnp.float32
    )


def on_device(embeddings, directions, level_basis, neighbours, counts):
    values = directions.astype(jnp.bfloat16)
    local_points = embeddings.shape[1]
    local_leaves = local_points // LEAF
    first_leaf = lax.axis_index(("leaf", "sub")) * local_leaves
    outer_points, outer_values = (
        padded(embeddings, ((("leaf", "sub"), 1),), local_points),
        padded(values, ((("leaf", "sub"), 1),), local_points),
    )

    def fetch_leaf(position):
        start = position * LEAF
        return (
            lax.dynamic_slice_in_dim(outer_points, start, LEAF, 1),
            lax.dynamic_slice_in_dim(outer_values, start, LEAF, 1),
        )

    near_parts = []
    for leaf_local in range(local_leaves):
        own_points = embeddings[:, leaf_local * LEAF : (leaf_local + 1) * LEAF]
        own_values = values[:, leaf_local * LEAF : (leaf_local + 1) * LEAF]
        total = kernel_apply(own_points, own_points, own_values)

        def add_slot(slot_index, running, leaf_local=leaf_local, own_points=own_points):
            position = neighbours[leaf_local, slot_index] - first_leaf + local_leaves
            source_points, source_values = fetch_leaf(position)
            return running + kernel_apply(own_points, source_points, source_values)

        total = lax.fori_loop(0, counts[leaf_local], add_slot, total)
        near_parts.append(total)
    near = jnp.concatenate(near_parts, axis=1)
    rank = level_basis.shape[1]
    nrhs = directions.shape[0]
    dev_bits = lax.axis_size(("leaf", "sub")).bit_length() - 1
    loc_bits = level_basis.shape[0] - dev_bits
    width = LEAF * 2**0
    blocks = local_points // width
    basis_view = level_basis[0].reshape(rank, blocks, width)
    value_view = values.reshape(nrhs, blocks, width)
    coeffs = jnp.einsum("rqn,tqn->qrt", basis_view, value_view, preferred_element_type=jnp.float32)
    scaled = (coeffs * (1.0 / math.sqrt(rank * width))).astype(jnp.bfloat16)
    swapped = scaled.reshape(blocks // 2, 2, rank, nrhs)[:, ::-1].reshape(blocks, rank, nrhs)
    far = jnp.einsum(
        "qrt,rqn->tqn", swapped, basis_view, preferred_element_type=jnp.float32
    ).reshape(nrhs, local_points)
    partials = [
        jnp.einsum(
            "rn,tn->rt",
            level_basis[loc_bits + bit_index],
            values,
            preferred_element_type=jnp.float32,
        )
        for bit_index in range(dev_bits)
    ]
    siblings = []
    for bit_index in range(dev_bits):
        running = partials[bit_index]
        for lower_bit in range(bit_index):
            running = running + from_partner(running, ("leaf", "sub"), lower_bit)
        siblings.append(from_partner(running, ("leaf", "sub"), bit_index))
    for bit_index in range(dev_bits):
        width = local_points * 2**bit_index
        scaled = (siblings[bit_index] * (1.0 / math.sqrt(rank * width))).astype(jnp.bfloat16)
        far = far + jnp.einsum(
            "rt,rn->tn",
            scaled,
            level_basis[loc_bits + bit_index],
            preferred_element_type=jnp.float32,
        )
    return RIDGE * directions + near + far


def solution(mesh):
    placed = (
        P(None, ("groups", "leaf", "sub")),
        P(None, ("groups", "leaf", "sub")),
        P(None, None, ("groups", "leaf", "sub")),
        P(("groups", "leaf", "sub"), None),
        P(("groups", "leaf", "sub")),
    )
    return jax.shard_map(
        on_device,
        mesh=mesh,
        in_specs=placed,
        out_specs=P(None, ("groups", "leaf", "sub")),
        check_vma=False,
    )
```

profile of v0, /device:TPU:29, one launch (start us, length us, event | category | flops | bytes accessed | tf_op | source)
XLA Modules:
  0.0 79.0 jit_solution(13396373009529567191)
XLA Ops:
  0.0 0.9 %convert_element_type.52 = bf16[32,1024]{1,0:T(8,128)(2,1)S(1)} convert(f32[32,1024]{1,0:T(8,128)} %param.10) | non-fusion elementwise | flops 32768 | bytes 196608 | tf_op jit(solution)/shard_map/convert_element_type | solution.py:51
  0.9 3.3 %collective-permute-start = (bf16[32,1024]{1,0:T(8,128)(2,1)S(1)}, bf16[32,1024]{1,0:T(8,128)(2,1)S(1)}, u32[]{:S(2)}, u32[]{:S(2)}) collective-permute-start(bf16[32,1024]{1,0:T(8,128)(2,1)S(1)} %convert_element_type.52), channel_id=1, source_target_pairs={{0,1},{1,2},{2,3},{3,4},{4,5},{5,6},{6,7},{7,8},{8,9},{9,10},{10,1... | collective-permute-start | bytes 196616 | tf_op jit(solution)/shard_map/ppermute | solution.py:23
  4.3 1.9 %collective-permute-start.1 = (bf16[32,1024]{1,0:T(8,128)(2,1)S(1)}, bf16[32,1024]{1,0:T(8,128)(2,1)S(1)}, u32[]{:S(2)}, u32[]{:S(2)}) collective-permute-start(bf16[32,1024]{1,0:T(8,128)(2,1)S(1)} %convert_element_type.52), channel_id=1, source_target_pairs={{1,0},{2,1},{3,2},{4,3},{5,4},{6,5},{7,6},{8,7},{9,8},{10,9},{11,1... | collective-permute-start | bytes 196616 | tf_op jit(solution)/shard_map/ppermute | solution.py:24
  6.2 1.0 %fusion.77 = f32[64,32]{0,1:T(8,128)S(1)} fusion(bf16[32,1024]{1,0:T(8,128)(2,1)S(1)} %convert_element_type.52, bf16[5,64,1024]{2,1,0:T(8,128)(2,1)} %param.11), kind=kOutput, calls=%fused_computation.90 | convolution fusion | flops 4194304 | bytes 204800 | tf_op jit(solution)/shard_map/rn,tn->rt/dot_general | solution.py:96
  7.5 1.0 %fusion.81 = f32[64,32]{0,1:T(8,128)S(1)} fusion(bf16[32,1024]{1,0:T(8,128)(2,1)S(1)} %convert_element_type.52, bf16[5,64,1024]{2,1,0:T(8,128)(2,1)} %param.11), kind=kOutput, calls=%fused_computation.94 | convolution fusion | flops 4194304 | bytes 204800 | tf_op jit(solution)/shard_map/rn,tn->rt/dot_general | solution.py:96
  8.5 1.4 %collective-permute-start.7 = (f32[64,32]{0,1:T(8,128)S(1)}, f32[64,32]{0,1:T(8,128)S(1)}, u32[]{:S(2)}, u32[]{:S(2)}) collective-permute-start(f32[64,32]{0,1:T(8,128)S(1)} %fusion.81), channel_id=1, source_target_pairs={{0,1},{1,0},{2,3},{3,2},{4,5},{5,4},{6,7},{7,6},{8,9},{9,8},{10,11... | collective-permute-start | bytes 24584 | tf_op jit(solution)/shard_map/ppermute | solution.py:32
  9.9 1.0 %fusion.85 = f32[64,32]{0,1:T(8,128)S(1)} fusion(bf16[32,1024]{1,0:T(8,128)(2,1)S(1)} %convert_element_type.52, bf16[5,64,1024]{2,1,0:T(8,128)(2,1)} %param.11), kind=kOutput, calls=%fused_computation.98 | convolution fusion | flops 4194304 | bytes 204800 | tf_op jit(solution)/shard_map/rn,tn->rt/dot_general | solution.py:96
  12.0 0.6 fusion.60
  13.3 2.6 %collective-permute-start.11 = (f32[64,32]{0,1:T(8,128)S(1)}, f32[64,32]{0,1:T(8,128)S(1)}, u32[]{:S(2)}, u32[]{:S(2)}) collective-permute-start(f32[64,32]{0,1:T(8,128)S(1)} %add.137), channel_id=1, source_target_pairs={{0,2},{1,3},{2,0},{3,1},{4,6},{5,7},{6,4},{7,5},{8,10},{9,11},{10,... | collective-permute-start | bytes 24584 | tf_op jit(solution)/shard_map/ppermute | solution.py:32
  16.0 2.4 %collective-permute-start.6 = (f32[64,32]{0,1:T(8,128)S(1)}, f32[64,32]{0,1:T(8,128)S(1)}, u32[]{:S(2)}, u32[]{:S(2)}) collective-permute-start(f32[64,32]{0,1:T(8,128)S(1)} %add.132), channel_id=1, source_target_pairs={{0,2},{1,3},{2,0},{3,1},{4,6},{5,7},{6,4},{7,5},{8,10},{9,11},{10,... | collective-permute-start | bytes 24584 | tf_op jit(solution)/shard_map/ppermute | solution.py:32
  18.4 0.6 fusion.123
  19.1 6.5 %collective-permute-start.2 = (bf16[128,1024]{1,0:T(8,128)(2,1)S(1)}, bf16[128,1024]{1,0:T(8,128)(2,1)S(1)}, u32[]{:S(2)}, u32[]{:S(2)}) collective-permute-start(bf16[128,1024]{1,0:T(8,128)(2,1)S(1)} %copy-done), channel_id=1, source_target_pairs={{0,1},{1,2},{2,3},{3,4},{4,5},{5,6},{6,7},{7,8},{8,9},{9,10},{10,1... | collective-permute-start | bytes 786440 | tf_op jit(solution)/shard_map/ppermute | solution.py:23
  26.9 1.9 %collective-permute-start.3 = (bf16[128,1024]{1,0:T(8,128)(2,1)S(1)}, bf16[128,1024]{1,0:T(8,128)(2,1)S(1)}, u32[]{:S(2)}, u32[]{:S(2)}) collective-permute-start(bf16[128,1024]{1,0:T(8,128)(2,1)S(1)} %copy-done), channel_id=1, source_target_pairs={{1,0},{2,1},{3,2},{4,3},{5,4},{6,5},{7,6},{8,7},{9,8},{10,9},{11,1... | collective-permute-start | bytes 786440 | tf_op jit(solution)/shard_map/ppermute | solution.py:24
  28.8 1.0 %collective-permute-start.13 = (f32[64,32]{0,1:T(8,128)S(1)}, f32[64,32]{0,1:T(8,128)S(1)}, u32[]{:S(2)}, u32[]{:S(2)}) collective-permute-start(f32[64,32]{0,1:T(8,128)S(1)} %add.139), channel_id=1, source_target_pairs={{0,8},{1,9},{2,10},{3,11},{4,12},{5,13},{6,14},{7,15},{8,0},{9,1},... | collective-permute-start | bytes 24584 | tf_op jit(solution)/shard_map/ppermute | solution.py:32
  29.9 1.6 %collective-permute-done.13 = f32[64,32]{0,1:T(8,128)S(1)} collective-permute-done((f32[64,32]{0,1:T(8,128)S(1)}, f32[64,32]{0,1:T(8,128)S(1)}, u32[]{:S(2)}, u32[]{:S(2)}) %collective-permute-start.13) | collective-permute-done | bytes 8224 | tf_op jit(solution)/shard_map/ppermute | solution.py:32
  31.7 6.4 %collective-permute-done.3 = bf16[128,1024]{1,0:T(8,128)(2,1)S(1)} collective-permute-done((bf16[128,1024]{1,0:T(8,128)(2,1)S(1)}, bf16[128,1024]{1,0:T(8,128)(2,1)S(1)}, u32[]{:S(2)}, u32[]{:S(2)}) %collective-permute-start.3) | collective-permute-done | bytes 262176 | tf_op jit(solution)/shard_map/ppermute | solution.py:24
  38.2 0.7 copy-done.5
  38.8 21.0 %while.20 = (s32[]{:T(128)}, f32[32,512]{1,0:T(8,128)S(1)}, s32[]{:T(128)}, s32[2,8]{1,0:T(2,128)S(1)}, s32[]{:T(128)}, /*index=5*/bf16[32,3072]{1,0:T(8,128)(2,...) while((s32[]{:T(128)}, f32[32,512]{1,0:T(8,128)S(1)}, ...), condition=%wide.region_4.5_spmd, body=%wide.region_1.4_spmd.sunk | while | flops 85867528 | bytes 697597 | solution.py:78
  39.4 0.6 constant_dynamic-slice_fusion.4
  40.7 0.6 fusion.142
  42.0 0.6 constant_dynamic-slice_fusion.4
  43.3 0.6 fusion.142
  44.5 0.6 constant_dynamic-slice_fusion.4
  45.9 0.6 fusion.142
  47.1 0.6 constant_dynamic-slice_fusion.4
  48.4 0.6 fusion.142
  49.6 0.6 constant_dynamic-slice_fusion.4
  51.0 0.6 fusion.142
  52.2 0.6 constant_dynamic-slice_fusion.4
  53.5 0.6 fusion.142
  54.7 0.6 constant_dynamic-slice_fusion.4
  56.1 0.6 fusion.142
  57.3 0.6 constant_dynamic-slice_fusion.4
  58.6 0.6 fusion.142
  59.9 18.3 %while.21 = (s32[]{:T(128)}, f32[32,512]{1,0:T(8,128)S(1)}, s32[]{:T(128)}, s32[2,8]{1,0:T(2,128)S(1)}, s32[]{:T(128)}, /*index=5*/bf16[32,3072]{1,0:T(8,128)(2,...) while((s32[]{:T(128)}, f32[32,512]{1,0:T(8,128)S(1)}, ...), condition=%wide.region_9.10_spmd, body=%wide.region_6.9_spmd.sunk | while | flops 85867528 | bytes 697597 | solution.py:78
  60.5 0.6 constant_dynamic-slice_fusion.5
  61.8 0.6 fusion.146
  64.3 0.6 fusion.146
  65.6 0.6 constant_dynamic-slice_fusion.5
  66.8 0.6 fusion.146
  69.3 0.6 fusion.146
  70.6 0.6 constant_dynamic-slice_fusion.5
  71.8 0.6 fusion.146
  73.1 0.6 constant_dynamic-slice_fusion.5
  74.3 0.6 fusion.146
  75.6 0.6 constant_dynamic-slice_fusion.5
  76.9 0.6 fusion.146
  78.2 0.9 %fusion.59 = f32[32,1024]{1,0:T(8,128)} fusion(f32[32,1024]{1,0:T(8,128)S(1)} %fusion.75, f32[32,1024]{1,0:T(8,128)S(1)} %fusion.79, f32[32,1024]{1,0:T(8,128)S(1)} %fusion.83, f32[32,1024]{1,0:T(8,128)S(1)} %bitcast.87, f32[32,512]{1,0:T(8,128)S(1)} %get-tuple-element.92, f32[32,512]{1,0:T(8,128)S(1)} %get-tuple-element.91, f32[32,1024]{1,0:T(8,128)S(1)} %copy-done.3, ...), kind=kOutput, calls=%fused_computation.67 | convolution fusion | flops 4460544 | bytes 1081344 | tf_op jit(solution)/shard_map/rt,rn->tn/dot_general | solution.py:113
  (70 shorter events, 6.0 us)
Async XLA Ops:
  0.9 30.7 %collective-permute-start = (bf16[32,1024]{1,0:T(8,128)(2,1)S(1)}, bf16[32,1024]{1,0:T(8,128)(2,1)S(1)}, u32[]{:S(2)}, u32[]{:S(2)}) collective-permute-start(bf16[32,1024]{1,0:T(8,128)(2,1)S(1)} %convert_element_type.52), channel_id=1, source_target_pairs={{0,1},{1,2},{2,3},{3,4},{4,5},{5,6},{6,7},{7,8},{8,9},{9,10},{10,1... | collective-permute-start | bytes 196616 | tf_op jit(solution)/shard_map/ppermute | solution.py:23
  4.3 27.4 %collective-permute-start.1 = (bf16[32,1024]{1,0:T(8,128)(2,1)S(1)}, bf16[32,1024]{1,0:T(8,128)(2,1)S(1)}, u32[]{:S(2)}, u32[]{:S(2)}) collective-permute-start(bf16[32,1024]{1,0:T(8,128)(2,1)S(1)} %convert_element_type.52), channel_id=1, source_target_pairs={{1,0},{2,1},{3,2},{4,3},{5,4},{6,5},{7,6},{8,7},{9,8},{10,9},{11,1... | collective-permute-start | bytes 196616 | tf_op jit(solution)/shard_map/ppermute | solution.py:24
  7.3 3.9 %copy-start = (bf16[128,1024]{1,0:T(8,128)(2,1)S(1)}, bf16[128,1024]{1,0:T(8,128)(2,1)}, u32[]{:S(2)}) copy-start(bf16[128,1024]{1,0:T(8,128)(2,1)} %param.9) | copy-start | bytes 786436
  7.3 6.1 %collective-permute-start.10 = (f32[64,32]{0,1:T(8,128)S(1)}, f32[64,32]{0,1:T(8,128)S(1)}, u32[]{:S(2)}, u32[]{:S(2)}) collective-permute-start(f32[64,32]{0,1:T(8,128)S(1)} %fusion.77), channel_id=1, source_target_pairs={{0,1},{1,0},{2,3},{3,2},{4,5},{5,4},{6,7},{7,6},{8,9},{9,8},{10,11... | collective-permute-start | bytes 24584 | tf_op jit(solution)/shard_map/ppermute | solution.py:32
  8.5 2.7 %copy-start.1 = (bf16[5,64,1024]{2,1,0:T(8,128)(2,1)S(1)}, bf16[5,64,1024]{2,1,0:T(8,128)(2,1)}, u32[]{:S(2)}) copy-start(bf16[5,64,1024]{2,1,0:T(8,128)(2,1)} %param.11) | copy-start | bytes 1966084
  8.5 7.4 %collective-permute-start.7 = (f32[64,32]{0,1:T(8,128)S(1)}, f32[64,32]{0,1:T(8,128)S(1)}, u32[]{:S(2)}, u32[]{:S(2)}) collective-permute-start(f32[64,32]{0,1:T(8,128)S(1)} %fusion.81), channel_id=1, source_target_pairs={{0,1},{1,0},{2,3},{3,2},{4,5},{5,4},{6,7},{7,6},{8,9},{9,8},{10,11... | collective-permute-start | bytes 24584 | tf_op jit(solution)/shard_map/ppermute | solution.py:32
  10.9 5.1 %collective-permute-start.5 = (f32[64,32]{0,1:T(8,128)S(1)}, f32[64,32]{0,1:T(8,128)S(1)}, u32[]{:S(2)}, u32[]{:S(2)}) collective-permute-start(f32[64,32]{0,1:T(8,128)S(1)} %fusion.85), channel_id=1, source_target_pairs={{0,1},{1,0},{2,3},{3,2},{4,5},{5,4},{6,7},{7,6},{8,9},{9,8},{10,11... | collective-permute-start | bytes 24584 | tf_op jit(solution)/shard_map/ppermute | solution.py:32
  12.0 0.9 %slice-start = ((bf16[5,64,1024]{2,1,0:T(8,128)(2,1)}), bf16[1,64,1024]{2,1,0:T(8,128)(2,1)S(1)}, s32[]{:S(2)}) async-start(bf16[5,64,1024]{2,1,0:T(8,128)(2,1)} %param.11), calls=%async_computation | async-start | bytes 262144 | tf_op jit(solution)/shard_map/slice | solution.py:87
  12.9 13.4 %copy-start.2 = (bf16[5,64,1024]{2,1,0:T(8,128)(2,1)S(1)}, bf16[5,64,1024]{2,1,0:T(8,128)(2,1)}, u32[]{:S(2)}) copy-start(bf16[5,64,1024]{2,1,0:T(8,128)(2,1)} %param.11) | copy-start | bytes 1966084
  13.3 5.7 %collective-permute-start.11 = (f32[64,32]{0,1:T(8,128)S(1)}, f32[64,32]{0,1:T(8,128)S(1)}, u32[]{:S(2)}, u32[]{:S(2)}) collective-permute-start(f32[64,32]{0,1:T(8,128)S(1)} %add.137), channel_id=1, source_target_pairs={{0,2},{1,3},{2,0},{3,1},{4,6},{5,7},{6,4},{7,5},{8,10},{9,11},{10,... | collective-permute-start | bytes 24584 | tf_op jit(solution)/shard_map/ppermute | solution.py:32
  15.9 2.5 %copy-start.4 = (s32[2]{0:T(128)S(1)}, s32[2]{0:T(128)}, u32[]{:S(2)}) copy-start(s32[2]{0:T(128)} %param.13) | copy-start | bytes 28
  15.9 9.7 %collective-permute-start.8 = (f32[64,32]{0,1:T(8,128)S(1)}, f32[64,32]{0,1:T(8,128)S(1)}, u32[]{:S(2)}, u32[]{:S(2)}) collective-permute-start(f32[64,32]{0,1:T(8,128)S(1)} %add.134), channel_id=1, source_target_pairs={{0,2},{1,3},{2,0},{3,1},{4,6},{5,7},{6,4},{7,5},{8,10},{9,11},{10,... | collective-permute-start | bytes 24584 | tf_op jit(solution)/shard_map/ppermute | solution.py:32
  16.0 9.7 %collective-permute-start.6 = (f32[64,32]{0,1:T(8,128)S(1)}, f32[64,32]{0,1:T(8,128)S(1)}, u32[]{:S(2)}, u32[]{:S(2)}) collective-permute-start(f32[64,32]{0,1:T(8,128)S(1)} %add.132), channel_id=1, source_target_pairs={{0,2},{1,3},{2,0},{3,1},{4,6},{5,7},{6,4},{7,5},{8,10},{9,11},{10,... | collective-permute-start | bytes 24584 | tf_op jit(solution)/shard_map/ppermute | solution.py:32
  19.1 12.6 %collective-permute-start.2 = (bf16[128,1024]{1,0:T(8,128)(2,1)S(1)}, bf16[128,1024]{1,0:T(8,128)(2,1)S(1)}, u32[]{:S(2)}, u32[]{:S(2)}) collective-permute-start(bf16[128,1024]{1,0:T(8,128)(2,1)S(1)} %copy-done), channel_id=1, source_target_pairs={{0,1},{1,2},{2,3},{3,4},{4,5},{5,6},{6,7},{7,8},{8,9},{9,10},{10,1... | collective-permute-start | bytes 786440 | tf_op jit(solution)/shard_map/ppermute | solution.py:23
  25.6 1.2 %collective-permute-start.12 = (f32[64,32]{0,1:T(8,128)S(1)}, f32[64,32]{0,1:T(8,128)S(1)}, u32[]{:S(2)}, u32[]{:S(2)}) collective-permute-start(f32[64,32]{0,1:T(8,128)S(1)} %add.138), channel_id=1, source_target_pairs={{0,4},{1,5},{2,6},{3,7},{4,0},{5,1},{6,2},{7,3},{8,12},{9,13},{10,... | collective-permute-start | bytes 24584 | tf_op jit(solution)/shard_map/ppermute | solution.py:32
  25.7 3.1 %collective-permute-start.9 = (f32[64,32]{0,1:T(8,128)S(1)}, f32[64,32]{0,1:T(8,128)S(1)}, u32[]{:S(2)}, u32[]{:S(2)}) collective-permute-start(f32[64,32]{0,1:T(8,128)S(1)} %add.135), channel_id=1, source_target_pairs={{0,4},{1,5},{2,6},{3,7},{4,0},{5,1},{6,2},{7,3},{8,12},{9,13},{10,... | collective-permute-start | bytes 24584 | tf_op jit(solution)/shard_map/ppermute | solution.py:32
  26.9 11.2 %collective-permute-start.3 = (bf16[128,1024]{1,0:T(8,128)(2,1)S(1)}, bf16[128,1024]{1,0:T(8,128)(2,1)S(1)}, u32[]{:S(2)}, u32[]{:S(2)}) collective-permute-start(bf16[128,1024]{1,0:T(8,128)(2,1)S(1)} %copy-done), channel_id=1, source_target_pairs={{1,0},{2,1},{3,2},{4,3},{5,4},{6,5},{7,6},{8,7},{9,8},{10,9},{11,1... | collective-permute-start | bytes 786440 | tf_op jit(solution)/shard_map/ppermute | solution.py:24
  28.8 2.7 %collective-permute-start.13 = (f32[64,32]{0,1:T(8,128)S(1)}, f32[64,32]{0,1:T(8,128)S(1)}, u32[]{:S(2)}, u32[]{:S(2)}) collective-permute-start(f32[64,32]{0,1:T(8,128)S(1)} %add.139), channel_id=1, source_target_pairs={{0,8},{1,9},{2,10},{3,11},{4,12},{5,13},{6,14},{7,15},{8,0},{9,1},... | collective-permute-start | bytes 24584 | tf_op jit(solution)/shard_map/ppermute | solution.py:32
  31.5 46.6 %collective-permute-start.4 = (f32[64,32]{1,0:T(8,128)S(1)}, f32[64,32]{1,0:T(8,128)S(1)}, u32[]{:S(2)}, u32[]{:S(2)}) collective-permute-start(f32[64,32]{1,0:T(8,128)S(1)} %fusion.88), channel_id=1, source_target_pairs={{0,1},{1,0},{2,3},{3,2},{4,5},{5,4},{6,7},{7,6},{8,9},{9,8},{10,11... | collective-permute-start | bytes 24584 | tf_op jit(solution)/shard_map/ppermute | solution.py:32
  38.1 0.7 copy-start.5
  59.8 18.3 %copy-start.3 = (f32[32,1024]{1,0:T(8,128)S(1)}, f32[32,1024]{1,0:T(8,128)}, u32[]{:S(2)}) copy-start(f32[32,1024]{1,0:T(8,128)} %param.10) | copy-start | bytes 393220
where the time goes:
time: 79.2 us; the launch traced here: 79 us
  starting transfers between devices  22.1 us (28%)
  loops' own time  20.1 us (25%)
  matrix products  15.1 us (19%)
  local copies, waits for them, and re-layouts  10.9 us (14%)
  waiting for transfers between devices  8.43 us (11%)
  other arithmetic  2.11 us (3%)
    another operation x2, loops' own time, on_device(): total = lax.fori_loop(0, counts[leaf_local], add_slot, total)  20.1 us
    dot_general x17, matrix products, kernel_apply(): lax.dot_general(source_values, weights, (((1,), (1,)), ((), ())), preferr...  10.2 us
    ppermute x2, starting transfers between devices, padded(): before = lax.ppermute(last, axis, up)  9.87 us
    dynamic_slice x15, local copies, waits for them, and re-layouts, add_slot(): position = neighbours[leaf_local, slot_index] - first_leaf + local_leaves  9.07 us
    ppermute x10, starting transfers between devices, from_partner(): return lax.ppermute(value, axis, pairs)  8.38 us
    ppermute x2, waiting for transfers between devices, padded(): after = lax.ppermute(leading, axis, down)  6.38 us
    ppermute x2, starting transfers between devices, padded(): after = lax.ppermute(leading, axis, down)  3.85 us
    dot_general x4, matrix products, on_device(): jnp.einsum('rn,tn->rt', level_basis[loc_bits + bit_index], values, prefer...  3.3 us
  transfers between devices with their start and end apart: 14, of which 3 were waited for; matrix products, arithmetic and copies ran while one was open for 32% of the time, Pallas kernels for 0%

commit v1 on v0

v1 whole, which is shorter than its diff:
```python
import math

import jax
import jax.numpy as jnp
from jax import lax
from jax.sharding import PartitionSpec as P

LEAF = 512


AMPLITUDE = 0.5
DISTANCE_SCALE = 0.125
RIDGE = 0.5


def shifted(x, axis, step):
    count = lax.axis_size(axis)
    if step > 0:
        pairs = [(i, i + step) for i in range(count - step)]
    else:
        pairs = [(i - step, i) for i in range(count + step)]
    return lax.ppermute(x, axis, pairs)


def from_mask(x, axis, mask):
    pairs = [(i, i ^ mask) for i in range(lax.axis_size(axis))]
    return lax.ppermute(x, axis, pairs)


def kernel_block(target_points, source_points):
    inner = lax.dot_general(
        target_points, source_points, (((0,), (0,)), ((), ())), preferred_element_type=jnp.float32
    )
    target_float = target_points.astype(jnp.float32)
    source_float = source_points.astype(jnp.float32)
    target_norms = jnp.sum(target_float * target_float, axis=0)
    source_norms = jnp.sum(source_float * source_float, axis=0)
    distance = target_norms[:, None] + source_norms[None, :] - 2.0 * inner
    return (AMPLITUDE * jnp.exp(-DISTANCE_SCALE * distance)).astype(jnp.bfloat16)


def apply_rows(weights, source_values):
    return lax.dot_general(
        source_values, weights, (((1,), (1,)), ((), ())), preferred_element_type=jnp.float32
    )


def apply_cols(weights, source_values):
    return lax.dot_general(
        source_values, weights, (((1,), (0,)), ((), ())), preferred_element_type=jnp.float32
    )


def on_device(embeddings, directions, level_basis, neighbours, counts):
    axes = ("leaf", "sub")
    values = directions.astype(jnp.bfloat16)
    width_e = embeddings.shape[0]
    local_points = embeddings.shape[1]
    local_leaves = local_points // LEAF
    me = lax.axis_index(axes)

    packed = jnp.concatenate([embeddings, values], axis=0)
    from_left = shifted(packed[:, local_points - LEAF :], axes, 1)
    from_right = shifted(packed[:, :LEAF], axes, -1)

    slots = neighbours.shape[1]
    live = jnp.arange(slots, dtype=jnp.int32)[None, :] < counts[:, None]
    leaf_ids = me * local_leaves + jnp.arange(local_leaves, dtype=jnp.int32)
    below = jnp.sum((live & (neighbours == (leaf_ids - 1)[:, None])).astype(jnp.float32), axis=1)
    above = jnp.sum((live & (neighbours == (leaf_ids + 1)[:, None])).astype(jnp.float32), axis=1)

    points = [embeddings[:, j * LEAF : (j + 1) * LEAF] for j in range(local_leaves)]
    leaf_values = [values[:, j * LEAF : (j + 1) * LEAF] for j in range(local_leaves)]
    near = [apply_rows(kernel_block(points[j], points[j]), leaf_values[j]) for j in range(local_leaves)]
    for j in range(local_leaves - 1):
        pair = kernel_block(points[j], points[j + 1])
        near[j] = near[j] + above[j] * apply_rows(pair, leaf_values[j + 1])
        near[j + 1] = near[j + 1] + below[j + 1] * apply_cols(pair, leaf_values[j])
    lower = kernel_block(points[0], from_left[:width_e])
    near[0] = near[0] + below[0] * apply_rows(lower, from_left[width_e:])
    last = local_leaves - 1
    upper = kernel_block(points[last], from_right[:width_e])
    near[last] = near[last] + above[last] * apply_rows(upper, from_right[width_e:])
    near = jnp.concatenate(near, axis=1)

    rank = level_basis.shape[1]
    nrhs = directions.shape[0]
    sub_size = lax.axis_size("sub")
    leaf_size = lax.axis_size("leaf")
    sub_bits = sub_size.bit_length() - 1
    leaf_bits = leaf_size.bit_length() - 1
    dev_bits = sub_bits + leaf_bits
    loc_bits = level_basis.shape[0] - dev_bits

    width = LEAF
    blocks = local_points // width
    basis_view = level_basis[0].reshape(rank, blocks, width)
    value_view = values.reshape(nrhs, blocks, width)
    coeffs = jnp.einsum("rqn,tqn->qrt", basis_view, value_view, preferred_element_type=jnp.float32)
    scaled = (coeffs * (1.0 / math.sqrt(rank * width))).astype(jnp.bfloat16)
    swapped = scaled.reshape(blocks // 2, 2, rank, nrhs)[:, ::-1].reshape(blocks, rank, nrhs)
    far = jnp.einsum(
        "qrt,rqn->tqn", swapped, basis_view, preferred_element_type=jnp.float32
    ).reshape(nrhs, local_points)

    upper_basis = level_basis[loc_bits:]
    partials = jnp.einsum("krn,tn->krt", upper_basis, values, preferred_element_type=jnp.float32)

    sibling = [None] * dev_bits
    line = partials[sub_bits:]
    for mask in range(1, sub_size):
        level = mask.bit_length() - 1
        got = from_mask(jnp.concatenate([partials[level : level + 1], partials[sub_bits:]], axis=0), "sub", mask)
        sibling[level] = got[0] if sibling[level] is None else sibling[level] + got[0]
        line = line + got[1:]
    for mask in range(1, leaf_size):
        level = mask.bit_length() - 1
        got = from_mask(line[level], "leaf", mask)
        index = sub_bits + level
        sibling[index] = got if sibling[index] is None else sibling[index] + got

    factors = jnp.array(
        [1.0 / math.sqrt(rank * local_points * 2**bit) for bit in range(dev_bits)], jnp.float32
    )
    scaled_upper = (jnp.stack(sibling) * factors[:, None, None]).astype(jnp.bfloat16)
    far = far + jnp.einsum("krt,krn->tn", scaled_upper, upper_basis, preferred_element_type=jnp.float32)
    return RIDGE * directions + near + far


def solution(mesh):
    placed = (
        P(None, ("groups", "leaf", "sub")),
        P(None, ("groups", "leaf", "sub")),
        P(None, None, ("groups", "leaf", "sub")),
        P(("groups", "leaf", "sub"), None),
        P(("groups", "leaf", "sub")),
    )
    return jax.shard_map(
        on_device,
        mesh=mesh,
        in_specs=placed,
        out_specs=P(None, ("groups", "leaf", "sub")),
        check_vma=False,
    )
```

time: 79.2 us -> 42.1 us (0.53)
  the two profiles are of different devices: /device:TPU:29 before, /device:TPU:0 now
where the time goes in v1:
time: 42.1 us; the launch traced here: 41.5 us
  starting transfers between devices  14.6 us (35%)
  matrix products  11.3 us (27%)
  local copies, waits for them, and re-layouts  8.18 us (19%)
  other arithmetic  5.3 us (13%)
  waiting for transfers between devices  1.8 us (4%)
    ppermute x6, starting transfers between devices, from_mask(): return lax.ppermute(x, axis, pairs)  8.09 us
    ppermute x2, starting transfers between devices, shifted(): return lax.ppermute(x, axis, pairs)  6.5 us
    dot_general x5, matrix products, apply_rows(): lax.dot_general(source_values, weights, (((1,), (1,)), ((), ())), preferr...  5.9 us
    unnamed x26, local copies, waits for them, and re-layouts  2.77 us
    dot_general x2, matrix products, kernel_block(): lax.dot_general(target_points, source_points, (((0,), (0,)), ((), ())), p...  1.95 us
    ppermute x6, waiting for transfers between devices, from_mask(): return lax.ppermute(x, axis, pairs)  1.79 us
    add x2, local copies, waits for them, and re-layouts, kernel_block(): distance = target_norms[:, None] + source_norms[None, :] - 2.0 * inner  1.65 us
    dot_general x1, matrix products, on_device(): jnp.einsum('krn,tn->krt', upper_basis, values, preferred_element_type=jnp...  1.42 us
  transfers between devices with their start and end apart: 8, of which 2 were waited for; matrix products, arithmetic and copies ran while one was open for 42% of the time, Pallas kernels for 0%

profile of v1, /device:TPU:0, one launch (start us, length us, event | category | flops | bytes accessed | tf_op | source)
XLA Modules:
  0.0 41.5 jit_solution(9174138403219297233)
XLA Ops:
  0.0 0.9 %convert_element_type.50 = bf16[32,1024]{1,0:T(8,128)(2,1)S(1)} convert(f32[32,1024]{1,0:T(8,128)} %param.7) | non-fusion elementwise | flops 32768 | bytes 196608 | tf_op jit(solution)/shard_map/convert_element_type | solution.py:56
  0.9 1.4 %fusion.72 = f32[4,64,32]{1,2,0:T(8,128)S(1)} fusion(bf16[5,64,1024]{2,1,0:T(8,128)(2,1)} %param.8, bf16[32,1024]{1,0:T(8,128)(2,1)S(1)} %convert_element_type.50), kind=kOutput, calls=%fused_computation.91 | convolution fusion | flops 16777216 | bytes 753664 | tf_op jit(solution)/shard_map/krn,tn->krt/dot_general | solution.py:107
  2.3 0.6 %concatenate.17 = f32[3,64,32]{1,2,0:T(8,128)} slice(f32[4,64,32]{1,2,0:T(8,128)S(1)} %fusion.72), slice={[1:4], [0:64], [0:32]} | slice | bytes 49152 | tf_op jit(solution)/shard_map/concatenate | solution.py:113
  3.0 5.0 %collective-permute-start.4 = (f32[3,64,32]{1,2,0:T(8,128)}, f32[3,64,32]{1,2,0:T(8,128)}, u32[]{:S(2)}, u32[]{:S(2)}) collective-permute-start(f32[3,64,32]{1,2,0:T(8,128)} %concatenate.17), channel_id=1, source_target_pairs={{0,3},{1,2},{2,1},{3,0},{4,7},{5,6},{6,5},{7,4},{8,11},{9,10},{10,... | collective-permute-start | bytes 73736 | tf_op jit(solution)/shard_map/ppermute | solution.py:27
  8.0 0.8 %fusion.54 = (bf16[160,512]{1,0:T(8,128)(2,1)}, bf16[160,512]{1,0:T(8,128)(2,1)}) fusion(bf16[128,1024]{1,0:T(8,128)(2,1)S(1)} %copy-done, bf16[32,1024]{1,0:T(8,128)(2,1)S(1)} %convert_element_type.50), kind=kLoop, calls=%fused_computation.74 | loop fusion | flops 655360 | bytes 655360 | tf_op jit(solution)/shard_map/concatenate | solution.py:62
  8.8 1.3 %collective-permute-start.1 = (bf16[160,512]{1,0:T(8,128)(2,1)}, bf16[160,512]{1,0:T(8,128)(2,1)S(1)}, u32[]{:S(2)}, u32[]{:S(2)}) collective-permute-start(bf16[160,512]{1,0:T(8,128)(2,1)} %get-tuple-element.10), channel_id=1, source_target_pairs={{1,0},{2,1},{3,2},{4,3},{5,4},{6,5},{7,6},{8,7},{9,8},{10,9},{11,1... | collective-permute-start | bytes 491528 | tf_op jit(solution)/shard_map/ppermute | solution.py:22
  10.1 5.2 %collective-permute-start = (bf16[160,512]{1,0:T(8,128)(2,1)}, bf16[160,512]{1,0:T(8,128)(2,1)}, u32[]{:S(2)}, u32[]{:S(2)}) collective-permute-start(bf16[160,512]{1,0:T(8,128)(2,1)} %get-tuple-element.9), channel_id=1, source_target_pairs={{0,1},{1,2},{2,3},{3,4},{4,5},{5,6},{6,7},{7,8},{8,9},{9,10},{10,1... | collective-permute-start | bytes 491528 | tf_op jit(solution)/shard_map/ppermute | solution.py:22
  15.3 0.6 %pad_maximum_fusion.1 = f32[3,64,32]{1,2,0:T(8,128)} fusion(f32[2,64,32]{1,2,0:T(8,128)S(1)} %slice.120, f32[1,64,32]{1,2,0:T(8,128)S(1)} %slice.119), kind=kLoop, calls=%fused_computation.93 | loop fusion | flops 6144 | bytes 49152 | tf_op jit(solution)/shard_map/concatenate | solution.py:113
  15.9 0.8 %collective-permute-start.2 = (f32[3,64,32]{1,2,0:T(8,128)}, f32[3,64,32]{1,2,0:T(8,128)S(1)}, u32[]{:S(2)}, u32[]{:S(2)}) collective-permute-start(f32[3,64,32]{1,2,0:T(8,128)} %pad_maximum_fusion.1), channel_id=1, source_target_pairs={{0,1},{1,0},{2,3},{3,2},{4,5},{5,4},{6,7},{7,6},{8,9},{9,8},{10,11... | collective-permute-start | bytes 73736 | tf_op jit(solution)/shard_map/ppermute | solution.py:27
  16.8 0.1 multiply_reduce_fusion.3
  16.8 0.8 %slice-done = bf16[1,64,1024]{2,1,0:T(8,128)(2,1)S(1)} async-done(((bf16[5,64,1024]{2,1,0:T(8,128)(2,1)}), bf16[1,64,1024]{2,1,0:T(8,128)(2,1)S(1)}, s32[]{:S(2)}) %slice-start) | async-done | bytes 131096 | tf_op jit(solution)/shard_map/slice | solution.py:97
  17.7 0.1 reshape_squeeze.3
  17.7 0.1 fusion.35
  17.9 0.6 %reshape.29 = bf16[2,64,32]{1,2,0:T(8,128)(2,1)} reverse(bf16[2,64,32]{1,2,0:T(8,128)(2,1)S(1)} %fusion.35), dimensions={0} | reverse | bytes 16384 | tf_op jit(solution)/shard_map/reshape | solution.py:101
  18.5 0.2 broadcast_add_fusion
  18.7 1.3 %copy.19 = f32[512,512]{1,0:T(8,128)} copy(f32[512,512]{0,1:T(8,128)S(1)} %get-tuple-element.14) | data formatting | bytes 2097152 | tf_op jit(solution)/shard_map/add | solution.py:38
  20.0 1.6 %fusion.21 = bf16[512,512]{1,0:T(8,128)(2,1)S(1)} fusion(f32[512,512]{1,0:T(8,128)} %copy.19, bf16[128,1024]{1,0:T(8,128)(2,1)S(1)} %copy-done), kind=kOutput, calls=%fused_computation.26 | convolution fusion | flops 68419584 | bytes 1835008 | tf_op jit(solution)/shard_map/dot_general | solution.py:31
  21.7 0.0 copy-start.9
  21.7 0.0 copy-start.11
  21.7 0.7 %copy-done.9 = s32[2,8]{1,0:T(2,128)S(1)} copy-done((s32[2,8]{1,0:T(2,128)S(1)}, s32[2,8]{1,0:T(2,128)}, u32[]{:S(2)}) %copy-start.9) | copy-done | bytes 88
  22.4 0.2 fusion.82
  22.6 0.6 %fusion.98 = (f32[1]{0:T(128)}, f32[1]{0:T(128)}) fusion(f32[2]{0:T(128)S(1)} %get-tuple-element.8), kind=kLoop, calls=%fused_computation.128 | loop fusion | bytes 16 | tf_op jit(solution)/shard_map/slice | solution.py:80
  23.2 0.3 copy.22
  23.5 0.7 %fusion.99 = (f32[1]{0:T(128)}, f32[1]{0:T(128)}) fusion(f32[2]{0:T(128)S(1)} %get-tuple-element.7), kind=kLoop, calls=%fused_computation.129 | loop fusion | bytes 16 | tf_op jit(solution)/shard_map/slice | solution.py:77
  24.2 0.8 %convolution_multiply_fusion.5 = f32[512,32]{0,1:T(8,128)S(1)} fusion(bf16[512,512]{1,0:T(8,128)(2,1)S(1)} %fusion.21, f32[]{:T(128)} %bitcast.4, bf16[32,1024]{1,0:T(8,128)(2,1)S(1)} %convert_element_type.50), kind=kOutput, calls=%fused_computation.40 | convolution fusion | flops 16793600 | bytes 622596 | tf_op jit(solution)/shard_map/dot_general | solution.py:49
  25.0 0.9 %convolution_multiply_fusion.7 = f32[512,32]{0,1:T(8,128)S(1)} fusion(bf16[512,512]{1,0:T(8,128)(2,1)S(1)} %fusion.21, f32[]{:T(128)} %bitcast, bf16[32,1024]{1,0:T(8,128)(2,1)S(1)} %convert_element_type.50), kind=kOutput, calls=%fused_computation.42 | convolution fusion | flops 16793600 | bytes 622596 | tf_op jit(solution)/shard_map/dot_general | solution.py:43
  25.9 0.0 copy-done.7
  25.9 1.2 %fusion.32 = f32[32,512]{1,0:T(8,128)} fusion(f32[512,32]{0,1:T(8,128)S(1)} %convolution_multiply_fusion.7, f32[512]{0:T(512)S(1)} %get-tuple-element.5, bf16[128,1024]{1,0:T(8,128)(2,1)S(1)} %copy-done, bf16[32,1024]{1,0:T(8,128)(2,1)S(1)} %convert_element_type.50), kind=kOutput, calls=%fused_computation.39 | convolution fusion | flops 85475328 | bytes 299008 | tf_op jit(solution)/shard_map/dot_general | solution.py:43
  27.1 0.5 %fusion.29 = f32[32,512]{1,0:T(8,128)S(1)} fusion(f32[512,32]{0,1:T(8,128)S(1)} %convolution_multiply_fusion.5, f32[512,512]{1,0:T(8,128)S(1)} %copy.22, bf16[128,1024]{1,0:T(8,128)(2,1)S(1)} %copy-done, bf16[32,1024]{1,0:T(8,128)(2,1)S(1)} %convert_element_type.50), kind=kOutput, calls=%fused_computation.36 | convolution fusion | flops 85213184 | bytes 1343488 | tf_op jit(solution)/shard_map/dot_general | solution.py:43
  27.7 0.2 copy-done.4
  27.8 0.1 convolution_bitcast_fusion.1
  28.0 0.0 collective-permute-done.4
  28.0 0.8 %slice_add_fusion = f32[2,64,32]{1,2,0:T(8,128)S(1)} fusion(f32[3,64,32]{1,2,0:T(8,128)} %collective-permute-done.4, f32[3,64,32]{1,2,0:T(8,128)} %collective-permute-done.3, f32[3,64,32]{1,2,0:T(8,128)S(1)} %collective-permute-done.2, f32[4,64,32]{1,2,0:T(8,128)S(1)} %fusion.72), kind=kLoop, calls=%fused_computation.94 | loop fusion | flops 12288 | bytes 81920 | tf_op jit(solution)/shard_map/add | solution.py:115
  28.9 1.6 %collective-permute-start.6 = (f32[64,32]{0,1:T(8,128)S(1)}, f32[64,32]{0,1:T(8,128)S(1)}, u32[]{:S(2)}, u32[]{:S(2)}) collective-permute-start(f32[64,32]{0,1:T(8,128)S(1)} %get-tuple-element.12), channel_id=1, source_target_pairs={{0,8},{4,12},{8,0},{12,4},{1,9},{5,13},{9,1},{13,5},{2,10},{6,14},... | collective-permute-start | bytes 24584 | tf_op jit(solution)/shard_map/ppermute | solution.py:27
  30.4 0.6 %collective-permute-start.5 = (f32[64,32]{0,1:T(8,128)S(1)}, f32[64,32]{0,1:T(8,128)S(1)}, u32[]{:S(2)}, u32[]{:S(2)}) collective-permute-start(f32[64,32]{0,1:T(8,128)S(1)} %get-tuple-element.11), channel_id=1, source_target_pairs={{0,4},{4,0},{8,12},{12,8},{1,5},{5,1},{9,13},{13,9},{2,6},{6,2},{1... | collective-permute-start | bytes 24584 | tf_op jit(solution)/shard_map/ppermute | solution.py:27
  31.1 0.7 %slice_add_fusion.3 = f32[1,64,32]{1,2,0:T(8,128)S(1)} fusion(f32[3,64,32]{1,2,0:T(8,128)} %collective-permute-done.4, f32[3,64,32]{1,2,0:T(8,128)} %collective-permute-done.3), kind=kLoop, calls=%fused_computation.106 | loop fusion | flops 2048 | bytes 24576 | tf_op jit(solution)/shard_map/add | solution.py:114
  31.8 0.9 %collective-permute-done.6 = f32[64,32]{0,1:T(8,128)S(1)} collective-permute-done((f32[64,32]{0,1:T(8,128)S(1)}, f32[64,32]{0,1:T(8,128)S(1)}, u32[]{:S(2)}, u32[]{:S(2)}) %collective-permute-start.6) | collective-permute-done | bytes 8224 | tf_op jit(solution)/shard_map/ppermute | solution.py:27
  32.7 0.9 %collective-permute-done.7 = f32[64,32]{0,1:T(8,128)S(1)} collective-permute-done((f32[64,32]{0,1:T(8,128)S(1)}, f32[64,32]{0,1:T(8,128)S(1)}, u32[]{:S(2)}, u32[]{:S(2)}) %collective-permute-start.7) | collective-permute-done | bytes 8224 | tf_op jit(solution)/shard_map/ppermute | solution.py:27
  33.7 0.6 %copy-done.6 = f32[512]{0:T(512)S(1)} copy-done((f32[512]{0:T(512)S(1)}, f32[512]{0:T(512)}, u32[]{:S(2)}) %copy-start.6) | copy-done | bytes 2072
  34.3 0.3 fusion.18
  34.6 0.3 copy.23
  34.9 1.0 %multiply_reduce_fusion.1 = f32[512]{0:T(512)S(1)} fusion(bf16[160,512]{1,0:T(8,128)(2,1)} %collective-permute-done), kind=kLoop, calls=%fused_computation.71 | loop fusion | flops 196096 | bytes 133120 | tf_op jit(solution)/shard_map/reduce_sum | solution.py:37
  35.9 1.0 %fusion.33 = f32[32,512]{1,0:T(8,128)S(1)} fusion(f32[32,512]{1,0:T(8,128)S(1)} %fusion.29, f32[512,512]{1,0:T(8,128)S(1)} %copy.23, bf16[160,512]{1,0:T(8,128)(2,1)S(1)} %collective-permute-done.1, f32[]{:T(128)} %bitcast.6), kind=kOutput, calls=%fused_computation.43 | convolution fusion | flops 17596416 | bytes 1212420 | tf_op jit(solution)/shard_map/dot_general | solution.py:43
  36.9 0.7 %copy-done.8 = f32[512]{0:T(512)S(1)} copy-done((f32[512]{0:T(512)S(1)}, f32[512]{0:T(512)}, u32[]{:S(2)}) %copy-start.8) | copy-done | bytes 2072
  37.6 2.2 %fusion.34 = f32[32,512]{1,0:T(8,128)S(1)} fusion(f32[32,512]{1,0:T(8,128)S(1)} %copy-done.12, f32[512]{0:T(512)S(1)} %multiply_reduce_fusion.1, f32[512]{0:T(512)S(1)} %copy-done.8, bf16[160,512]{1,0:T(8,128)(2,1)} %collective-permute-done, bf16[128,1024]{1,0:T(8,128)(2,1)S(1)} %copy-done, f32[]{:T(128)} %bitcast.2), kind=kOutput, calls=%fused_computation.44 | convolution fusion | flops 85491712 | bytes 430084 | tf_op jit(solution)/shard_map/dot_general | solution.py:43
  39.9 0.0 copy-start.10
  39.9 0.6 %copy-done.10 = f32[4]{0:T(128)S(1)} copy-done((f32[4]{0:T(128)S(1)}, f32[4]{0:T(128)}, u32[]{:S(2)}) %copy-start.10) | copy-done | bytes 40
  40.5 1.0 %fusion.27 = f32[32,1024]{1,0:T(8,128)} fusion(f32[32,1024]{1,0:T(8,128)S(1)} %bitcast.59, bf16[5,64,1024]{2,1,0:T(8,128)(2,1)S(1)} %copy-done.1, f32[32,512]{1,0:T(8,128)S(1)} %fusion.33, f32[32,512]{1,0:T(8,128)S(1)} %fusion.34, f32[32,1024]{1,0:T(8,128)S(1)} %copy-done.2, f32[1,64,32]{1,2,0:T(8,128)S(1)} %add_bitcast_fusion, ...), kind=kOutput, calls=%fused_computation.34 | convolution fusion | flops 16982016 | bytes 1114624 | tf_op jit(solution)/shard_map/krt,krn->tn/dot_general | solution.py:126
  (34 shorter events, 0.1 us)
Async XLA Ops:
  0.9 7.1 %copy-start = (bf16[128,1024]{1,0:T(8,128)(2,1)S(1)}, bf16[128,1024]{1,0:T(8,128)(2,1)}, u32[]{:S(2)}) copy-start(bf16[128,1024]{1,0:T(8,128)(2,1)} %param.6) | copy-start | bytes 786436
  3.0 25.0 %collective-permute-start.4 = (f32[3,64,32]{1,2,0:T(8,128)}, f32[3,64,32]{1,2,0:T(8,128)}, u32[]{:S(2)}, u32[]{:S(2)}) collective-permute-start(f32[3,64,32]{1,2,0:T(8,128)} %concatenate.17), channel_id=1, source_target_pairs={{0,3},{1,2},{2,1},{3,0},{4,7},{5,6},{6,5},{7,4},{8,11},{9,10},{10,... | collective-permute-start | bytes 73736 | tf_op jit(solution)/shard_map/ppermute | solution.py:27
  8.0 20.0 %collective-permute-start.3 = (f32[3,64,32]{1,2,0:T(8,128)}, f32[3,64,32]{1,2,0:T(8,128)}, u32[]{:S(2)}, u32[]{:S(2)}) collective-permute-start(f32[3,64,32]{1,2,0:T(8,128)} %concatenate.17), channel_id=1, source_target_pairs={{0,2},{1,3},{2,0},{3,1},{4,6},{5,7},{6,4},{7,5},{8,10},{9,11},{10,... | collective-permute-start | bytes 73736 | tf_op jit(solution)/shard_map/ppermute | solution.py:27
  8.8 24.8 %collective-permute-start.1 = (bf16[160,512]{1,0:T(8,128)(2,1)}, bf16[160,512]{1,0:T(8,128)(2,1)S(1)}, u32[]{:S(2)}, u32[]{:S(2)}) collective-permute-start(bf16[160,512]{1,0:T(8,128)(2,1)} %get-tuple-element.10), channel_id=1, source_target_pairs={{1,0},{2,1},{3,2},{4,3},{5,4},{6,5},{7,6},{8,7},{9,8},{10,9},{11,1... | collective-permute-start | bytes 491528 | tf_op jit(solution)/shard_map/ppermute | solution.py:22
  10.1 24.9 %collective-permute-start = (bf16[160,512]{1,0:T(8,128)(2,1)}, bf16[160,512]{1,0:T(8,128)(2,1)}, u32[]{:S(2)}, u32[]{:S(2)}) collective-permute-start(bf16[160,512]{1,0:T(8,128)(2,1)} %get-tuple-element.9), channel_id=1, source_target_pairs={{0,1},{1,2},{2,3},{3,4},{4,5},{5,6},{6,7},{7,8},{8,9},{9,10},{10,1... | collective-permute-start | bytes 491528 | tf_op jit(solution)/shard_map/ppermute | solution.py:22
  15.9 12.1 %collective-permute-start.2 = (f32[3,64,32]{1,2,0:T(8,128)}, f32[3,64,32]{1,2,0:T(8,128)S(1)}, u32[]{:S(2)}, u32[]{:S(2)}) collective-permute-start(f32[3,64,32]{1,2,0:T(8,128)} %pad_maximum_fusion.1), channel_id=1, source_target_pairs={{0,1},{1,0},{2,3},{3,2},{4,5},{5,4},{6,7},{7,6},{8,9},{9,8},{10,11... | collective-permute-start | bytes 73736 | tf_op jit(solution)/shard_map/ppermute | solution.py:27
  16.8 0.9 %slice-start = ((bf16[5,64,1024]{2,1,0:T(8,128)(2,1)}), bf16[1,64,1024]{2,1,0:T(8,128)(2,1)S(1)}, s32[]{:S(2)}) async-start(bf16[5,64,1024]{2,1,0:T(8,128)(2,1)} %param.8), calls=%async_computation | async-start | bytes 262144 | tf_op jit(solution)/shard_map/slice | solution.py:97
  16.8 1.7 %copy-start.5 = (f32[512]{0:T(512)}, f32[512]{0:T(512)S(1)}, u32[]{:S(2)}) copy-start(f32[512]{0:T(512)S(1)} %get-tuple-element.6) | copy-start | bytes 6148
  16.8 9.1 %copy-start.7 = (f32[512]{0:T(512)}, f32[512]{0:T(512)S(1)}, u32[]{:S(2)}) copy-start(f32[512]{0:T(512)S(1)} %get-tuple-element.5) | copy-start | bytes 6148
  21.7 0.7 %copy-start.9 = (s32[2,8]{1,0:T(2,128)S(1)}, s32[2,8]{1,0:T(2,128)}, u32[]{:S(2)}) copy-start(s32[2,8]{1,0:T(2,128)} %param.9) | copy-start | bytes 196
  21.7 0.7 %copy-start.11 = (s32[2]{0:T(128)S(1)}, s32[2]{0:T(128)}, u32[]{:S(2)}) copy-start(s32[2]{0:T(128)} %param.10) | copy-start | bytes 28
  27.1 0.7 %copy-start.4 = (bf16[2,64,32]{1,2,0:T(8,128)(2,1)S(1)}, bf16[2,64,32]{1,2,0:T(8,128)(2,1)}, u32[]{:S(2)}) copy-start(bf16[2,64,32]{1,2,0:T(8,128)(2,1)} %reshape.29) | copy-start | bytes 24580
  28.0 3.8 %copy-start.3 = (f32[3,64,32]{1,2,0:T(8,128)}, f32[3,64,32]{1,2,0:T(8,128)S(1)}, u32[]{:S(2)}) copy-start(f32[3,64,32]{1,2,0:T(8,128)S(1)} %collective-permute-done.2) | copy-start | bytes 73732
  28.9 3.8 %collective-permute-start.6 = (f32[64,32]{0,1:T(8,128)S(1)}, f32[64,32]{0,1:T(8,128)S(1)}, u32[]{:S(2)}, u32[]{:S(2)}) collective-permute-start(f32[64,32]{0,1:T(8,128)S(1)} %get-tuple-element.12), channel_id=1, source_target_pairs={{0,8},{4,12},{8,0},{12,4},{1,9},{5,13},{9,1},{13,5},{2,10},{6,14},... | collective-permute-start | bytes 24584 | tf_op jit(solution)/shard_map/ppermute | solution.py:27
  30.4 3.2 %collective-permute-start.7 = (f32[64,32]{0,1:T(8,128)S(1)}, f32[64,32]{0,1:T(8,128)S(1)}, u32[]{:S(2)}, u32[]{:S(2)}) collective-permute-start(f32[64,32]{0,1:T(8,128)S(1)} %get-tuple-element.12), channel_id=1, source_target_pairs={{0,12},{4,8},{8,4},{12,0},{1,13},{5,9},{9,5},{13,1},{2,14},{6,10},... | collective-permute-start | bytes 24584 | tf_op jit(solution)/shard_map/ppermute | solution.py:27
  30.4 9.4 %collective-permute-start.5 = (f32[64,32]{0,1:T(8,128)S(1)}, f32[64,32]{0,1:T(8,128)S(1)}, u32[]{:S(2)}, u32[]{:S(2)}) collective-permute-start(f32[64,32]{0,1:T(8,128)S(1)} %get-tuple-element.11), channel_id=1, source_target_pairs={{0,4},{4,0},{8,12},{12,8},{1,5},{5,1},{9,13},{13,9},{2,6},{6,2},{1... | collective-permute-start | bytes 24584 | tf_op jit(solution)/shard_map/ppermute | solution.py:27
  33.6 0.7 %copy-start.6 = (f32[512]{0:T(512)S(1)}, f32[512]{0:T(512)}, u32[]{:S(2)}) copy-start(f32[512]{0:T(512)} %copy-done.5) | copy-start | bytes 6148
  35.9 1.0 %copy-start.12 = (f32[32,512]{1,0:T(8,128)S(1)}, f32[32,512]{1,0:T(8,128)}, u32[]{:S(2)}) copy-start(f32[32,512]{1,0:T(8,128)} %fusion.32) | copy-start | bytes 196612
  36.9 0.7 %copy-start.8 = (f32[512]{0:T(512)S(1)}, f32[512]{0:T(512)}, u32[]{:S(2)}) copy-start(f32[512]{0:T(512)} %copy-done.7) | copy-start | bytes 6148
  37.6 2.3 %copy-start.1 = (bf16[5,64,1024]{2,1,0:T(8,128)(2,1)S(1)}, bf16[5,64,1024]{2,1,0:T(8,128)(2,1)}, u32[]{:S(2)}) copy-start(bf16[5,64,1024]{2,1,0:T(8,128)(2,1)} %param.8) | copy-start | bytes 1966084
  37.6 2.3 %copy-start.2 = (f32[32,1024]{1,0:T(8,128)S(1)}, f32[32,1024]{1,0:T(8,128)}, u32[]{:S(2)}) copy-start(f32[32,1024]{1,0:T(8,128)} %param.7) | copy-start | bytes 393220
  37.6 2.3 %slice-start.1 = ((f32[3,64,32]{1,2,0:T(8,128)}), f32[1,64,32]{1,2,0:T(8,128)S(1)}, s32[]{:S(2)}) async-start(f32[3,64,32]{1,2,0:T(8,128)} %copy-done.3), calls=%async_computation.1 | async-start | bytes 32768 | tf_op jit(solution)/shard_map/slice | solution.py:114
  39.9 0.7 %copy-start.10 = (f32[4]{0:T(128)S(1)}, f32[4]{0:T(128)}, u32[]{:S(2)}) copy-start(f32[4]{0:T(128)} %constant.28.clone) | copy-start | bytes 52

commit v2 on v1

--- a/solution.py
+++ b/solution.py
@@ -106,23 +106,18 @@
     upper_basis = level_basis[loc_bits:]
     partials = jnp.einsum("krn,tn->krt", upper_basis, values, preferred_element_type=jnp.float32)
 
-    sibling = [None] * dev_bits
-    line = partials[sub_bits:]
-    for mask in range(1, sub_size):
-        level = mask.bit_length() - 1
-        got = from_mask(jnp.concatenate([partials[level : level + 1], partials[sub_bits:]], axis=0), "sub", mask)
-        sibling[level] = got[0] if sibling[level] is None else sibling[level] + got[0]
-        line = line + got[1:]
-    for mask in range(1, leaf_size):
-        level = mask.bit_length() - 1
-        got = from_mask(line[level], "leaf", mask)
-        index = sub_bits + level
-        sibling[index] = got if sibling[index] is None else sibling[index] + got
+    ndev = lax.axis_size(axes)
+    others = jnp.arange(ndev, dtype=jnp.int32) ^ me
+    level_of = sum((others >= 2**bit).astype(jnp.int32) for bit in range(1, dev_bits))
+    outgoing = jnp.take(partials, level_of, axis=0)
+    incoming = lax.all_to_all(outgoing, axes, 0, 0, tiled=True)
+    picks = (level_of[None, :] == jnp.arange(dev_bits, dtype=jnp.int32)[:, None]) & (others > 0)[None, :]
+    sibling = jnp.sum(jnp.where(picks[:, :, None, None], incoming[None], 0.0), axis=1)
 
     factors = jnp.array(
         [1.0 / math.sqrt(rank * local_points * 2**bit) for bit in range(dev_bits)], jnp.float32
     )
-    scaled_upper = (jnp.stack(sibling) * factors[:, None, None]).astype(jnp.bfloat16)
+    scaled_upper = (sibling * factors[:, None, None]).astype(jnp.bfloat16)
     far = far + jnp.einsum("krt,krn->tn", scaled_upper, upper_basis, preferred_element_type=jnp.float32)
     return RIDGE * directions + near + far
 

time: 42.1 us -> 40.9 us (0.971)
  other arithmetic: 5.3 us -> 7.32 us
  waiting for transfers between devices: 1.8 us -> 0.01 us
  matrix products: 11.3 us -> 9.87 us
    ppermute x6 -> x0, starting transfers between devices: 8.09 us -> none  [from_mask(): return lax.ppermute(x, axis, pairs)]
    all_to_all x0 -> x1, starting transfers between devices: none -> 7.28 us  [on_device(): incoming = lax.all_to_all(outgoing, axes, 0, 0, tiled=True)]
    all_to_all x0 -> x1, other arithmetic: none -> 1.86 us  [on_device(): incoming = lax.all_to_all(outgoing, axes, 0, 0, tiled=True)]
    ppermute x6 -> x0, waiting for transfers between devices: 1.79 us -> none  [from_mask(): return lax.ppermute(x, axis, pairs)]
    add x2 -> x1, other arithmetic: 1.54 us -> 0.01 us  [on_device(): sum(((others >= 2 ** bit).astype(jnp.int32) for bit in range(1, dev_bits)))]
    dot_general x1, matrix products: 1.42 us -> 0.34 us  [on_device(): jnp.einsum('krn,tn->krt', upper_basis, values, preferred_element_type=jnp...]
    concatenate x1, other arithmetic: 0.75 us -> 1.76 us  [on_device(): packed = jnp.concatenate([embeddings, values], axis=0)]
    ppermute x2, starting transfers between devices: 6.5 us -> 7.5 us  [shifted(): return lax.ppermute(x, axis, pairs)]
  transfers between devices with their start and end apart: 8 -> 3, of which waited for: 2 -> 0; matrix products, arithmetic and copies ran while one was open for 42% -> 40% of each run, Pallas kernels for 0% -> 0%
where the time goes in v2:
time: 40.9 us; the launch traced here: 40.3 us
  starting transfers between devices  14.8 us (36%)
  matrix products  9.87 us (24%)
  local copies, waits for them, and re-layouts  8.05 us (20%)
  other arithmetic  7.32 us (18%)
    ppermute x2, starting transfers between devices, shifted(): return lax.ppermute(x, axis, pairs)  7.5 us
    all_to_all x1, starting transfers between devices, on_device(): incoming = lax.all_to_all(outgoing, axes, 0, 0, tiled=True)  7.28 us
    dot_general x5, matrix products, apply_rows(): lax.dot_general(source_values, weights, (((1,), (1,)), ((), ())), preferr...  5.72 us
    unnamed x22, local copies, waits for them, and re-layouts  3.14 us
    reduce_sum x2, other arithmetic, kernel_block(): source_norms = jnp.sum(source_float * source_float, axis=0)  1.9 us
    all_to_all x1, other arithmetic, on_device(): incoming = lax.all_to_all(outgoing, axes, 0, 0, tiled=True)  1.86 us
    concatenate x1, other arithmetic, on_device(): packed = jnp.concatenate([embeddings, values], axis=0)  1.76 us
    dot_general x2, matrix products, kernel_block(): lax.dot_general(target_points, source_points, (((0,), (0,)), ((), ())), p...  1.69 us
  transfers between devices with their start and end apart: 3, of which 0 were waited for; matrix products, arithmetic and copies ran while one was open for 40% of the time, Pallas kernels for 0%

profile of v2, /device:TPU:0, one launch (start us, length us, event | category | flops | bytes accessed | tf_op | source)
XLA Modules:
  0.0 40.3 jit_solution(2009166385580942360)
XLA Ops:
  0.0 1.0 %convert_element_type.104 = bf16[32,1024]{1,0:T(8,128)(2,1)S(1)} convert(f32[32,1024]{1,0:T(8,128)} %param.7) | non-fusion elementwise | flops 32768 | bytes 196608 | tf_op jit(solution)/shard_map/convert_element_type | solution.py:56
  1.0 1.8 %fusion.51 = (bf16[160,512]{1,0:T(8,128)(2,1)}, bf16[160,512]{1,0:T(8,128)(2,1)}) fusion(bf16[128,1024]{1,0:T(8,128)(2,1)} %param.6, bf16[32,1024]{1,0:T(8,128)(2,1)S(1)} %convert_element_type.104), kind=kLoop, calls=%fused_computation.73 | loop fusion | flops 655360 | bytes 655360 | tf_op jit(solution)/shard_map/concatenate | solution.py:62
  2.7 1.3 %collective-permute-start.1 = (bf16[160,512]{1,0:T(8,128)(2,1)}, bf16[160,512]{1,0:T(8,128)(2,1)}, u32[]{:S(2)}, u32[]{:S(2)}) collective-permute-start(bf16[160,512]{1,0:T(8,128)(2,1)} %get-tuple-element.10), channel_id=1, source_target_pairs={{1,0},{2,1},{3,2},{4,3},{5,4},{6,5},{7,6},{8,7},{9,8},{10,9},{11,1... | collective-permute-start | bytes 491528 | tf_op jit(solution)/shard_map/ppermute | solution.py:22
  4.0 6.2 %collective-permute-start = (bf16[160,512]{1,0:T(8,128)(2,1)}, bf16[160,512]{1,0:T(8,128)(2,1)}, u32[]{:S(2)}, u32[]{:S(2)}) collective-permute-start(bf16[160,512]{1,0:T(8,128)(2,1)} %get-tuple-element.9), channel_id=1, source_target_pairs={{0,1},{1,2},{2,3},{3,4},{4,5},{5,6},{6,7},{7,8},{8,9},{9,10},{10,1... | collective-permute-start | bytes 491528 | tf_op jit(solution)/shard_map/ppermute | solution.py:22
  10.3 0.3 fusion.68
  10.7 0.6 %gather_fusion = f32[16,64,32]{1,2,0:T(8,128)S(1)} fusion(f32[4,64,32]{1,2,0:T(8,128)S(1)} %fusion.68, s32[1024]{0:T(1024)S(1)} %pad_clamp_fusion), kind=kCustom, calls=%fused_computation | custom fusion | bytes 262208 | tf_op jit(solution)/shard_map/jit(_take)/gather | solution.py:112
  11.2 0.1 fusion.101
  11.3 0.0 copy-start.2
  11.3 0.8 %reshape.134 = f32[16,1,2048]{2,1,0:T(1,128)} reshape(f32[16,32,64]{2,1,0:T(8,128)S(1)} %fusion.101) | data formatting | bytes 262144
  12.2 7.3 %all-to-all-start = ((f32[16,1,2048]{2,1,0:T(1,128)}), f32[16,1,2048]{2,1,0:T(1,128)}, u32[]{:S(2)}, u32[]{:S(2)}) async-start(f32[16,1,2048]{2,1,0:T(1,128)} %reshape.134), calls=%async_computation | async-start | bytes 262144 | tf_op jit(solution)/shard_map/all_to_all | solution.py:113
  19.5 0.1 multiply_reduce_fusion.3
  19.6 0.5 %fusion.21 = bf16[512,512]{0,1:T(8,128)(2,1)S(1)} fusion(f32[512]{0:T(512)S(1)} %get-tuple-element.6, f32[512]{0:T(512)S(1)} %get-tuple-element.5, bf16[128,1024]{1,0:T(8,128)(2,1)S(1)} %copy-done.2), kind=kOutput, calls=%fused_computation.27 | convolution fusion | flops 68681728 | bytes 790528 | tf_op jit(solution)/shard_map/dot_general | solution.py:31
  20.0 0.2 broadcast_add_fusion
  20.3 0.0 copy-start.7
  20.3 0.0 copy-start.9
  20.3 0.7 %copy-done.7 = s32[2,8]{1,0:T(2,128)S(1)} copy-done((s32[2,8]{1,0:T(2,128)S(1)}, s32[2,8]{1,0:T(2,128)}, u32[]{:S(2)}) %copy-start.7) | copy-done | bytes 88
  21.0 0.2 fusion.78
  21.1 0.6 %fusion.99 = (f32[1]{0:T(128)}, f32[1]{0:T(128)}) fusion(f32[2]{0:T(128)S(1)} %get-tuple-element.8), kind=kLoop, calls=%fused_computation.137 | loop fusion | bytes 16 | tf_op jit(solution)/shard_map/slice | solution.py:80
  21.7 1.3 %copy.47 = f32[512,512]{1,0:T(8,128)} copy(f32[512,512]{0,1:T(8,128)S(1)} %get-tuple-element.17) | data formatting | bytes 2097152 | tf_op jit(solution)/shard_map/add | solution.py:38
  23.1 0.6 %fusion.100 = (f32[1]{0:T(128)}, f32[1]{0:T(128)}) fusion(f32[2]{0:T(128)S(1)} %get-tuple-element.7), kind=kLoop, calls=%fused_computation.138 | loop fusion | bytes 16 | tf_op jit(solution)/shard_map/slice | solution.py:77
  23.7 0.9 %convolution_multiply_fusion.7 = f32[512,32]{0,1:T(8,128)S(1)} fusion(bf16[512,512]{0,1:T(8,128)(2,1)S(1)} %fusion.21, f32[]{:T(128)} %bitcast.4, bf16[32,1024]{1,0:T(8,128)(2,1)S(1)} %copy-done.4), kind=kOutput, calls=%fused_computation.43 | convolution fusion | flops 16793600 | bytes 622596 | tf_op jit(solution)/shard_map/dot_general | solution.py:49
  24.5 0.8 %convolution_multiply_fusion.5 = f32[512,32]{0,1:T(8,128)S(1)} fusion(bf16[512,512]{0,1:T(8,128)(2,1)S(1)} %fusion.21, f32[]{:T(128)} %bitcast, bf16[32,1024]{1,0:T(8,128)(2,1)S(1)} %copy-done.4), kind=kOutput, calls=%fused_computation.41 | convolution fusion | flops 16793600 | bytes 622596 | tf_op jit(solution)/shard_map/dot_general | solution.py:43
  25.4 0.3 copy.40
  25.7 0.6 %slice-done = bf16[1,64,1024]{2,1,0:T(8,128)(2,1)S(1)} async-done(((bf16[5,64,1024]{2,1,0:T(8,128)(2,1)}), bf16[1,64,1024]{2,1,0:T(8,128)(2,1)S(1)}, s32[]{:S(2)}) %slice-start) | async-done | bytes 131096 | tf_op jit(solution)/shard_map/slice | solution.py:97
  26.3 0.1 reshape_squeeze.3
  26.4 0.1 fusion.35
  26.5 0.2 convolution_bitcast_fusion.1
  26.7 0.8 %copy-done.5 = f32[512,512]{1,0:T(8,128)S(1)} copy-done((f32[512,512]{1,0:T(8,128)S(1)}, f32[512,512]{1,0:T(8,128)}, u32[]{:S(2)}) %copy-start.5) | copy-done | bytes 1048600
  27.5 0.5 %fusion.29 = f32[32,512]{1,0:T(8,128)S(1)} fusion(f32[512,32]{0,1:T(8,128)S(1)} %convolution_multiply_fusion.7, f32[512,512]{1,0:T(8,128)S(1)} %copy-done.5, bf16[128,1024]{1,0:T(8,128)(2,1)S(1)} %copy-done.2, bf16[32,1024]{1,0:T(8,128)(2,1)S(1)} %copy-done.4), kind=kOutput, calls=%fused_computation.37 | convolution fusion | flops 85213184 | bytes 1343488 | tf_op jit(solution)/shard_map/dot_general | solution.py:43
  28.0 0.6 %fusion.32 = f32[32,512]{1,0:T(8,128)S(1)} fusion(f32[512,32]{0,1:T(8,128)S(1)} %convolution_multiply_fusion.5, f32[512,512]{1,0:T(8,128)S(1)} %copy.40, bf16[128,1024]{1,0:T(8,128)(2,1)S(1)} %copy-done.2, bf16[32,1024]{1,0:T(8,128)(2,1)S(1)} %copy-done.4), kind=kOutput, calls=%fused_computation.40 | convolution fusion | flops 85213184 | bytes 1343488 | tf_op jit(solution)/shard_map/dot_general | solution.py:43
  28.7 0.0 collective-permute-done.1
  28.7 1.0 %multiply_reduce_fusion = f32[512]{0:T(512)S(1)} fusion(bf16[160,512]{1,0:T(8,128)(2,1)} %collective-permute-done.1), kind=kLoop, calls=%fused_computation.69 | loop fusion | flops 196096 | bytes 133120 | tf_op jit(solution)/shard_map/reduce_sum | solution.py:37
  29.6 1.2 %fusion.18 = f32[512,512]{0,1:T(8,128)S(1)} fusion(f32[512]{0:T(512)S(1)} %multiply_reduce_fusion, f32[512]{0:T(512)S(1)} %get-tuple-element.6, bf16[160,512]{1,0:T(8,128)(2,1)} %collective-permute-done.1, bf16[128,1024]{1,0:T(8,128)(2,1)S(1)} %copy-done.2), kind=kOutput, calls=%fused_computation.24 | convolution fusion | flops 67895296 | bytes 1314816 | tf_op jit(solution)/shard_map/dot_general | solution.py:31
  30.9 0.3 copy.48
  31.2 0.0 collective-permute-done
  31.2 1.0 %multiply_reduce_fusion.1 = f32[512]{0:T(512)S(1)} fusion(bf16[160,512]{1,0:T(8,128)(2,1)} %collective-permute-done), kind=kLoop, calls=%fused_computation.70 | loop fusion | flops 196096 | bytes 133120 | tf_op jit(solution)/shard_map/reduce_sum | solution.py:37
  32.2 2.2 %fusion.34 = f32[32,512]{1,0:T(8,128)S(1)} fusion(f32[32,512]{1,0:T(8,128)S(1)} %fusion.32, f32[512]{0:T(512)S(1)} %multiply_reduce_fusion.1, f32[512]{0:T(512)S(1)} %get-tuple-element.5, bf16[160,512]{1,0:T(8,128)(2,1)} %collective-permute-done, bf16[128,1024]{1,0:T(8,128)(2,1)S(1)} %copy-done.2, f32[]{:T(128)} %bitcast.2), kind=kOutput, calls=%fused_computation.45 | convolution fusion | flops 85491712 | bytes 430084 | tf_op jit(solution)/shard_map/dot_general | solution.py:43
  34.3 1.6 %fusion.33 = f32[32,512]{1,0:T(8,128)S(1)} fusion(f32[32,512]{1,0:T(8,128)S(1)} %fusion.29, f32[512,512]{1,0:T(8,128)S(1)} %copy.48, bf16[160,512]{1,0:T(8,128)(2,1)} %collective-permute-done.1, f32[]{:T(128)} %bitcast.6), kind=kOutput, calls=%fused_computation.44 | convolution fusion | flops 17596416 | bytes 1212928 | tf_op jit(solution)/shard_map/dot_general | solution.py:43
  35.9 0.0 copy-start.1
  35.9 0.0 all-to-all-done
  36.0 0.5 %broadcast.246 = f32[]{:T(128)} broadcast(f32[]{:T(128)} %constant.147), dimensions={} | broadcast | bytes 8 | tf_op jit(solution)/shard_map/all_to_all | solution.py:113
  36.5 1.9 %reduce = f32[16,2048]{1,0:T(8,128)S(1)} reduce(f32[16,1,2048]{2,1,0:T(1,128)} %all-to-all-done, f32[]{:T(128)} %broadcast.246), dimensions={1}, to_apply=%all_to_all.3.reduce_sub_computation | reduce | bytes 262148 | tf_op jit(solution)/shard_map/all_to_all | solution.py:113
  38.3 0.1 reshape.135
  38.4 0.0 copy-start.6
  38.5 0.2 select_reduce_fusion
  38.6 0.0 copy-start.8
  38.7 0.7 %copy-done.6 = f32[32,1024]{1,0:T(8,128)S(1)} copy-done((f32[32,1024]{1,0:T(8,128)S(1)}, f32[32,1024]{1,0:T(8,128)}, u32[]{:S(2)}) %copy-start.6) | copy-done | bytes 131096
  39.4 1.0 %fusion.27 = f32[32,1024]{1,0:T(8,128)} fusion(f32[32,1024]{1,0:T(8,128)S(1)} %bitcast.58, bf16[5,64,1024]{2,1,0:T(8,128)(2,1)S(1)} %copy-done.1, f32[32,512]{1,0:T(8,128)S(1)} %fusion.33, f32[32,512]{1,0:T(8,128)S(1)} %fusion.34, f32[32,1024]{1,0:T(8,128)S(1)} %copy-done.6, f32[4,64,32]{1,2,0:T(8,128)S(1)} %select_reduce_fusion, f32[4]{0:T(128)S(1)} %copy-done.8), kind=kOutput, calls=%fused_computation.35 | convolution fusion | flops 16957440 | bytes 1114624 | tf_op jit(solution)/shard_map/krt,krn->tn/dot_general | solution.py:121
  (21 shorter events, 0.1 us)
Async XLA Ops:
  0.0 10.3 %copy-start = (bf16[5,64,1024]{2,1,0:T(8,128)(2,1)S(1)}, bf16[5,64,1024]{2,1,0:T(8,128)(2,1)}, u32[]{:S(2)}) copy-start(bf16[5,64,1024]{2,1,0:T(8,128)(2,1)} %param.8) | copy-start | bytes 1966084
  1.0 9.3 %copy-start.3 = (bf16[32,1024]{1,0:T(8,128)(2,1)}, bf16[32,1024]{1,0:T(8,128)(2,1)S(1)}, u32[]{:S(2)}) copy-start(bf16[32,1024]{1,0:T(8,128)(2,1)S(1)} %convert_element_type.104) | copy-start | bytes 196612
  2.7 25.9 %collective-permute-start.1 = (bf16[160,512]{1,0:T(8,128)(2,1)}, bf16[160,512]{1,0:T(8,128)(2,1)}, u32[]{:S(2)}, u32[]{:S(2)}) collective-permute-start(bf16[160,512]{1,0:T(8,128)(2,1)} %get-tuple-element.10), channel_id=1, source_target_pairs={{1,0},{2,1},{3,2},{4,3},{5,4},{6,5},{7,6},{8,7},{9,8},{10,9},{11,1... | collective-permute-start | bytes 491528 | tf_op jit(solution)/shard_map/ppermute | solution.py:22
  4.0 27.2 %collective-permute-start = (bf16[160,512]{1,0:T(8,128)(2,1)}, bf16[160,512]{1,0:T(8,128)(2,1)}, u32[]{:S(2)}, u32[]{:S(2)}) collective-permute-start(bf16[160,512]{1,0:T(8,128)(2,1)} %get-tuple-element.9), channel_id=1, source_target_pairs={{0,1},{1,2},{2,3},{3,4},{4,5},{5,6},{6,7},{7,8},{8,9},{9,10},{10,1... | collective-permute-start | bytes 491528 | tf_op jit(solution)/shard_map/ppermute | solution.py:22
  11.3 8.1 %copy-start.2 = (bf16[128,1024]{1,0:T(8,128)(2,1)S(1)}, bf16[128,1024]{1,0:T(8,128)(2,1)}, u32[]{:S(2)}) copy-start(bf16[128,1024]{1,0:T(8,128)(2,1)} %param.6) | copy-start | bytes 786436
  12.2 23.8 %all-to-all-start = ((f32[16,1,2048]{2,1,0:T(1,128)}), f32[16,1,2048]{2,1,0:T(1,128)}, u32[]{:S(2)}, u32[]{:S(2)}) async-start(f32[16,1,2048]{2,1,0:T(1,128)} %reshape.134), calls=%async_computation | async-start | bytes 262144 | tf_op jit(solution)/shard_map/all_to_all | solution.py:113
  20.3 0.7 %copy-start.7 = (s32[2,8]{1,0:T(2,128)S(1)}, s32[2,8]{1,0:T(2,128)}, u32[]{:S(2)}) copy-start(s32[2,8]{1,0:T(2,128)} %param.9) | copy-start | bytes 196
  20.3 0.7 %copy-start.9 = (s32[2]{0:T(128)S(1)}, s32[2]{0:T(128)}, u32[]{:S(2)}) copy-start(s32[2]{0:T(128)} %param.10) | copy-start | bytes 28
  21.7 1.9 %copy-start.4 = (bf16[32,1024]{1,0:T(8,128)(2,1)S(1)}, bf16[32,1024]{1,0:T(8,128)(2,1)}, u32[]{:S(2)}) copy-start(bf16[32,1024]{1,0:T(8,128)(2,1)} %copy-done.3) | copy-start | bytes 196612
  25.4 0.9 %slice-start = ((bf16[5,64,1024]{2,1,0:T(8,128)(2,1)}), bf16[1,64,1024]{2,1,0:T(8,128)(2,1)S(1)}, s32[]{:S(2)}) async-start(bf16[5,64,1024]{2,1,0:T(8,128)(2,1)} %param.8), calls=%async_computation.1 | async-start | bytes 262144 | tf_op jit(solution)/shard_map/slice | solution.py:97
  26.3 1.2 %copy-start.5 = (f32[512,512]{1,0:T(8,128)S(1)}, f32[512,512]{1,0:T(8,128)}, u32[]{:S(2)}) copy-start(f32[512,512]{1,0:T(8,128)} %copy.47) | copy-start | bytes 3145732
  35.9 2.7 %copy-start.1 = (bf16[5,64,1024]{2,1,0:T(8,128)(2,1)S(1)}, bf16[5,64,1024]{2,1,0:T(8,128)(2,1)}, u32[]{:S(2)}) copy-start(bf16[5,64,1024]{2,1,0:T(8,128)(2,1)} %param.8) | copy-start | bytes 1966084
  38.4 0.9 %copy-start.6 = (f32[32,1024]{1,0:T(8,128)S(1)}, f32[32,1024]{1,0:T(8,128)}, u32[]{:S(2)}) copy-start(f32[32,1024]{1,0:T(8,128)} %param.7) | copy-start | bytes 393220
  38.6 0.7 %copy-start.8 = (f32[4]{0:T(128)S(1)}, f32[4]{0:T(128)}, u32[]{:S(2)}) copy-start(f32[4]{0:T(128)} %constant.48.clone) | copy-start | bytes 52

commit v3 on v2

v3 whole, which is shorter than its diff:
```python
import functools
import math

import jax
import jax.numpy as jnp
from jax import lax
from jax.experimental import pallas as pl
from jax.experimental.pallas import tpu as pltpu
from jax.sharding import PartitionSpec as P

LEAF = 512


AMPLITUDE = 0.5
DISTANCE_SCALE = 0.125
RIDGE = 0.5

VMEM = pl.BlockSpec(memory_space=pltpu.VMEM)
SMEM = pl.BlockSpec(memory_space=pltpu.SMEM)


def shifted(x, axis, step):
    count = lax.axis_size(axis)
    if step > 0:
        pairs = [(i, i + step) for i in range(count - step)]
    else:
        pairs = [(i - step, i) for i in range(count + step)]
    return lax.ppermute(x, axis, pairs)


def top_bit(x, dev_bits):
    level = jnp.int32(0)
    for bit in range(1, dev_bits):
        level = level + (x >= 2**bit).astype(jnp.int32)
    return level


def nt_dot(a, b):
    return lax.dot_general(a, b, (((1,), (1,)), ((), ())), preferred_element_type=jnp.float32)


def nn_dot(a, b):
    return lax.dot_general(a, b, (((1,), (0,)), ((), ())), preferred_element_type=jnp.float32)


def send_kernel(sub_size, dev_bits, ndev, emb_ref, dirs_ref, basis_ref, first_ref, last_ref, out_ref, part_ref):
    width_e = emb_ref.shape[0]
    local_points = emb_ref.shape[1]
    values = dirs_ref[...].astype(jnp.bfloat16)
    first_ref[:width_e, :] = emb_ref[:, :LEAF]
    first_ref[width_e:, :] = values[:, :LEAF]
    last_ref[:width_e, :] = emb_ref[:, local_points - LEAF :]
    last_ref[width_e:, :] = values[:, local_points - LEAF :]
    for level in range(dev_bits):
        part_ref[level] = nt_dot(values, basis_ref[level])
    me = lax.axis_index("leaf") * sub_size + lax.axis_index("sub")

    def one(target, carry):
        other = jnp.bitwise_xor(target, me)
        level = top_bit(jnp.maximum(other, 1), dev_bits)
        out_ref[target] = part_ref[level]
        return carry

    lax.fori_loop(0, ndev, one, 0)


def main_kernel(
    sub_size, dev_bits, ndev, loc_bits,
    emb_ref, dirs_ref, left_ref, right_ref, basis_ref, incoming_ref, neighbours_ref, counts_ref,
    out_ref, sibling_ref,
):
    width_e = emb_ref.shape[0]
    local_points = emb_ref.shape[1]
    local_leaves = local_points // LEAF
    rank = basis_ref.shape[1]
    slots = neighbours_ref.shape[1]
    me = lax.axis_index("leaf") * sub_size + lax.axis_index("sub")

    directions = dirs_ref[...]
    values = directions.astype(jnp.bfloat16)
    emb_float = emb_ref[...].astype(jnp.float32)
    row_norms = jnp.sum(emb_float * emb_float, axis=0, keepdims=True)
    emb_t = emb_float.T
    col_norms = jnp.sum(emb_t * emb_t, axis=1, keepdims=True)
    emb_t = emb_t.astype(jnp.bfloat16)

    def block(j, source_points, source_norms):
        inner = nn_dot(emb_t[j * LEAF : (j + 1) * LEAF], source_points)
        distance = col_norms[j * LEAF : (j + 1) * LEAF] + source_norms - 2.0 * inner
        return (AMPLITUDE * jnp.exp(-DISTANCE_SCALE * distance)).astype(jnp.bfloat16)

    def weight(j, offset):
        leaf = me * local_leaves + j
        total = jnp.int32(0)
        for slot in range(slots):
            hit = (slot < counts_ref[j]) & (neighbours_ref[j, slot] == leaf + offset)
            total = total + hit.astype(jnp.int32)
        return total.astype(jnp.float32)

    points = [emb_ref[:, j * LEAF : (j + 1) * LEAF] for j in range(local_leaves)]
    norms = [row_norms[:, j * LEAF : (j + 1) * LEAF] for j in range(local_leaves)]
    leaf_values = [values[:, j * LEAF : (j + 1) * LEAF] for j in range(local_leaves)]
    near = [nt_dot(leaf_values[j], block(j, points[j], norms[j])) for j in range(local_leaves)]
    for j in range(local_leaves - 1):
        pair = block(j, points[j + 1], norms[j + 1])
        near[j] = near[j] + weight(j, 1) * nt_dot(leaf_values[j + 1], pair)
        near[j + 1] = near[j + 1] + weight(j + 1, -1) * nn_dot(leaf_values[j], pair)
    for j, halo_ref, offset in ((0, left_ref, -1), (local_leaves - 1, right_ref, 1)):
        halo_points = halo_ref[:width_e, :]
        halo_float = halo_points.astype(jnp.float32)
        halo_norms = jnp.sum(halo_float * halo_float, axis=0, keepdims=True)
        lower = block(j, halo_points, halo_norms)
        near[j] = near[j] + weight(j, offset) * nt_dot(halo_ref[width_e:, :], lower)

    sibling_ref[...] = jnp.zeros_like(sibling_ref)

    def gather(source, carry):
        other = jnp.bitwise_xor(source, me)
        level = top_bit(jnp.maximum(other, 1), dev_bits)

        @pl.when(other > 0)
        def _():
            sibling_ref[level] = sibling_ref[level] + incoming_ref[source]

        return carry

    lax.fori_loop(0, ndev, gather, 0)

    far = jnp.zeros((values.shape[0], local_points), jnp.float32)
    for bit in range(dev_bits):
        factor = 1.0 / math.sqrt(rank * local_points * 2**bit)
        scaled = (sibling_ref[bit] * factor).astype(jnp.bfloat16)
        far = far + nn_dot(scaled, basis_ref[loc_bits + bit])

    basis0 = basis_ref[0]
    coeffs = [nt_dot(leaf_values[q], basis0[:, q * LEAF : (q + 1) * LEAF]) for q in range(local_leaves)]
    factor0 = 1.0 / math.sqrt(rank * LEAF)
    scaled0 = [(c * factor0).astype(jnp.bfloat16) for c in coeffs]
    for q in range(local_leaves):
        near[q] = near[q] + nn_dot(scaled0[q ^ 1], basis0[:, q * LEAF : (q + 1) * LEAF])
    for j in range(local_leaves):
        out_ref[:, j * LEAF : (j + 1) * LEAF] = (
            RIDGE * directions[:, j * LEAF : (j + 1) * LEAF] + near[j] + far[:, j * LEAF : (j + 1) * LEAF]
        )


def on_device(embeddings, directions, level_basis, neighbours, counts):
    axes = ("leaf", "sub")
    width_e = embeddings.shape[0]
    local_points = embeddings.shape[1]
    rank = level_basis.shape[1]
    nrhs = directions.shape[0]
    sub_size = lax.axis_size("sub")
    leaf_size = lax.axis_size("leaf")
    ndev = sub_size * leaf_size
    dev_bits = ndev.bit_length() - 1
    loc_bits = level_basis.shape[0] - dev_bits

    halo = jax.ShapeDtypeStruct((width_e + nrhs, LEAF), jnp.bfloat16)
    first, last, outgoing = pl.pallas_call(
        functools.partial(send_kernel, sub_size, dev_bits, ndev),
        out_shape=(halo, halo, jax.ShapeDtypeStruct((ndev, nrhs, rank), jnp.float32)),
        in_specs=[VMEM, VMEM, VMEM],
        out_specs=(VMEM, VMEM, VMEM),
        scratch_shapes=[pltpu.VMEM((dev_bits, nrhs, rank), jnp.float32)],
    )(embeddings, directions, level_basis[loc_bits:])

    from_left = shifted(last, axes, 1)
    from_right = shifted(first, axes, -1)
    incoming = lax.all_to_all(outgoing, axes, 0, 0, tiled=True)

    return pl.pallas_call(
        functools.partial(main_kernel, sub_size, dev_bits, ndev, loc_bits),
        out_shape=jax.ShapeDtypeStruct((nrhs, local_points), jnp.float32),
        in_specs=[VMEM, VMEM, VMEM, VMEM, VMEM, VMEM, SMEM, SMEM],
        out_specs=VMEM,
        scratch_shapes=[pltpu.VMEM((dev_bits, nrhs, rank), jnp.float32)],
    )(embeddings, directions, from_left, from_right, level_basis, incoming, neighbours, counts)


def solution(mesh):
    placed = (
        P(None, ("groups", "leaf", "sub")),
        P(None, ("groups", "leaf", "sub")),
        P(None, None, ("groups", "leaf", "sub")),
        P(("groups", "leaf", "sub"), None),
        P(("groups", "leaf", "sub")),
    )
    return jax.shard_map(
        on_device,
        mesh=mesh,
        in_specs=placed,
        out_specs=P(None, ("groups", "leaf", "sub")),
        check_vma=False,
    )
```

time: 40.9 us -> 33.7 us (0.82)
  matrix products: 9.87 us -> 0 us
  Pallas kernels: 0 us -> 7.19 us
  waiting for transfers between devices: 0.01 us -> 6.86 us
  other arithmetic: 7.32 us -> 0.95 us
  local copies, waits for them, and re-layouts: 8.05 us -> 5.68 us
  starting transfers between devices: 14.8 us -> 12.6 us
    dot_general x12 -> x0, matrix products: 9.87 us -> none  [the longest x5 5.72 us: apply_rows(): lax.dot_general(source_values, weights, (((1,), (1,)), ((), ())), preferr...]
    pallas_call x0 -> x2, Pallas kernels: none -> 7.19 us  [the longest x1 4.78 us: on_device(): pl.pallas_call(functools.partial(main_kernel, sub_size, dev_bits, ndev, l...]
    ppermute x2, waiting for transfers between devices: 0.01 us -> 4.67 us  [shifted(): return lax.ppermute(x, axis, pairs)]
    ppermute x2, starting transfers between devices: 7.5 us -> 5.13 us  [shifted(): return lax.ppermute(x, axis, pairs)]
    reduce_sum x5 -> x0, other arithmetic: 2.34 us -> none  [the longest x2 1.9 us: kernel_block(): source_norms = jnp.sum(source_float * source_float, axis=0)]
    all_to_all x1, waiting for transfers between devices: 0.01 us -> 2.19 us  [on_device(): incoming = lax.all_to_all(outgoing, axes, 0, 0, tiled=True)]
    concatenate x1 -> x0, other arithmetic: 1.76 us -> none  [on_device(): packed = jnp.concatenate([embeddings, values], axis=0)]
    add x2 -> x0, local copies, waits for them, and re-layouts: 1.66 us -> none  [kernel_block(): distance = target_norms[:, None] + source_norms[None, :] - 2.0 * inner]
  transfers between devices with their start and end apart: 3 -> 3, of which waited for: 0 -> 2; matrix products, arithmetic and copies ran while one was open for 40% -> 7% of each run, Pallas kernels for 0% -> 0%
where the time goes in v3:
time: 33.7 us; the launch traced here: 33.4 us
  starting transfers between devices  12.6 us (37%)
  Pallas kernels  7.19 us (21%)
  waiting for transfers between devices  6.86 us (20%)
  local copies, waits for them, and re-layouts  5.68 us (17%)
  other arithmetic  0.95 us (3%)
    all_to_all x1, starting transfers between devices, on_device(): incoming = lax.all_to_all(outgoing, axes, 0, 0, tiled=True)  7.49 us
    ppermute x2, starting transfers between devices, shifted(): return lax.ppermute(x, axis, pairs)  5.13 us
    pallas_call x1, Pallas kernels, on_device(): pl.pallas_call(functools.partial(main_kernel, sub_size, dev_bits, ndev, l...  4.78 us
    ppermute x2, waiting for transfers between devices, shifted(): return lax.ppermute(x, axis, pairs)  4.67 us
    unnamed x10, local copies, waits for them, and re-layouts  3.31 us
    pallas_call x1, Pallas kernels, on_device(): pl.pallas_call(functools.partial(send_kernel, sub_size, dev_bits, ndev),...  2.41 us
    all_to_all x1, waiting for transfers between devices, on_device(): incoming = lax.all_to_all(outgoing, axes, 0, 0, tiled=True)  2.19 us
    slice x1, local copies, waits for them, and re-layouts, on_device(): level_basis[loc_bits:]  1.87 us
  transfers between devices with their start and end apart: 3, of which 2 were waited for; matrix products, arithmetic and copies ran while one was open for 7% of the time, Pallas kernels for 0%

profile of v3, /device:TPU:0, one launch (start us, length us, event | category | flops | bytes accessed | tf_op | source)
XLA Modules:
  0.0 33.4 jit_solution(4085339034603616811)
XLA Ops:
  0.0 1.9 %slice.3.basis_ref = bf16[4,64,1024]{2,1,0:T(8,128)(2,1)} slice(bf16[5,64,1024]{2,1,0:T(8,128)(2,1)} %basis_ref.1), slice={[1:5], [0:64], [0:1024]} | slice | bytes 1048576 | tf_op jit(solution)/shard_map/slice | solution.py:166
  1.9 2.4 %shard_map.55 = (bf16[160,512]{1,0:T(8,128)(2,1)}, bf16[160,512]{1,0:T(8,128)(2,1)}, f32[16,32,64]{2,1,0:T(8,128)}) custom-call(bf16[128,1024]{1,0:T(8,128)(2,1)} %emb_ref.3, f32[32,1024]{1,0:T(8,128)} %dirs_ref.3, bf16[4,64,1024]{2,1,0:T(8,128)(2,1)} %slice.3.basis_ref), custom_call_target="tpu_custom_call" | custom-call | tf_op jit(solution)/shard_map/pallas_call | solution.py:160
  4.3 0.0 copy-start.3
  4.3 1.8 %reshape = f32[16,1,2048]{2,1,0:T(1,128)} reshape(f32[16,32,64]{2,1,0:T(8,128)} %get-tuple-element.10) | data formatting | bytes 262144
  6.1 0.0 copy-start.2
  6.1 7.5 %all-to-all-start = ((f32[16,1,2048]{2,1,0:T(1,128)}), f32[16,1,2048]{2,1,0:T(1,128)S(1)}, u32[]{:S(2)}, u32[]{:S(2)}) async-start(f32[16,1,2048]{2,1,0:T(1,128)} %reshape), calls=%async_computation | async-start | bytes 262144 | tf_op jit(solution)/shard_map/all_to_all | solution.py:170
  13.6 0.0 copy-done.3
  13.6 3.8 %collective-permute-start = (bf16[160,512]{1,0:T(8,128)(2,1)S(1)}, bf16[160,512]{1,0:T(8,128)(2,1)S(1)}, u32[]{:S(2)}, u32[]{:S(2)}) collective-permute-start(bf16[160,512]{1,0:T(8,128)(2,1)S(1)} %copy-done.3), channel_id=1, source_target_pairs={{0,1},{1,2},{2,3},{3,4},{4,5},{5,6},{6,7},{7,8},{8,9},{9,10},{10,1... | collective-permute-start | bytes 491528 | tf_op jit(solution)/shard_map/ppermute | solution.py:28
  17.5 0.0 copy-done.2
  17.5 1.3 %collective-permute-start.1 = (bf16[160,512]{1,0:T(8,128)(2,1)S(1)}, bf16[160,512]{1,0:T(8,128)(2,1)S(1)}, u32[]{:S(2)}, u32[]{:S(2)}) collective-permute-start(bf16[160,512]{1,0:T(8,128)(2,1)S(1)} %copy-done.2), channel_id=1, source_target_pairs={{1,0},{2,1},{3,2},{4,3},{5,4},{6,5},{7,6},{8,7},{9,8},{10,9},{11,1... | collective-permute-start | bytes 491528 | tf_op jit(solution)/shard_map/ppermute | solution.py:28
  18.8 2.2 %all-to-all-done = f32[16,1,2048]{2,1,0:T(1,128)S(1)} async-done(((f32[16,1,2048]{2,1,0:T(1,128)}), f32[16,1,2048]{2,1,0:T(1,128)S(1)}, u32[]{:S(2)}, u32[]{:S(2)}) %all-to-all-start) | async-done | bytes 131104 | tf_op jit(solution)/shard_map/all_to_all | solution.py:170
  21.0 0.5 %broadcast = f32[]{:T(128)} broadcast(f32[]{:T(128)} %constant.2), dimensions={} | broadcast | bytes 8 | tf_op jit(solution)/shard_map/all_to_all | solution.py:170
  21.5 0.9 %reduce = f32[16,2048]{1,0:T(8,128)S(1)} reduce(f32[16,1,2048]{2,1,0:T(1,128)S(1)} %all-to-all-done, f32[]{:T(128)} %broadcast), dimensions={1}, to_apply=%all_to_all.3.reduce_sub_computation | reduce | bytes 262148 | tf_op jit(solution)/shard_map/all_to_all | solution.py:170
  22.4 0.8 %reshape.1.incoming_ref = f32[16,32,64]{2,1,0:T(8,128)} reshape(f32[16,2048]{1,0:T(8,128)S(1)} %reduce) | data formatting | bytes 262144
  23.2 0.0 collective-permute-done.left_ref
  23.2 0.0 copy-start
  23.2 4.7 %collective-permute-done.1.right_ref = bf16[160,512]{1,0:T(8,128)(2,1)S(1)} collective-permute-done((bf16[160,512]{1,0:T(8,128)(2,1)S(1)}, bf16[160,512]{1,0:T(8,128)(2,1)S(1)}, u32[]{:S(2)}, u32[]{:S(2)}) %collective-permute-start.1) | collective-permute-done | bytes 163872 | tf_op jit(solution)/shard_map/ppermute | solution.py:28
  27.9 0.0 copy-done
  27.9 0.0 copy-start.1
  27.9 0.7 %copy-done.1 = bf16[160,512]{1,0:T(8,128)(2,1)} copy-done((bf16[160,512]{1,0:T(8,128)(2,1)}, bf16[160,512]{1,0:T(8,128)(2,1)S(1)}, u32[]{:S(2)}) %copy-start.1) | copy-done | bytes 163864
  28.6 4.8 %shard_map.56 = f32[32,1024]{1,0:T(8,128)} custom-call(bf16[128,1024]{1,0:T(8,128)(2,1)} %emb_ref.3, f32[32,1024]{1,0:T(8,128)} %dirs_ref.3, bf16[160,512]{1,0:T(8,128)(2,1)} %copy-done, bf16[160,512]{1,0:T(8,128)(2,1)} %copy-done.1, bf16[5,64,1024]{2,1,0:T(8,128)(2,1)} %basis_ref.1, f32[16,32,64]{2,1,0:T(8,128)} %reshape.1.incoming_ref, ...), custom_call_target="tpu_custom_call" | custom-call | tf_op jit(solution)/shard_map/pallas_call | solution.py:172
Async XLA Ops:
  4.3 9.3 %copy-start.3 = (bf16[160,512]{1,0:T(8,128)(2,1)S(1)}, bf16[160,512]{1,0:T(8,128)(2,1)}, u32[]{:S(2)}) copy-start(bf16[160,512]{1,0:T(8,128)(2,1)} %get-tuple-element.8) | copy-start | bytes 491524
  6.1 11.4 %copy-start.2 = (bf16[160,512]{1,0:T(8,128)(2,1)S(1)}, bf16[160,512]{1,0:T(8,128)(2,1)}, u32[]{:S(2)}) copy-start(bf16[160,512]{1,0:T(8,128)(2,1)} %get-tuple-element.9) | copy-start | bytes 491524
  6.1 14.8 %all-to-all-start = ((f32[16,1,2048]{2,1,0:T(1,128)}), f32[16,1,2048]{2,1,0:T(1,128)S(1)}, u32[]{:S(2)}, u32[]{:S(2)}) async-start(f32[16,1,2048]{2,1,0:T(1,128)} %reshape), calls=%async_computation | async-start | bytes 262144 | tf_op jit(solution)/shard_map/all_to_all | solution.py:170
  13.6 9.6 %collective-permute-start = (bf16[160,512]{1,0:T(8,128)(2,1)S(1)}, bf16[160,512]{1,0:T(8,128)(2,1)S(1)}, u32[]{:S(2)}, u32[]{:S(2)}) collective-permute-start(bf16[160,512]{1,0:T(8,128)(2,1)S(1)} %copy-done.3), channel_id=1, source_target_pairs={{0,1},{1,2},{2,3},{3,4},{4,5},{5,6},{6,7},{7,8},{8,9},{9,10},{10,1... | collective-permute-start | bytes 491528 | tf_op jit(solution)/shard_map/ppermute | solution.py:28
  17.5 10.4 %collective-permute-start.1 = (bf16[160,512]{1,0:T(8,128)(2,1)S(1)}, bf16[160,512]{1,0:T(8,128)(2,1)S(1)}, u32[]{:S(2)}, u32[]{:S(2)}) collective-permute-start(bf16[160,512]{1,0:T(8,128)(2,1)S(1)} %copy-done.2), channel_id=1, source_target_pairs={{1,0},{2,1},{3,2},{4,3},{5,4},{6,5},{7,6},{8,7},{9,8},{10,9},{11,1... | collective-permute-start | bytes 491528 | tf_op jit(solution)/shard_map/ppermute | solution.py:28
  23.2 4.7 %copy-start = (bf16[160,512]{1,0:T(8,128)(2,1)}, bf16[160,512]{1,0:T(8,128)(2,1)S(1)}, u32[]{:S(2)}) copy-start(bf16[160,512]{1,0:T(8,128)(2,1)S(1)} %collective-permute-done.left_ref) | copy-start | bytes 491524
  27.9 0.7 %copy-start.1 = (bf16[160,512]{1,0:T(8,128)(2,1)}, bf16[160,512]{1,0:T(8,128)(2,1)S(1)}, u32[]{:S(2)}) copy-start(bf16[160,512]{1,0:T(8,128)(2,1)S(1)} %collective-permute-done.1.right_ref) | copy-start | bytes 491524

commit v4 on v3

--- a/solution.py
+++ b/solution.py
@@ -43,7 +43,7 @@
     return lax.dot_general(a, b, (((1,), (0,)), ((), ())), preferred_element_type=jnp.float32)
 
 
-def send_kernel(sub_size, dev_bits, ndev, emb_ref, dirs_ref, basis_ref, first_ref, last_ref, out_ref, part_ref):
+def send_kernel(loc_bits, emb_ref, dirs_ref, basis_ref, first_ref, last_ref, part_ref):
     width_e = emb_ref.shape[0]
     local_points = emb_ref.shape[1]
     values = dirs_ref[...].astype(jnp.bfloat16)
@@ -51,17 +51,8 @@
     first_ref[width_e:, :] = values[:, :LEAF]
     last_ref[:width_e, :] = emb_ref[:, local_points - LEAF :]
     last_ref[width_e:, :] = values[:, local_points - LEAF :]
-    for level in range(dev_bits):
-        part_ref[level] = nt_dot(values, basis_ref[level])
-    me = lax.axis_index("leaf") * sub_size + lax.axis_index("sub")
-
-    def one(target, carry):
-        other = jnp.bitwise_xor(target, me)
-        level = top_bit(jnp.maximum(other, 1), dev_bits)
-        out_ref[target] = part_ref[level]
-        return carry
-
-    lax.fori_loop(0, ndev, one, 0)
+    for level in range(part_ref.shape[0]):
+        part_ref[level] = nt_dot(values, basis_ref[loc_bits + level])
 
 
 def main_kernel(
@@ -120,7 +111,7 @@
 
         @pl.when(other > 0)
         def _():
-            sibling_ref[level] = sibling_ref[level] + incoming_ref[source]
+            sibling_ref[level] = sibling_ref[level] + incoming_ref[source, level]
 
         return carry
 
@@ -157,17 +148,16 @@
     loc_bits = level_basis.shape[0] - dev_bits
 
     halo = jax.ShapeDtypeStruct((width_e + nrhs, LEAF), jnp.bfloat16)
-    first, last, outgoing = pl.pallas_call(
-        functools.partial(send_kernel, sub_size, dev_bits, ndev),
-        out_shape=(halo, halo, jax.ShapeDtypeStruct((ndev, nrhs, rank), jnp.float32)),
+    first, last, partials = pl.pallas_call(
+        functools.partial(send_kernel, loc_bits),
+        out_shape=(halo, halo, jax.ShapeDtypeStruct((dev_bits, nrhs, rank), jnp.float32)),
         in_specs=[VMEM, VMEM, VMEM],
         out_specs=(VMEM, VMEM, VMEM),
-        scratch_shapes=[pltpu.VMEM((dev_bits, nrhs, rank), jnp.float32)],
-    )(embeddings, directions, level_basis[loc_bits:])
+    )(embeddings, directions, level_basis)
 
     from_left = shifted(last, axes, 1)
     from_right = shifted(first, axes, -1)
-    incoming = lax.all_to_all(outgoing, axes, 0, 0, tiled=True)
+    incoming = lax.all_gather(partials, axes, axis=0, tiled=False)
 
     return pl.pallas_call(
         functools.partial(main_kernel, sub_size, dev_bits, ndev, loc_bits),

time: 33.7 us -> 61.9 us (1.84)
  blocking collectives: 0 us -> 47.5 us
  waiting for transfers between devices: 6.86 us -> 0.01 us
  starting transfers between devices: 12.6 us -> 6.22 us
  local copies, waits for them, and re-layouts: 5.68 us -> 0.73 us
  other arithmetic: 0.95 us -> 0 us
    all_gather x0 -> x1, blocking collectives: none -> 47.5 us  [on_device(): incoming = lax.all_gather(partials, axes, axis=0, tiled=False)]
    all_to_all x1 -> x0, starting transfers between devices: 7.49 us -> none  [on_device(): incoming = lax.all_to_all(outgoing, axes, 0, 0, tiled=True)]
    ppermute x2, waiting for transfers between devices: 4.67 us -> 0.01 us  [shifted(): return lax.ppermute(x, axis, pairs)]
    unnamed x10 -> x4, local copies, waits for them, and re-layouts: 3.31 us -> 0.73 us
    all_to_all x1 -> x0, waiting for transfers between devices: 2.19 us -> none  [on_device(): incoming = lax.all_to_all(outgoing, axes, 0, 0, tiled=True)]
    slice x1 -> x0, local copies, waits for them, and re-layouts: 1.87 us -> none  [on_device(): level_basis[loc_bits:]]
    ppermute x2, starting transfers between devices: 5.13 us -> 6.22 us  [shifted(): return lax.ppermute(x, axis, pairs)]
    all_to_all x1 -> x0, other arithmetic: 0.95 us -> none  [on_device(): incoming = lax.all_to_all(outgoing, axes, 0, 0, tiled=True)]
  transfers between devices with their start and end apart: 3 -> 2, of which waited for: 2 -> 0; matrix products, arithmetic and copies ran while one was open for 7% -> 0% of each run, Pallas kernels for 0% -> 0%
where the time goes in v4:
time: 61.9 us; the launch traced here: 61.7 us
  blocking collectives  47.5 us (77%)
  Pallas kernels  7.21 us (12%)
  starting transfers between devices  6.22 us (10%)
  local copies, waits for them, and re-layouts  0.73 us (1%)
    all_gather x1, blocking collectives, on_device(): incoming = lax.all_gather(partials, axes, axis=0, tiled=False)  47.5 us
    ppermute x2, starting transfers between devices, shifted(): return lax.ppermute(x, axis, pairs)  6.22 us
    pallas_call x1, Pallas kernels, on_device(): pl.pallas_call(functools.partial(main_kernel, sub_size, dev_bits, ndev, l...  5.08 us
    pallas_call x1, Pallas kernels, on_device(): pl.pallas_call(functools.partial(send_kernel, loc_bits), out_shape=(halo,...  2.14 us
  transfers between devices with their start and end apart: 2, of which 0 were waited for; matrix products, arithmetic and copies ran while one was open for 0% of the time, Pallas kernels for 0%

profile of v4, /device:TPU:0, one launch (start us, length us, event | category | flops | bytes accessed | tf_op | source)
XLA Modules:
  0.0 61.7 jit_solution(7949701378653870414)
XLA Ops:
  0.0 2.1 %shard_map.55 = (bf16[160,512]{1,0:T(8,128)(2,1)}, bf16[160,512]{1,0:T(8,128)(2,1)}, f32[4,32,64]{2,1,0:T(8,128)}) custom-call(bf16[128,1024]{1,0:T(8,128)(2,1)} %emb_ref.3, f32[32,1024]{1,0:T(8,128)} %dirs_ref.3, bf16[5,64,1024]{2,1,0:T(8,128)(2,1)} %basis_ref.3), custom_call_target="tpu_custom_call" | custom-call | tf_op jit(solution)/shard_map/pallas_call | solution.py:151
  2.1 4.9 %collective-permute-start = (bf16[160,512]{1,0:T(8,128)(2,1)}, bf16[160,512]{1,0:T(8,128)(2,1)S(1)}, u32[]{:S(2)}, u32[]{:S(2)}) collective-permute-start(bf16[160,512]{1,0:T(8,128)(2,1)} %get-tuple-element.8), channel_id=1, source_target_pairs={{0,1},{1,2},{2,3},{3,4},{4,5},{5,6},{6,7},{7,8},{8,9},{9,10},{10,1... | collective-permute-start | bytes 491528 | tf_op jit(solution)/shard_map/ppermute | solution.py:28
  7.1 1.3 %collective-permute-start.1 = (bf16[160,512]{1,0:T(8,128)(2,1)}, bf16[160,512]{1,0:T(8,128)(2,1)S(1)}, u32[]{:S(2)}, u32[]{:S(2)}) collective-permute-start(bf16[160,512]{1,0:T(8,128)(2,1)} %get-tuple-element.9), channel_id=1, source_target_pairs={{1,0},{2,1},{3,2},{4,3},{5,4},{6,5},{7,6},{8,7},{9,8},{10,9},{11,1... | collective-permute-start | bytes 491528 | tf_op jit(solution)/shard_map/ppermute | solution.py:28
  8.4 47.5 %all-gather = f32[64,32,64]{2,1,0:T(8,128)} all-gather(f32[4,32,64]{2,1,0:T(8,128)} %get-tuple-element.10), channel_id=2, replica_groups=mesh['groups'=2,'leaf'=4,'sub'=4] {'leaf','sub'}, dimensions={0}, use_global_device_ids=true | all-gather | bytes 557056 | tf_op jit(solution)/shard_map/all_gather | solution.py:160
  55.8 0.0 collective-permute-done.left_ref
  55.9 0.0 copy-start
  55.9 0.0 collective-permute-done.1.right_ref
  55.9 0.0 copy-start.1
  55.9 0.7 %copy-done = bf16[160,512]{1,0:T(8,128)(2,1)} copy-done((bf16[160,512]{1,0:T(8,128)(2,1)}, bf16[160,512]{1,0:T(8,128)(2,1)S(1)}, u32[]{:S(2)}) %copy-start) | copy-done | bytes 163864
  56.5 0.1 copy-done.1
  56.6 5.1 %shard_map.56 = f32[32,1024]{1,0:T(8,128)} custom-call(bf16[128,1024]{1,0:T(8,128)(2,1)} %emb_ref.3, f32[32,1024]{1,0:T(8,128)} %dirs_ref.3, bf16[160,512]{1,0:T(8,128)(2,1)} %copy-done, bf16[160,512]{1,0:T(8,128)(2,1)} %copy-done.1, bf16[5,64,1024]{2,1,0:T(8,128)(2,1)} %basis_ref.3, f32[16,4,32,64]{3,2,1,0:T(8,128)} %bitcast.1, s32[2,8]{1,0:T(2,128)} %neighbours_ref.1, ...), custom_call_target="tpu_custom_call" | custom-call | tf_op jit(solution)/shard_map/pallas_call | solution.py:162
Async XLA Ops:
  2.1 53.7 %collective-permute-start = (bf16[160,512]{1,0:T(8,128)(2,1)}, bf16[160,512]{1,0:T(8,128)(2,1)S(1)}, u32[]{:S(2)}, u32[]{:S(2)}) collective-permute-start(bf16[160,512]{1,0:T(8,128)(2,1)} %get-tuple-element.8), channel_id=1, source_target_pairs={{0,1},{1,2},{2,3},{3,4},{4,5},{5,6},{6,7},{7,8},{8,9},{9,10},{10,1... | collective-permute-start | bytes 491528 | tf_op jit(solution)/shard_map/ppermute | solution.py:28
  7.1 48.8 %collective-permute-start.1 = (bf16[160,512]{1,0:T(8,128)(2,1)}, bf16[160,512]{1,0:T(8,128)(2,1)S(1)}, u32[]{:S(2)}, u32[]{:S(2)}) collective-permute-start(bf16[160,512]{1,0:T(8,128)(2,1)} %get-tuple-element.9), channel_id=1, source_target_pairs={{1,0},{2,1},{3,2},{4,3},{5,4},{6,5},{7,6},{8,7},{9,8},{10,9},{11,1... | collective-permute-start | bytes 491528 | tf_op jit(solution)/shard_map/ppermute | solution.py:28
  55.9 0.7 %copy-start = (bf16[160,512]{1,0:T(8,128)(2,1)}, bf16[160,512]{1,0:T(8,128)(2,1)S(1)}, u32[]{:S(2)}) copy-start(bf16[160,512]{1,0:T(8,128)(2,1)S(1)} %collective-permute-done.left_ref) | copy-start | bytes 491524
  55.9 0.7 %copy-start.1 = (bf16[160,512]{1,0:T(8,128)(2,1)}, bf16[160,512]{1,0:T(8,128)(2,1)S(1)}, u32[]{:S(2)}) copy-start(bf16[160,512]{1,0:T(8,128)(2,1)S(1)} %collective-permute-done.1.right_ref) | copy-start | bytes 491524

commit v5 on v4

v5 whole, which is shorter than its diff:
```python
import functools
import math

import jax
import jax.numpy as jnp
from jax import lax
from jax.experimental import pallas as pl
from jax.experimental.pallas import tpu as pltpu
from jax.sharding import PartitionSpec as P

LEAF = 512


AMPLITUDE = 0.5
DISTANCE_SCALE = 0.125
RIDGE = 0.5

VMEM = pl.BlockSpec(memory_space=pltpu.VMEM)
SMEM = pl.BlockSpec(memory_space=pltpu.SMEM)


def shifted(x, axis, step):
    count = lax.axis_size(axis)
    if step > 0:
        pairs = [(i, i + step) for i in range(count - step)]
    else:
        pairs = [(i - step, i) for i in range(count + step)]
    return lax.ppermute(x, axis, pairs)


def from_mask(x, axis, mask):
    pairs = [(i, i ^ mask) for i in range(lax.axis_size(axis))]
    return lax.ppermute(x, axis, pairs)


def nt_dot(a, b):
    return lax.dot_general(a, b, (((1,), (1,)), ((), ())), preferred_element_type=jnp.float32)


def nn_dot(a, b):
    return lax.dot_general(a, b, (((1,), (0,)), ((), ())), preferred_element_type=jnp.float32)


def send_kernel(loc_bits, sub_bits, emb_ref, dirs_ref, basis_ref, first_ref, last_ref, upper_ref, *payload_refs):
    width_e = emb_ref.shape[0]
    local_points = emb_ref.shape[1]
    values = dirs_ref[...].astype(jnp.bfloat16)
    first_ref[:width_e, :] = emb_ref[:, :LEAF]
    first_ref[width_e:, :] = values[:, :LEAF]
    last_ref[:width_e, :] = emb_ref[:, local_points - LEAF :]
    last_ref[width_e:, :] = values[:, local_points - LEAF :]
    for level in range(upper_ref.shape[0]):
        part = nt_dot(values, basis_ref[loc_bits + sub_bits + level])
        upper_ref[level] = part
        for payload_ref in payload_refs:
            payload_ref[1 + level] = part
    for level, payload_ref in enumerate(payload_refs):
        payload_ref[0] = nt_dot(values, basis_ref[loc_bits + level])


class Leaves:
    def __init__(self, emb_ref, dirs_ref, neighbours_ref, counts_ref, sub_size):
        self.width_e = emb_ref.shape[0]
        self.local_points = emb_ref.shape[1]
        self.count = self.local_points // LEAF
        self.directions = dirs_ref[...]
        self.values = self.directions.astype(jnp.bfloat16)
        emb_float = emb_ref[...].astype(jnp.float32)
        row_norms = jnp.sum(emb_float * emb_float, axis=0, keepdims=True)
        emb_t = emb_float.T
        self.col_norms = jnp.sum(emb_t * emb_t, axis=1, keepdims=True)
        self.emb_t = emb_t.astype(jnp.bfloat16)
        self.points = [emb_ref[:, j * LEAF : (j + 1) * LEAF] for j in range(self.count)]
        self.norms = [row_norms[:, j * LEAF : (j + 1) * LEAF] for j in range(self.count)]
        self.leaf_values = [self.values[:, j * LEAF : (j + 1) * LEAF] for j in range(self.count)]
        self.neighbours_ref = neighbours_ref
        self.counts_ref = counts_ref
        self.me = lax.axis_index("leaf") * sub_size + lax.axis_index("sub")

    def block(self, j, source_points, source_norms):
        inner = nn_dot(self.emb_t[j * LEAF : (j + 1) * LEAF], source_points)
        distance = self.col_norms[j * LEAF : (j + 1) * LEAF] + source_norms - 2.0 * inner
        return (AMPLITUDE * jnp.exp(-DISTANCE_SCALE * distance)).astype(jnp.bfloat16)

    def weight(self, j, offset):
        leaf = self.me * self.count + j
        total = jnp.int32(0)
        for slot in range(self.neighbours_ref.shape[1]):
            hit = (slot < self.counts_ref[j]) & (self.neighbours_ref[j, slot] == leaf + offset)
            total = total + hit.astype(jnp.int32)
        return total.astype(jnp.float32)


def local_kernel(sub_size, emb_ref, dirs_ref, basis_ref, neighbours_ref, counts_ref, out_ref):
    lv = Leaves(emb_ref, dirs_ref, neighbours_ref, counts_ref, sub_size)
    rank = basis_ref.shape[1]
    near = [nt_dot(lv.leaf_values[j], lv.block(j, lv.points[j], lv.norms[j])) for j in range(lv.count)]
    for j in range(lv.count - 1):
        pair = lv.block(j, lv.points[j + 1], lv.norms[j + 1])
        near[j] = near[j] + lv.weight(j, 1) * nt_dot(lv.leaf_values[j + 1], pair)
        near[j + 1] = near[j + 1] + lv.weight(j + 1, -1) * nn_dot(lv.leaf_values[j], pair)
    basis0 = basis_ref[0]
    factor0 = 1.0 / math.sqrt(rank * LEAF)
    scaled0 = [
        (nt_dot(lv.leaf_values[q], basis0[:, q * LEAF : (q + 1) * LEAF]) * factor0).astype(jnp.bfloat16)
        for q in range(lv.count)
    ]
    for q in range(lv.count):
        far0 = nn_dot(scaled0[q ^ 1], basis0[:, q * LEAF : (q + 1) * LEAF])
        out_ref[:, q * LEAF : (q + 1) * LEAF] = (
            RIDGE * lv.directions[:, q * LEAF : (q + 1) * LEAF] + near[q] + far0
        )


def final_kernel(sub_size, sub_bits, leaf_bits, loc_bits, *refs):
    sub_masks = 2**sub_bits - 1
    leaf_masks = 2**leaf_bits - 1
    emb_ref, dirs_ref, local_ref, left_ref, right_ref, basis_ref, neighbours_ref, counts_ref = refs[:8]
    round_one = refs[8 : 8 + sub_masks]
    round_two = refs[8 + sub_masks : 8 + sub_masks + leaf_masks]
    out_ref = refs[8 + sub_masks + leaf_masks]
    lv = Leaves(emb_ref, dirs_ref, neighbours_ref, counts_ref, sub_size)
    rank = basis_ref.shape[1]
    local_points = lv.local_points

    sibling = [None] * (sub_bits + leaf_bits)
    line = None
    for mask, got_ref in enumerate(round_one, start=1):
        level = mask.bit_length() - 1
        got = got_ref[0]
        sibling[level] = got if sibling[level] is None else sibling[level] + got
    for mask, got_ref in enumerate(round_two, start=1):
        level = sub_bits + mask.bit_length() - 1
        got = got_ref[level - sub_bits]
        sibling[level] = got if sibling[level] is None else sibling[level] + got

    far = None
    for bit in range(sub_bits + leaf_bits):
        factor = 1.0 / math.sqrt(rank * local_points * 2**bit)
        scaled = (sibling[bit] * factor).astype(jnp.bfloat16)
        term = nn_dot(scaled, basis_ref[loc_bits + bit])
        far = term if far is None else far + term

    halo = {}
    for j, halo_ref, offset in ((0, left_ref, -1), (lv.count - 1, right_ref, 1)):
        halo_points = halo_ref[: lv.width_e, :]
        halo_float = halo_points.astype(jnp.float32)
        halo_norms = jnp.sum(halo_float * halo_float, axis=0, keepdims=True)
        weights = lv.block(j, halo_points, halo_norms)
        term = lv.weight(j, offset) * nt_dot(halo_ref[lv.width_e :, :], weights)
        halo[j] = term if j not in halo else halo[j] + term
    for j in range(lv.count):
        total = local_ref[:, j * LEAF : (j + 1) * LEAF] + far[:, j * LEAF : (j + 1) * LEAF]
        if j in halo:
            total = total + halo[j]
        out_ref[:, j * LEAF : (j + 1) * LEAF] = total


def on_device(embeddings, directions, level_basis, neighbours, counts):
    axes = ("leaf", "sub")
    width_e = embeddings.shape[0]
    local_points = embeddings.shape[1]
    rank = level_basis.shape[1]
    nrhs = directions.shape[0]
    sub_size = lax.axis_size("sub")
    leaf_size = lax.axis_size("leaf")
    sub_bits = sub_size.bit_length() - 1
    leaf_bits = leaf_size.bit_length() - 1
    dev_bits = sub_bits + leaf_bits
    loc_bits = level_basis.shape[0] - dev_bits

    halo = jax.ShapeDtypeStruct((width_e + nrhs, LEAF), jnp.bfloat16)
    upper = jax.ShapeDtypeStruct((leaf_bits, nrhs, rank), jnp.float32)
    payload = jax.ShapeDtypeStruct((1 + leaf_bits, nrhs, rank), jnp.float32)
    first, last, upper_own, *payloads = pl.pallas_call(
        functools.partial(send_kernel, loc_bits, sub_bits),
        out_shape=(halo, halo, upper) + (payload,) * sub_bits,
        in_specs=[VMEM, VMEM, VMEM],
        out_specs=(VMEM,) * (3 + sub_bits),
    )(embeddings, directions, level_basis)

    from_left = shifted(last, axes, 1)
    from_right = shifted(first, axes, -1)
    round_one = [from_mask(payloads[mask.bit_length() - 1], "sub", mask) for mask in range(1, sub_size)]
    line = upper_own
    for got in round_one:
        line = line + got[1:]
    round_two = [from_mask(line, "leaf", mask) for mask in range(1, leaf_size)]

    out = jax.ShapeDtypeStruct((nrhs, local_points), jnp.float32)
    local = pl.pallas_call(
        functools.partial(local_kernel, sub_size),
        out_shape=out,
        in_specs=[VMEM, VMEM, VMEM, SMEM, SMEM],
        out_specs=VMEM,
    )(embeddings, directions, level_basis, neighbours, counts)

    remote = round_one + round_two
    return pl.pallas_call(
        functools.partial(final_kernel, sub_size, sub_bits, leaf_bits, loc_bits),
        out_shape=out,
        in_specs=[VMEM] * 6 + [SMEM, SMEM] + [VMEM] * len(remote),
        out_specs=VMEM,
        input_output_aliases={2: 0},
    )(embeddings, directions, local, from_left, from_right, level_basis, neighbours, counts, *remote)


def solution(mesh):
    placed = (
        P(None, ("groups", "leaf", "sub")),
        P(None, ("groups", "leaf", "sub")),
        P(None, None, ("groups", "leaf", "sub")),
        P(("groups", "leaf", "sub"), None),
        P(("groups", "leaf", "sub")),
    )
    return jax.shard_map(
        on_device,
        mesh=mesh,
        in_specs=placed,
        out_specs=P(None, ("groups", "leaf", "sub")),
        check_vma=False,
    )
```

time: 61.9 us -> 26.9 us (0.43)
  blocking collectives: 47.5 us -> 0 us
  starting transfers between devices: 6.22 us -> 15.6 us
  Pallas kernels: 7.21 us -> 8.73 us
  other arithmetic: 0 us -> 0.78 us
  local copies, waits for them, and re-layouts: 0.73 us -> 1.35 us
    all_gather x1 -> x0, blocking collectives: 47.5 us -> none  [on_device(): incoming = lax.all_gather(partials, axes, axis=0, tiled=False)]
    ppermute x0 -> x6, starting transfers between devices: none -> 10.6 us  [from_mask(): return lax.ppermute(x, axis, pairs)]
    pallas_call x2 -> x3, Pallas kernels: 7.21 us -> 8.73 us  [the longest x1 3.49 us: on_device(): pl.pallas_call(functools.partial(local_kernel, sub_size), out_shape=out,...]
    ppermute x2, starting transfers between devices: 6.22 us -> 4.99 us  [shifted(): return lax.ppermute(x, axis, pairs)]
    add x0 -> x1, other arithmetic: none -> 0.78 us  [on_device(): line = line + got[1:]]
    unnamed x4 -> x16, local copies, waits for them, and re-layouts: 0.73 us -> 1.35 us
  transfers between devices with their start and end apart: 2 -> 8, of which waited for: 0 -> 0; matrix products, arithmetic and copies ran while one was open for 0% -> 3% of each run, Pallas kernels for 0% -> 13%
where the time goes in v5:
time: 26.9 us; the launch traced here: 26.6 us
  starting transfers between devices  15.6 us (58%)
  Pallas kernels  8.73 us (32%)
  local copies, waits for them, and re-layouts  1.35 us (5%)
  other arithmetic  0.78 us (3%)
    ppermute x6, starting transfers between devices, from_mask(): return lax.ppermute(x, axis, pairs)  10.6 us
    ppermute x2, starting transfers between devices, shifted(): return lax.ppermute(x, axis, pairs)  4.99 us
    pallas_call x1, Pallas kernels, on_device(): pl.pallas_call(functools.partial(local_kernel, sub_size), out_shape=out,...  3.49 us
    pallas_call x1, Pallas kernels, on_device(): pl.pallas_call(functools.partial(final_kernel, sub_size, sub_bits, leaf_b...  3.1 us
    pallas_call x1, Pallas kernels, on_device(): pl.pallas_call(functools.partial(send_kernel, loc_bits, sub_bits), out_sh...  2.13 us
    unnamed x16, local copies, waits for them, and re-layouts  1.35 us
    add x1, other arithmetic, on_device(): line = line + got[1:]  0.78 us
  transfers between devices with their start and end apart: 8, of which 0 were waited for; matrix products, arithmetic and copies ran while one was open for 3% of the time, Pallas kernels for 13%

profile of v5, /device:TPU:0, one launch (start us, length us, event | category | flops | bytes accessed | tf_op | source)
XLA Modules:
  0.0 26.6 jit_solution(14794228680556276606)
XLA Ops:
  0.0 2.1 %shard_map.56 = (bf16[160,512]{1,0:T(8,128)(2,1)}, bf16[160,512]{1,0:T(8,128)(2,1)}, f32[2,32,64]{2,1,0:T(8,128)}, f32[3,32,64]{2,1,0:T(8,128)}, f32[3,32,64]{2,1,0:T(8,128)}) custom-call(bf16[128,1024]{1,0:T(8,128)(2,1)} %refs_0_.1, f32[32,1024]{1,0:T(8,128)} %refs_1_.1, bf16[5,64,1024]{2,1,0:T(8,128)(2,1)} %refs_5_.1), custom_call_target="tpu_custom_call" | custom-call | tf_op jit(solution)/shard_map/pallas_call | solution.py:175
  2.1 4.0 %collective-permute-start.3 = (f32[3,32,64]{2,1,0:T(8,128)}, f32[3,32,64]{2,1,0:T(8,128)S(1)}, u32[]{:S(2)}, u32[]{:S(2)}) collective-permute-start(f32[3,32,64]{2,1,0:T(8,128)} %get-tuple-element.13), channel_id=1, source_target_pairs={{0,2},{1,3},{2,0},{3,1},{4,6},{5,7},{6,4},{7,5},{8,10},{9,11},{10,... | collective-permute-start | bytes 73736 | tf_op jit(solution)/shard_map/ppermute | solution.py:33
  6.2 1.3 %collective-permute-start.4 = (f32[3,32,64]{2,1,0:T(8,128)}, f32[3,32,64]{2,1,0:T(8,128)S(1)}, u32[]{:S(2)}, u32[]{:S(2)}) collective-permute-start(f32[3,32,64]{2,1,0:T(8,128)} %get-tuple-element.13), channel_id=1, source_target_pairs={{0,3},{1,2},{2,1},{3,0},{4,7},{5,6},{6,5},{7,4},{8,11},{9,10},{10,... | collective-permute-start | bytes 73736 | tf_op jit(solution)/shard_map/ppermute | solution.py:33
  7.5 0.2 collective-permute-start.2
  7.8 3.7 %collective-permute-start = (bf16[160,512]{1,0:T(8,128)(2,1)}, bf16[160,512]{1,0:T(8,128)(2,1)S(1)}, u32[]{:S(2)}, u32[]{:S(2)}) collective-permute-start(bf16[160,512]{1,0:T(8,128)(2,1)} %get-tuple-element.10), channel_id=1, source_target_pairs={{0,1},{1,2},{2,3},{3,4},{4,5},{5,6},{6,7},{7,8},{8,9},{9,10},{10,1... | collective-permute-start | bytes 491528 | tf_op jit(solution)/shard_map/ppermute | solution.py:28
  11.5 1.3 %collective-permute-start.1 = (bf16[160,512]{1,0:T(8,128)(2,1)}, bf16[160,512]{1,0:T(8,128)(2,1)S(1)}, u32[]{:S(2)}, u32[]{:S(2)}) collective-permute-start(bf16[160,512]{1,0:T(8,128)(2,1)} %get-tuple-element.11), channel_id=1, source_target_pairs={{1,0},{2,1},{3,2},{4,3},{5,4},{6,5},{7,6},{8,7},{9,8},{10,9},{11,1... | collective-permute-start | bytes 491528 | tf_op jit(solution)/shard_map/ppermute | solution.py:28
  12.8 0.0 collective-permute-done.3.refs_9_
  12.8 0.0 copy-start.2
  12.8 0.0 collective-permute-done.4.refs_10_
  12.8 0.0 copy-start.3
  12.8 0.0 collective-permute-done.2.refs_8_
  12.8 0.0 copy-start.4
  12.8 0.8 %slice_add_fusion = f32[2,32,64]{2,1,0:T(8,128)S(1)} fusion(f32[3,32,64]{2,1,0:T(8,128)S(1)} %collective-permute-done.4.refs_10_, f32[3,32,64]{2,1,0:T(8,128)S(1)} %collective-permute-done.3.refs_9_, f32[2,32,64]{2,1,0:T(8,128)} %get-tuple-element.14, f32[3,32,64]{2,1,0:T(8,128)S(1)} %collective-permute-done.2.refs_8_), kind=kLoop, calls=%fused_computation | loop fusion | flops 12288 | bytes 81920 | tf_op jit(solution)/shard_map/add | solution.py:187
  13.6 0.0 copy-done.2
  13.6 0.0 copy-done.3
  13.6 0.0 copy-done.4
  13.6 1.9 %collective-permute-start.5 = (f32[2,32,64]{2,1,0:T(8,128)S(1)}, f32[2,32,64]{2,1,0:T(8,128)S(1)}, u32[]{:S(2)}, u32[]{:S(2)}) collective-permute-start(f32[2,32,64]{2,1,0:T(8,128)S(1)} %slice_add_fusion), channel_id=1, source_target_pairs={{0,4},{4,0},{8,12},{12,8},{1,5},{5,1},{9,13},{13,9},{2,6},{6,2},{1... | collective-permute-start | bytes 49160 | tf_op jit(solution)/shard_map/ppermute | solution.py:33
  15.6 3.0 %collective-permute-start.6 = (f32[2,32,64]{2,1,0:T(8,128)S(1)}, f32[2,32,64]{2,1,0:T(8,128)S(1)}, u32[]{:S(2)}, u32[]{:S(2)}) collective-permute-start(f32[2,32,64]{2,1,0:T(8,128)S(1)} %slice_add_fusion), channel_id=1, source_target_pairs={{0,8},{4,12},{8,0},{12,4},{1,9},{5,13},{9,1},{13,5},{2,10},{6,14},... | collective-permute-start | bytes 49160 | tf_op jit(solution)/shard_map/ppermute | solution.py:33
  18.5 0.1 collective-permute-start.7
  18.6 3.5 %shard_map.55.refs_2_ = f32[32,1024]{1,0:T(8,128)} custom-call(bf16[128,1024]{1,0:T(8,128)(2,1)} %refs_0_.1, f32[32,1024]{1,0:T(8,128)} %refs_1_.1, bf16[5,64,1024]{2,1,0:T(8,128)(2,1)} %refs_5_.1, s32[2,8]{1,0:T(2,128)} %refs_6_.1, s32[2]{0:T(128)} %refs_7_.1), custom_call_target="tpu_custom_call" | custom-call | tf_op jit(solution)/shard_map/pallas_call | solution.py:191
  22.1 0.0 collective-permute-done.5.refs_11_
  22.1 0.0 copy-start.5
  22.1 0.0 collective-permute-done.6.refs_12_
  22.1 0.0 copy-start.6
  22.1 0.0 collective-permute-done.7.refs_13_
  22.1 0.0 copy-start.7
  22.1 0.0 collective-permute-done.refs_3_
  22.1 0.0 copy-start
  22.2 0.0 collective-permute-done.1.refs_4_
  22.2 0.5 %copy-done.5 = f32[2,32,64]{2,1,0:T(8,128)} copy-done((f32[2,32,64]{2,1,0:T(8,128)}, f32[2,32,64]{2,1,0:T(8,128)S(1)}, u32[]{:S(2)}) %copy-start.5) | copy-done | bytes 16408
  22.7 0.0 copy-done.6
  22.7 0.0 copy-done.7
  22.7 0.1 copy-done
  22.8 0.0 copy-start.1
  22.8 0.7 %copy-done.1 = bf16[160,512]{1,0:T(8,128)(2,1)} copy-done((bf16[160,512]{1,0:T(8,128)(2,1)}, bf16[160,512]{1,0:T(8,128)(2,1)S(1)}, u32[]{:S(2)}) %copy-start.1) | copy-done | bytes 163864
  23.5 3.1 %shard_map.57 = f32[32,1024]{1,0:T(8,128)} custom-call(bf16[128,1024]{1,0:T(8,128)(2,1)} %refs_0_.1, f32[32,1024]{1,0:T(8,128)} %refs_1_.1, f32[32,1024]{1,0:T(8,128)} %shard_map.55.refs_2_, bf16[160,512]{1,0:T(8,128)(2,1)} %copy-done, bf16[160,512]{1,0:T(8,128)(2,1)} %copy-done.1, bf16[5,64,1024]{2,1,0:T(8,128)(2,1)} %refs_5_.1, ...), custom_call_target="tpu_custom_call", output_to_operand_aliasing={{}: (2, {})} | custom-call | tf_op jit(solution)/shard_map/pallas_call | solution.py:199
Async XLA Ops:
  2.1 10.6 %collective-permute-start.3 = (f32[3,32,64]{2,1,0:T(8,128)}, f32[3,32,64]{2,1,0:T(8,128)S(1)}, u32[]{:S(2)}, u32[]{:S(2)}) collective-permute-start(f32[3,32,64]{2,1,0:T(8,128)} %get-tuple-element.13), channel_id=1, source_target_pairs={{0,2},{1,3},{2,0},{3,1},{4,6},{5,7},{6,4},{7,5},{8,10},{9,11},{10,... | collective-permute-start | bytes 73736 | tf_op jit(solution)/shard_map/ppermute | solution.py:33
  6.2 6.6 %collective-permute-start.4 = (f32[3,32,64]{2,1,0:T(8,128)}, f32[3,32,64]{2,1,0:T(8,128)S(1)}, u32[]{:S(2)}, u32[]{:S(2)}) collective-permute-start(f32[3,32,64]{2,1,0:T(8,128)} %get-tuple-element.13), channel_id=1, source_target_pairs={{0,3},{1,2},{2,1},{3,0},{4,7},{5,6},{6,5},{7,4},{8,11},{9,10},{10,... | collective-permute-start | bytes 73736 | tf_op jit(solution)/shard_map/ppermute | solution.py:33
  7.5 5.3 %collective-permute-start.2 = (f32[3,32,64]{2,1,0:T(8,128)}, f32[3,32,64]{2,1,0:T(8,128)S(1)}, u32[]{:S(2)}, u32[]{:S(2)}) collective-permute-start(f32[3,32,64]{2,1,0:T(8,128)} %get-tuple-element.12), channel_id=1, source_target_pairs={{0,1},{1,0},{2,3},{3,2},{4,5},{5,4},{6,7},{7,6},{8,9},{9,8},{10,11... | collective-permute-start | bytes 73736 | tf_op jit(solution)/shard_map/ppermute | solution.py:33
  7.8 14.4 %collective-permute-start = (bf16[160,512]{1,0:T(8,128)(2,1)}, bf16[160,512]{1,0:T(8,128)(2,1)S(1)}, u32[]{:S(2)}, u32[]{:S(2)}) collective-permute-start(bf16[160,512]{1,0:T(8,128)(2,1)} %get-tuple-element.10), channel_id=1, source_target_pairs={{0,1},{1,2},{2,3},{3,4},{4,5},{5,6},{6,7},{7,8},{8,9},{9,10},{10,1... | collective-permute-start | bytes 491528 | tf_op jit(solution)/shard_map/ppermute | solution.py:28
  11.5 10.7 %collective-permute-start.1 = (bf16[160,512]{1,0:T(8,128)(2,1)}, bf16[160,512]{1,0:T(8,128)(2,1)S(1)}, u32[]{:S(2)}, u32[]{:S(2)}) collective-permute-start(bf16[160,512]{1,0:T(8,128)(2,1)} %get-tuple-element.11), channel_id=1, source_target_pairs={{1,0},{2,1},{3,2},{4,3},{5,4},{6,5},{7,6},{8,7},{9,8},{10,9},{11,1... | collective-permute-start | bytes 491528 | tf_op jit(solution)/shard_map/ppermute | solution.py:28
  12.8 0.8 %copy-start.2 = (f32[3,32,64]{2,1,0:T(8,128)}, f32[3,32,64]{2,1,0:T(8,128)S(1)}, u32[]{:S(2)}) copy-start(f32[3,32,64]{2,1,0:T(8,128)S(1)} %collective-permute-done.3.refs_9_) | copy-start | bytes 73732
  12.8 0.8 %copy-start.3 = (f32[3,32,64]{2,1,0:T(8,128)}, f32[3,32,64]{2,1,0:T(8,128)S(1)}, u32[]{:S(2)}) copy-start(f32[3,32,64]{2,1,0:T(8,128)S(1)} %collective-permute-done.4.refs_10_) | copy-start | bytes 73732
  12.8 0.8 %copy-start.4 = (f32[3,32,64]{2,1,0:T(8,128)}, f32[3,32,64]{2,1,0:T(8,128)S(1)}, u32[]{:S(2)}) copy-start(f32[3,32,64]{2,1,0:T(8,128)S(1)} %collective-permute-done.2.refs_8_) | copy-start | bytes 73732
  13.6 8.5 %collective-permute-start.5 = (f32[2,32,64]{2,1,0:T(8,128)S(1)}, f32[2,32,64]{2,1,0:T(8,128)S(1)}, u32[]{:S(2)}, u32[]{:S(2)}) collective-permute-start(f32[2,32,64]{2,1,0:T(8,128)S(1)} %slice_add_fusion), channel_id=1, source_target_pairs={{0,4},{4,0},{8,12},{12,8},{1,5},{5,1},{9,13},{13,9},{2,6},{6,2},{1... | collective-permute-start | bytes 49160 | tf_op jit(solution)/shard_map/ppermute | solution.py:33
  15.6 6.5 %collective-permute-start.6 = (f32[2,32,64]{2,1,0:T(8,128)S(1)}, f32[2,32,64]{2,1,0:T(8,128)S(1)}, u32[]{:S(2)}, u32[]{:S(2)}) collective-permute-start(f32[2,32,64]{2,1,0:T(8,128)S(1)} %slice_add_fusion), channel_id=1, source_target_pairs={{0,8},{4,12},{8,0},{12,4},{1,9},{5,13},{9,1},{13,5},{2,10},{6,14},... | collective-permute-start | bytes 49160 | tf_op jit(solution)/shard_map/ppermute | solution.py:33
  18.5 3.6 %collective-permute-start.7 = (f32[2,32,64]{2,1,0:T(8,128)S(1)}, f32[2,32,64]{2,1,0:T(8,128)S(1)}, u32[]{:S(2)}, u32[]{:S(2)}) collective-permute-start(f32[2,32,64]{2,1,0:T(8,128)S(1)} %slice_add_fusion), channel_id=1, source_target_pairs={{0,12},{4,8},{8,4},{12,0},{1,13},{5,9},{9,5},{13,1},{2,14},{6,10},... | collective-permute-start | bytes 49160 | tf_op jit(solution)/shard_map/ppermute | solution.py:33
  22.1 0.6 %copy-start.5 = (f32[2,32,64]{2,1,0:T(8,128)}, f32[2,32,64]{2,1,0:T(8,128)S(1)}, u32[]{:S(2)}) copy-start(f32[2,32,64]{2,1,0:T(8,128)S(1)} %collective-permute-done.5.refs_11_) | copy-start | bytes 49156
  22.1 0.6 %copy-start.6 = (f32[2,32,64]{2,1,0:T(8,128)}, f32[2,32,64]{2,1,0:T(8,128)S(1)}, u32[]{:S(2)}) copy-start(f32[2,32,64]{2,1,0:T(8,128)S(1)} %collective-permute-done.6.refs_12_) | copy-start | bytes 49156
  22.1 0.6 %copy-start.7 = (f32[2,32,64]{2,1,0:T(8,128)}, f32[2,32,64]{2,1,0:T(8,128)S(1)}, u32[]{:S(2)}) copy-start(f32[2,32,64]{2,1,0:T(8,128)S(1)} %collective-permute-done.7.refs_13_) | copy-start | bytes 49156
  22.1 0.7 %copy-start = (bf16[160,512]{1,0:T(8,128)(2,1)}, bf16[160,512]{1,0:T(8,128)(2,1)S(1)}, u32[]{:S(2)}) copy-start(bf16[160,512]{1,0:T(8,128)(2,1)S(1)} %collective-permute-done.refs_3_) | copy-start | bytes 491524
  22.8 0.7 %copy-start.1 = (bf16[160,512]{1,0:T(8,128)(2,1)}, bf16[160,512]{1,0:T(8,128)(2,1)S(1)}, u32[]{:S(2)}) copy-start(bf16[160,512]{1,0:T(8,128)(2,1)S(1)} %collective-permute-done.1.refs_4_) | copy-start | bytes 491524

commit v6 on v5

--- a/solution.py
+++ b/solution.py
@@ -19,15 +19,6 @@
 SMEM = pl.BlockSpec(memory_space=pltpu.SMEM)
 
 
-def shifted(x, axis, step):
-    count = lax.axis_size(axis)
-    if step > 0:
-        pairs = [(i, i + step) for i in range(count - step)]
-    else:
-        pairs = [(i - step, i) for i in range(count + step)]
-    return lax.ppermute(x, axis, pairs)
-
-
 def from_mask(x, axis, mask):
     pairs = [(i, i ^ mask) for i in range(lax.axis_size(axis))]
     return lax.ppermute(x, axis, pairs)
@@ -45,10 +36,13 @@
     width_e = emb_ref.shape[0]
     local_points = emb_ref.shape[1]
     values = dirs_ref[...].astype(jnp.bfloat16)
-    first_ref[:width_e, :] = emb_ref[:, :LEAF]
-    first_ref[width_e:, :] = values[:, :LEAF]
-    last_ref[:width_e, :] = emb_ref[:, local_points - LEAF :]
-    last_ref[width_e:, :] = values[:, local_points - LEAF :]
+    even = lax.axis_index("sub") % 2 == 0
+    head_points, tail_points = emb_ref[:, :LEAF], emb_ref[:, local_points - LEAF :]
+    head_values, tail_values = values[:, :LEAF], values[:, local_points - LEAF :]
+    first_ref[:width_e, :] = jnp.where(even, tail_points, head_points)
+    first_ref[width_e:, :] = jnp.where(even, tail_values, head_values)
+    last_ref[:width_e, :] = jnp.where(even, head_points, tail_points)
+    last_ref[width_e:, :] = jnp.where(even, head_values, tail_values)
     for level in range(upper_ref.shape[0]):
         part = nt_dot(values, basis_ref[loc_bits + sub_bits + level])
         upper_ref[level] = part
@@ -115,7 +109,7 @@
 def final_kernel(sub_size, sub_bits, leaf_bits, loc_bits, *refs):
     sub_masks = 2**sub_bits - 1
     leaf_masks = 2**leaf_bits - 1
-    emb_ref, dirs_ref, local_ref, left_ref, right_ref, basis_ref, neighbours_ref, counts_ref = refs[:8]
+    emb_ref, dirs_ref, local_ref, pair_ref, cross_ref, basis_ref, neighbours_ref, counts_ref = refs[:8]
     round_one = refs[8 : 8 + sub_masks]
     round_two = refs[8 + sub_masks : 8 + sub_masks + leaf_masks]
     out_ref = refs[8 + sub_masks + leaf_masks]
@@ -141,13 +135,16 @@
         term = nn_dot(scaled, basis_ref[loc_bits + bit])
         far = term if far is None else far + term
 
+    even = lax.axis_index("sub") % 2 == 0
+    pair, cross = pair_ref[...], cross_ref[...]
+    left, right = jnp.where(even, cross, pair), jnp.where(even, pair, cross)
     halo = {}
-    for j, halo_ref, offset in ((0, left_ref, -1), (lv.count - 1, right_ref, 1)):
-        halo_points = halo_ref[: lv.width_e, :]
+    for j, received, offset in ((0, left, -1), (lv.count - 1, right, 1)):
+        halo_points = received[: lv.width_e, :]
         halo_float = halo_points.astype(jnp.float32)
         halo_norms = jnp.sum(halo_float * halo_float, axis=0, keepdims=True)
         weights = lv.block(j, halo_points, halo_norms)
-        term = lv.weight(j, offset) * nt_dot(halo_ref[lv.width_e :, :], weights)
+        term = lv.weight(j, offset) * nt_dot(received[lv.width_e :, :], weights)
         halo[j] = term if j not in halo else halo[j] + term
     for j in range(lv.count):
         total = local_ref[:, j * LEAF : (j + 1) * LEAF] + far[:, j * LEAF : (j + 1) * LEAF]
@@ -179,8 +176,9 @@
         out_specs=(VMEM,) * (3 + sub_bits),
     )(embeddings, directions, level_basis)
 
-    from_left = shifted(last, axes, 1)
-    from_right = shifted(first, axes, -1)
+    ndev = sub_size * leaf_size
+    from_pair = lax.ppermute(first, axes, [(i, i ^ 1) for i in range(ndev)])
+    from_cross = lax.ppermute(last, axes, [(i, i - 1 + 2 * (i % 2)) for i in range(1, ndev - 1)])
     round_one = [from_mask(payloads[mask.bit_length() - 1], "sub", mask) for mask in range(1, sub_size)]
     line = upper_own
     for got in round_one:
@@ -202,7 +200,7 @@
         in_specs=[VMEM] * 6 + [SMEM, SMEM] + [VMEM] * len(remote),
         out_specs=VMEM,
         input_output_aliases={2: 0},
-    )(embeddings, directions, local, from_left, from_right, level_basis, neighbours, counts, *remote)
+    )(embeddings, directions, local, from_pair, from_cross, level_basis, neighbours, counts, *remote)
 
 
 def solution(mesh):

time: 26.9 us -> 25 us (0.929)
  starting transfers between devices: 15.6 us -> 10.8 us
  waiting for transfers between devices: 0.02 us -> 2.87 us
    ppermute x6, waiting for transfers between devices: 0.02 us -> 2.86 us  [from_mask(): return lax.ppermute(x, axis, pairs)]
    ppermute x2, starting transfers between devices: 4.99 us -> 2.45 us  [the longest x1 1.8 us: on_device(): from_pair = lax.ppermute(first, axes, [(i, i ^ 1) for i in range(ndev)])]
    ppermute x6, starting transfers between devices: 10.6 us -> 8.33 us  [from_mask(): return lax.ppermute(x, axis, pairs)]
  transfers between devices with their start and end apart: 8 -> 8, of which waited for: 0 -> 3; matrix products, arithmetic and copies ran while one was open for 3% -> 3% of each run, Pallas kernels for 13% -> 14%
where the time goes in v6:
time: 25 us; the launch traced here: 24.7 us
  starting transfers between devices  10.8 us (43%)
  Pallas kernels  8.8 us (35%)
  waiting for transfers between devices  2.87 us (11%)
  local copies, waits for them, and re-layouts  1.36 us (5%)
  other arithmetic  0.79 us (3%)
    ppermute x6, starting transfers between devices, from_mask(): return lax.ppermute(x, axis, pairs)  8.33 us
    pallas_call x1, Pallas kernels, on_device(): pl.pallas_call(functools.partial(local_kernel, sub_size), out_shape=out,...  3.49 us
    pallas_call x1, Pallas kernels, on_device(): pl.pallas_call(functools.partial(final_kernel, sub_size, sub_bits, leaf_b...  3.11 us
    ppermute x6, waiting for transfers between devices, from_mask(): return lax.ppermute(x, axis, pairs)  2.86 us
    pallas_call x1, Pallas kernels, on_device(): pl.pallas_call(functools.partial(send_kernel, loc_bits, sub_bits), out_sh...  2.19 us
    ppermute x1, starting transfers between devices, on_device(): from_pair = lax.ppermute(first, axes, [(i, i ^ 1) for i in range(ndev)])  1.8 us
    unnamed x16, local copies, waits for them, and re-layouts  1.36 us
    add x1, other arithmetic, on_device(): line = line + got[1:]  0.79 us
  transfers between devices with their start and end apart: 8, of which 3 were waited for; matrix products, arithmetic and copies ran while one was open for 3% of the time, Pallas kernels for 14%

profile of v6, /device:TPU:0, one launch (start us, length us, event | category | flops | bytes accessed | tf_op | source)
XLA Modules:
  0.0 24.7 jit_solution(14559077038720818339)
XLA Ops:
  0.0 2.2 %shard_map.56 = (bf16[160,512]{1,0:T(8,128)(2,1)}, bf16[160,512]{1,0:T(8,128)(2,1)}, f32[2,32,64]{2,1,0:T(8,128)}, f32[3,32,64]{2,1,0:T(8,128)}, f32[3,32,64]{2,1,0:T(8,128)}) custom-call(bf16[128,1024]{1,0:T(8,128)(2,1)} %refs_0_.1, f32[32,1024]{1,0:T(8,128)} %refs_1_.1, bf16[5,64,1024]{2,1,0:T(8,128)(2,1)} %refs_5_.1), custom_call_target="tpu_custom_call" | custom-call | tf_op jit(solution)/shard_map/pallas_call | solution.py:172
  2.2 4.0 %collective-permute-start.3 = (f32[3,32,64]{2,1,0:T(8,128)}, f32[3,32,64]{2,1,0:T(8,128)S(1)}, u32[]{:S(2)}, u32[]{:S(2)}) collective-permute-start(f32[3,32,64]{2,1,0:T(8,128)} %get-tuple-element.13), channel_id=1, source_target_pairs={{0,2},{1,3},{2,0},{3,1},{4,6},{5,7},{6,4},{7,5},{8,10},{9,11},{10,... | collective-permute-start | bytes 73736 | tf_op jit(solution)/shard_map/ppermute | solution.py:24
  6.2 1.3 %collective-permute-start.4 = (f32[3,32,64]{2,1,0:T(8,128)}, f32[3,32,64]{2,1,0:T(8,128)S(1)}, u32[]{:S(2)}, u32[]{:S(2)}) collective-permute-start(f32[3,32,64]{2,1,0:T(8,128)} %get-tuple-element.13), channel_id=1, source_target_pairs={{0,3},{1,2},{2,1},{3,0},{4,7},{5,6},{6,5},{7,4},{8,11},{9,10},{10,... | collective-permute-start | bytes 73736 | tf_op jit(solution)/shard_map/ppermute | solution.py:24
  7.6 0.2 collective-permute-start.2
  7.8 1.8 %collective-permute-start = (bf16[160,512]{1,0:T(8,128)(2,1)}, bf16[160,512]{1,0:T(8,128)(2,1)S(1)}, u32[]{:S(2)}, u32[]{:S(2)}) collective-permute-start(bf16[160,512]{1,0:T(8,128)(2,1)} %get-tuple-element.10), channel_id=1, source_target_pairs={{0,1},{1,0},{2,3},{3,2},{4,5},{5,4},{6,7},{7,6},{8,9},{9,8},{10,11... | collective-permute-start | bytes 491528 | tf_op jit(solution)/shard_map/ppermute | solution.py:180
  9.6 0.7 %collective-permute-start.1 = (bf16[160,512]{1,0:T(8,128)(2,1)}, bf16[160,512]{1,0:T(8,128)(2,1)S(1)}, u32[]{:S(2)}, u32[]{:S(2)}) collective-permute-start(bf16[160,512]{1,0:T(8,128)(2,1)} %get-tuple-element.11), channel_id=1, source_target_pairs={{1,2},{2,1},{3,4},{4,3},{5,6},{6,5},{7,8},{8,7},{9,10},{10,9},{11,... | collective-permute-start | bytes 491528 | tf_op jit(solution)/shard_map/ppermute | solution.py:181
  10.3 0.0 collective-permute-done.3.refs_9_
  10.3 0.0 copy-start.2
  10.3 2.5 %collective-permute-done.4.refs_10_ = f32[3,32,64]{2,1,0:T(8,128)S(1)} collective-permute-done((f32[3,32,64]{2,1,0:T(8,128)}, f32[3,32,64]{2,1,0:T(8,128)S(1)}, u32[]{:S(2)}, u32[]{:S(2)}) %collective-permute-start.4) | collective-permute-done | bytes 24608 | tf_op jit(solution)/shard_map/ppermute | solution.py:24
  12.8 0.0 copy-start.3
  12.8 0.2 collective-permute-done.2.refs_8_
  13.0 0.0 copy-start.4
  13.0 0.8 %slice_add_fusion = f32[2,32,64]{2,1,0:T(8,128)S(1)} fusion(f32[3,32,64]{2,1,0:T(8,128)S(1)} %collective-permute-done.4.refs_10_, f32[3,32,64]{2,1,0:T(8,128)S(1)} %collective-permute-done.3.refs_9_, f32[2,32,64]{2,1,0:T(8,128)} %get-tuple-element.14, f32[3,32,64]{2,1,0:T(8,128)S(1)} %collective-permute-done.2.refs_8_), kind=kLoop, calls=%fused_computation | loop fusion | flops 12288 | bytes 81920 | tf_op jit(solution)/shard_map/add | solution.py:185
  13.8 0.0 copy-done.2
  13.8 0.0 copy-done.3
  13.8 0.0 copy-done.4
  13.8 1.2 %collective-permute-start.5 = (f32[2,32,64]{2,1,0:T(8,128)S(1)}, f32[2,32,64]{2,1,0:T(8,128)S(1)}, u32[]{:S(2)}, u32[]{:S(2)}) collective-permute-start(f32[2,32,64]{2,1,0:T(8,128)S(1)} %slice_add_fusion), channel_id=1, source_target_pairs={{0,4},{4,0},{8,12},{12,8},{1,5},{5,1},{9,13},{13,9},{2,6},{6,2},{1... | collective-permute-start | bytes 49160 | tf_op jit(solution)/shard_map/ppermute | solution.py:24
  15.0 1.5 %collective-permute-start.6 = (f32[2,32,64]{2,1,0:T(8,128)S(1)}, f32[2,32,64]{2,1,0:T(8,128)S(1)}, u32[]{:S(2)}, u32[]{:S(2)}) collective-permute-start(f32[2,32,64]{2,1,0:T(8,128)S(1)} %slice_add_fusion), channel_id=1, source_target_pairs={{0,8},{4,12},{8,0},{12,4},{1,9},{5,13},{9,1},{13,5},{2,10},{6,14},... | collective-permute-start | bytes 49160 | tf_op jit(solution)/shard_map/ppermute | solution.py:24
  16.5 0.0 collective-permute-start.7
  16.5 3.5 %shard_map.55.refs_2_ = f32[32,1024]{1,0:T(8,128)} custom-call(bf16[128,1024]{1,0:T(8,128)(2,1)} %refs_0_.1, f32[32,1024]{1,0:T(8,128)} %refs_1_.1, bf16[5,64,1024]{2,1,0:T(8,128)(2,1)} %refs_5_.1, s32[2,8]{1,0:T(2,128)} %refs_6_.1, s32[2]{0:T(128)} %refs_7_.1), custom_call_target="tpu_custom_call" | custom-call | tf_op jit(solution)/shard_map/pallas_call | solution.py:189
  20.0 0.0 collective-permute-done.5.refs_11_
  20.0 0.0 copy-start.5
  20.0 0.0 collective-permute-done.6.refs_12_
  20.0 0.0 copy-start.6
  20.1 0.2 collective-permute-done.7.refs_13_
  20.2 0.0 copy-start.7
  20.2 0.0 collective-permute-done.refs_3_
  20.2 0.0 copy-start
  20.2 0.0 collective-permute-done.1.refs_4_
  20.2 0.4 %copy-done.5 = f32[2,32,64]{2,1,0:T(8,128)} copy-done((f32[2,32,64]{2,1,0:T(8,128)}, f32[2,32,64]{2,1,0:T(8,128)S(1)}, u32[]{:S(2)}) %copy-start.5) | copy-done | bytes 16408
  20.6 0.0 copy-done.6
  20.7 0.2 copy-done.7
  20.8 0.1 copy-done
  20.9 0.0 copy-start.1
  20.9 0.7 %copy-done.1 = bf16[160,512]{1,0:T(8,128)(2,1)} copy-done((bf16[160,512]{1,0:T(8,128)(2,1)}, bf16[160,512]{1,0:T(8,128)(2,1)S(1)}, u32[]{:S(2)}) %copy-start.1) | copy-done | bytes 163864
  21.6 3.1 %shard_map.57 = f32[32,1024]{1,0:T(8,128)} custom-call(bf16[128,1024]{1,0:T(8,128)(2,1)} %refs_0_.1, f32[32,1024]{1,0:T(8,128)} %refs_1_.1, f32[32,1024]{1,0:T(8,128)} %shard_map.55.refs_2_, bf16[160,512]{1,0:T(8,128)(2,1)} %copy-done, bf16[160,512]{1,0:T(8,128)(2,1)} %copy-done.1, bf16[5,64,1024]{2,1,0:T(8,128)(2,1)} %refs_5_.1, ...), custom_call_target="tpu_custom_call", output_to_operand_aliasing={{}: (2, {})} | custom-call | tf_op jit(solution)/shard_map/pallas_call | solution.py:197
Async XLA Ops:
  2.2 8.1 %collective-permute-start.3 = (f32[3,32,64]{2,1,0:T(8,128)}, f32[3,32,64]{2,1,0:T(8,128)S(1)}, u32[]{:S(2)}, u32[]{:S(2)}) collective-permute-start(f32[3,32,64]{2,1,0:T(8,128)} %get-tuple-element.13), channel_id=1, source_target_pairs={{0,2},{1,3},{2,0},{3,1},{4,6},{5,7},{6,4},{7,5},{8,10},{9,11},{10,... | collective-permute-start | bytes 73736 | tf_op jit(solution)/shard_map/ppermute | solution.py:24
  6.2 6.6 %collective-permute-start.4 = (f32[3,32,64]{2,1,0:T(8,128)}, f32[3,32,64]{2,1,0:T(8,128)S(1)}, u32[]{:S(2)}, u32[]{:S(2)}) collective-permute-start(f32[3,32,64]{2,1,0:T(8,128)} %get-tuple-element.13), channel_id=1, source_target_pairs={{0,3},{1,2},{2,1},{3,0},{4,7},{5,6},{6,5},{7,4},{8,11},{9,10},{10,... | collective-permute-start | bytes 73736 | tf_op jit(solution)/shard_map/ppermute | solution.py:24
  7.6 5.4 %collective-permute-start.2 = (f32[3,32,64]{2,1,0:T(8,128)}, f32[3,32,64]{2,1,0:T(8,128)S(1)}, u32[]{:S(2)}, u32[]{:S(2)}) collective-permute-start(f32[3,32,64]{2,1,0:T(8,128)} %get-tuple-element.12), channel_id=1, source_target_pairs={{0,1},{1,0},{2,3},{3,2},{4,5},{5,4},{6,7},{7,6},{8,9},{9,8},{10,11... | collective-permute-start | bytes 73736 | tf_op jit(solution)/shard_map/ppermute | solution.py:24
  7.8 12.4 %collective-permute-start = (bf16[160,512]{1,0:T(8,128)(2,1)}, bf16[160,512]{1,0:T(8,128)(2,1)S(1)}, u32[]{:S(2)}, u32[]{:S(2)}) collective-permute-start(bf16[160,512]{1,0:T(8,128)(2,1)} %get-tuple-element.10), channel_id=1, source_target_pairs={{0,1},{1,0},{2,3},{3,2},{4,5},{5,4},{6,7},{7,6},{8,9},{9,8},{10,11... | collective-permute-start | bytes 491528 | tf_op jit(solution)/shard_map/ppermute | solution.py:180
  9.6 10.6 %collective-permute-start.1 = (bf16[160,512]{1,0:T(8,128)(2,1)}, bf16[160,512]{1,0:T(8,128)(2,1)S(1)}, u32[]{:S(2)}, u32[]{:S(2)}) collective-permute-start(bf16[160,512]{1,0:T(8,128)(2,1)} %get-tuple-element.11), channel_id=1, source_target_pairs={{1,2},{2,1},{3,4},{4,3},{5,6},{6,5},{7,8},{8,7},{9,10},{10,9},{11,... | collective-permute-start | bytes 491528 | tf_op jit(solution)/shard_map/ppermute | solution.py:181
  10.3 3.5 %copy-start.2 = (f32[3,32,64]{2,1,0:T(8,128)}, f32[3,32,64]{2,1,0:T(8,128)S(1)}, u32[]{:S(2)}) copy-start(f32[3,32,64]{2,1,0:T(8,128)S(1)} %collective-permute-done.3.refs_9_) | copy-start | bytes 73732
  12.8 1.0 %copy-start.3 = (f32[3,32,64]{2,1,0:T(8,128)}, f32[3,32,64]{2,1,0:T(8,128)S(1)}, u32[]{:S(2)}) copy-start(f32[3,32,64]{2,1,0:T(8,128)S(1)} %collective-permute-done.4.refs_10_) | copy-start | bytes 73732
  13.0 0.8 %copy-start.4 = (f32[3,32,64]{2,1,0:T(8,128)}, f32[3,32,64]{2,1,0:T(8,128)S(1)}, u32[]{:S(2)}) copy-start(f32[3,32,64]{2,1,0:T(8,128)S(1)} %collective-permute-done.2.refs_8_) | copy-start | bytes 73732
  13.8 6.2 %collective-permute-start.5 = (f32[2,32,64]{2,1,0:T(8,128)S(1)}, f32[2,32,64]{2,1,0:T(8,128)S(1)}, u32[]{:S(2)}, u32[]{:S(2)}) collective-permute-start(f32[2,32,64]{2,1,0:T(8,128)S(1)} %slice_add_fusion), channel_id=1, source_target_pairs={{0,4},{4,0},{8,12},{12,8},{1,5},{5,1},{9,13},{13,9},{2,6},{6,2},{1... | collective-permute-start | bytes 49160 | tf_op jit(solution)/shard_map/ppermute | solution.py:24
  15.0 5.0 %collective-permute-start.6 = (f32[2,32,64]{2,1,0:T(8,128)S(1)}, f32[2,32,64]{2,1,0:T(8,128)S(1)}, u32[]{:S(2)}, u32[]{:S(2)}) collective-permute-start(f32[2,32,64]{2,1,0:T(8,128)S(1)} %slice_add_fusion), channel_id=1, source_target_pairs={{0,8},{4,12},{8,0},{12,4},{1,9},{5,13},{9,1},{13,5},{2,10},{6,14},... | collective-permute-start | bytes 49160 | tf_op jit(solution)/shard_map/ppermute | solution.py:24
  16.5 3.7 %collective-permute-start.7 = (f32[2,32,64]{2,1,0:T(8,128)S(1)}, f32[2,32,64]{2,1,0:T(8,128)S(1)}, u32[]{:S(2)}, u32[]{:S(2)}) collective-permute-start(f32[2,32,64]{2,1,0:T(8,128)S(1)} %slice_add_fusion), channel_id=1, source_target_pairs={{0,12},{4,8},{8,4},{12,0},{1,13},{5,9},{9,5},{13,1},{2,14},{6,10},... | collective-permute-start | bytes 49160 | tf_op jit(solution)/shard_map/ppermute | solution.py:24
  20.0 0.6 %copy-start.5 = (f32[2,32,64]{2,1,0:T(8,128)}, f32[2,32,64]{2,1,0:T(8,128)S(1)}, u32[]{:S(2)}) copy-start(f32[2,32,64]{2,1,0:T(8,128)S(1)} %collective-permute-done.5.refs_11_) | copy-start | bytes 49156
  20.0 0.6 %copy-start.6 = (f32[2,32,64]{2,1,0:T(8,128)}, f32[2,32,64]{2,1,0:T(8,128)S(1)}, u32[]{:S(2)}) copy-start(f32[2,32,64]{2,1,0:T(8,128)S(1)} %collective-permute-done.6.refs_12_) | copy-start | bytes 49156
  20.2 0.6 %copy-start.7 = (f32[2,32,64]{2,1,0:T(8,128)}, f32[2,32,64]{2,1,0:T(8,128)S(1)}, u32[]{:S(2)}) copy-start(f32[2,32,64]{2,1,0:T(8,128)S(1)} %collective-permute-done.7.refs_13_) | copy-start | bytes 49156
  20.2 0.7 %copy-start = (bf16[160,512]{1,0:T(8,128)(2,1)}, bf16[160,512]{1,0:T(8,128)(2,1)S(1)}, u32[]{:S(2)}) copy-start(bf16[160,512]{1,0:T(8,128)(2,1)S(1)} %collective-permute-done.refs_3_) | copy-start | bytes 491524
  20.9 0.7 %copy-start.1 = (bf16[160,512]{1,0:T(8,128)(2,1)}, bf16[160,512]{1,0:T(8,128)(2,1)S(1)}, u32[]{:S(2)}) copy-start(bf16[160,512]{1,0:T(8,128)(2,1)S(1)} %collective-permute-done.1.refs_4_) | copy-start | bytes 491524

commit v7 on v6

--- a/solution.py
+++ b/solution.py
@@ -177,12 +177,13 @@
     )(embeddings, directions, level_basis)
 
     ndev = sub_size * leaf_size
-    from_pair = lax.ppermute(first, axes, [(i, i ^ 1) for i in range(ndev)])
-    from_cross = lax.ppermute(last, axes, [(i, i - 1 + 2 * (i % 2)) for i in range(1, ndev - 1)])
     round_one = [from_mask(payloads[mask.bit_length() - 1], "sub", mask) for mask in range(1, sub_size)]
     line = upper_own
     for got in round_one:
         line = line + got[1:]
+    first, last, line = lax.optimization_barrier((first, last, line))
+    from_pair = lax.ppermute(first, axes, [(i, i ^ 1) for i in range(ndev)])
+    from_cross = lax.ppermute(last, axes, [(i, i - 1 + 2 * (i % 2)) for i in range(1, ndev - 1)])
     round_two = [from_mask(line, "leaf", mask) for mask in range(1, leaf_size)]
 
     out = jax.ShapeDtypeStruct((nrhs, local_points), jnp.float32)

time: 25 us -> 28.4 us (1.14)
  waiting for transfers between devices: 2.87 us -> 4.76 us
  starting transfers between devices: 10.8 us -> 12.3 us
    ppermute x6, starting transfers between devices: 8.33 us -> 11.4 us  [from_mask(): return lax.ppermute(x, axis, pairs)]
    ppermute x6, waiting for transfers between devices: 2.86 us -> 4.75 us  [from_mask(): return lax.ppermute(x, axis, pairs)]
    ppermute x1, starting transfers between devices: 1.8 us -> 0.27 us  [on_device(): from_pair = lax.ppermute(first, axes, [(i, i ^ 1) for i in range(ndev)])]
    unnamed x16 -> x18, local copies, waits for them, and re-layouts: 1.36 us -> 1.35 us
  transfers between devices with their start and end apart: 8 -> 8, of which waited for: 3 -> 3; matrix products, arithmetic and copies ran while one was open for 3% -> 0% of each run, Pallas kernels for 14% -> 12%
where the time goes in v7:
time: 28.4 us; the launch traced here: 28.1 us
  starting transfers between devices  12.3 us (43%)
  Pallas kernels  8.8 us (31%)
  waiting for transfers between devices  4.76 us (17%)
  local copies, waits for them, and re-layouts  1.35 us (5%)
  other arithmetic  0.79 us (3%)
    ppermute x6, starting transfers between devices, from_mask(): return lax.ppermute(x, axis, pairs)  11.4 us
    ppermute x6, waiting for transfers between devices, from_mask(): return lax.ppermute(x, axis, pairs)  4.75 us
    pallas_call x1, Pallas kernels, on_device(): pl.pallas_call(functools.partial(local_kernel, sub_size), out_shape=out,...  3.49 us
    pallas_call x1, Pallas kernels, on_device(): pl.pallas_call(functools.partial(final_kernel, sub_size, sub_bits, leaf_b...  3.11 us
    pallas_call x1, Pallas kernels, on_device(): pl.pallas_call(functools.partial(send_kernel, loc_bits, sub_bits), out_sh...  2.2 us
    unnamed x18, local copies, waits for them, and re-layouts  1.35 us
    add x1, other arithmetic, on_device(): line = line + got[1:]  0.79 us
    ppermute x1, starting transfers between devices, on_device(): lax.ppermute(last, axes, [(i, i - 1 + 2 * (i % 2)) for i in range(1, ndev...  0.66 us
  transfers between devices with their start and end apart: 8, of which 3 were waited for; matrix products, arithmetic and copies ran while one was open for 0% of the time, Pallas kernels for 12%

profile of v7, /device:TPU:0, one launch (start us, length us, event | category | flops | bytes accessed | tf_op | source)
XLA Modules:
  0.0 28.1 jit_solution(8084564091624087305)
XLA Ops:
  0.0 2.2 %shard_map.56 = (bf16[160,512]{1,0:T(8,128)(2,1)}, bf16[160,512]{1,0:T(8,128)(2,1)}, f32[2,32,64]{2,1,0:T(8,128)}, f32[3,32,64]{2,1,0:T(8,128)}, f32[3,32,64]{2,1,0:T(8,128)}) custom-call(bf16[128,1024]{1,0:T(8,128)(2,1)} %refs_0_.1, f32[32,1024]{1,0:T(8,128)} %refs_1_.1, bf16[5,64,1024]{2,1,0:T(8,128)(2,1)} %refs_5_.1), custom_call_target="tpu_custom_call" | custom-call | tf_op jit(solution)/shard_map/pallas_call | solution.py:172
  2.2 0.0 copy-start.8
  2.2 4.0 %collective-permute-start.1 = (f32[3,32,64]{2,1,0:T(8,128)}, f32[3,32,64]{2,1,0:T(8,128)S(1)}, u32[]{:S(2)}, u32[]{:S(2)}) collective-permute-start(f32[3,32,64]{2,1,0:T(8,128)} %get-tuple-element.17), channel_id=1, source_target_pairs={{0,2},{1,3},{2,0},{3,1},{4,6},{5,7},{6,4},{7,5},{8,10},{9,11},{10,... | collective-permute-start | bytes 73736 | tf_op jit(solution)/shard_map/ppermute | solution.py:24
  6.2 1.3 %collective-permute-start.2 = (f32[3,32,64]{2,1,0:T(8,128)}, f32[3,32,64]{2,1,0:T(8,128)S(1)}, u32[]{:S(2)}, u32[]{:S(2)}) collective-permute-start(f32[3,32,64]{2,1,0:T(8,128)} %get-tuple-element.17), channel_id=1, source_target_pairs={{0,3},{1,2},{2,1},{3,0},{4,7},{5,6},{6,5},{7,4},{8,11},{9,10},{10,... | collective-permute-start | bytes 73736 | tf_op jit(solution)/shard_map/ppermute | solution.py:24
  7.6 0.2 collective-permute-start
  7.8 1.2 %collective-permute-done.1.refs_9_ = f32[3,32,64]{2,1,0:T(8,128)S(1)} collective-permute-done((f32[3,32,64]{2,1,0:T(8,128)}, f32[3,32,64]{2,1,0:T(8,128)S(1)}, u32[]{:S(2)}, u32[]{:S(2)}) %collective-permute-start.1) | collective-permute-done | bytes 24608 | tf_op jit(solution)/shard_map/ppermute | solution.py:24
  9.0 0.0 copy-start.2
  9.0 3.4 %collective-permute-done.2.refs_10_ = f32[3,32,64]{2,1,0:T(8,128)S(1)} collective-permute-done((f32[3,32,64]{2,1,0:T(8,128)}, f32[3,32,64]{2,1,0:T(8,128)S(1)}, u32[]{:S(2)}, u32[]{:S(2)}) %collective-permute-start.2) | collective-permute-done | bytes 24608 | tf_op jit(solution)/shard_map/ppermute | solution.py:24
  12.4 0.0 copy-start.3
  12.4 0.0 collective-permute-done.refs_8_
  12.4 0.0 copy-start.4
  12.4 0.8 %slice_add_fusion = f32[2,32,64]{2,1,0:T(8,128)S(1)} fusion(f32[3,32,64]{2,1,0:T(8,128)S(1)} %collective-permute-done.2.refs_10_, f32[3,32,64]{2,1,0:T(8,128)S(1)} %collective-permute-done.1.refs_9_, f32[2,32,64]{2,1,0:T(8,128)} %get-tuple-element.15, f32[3,32,64]{2,1,0:T(8,128)S(1)} %collective-permute-done.refs_8_), kind=kLoop, calls=%fused_computation | loop fusion | flops 12288 | bytes 81920 | tf_op jit(solution)/shard_map/add | solution.py:183
  13.2 0.0 copy-done.2
  13.2 0.0 copy-done.3
  13.2 0.0 copy-done.4
  13.3 0.3 collective-permute-start.3
  13.5 0.0 copy-done.8
  13.5 0.7 %collective-permute-start.4 = (bf16[160,512]{1,0:T(8,128)(2,1)S(1)}, bf16[160,512]{1,0:T(8,128)(2,1)S(1)}, u32[]{:S(2)}, u32[]{:S(2)}) collective-permute-start(bf16[160,512]{1,0:T(8,128)(2,1)S(1)} %copy-done.8), channel_id=1, source_target_pairs={{1,2},{2,1},{3,4},{4,3},{5,6},{6,5},{7,8},{8,7},{9,10},{10,9},{11,... | collective-permute-start | bytes 491528 | tf_op jit(solution)/shard_map/ppermute | solution.py:186
  14.2 4.3 %collective-permute-start.5 = (f32[2,32,64]{2,1,0:T(8,128)S(1)}, f32[2,32,64]{2,1,0:T(8,128)S(1)}, u32[]{:S(2)}, u32[]{:S(2)}) collective-permute-start(f32[2,32,64]{2,1,0:T(8,128)S(1)} %slice_add_fusion), channel_id=1, source_target_pairs={{0,4},{4,0},{8,12},{12,8},{1,5},{5,1},{9,13},{13,9},{2,6},{6,2},{1... | collective-permute-start | bytes 49160 | tf_op jit(solution)/shard_map/ppermute | solution.py:24
  18.4 1.5 %collective-permute-start.6 = (f32[2,32,64]{2,1,0:T(8,128)S(1)}, f32[2,32,64]{2,1,0:T(8,128)S(1)}, u32[]{:S(2)}, u32[]{:S(2)}) collective-permute-start(f32[2,32,64]{2,1,0:T(8,128)S(1)} %slice_add_fusion), channel_id=1, source_target_pairs={{0,8},{4,12},{8,0},{12,4},{1,9},{5,13},{9,1},{13,5},{2,10},{6,14},... | collective-permute-start | bytes 49160 | tf_op jit(solution)/shard_map/ppermute | solution.py:24
  19.9 0.0 collective-permute-start.7
  19.9 3.5 %shard_map.55.refs_2_ = f32[32,1024]{1,0:T(8,128)} custom-call(bf16[128,1024]{1,0:T(8,128)(2,1)} %refs_0_.1, f32[32,1024]{1,0:T(8,128)} %refs_1_.1, bf16[5,64,1024]{2,1,0:T(8,128)(2,1)} %refs_5_.1, s32[2,8]{1,0:T(2,128)} %refs_6_.1, s32[2]{0:T(128)} %refs_7_.1), custom_call_target="tpu_custom_call" | custom-call | tf_op jit(solution)/shard_map/pallas_call | solution.py:190
  23.4 0.0 collective-permute-done.5.refs_11_
  23.4 0.0 copy-start.5
  23.4 0.0 collective-permute-done.6.refs_12_
  23.4 0.0 copy-start.6
  23.4 0.2 collective-permute-done.7.refs_13_
  23.6 0.0 copy-start.7
  23.6 0.0 collective-permute-done.3.refs_3_
  23.6 0.0 copy-start
  23.6 0.0 collective-permute-done.4.refs_4_
  23.6 0.4 %copy-done.5 = f32[2,32,64]{2,1,0:T(8,128)} copy-done((f32[2,32,64]{2,1,0:T(8,128)}, f32[2,32,64]{2,1,0:T(8,128)S(1)}, u32[]{:S(2)}) %copy-start.5) | copy-done | bytes 16408
  24.0 0.0 copy-done.6
  24.1 0.2 copy-done.7
  24.2 0.1 copy-done
  24.3 0.0 copy-start.1
  24.3 0.7 %copy-done.1 = bf16[160,512]{1,0:T(8,128)(2,1)} copy-done((bf16[160,512]{1,0:T(8,128)(2,1)}, bf16[160,512]{1,0:T(8,128)(2,1)S(1)}, u32[]{:S(2)}) %copy-start.1) | copy-done | bytes 163864
  25.0 3.1 %shard_map.57 = f32[32,1024]{1,0:T(8,128)} custom-call(bf16[128,1024]{1,0:T(8,128)(2,1)} %refs_0_.1, f32[32,1024]{1,0:T(8,128)} %refs_1_.1, f32[32,1024]{1,0:T(8,128)} %shard_map.55.refs_2_, bf16[160,512]{1,0:T(8,128)(2,1)} %copy-done, bf16[160,512]{1,0:T(8,128)(2,1)} %copy-done.1, bf16[5,64,1024]{2,1,0:T(8,128)(2,1)} %refs_5_.1, ...), custom_call_target="tpu_custom_call", output_to_operand_aliasing={{}: (2, {})} | custom-call | tf_op jit(solution)/shard_map/pallas_call | solution.py:198
Async XLA Ops:
  2.2 11.3 %copy-start.8 = (bf16[160,512]{1,0:T(8,128)(2,1)S(1)}, bf16[160,512]{1,0:T(8,128)(2,1)}, u32[]{:S(2)}) copy-start(bf16[160,512]{1,0:T(8,128)(2,1)} %get-tuple-element.19) | copy-start | bytes 491524
  2.2 6.8 %collective-permute-start.1 = (f32[3,32,64]{2,1,0:T(8,128)}, f32[3,32,64]{2,1,0:T(8,128)S(1)}, u32[]{:S(2)}, u32[]{:S(2)}) collective-permute-start(f32[3,32,64]{2,1,0:T(8,128)} %get-tuple-element.17), channel_id=1, source_target_pairs={{0,2},{1,3},{2,0},{3,1},{4,6},{5,7},{6,4},{7,5},{8,10},{9,11},{10,... | collective-permute-start | bytes 73736 | tf_op jit(solution)/shard_map/ppermute | solution.py:24
  6.2 6.2 %collective-permute-start.2 = (f32[3,32,64]{2,1,0:T(8,128)}, f32[3,32,64]{2,1,0:T(8,128)S(1)}, u32[]{:S(2)}, u32[]{:S(2)}) collective-permute-start(f32[3,32,64]{2,1,0:T(8,128)} %get-tuple-element.17), channel_id=1, source_target_pairs={{0,3},{1,2},{2,1},{3,0},{4,7},{5,6},{6,5},{7,4},{8,11},{9,10},{10,... | collective-permute-start | bytes 73736 | tf_op jit(solution)/shard_map/ppermute | solution.py:24
  7.6 4.8 %collective-permute-start = (f32[3,32,64]{2,1,0:T(8,128)}, f32[3,32,64]{2,1,0:T(8,128)S(1)}, u32[]{:S(2)}, u32[]{:S(2)}) collective-permute-start(f32[3,32,64]{2,1,0:T(8,128)} %get-tuple-element.16), channel_id=1, source_target_pairs={{0,1},{1,0},{2,3},{3,2},{4,5},{5,4},{6,7},{7,6},{8,9},{9,8},{10,11... | collective-permute-start | bytes 73736 | tf_op jit(solution)/shard_map/ppermute | solution.py:24
  9.0 4.2 %copy-start.2 = (f32[3,32,64]{2,1,0:T(8,128)}, f32[3,32,64]{2,1,0:T(8,128)S(1)}, u32[]{:S(2)}) copy-start(f32[3,32,64]{2,1,0:T(8,128)S(1)} %collective-permute-done.1.refs_9_) | copy-start | bytes 73732
  12.4 0.8 %copy-start.3 = (f32[3,32,64]{2,1,0:T(8,128)}, f32[3,32,64]{2,1,0:T(8,128)S(1)}, u32[]{:S(2)}) copy-start(f32[3,32,64]{2,1,0:T(8,128)S(1)} %collective-permute-done.2.refs_10_) | copy-start | bytes 73732
  12.4 0.8 %copy-start.4 = (f32[3,32,64]{2,1,0:T(8,128)}, f32[3,32,64]{2,1,0:T(8,128)S(1)}, u32[]{:S(2)}) copy-start(f32[3,32,64]{2,1,0:T(8,128)S(1)} %collective-permute-done.refs_8_) | copy-start | bytes 73732
  13.3 10.4 %collective-permute-start.3 = (bf16[160,512]{1,0:T(8,128)(2,1)}, bf16[160,512]{1,0:T(8,128)(2,1)S(1)}, u32[]{:S(2)}, u32[]{:S(2)}) collective-permute-start(bf16[160,512]{1,0:T(8,128)(2,1)} %get-tuple-element.18), channel_id=1, source_target_pairs={{0,1},{1,0},{2,3},{3,2},{4,5},{5,4},{6,7},{7,6},{8,9},{9,8},{10,11... | collective-permute-start | bytes 491528 | tf_op jit(solution)/shard_map/ppermute | solution.py:185
  13.5 10.1 %collective-permute-start.4 = (bf16[160,512]{1,0:T(8,128)(2,1)S(1)}, bf16[160,512]{1,0:T(8,128)(2,1)S(1)}, u32[]{:S(2)}, u32[]{:S(2)}) collective-permute-start(bf16[160,512]{1,0:T(8,128)(2,1)S(1)} %copy-done.8), channel_id=1, source_target_pairs={{1,2},{2,1},{3,4},{4,3},{5,6},{6,5},{7,8},{8,7},{9,10},{10,9},{11,... | collective-permute-start | bytes 491528 | tf_op jit(solution)/shard_map/ppermute | solution.py:186
  14.2 9.2 %collective-permute-start.5 = (f32[2,32,64]{2,1,0:T(8,128)S(1)}, f32[2,32,64]{2,1,0:T(8,128)S(1)}, u32[]{:S(2)}, u32[]{:S(2)}) collective-permute-start(f32[2,32,64]{2,1,0:T(8,128)S(1)} %slice_add_fusion), channel_id=1, source_target_pairs={{0,4},{4,0},{8,12},{12,8},{1,5},{5,1},{9,13},{13,9},{2,6},{6,2},{1... | collective-permute-start | bytes 49160 | tf_op jit(solution)/shard_map/ppermute | solution.py:24
  18.4 5.0 %collective-permute-start.6 = (f32[2,32,64]{2,1,0:T(8,128)S(1)}, f32[2,32,64]{2,1,0:T(8,128)S(1)}, u32[]{:S(2)}, u32[]{:S(2)}) collective-permute-start(f32[2,32,64]{2,1,0:T(8,128)S(1)} %slice_add_fusion), channel_id=1, source_target_pairs={{0,8},{4,12},{8,0},{12,4},{1,9},{5,13},{9,1},{13,5},{2,10},{6,14},... | collective-permute-start | bytes 49160 | tf_op jit(solution)/shard_map/ppermute | solution.py:24
  19.9 3.7 %collective-permute-start.7 = (f32[2,32,64]{2,1,0:T(8,128)S(1)}, f32[2,32,64]{2,1,0:T(8,128)S(1)}, u32[]{:S(2)}, u32[]{:S(2)}) collective-permute-start(f32[2,32,64]{2,1,0:T(8,128)S(1)} %slice_add_fusion), channel_id=1, source_target_pairs={{0,12},{4,8},{8,4},{12,0},{1,13},{5,9},{9,5},{13,1},{2,14},{6,10},... | collective-permute-start | bytes 49160 | tf_op jit(solution)/shard_map/ppermute | solution.py:24
  23.4 0.6 %copy-start.5 = (f32[2,32,64]{2,1,0:T(8,128)}, f32[2,32,64]{2,1,0:T(8,128)S(1)}, u32[]{:S(2)}) copy-start(f32[2,32,64]{2,1,0:T(8,128)S(1)} %collective-permute-done.5.refs_11_) | copy-start | bytes 49156
  23.4 0.6 %copy-start.6 = (f32[2,32,64]{2,1,0:T(8,128)}, f32[2,32,64]{2,1,0:T(8,128)S(1)}, u32[]{:S(2)}) copy-start(f32[2,32,64]{2,1,0:T(8,128)S(1)} %collective-permute-done.6.refs_12_) | copy-start | bytes 49156
  23.6 0.6 %copy-start.7 = (f32[2,32,64]{2,1,0:T(8,128)}, f32[2,32,64]{2,1,0:T(8,128)S(1)}, u32[]{:S(2)}) copy-start(f32[2,32,64]{2,1,0:T(8,128)S(1)} %collective-permute-done.7.refs_13_) | copy-start | bytes 49156
  23.6 0.7 %copy-start = (bf16[160,512]{1,0:T(8,128)(2,1)}, bf16[160,512]{1,0:T(8,128)(2,1)S(1)}, u32[]{:S(2)}) copy-start(bf16[160,512]{1,0:T(8,128)(2,1)S(1)} %collective-permute-done.3.refs_3_) | copy-start | bytes 491524
  24.3 0.7 %copy-start.1 = (bf16[160,512]{1,0:T(8,128)(2,1)}, bf16[160,512]{1,0:T(8,128)(2,1)S(1)}, u32[]{:S(2)}) copy-start(bf16[160,512]{1,0:T(8,128)(2,1)S(1)} %collective-permute-done.4.refs_4_) | copy-start | bytes 491524

commit v8 on v6

--- a/solution.py
+++ b/solution.py
@@ -62,19 +62,19 @@
         emb_float = emb_ref[...].astype(jnp.float32)
         row_norms = jnp.sum(emb_float * emb_float, axis=0, keepdims=True)
         emb_t = emb_float.T
-        self.col_norms = jnp.sum(emb_t * emb_t, axis=1, keepdims=True)
-        self.emb_t = emb_t.astype(jnp.bfloat16)
+        self.col_terms = -DISTANCE_SCALE * jnp.sum(emb_t * emb_t, axis=1, keepdims=True)
+        self.emb_t = (emb_t * (2.0 * DISTANCE_SCALE)).astype(jnp.bfloat16)
         self.points = [emb_ref[:, j * LEAF : (j + 1) * LEAF] for j in range(self.count)]
-        self.norms = [row_norms[:, j * LEAF : (j + 1) * LEAF] for j in range(self.count)]
+        self.norms = [-DISTANCE_SCALE * row_norms[:, j * LEAF : (j + 1) * LEAF] for j in range(self.count)]
         self.leaf_values = [self.values[:, j * LEAF : (j + 1) * LEAF] for j in range(self.count)]
         self.neighbours_ref = neighbours_ref
         self.counts_ref = counts_ref
         self.me = lax.axis_index("leaf") * sub_size + lax.axis_index("sub")
 
-    def block(self, j, source_points, source_norms):
+    def block(self, j, source_points, source_terms):
         inner = nn_dot(self.emb_t[j * LEAF : (j + 1) * LEAF], source_points)
-        distance = self.col_norms[j * LEAF : (j + 1) * LEAF] + source_norms - 2.0 * inner
-        return (AMPLITUDE * jnp.exp(-DISTANCE_SCALE * distance)).astype(jnp.bfloat16)
+        exponent = (self.col_terms[j * LEAF : (j + 1) * LEAF] + source_terms) + inner
+        return (AMPLITUDE * jnp.exp(exponent)).astype(jnp.bfloat16)
 
     def weight(self, j, offset):
         leaf = self.me * self.count + j
@@ -142,7 +142,7 @@
     for j, received, offset in ((0, left, -1), (lv.count - 1, right, 1)):
         halo_points = received[: lv.width_e, :]
         halo_float = halo_points.astype(jnp.float32)
-        halo_norms = jnp.sum(halo_float * halo_float, axis=0, keepdims=True)
+        halo_norms = -DISTANCE_SCALE * jnp.sum(halo_float * halo_float, axis=0, keepdims=True)
         weights = lv.block(j, halo_points, halo_norms)
         term = lv.weight(j, offset) * nt_dot(received[lv.width_e :, :], weights)
         halo[j] = term if j not in halo else halo[j] + term

time: 25 us -> 25.1 us (level)
  no operation moved by 1% of the time
where the time goes in v8:
time: 25.1 us; the launch traced here: 24.7 us
  starting transfers between devices  10.8 us (43%)
  Pallas kernels  8.86 us (35%)
  waiting for transfers between devices  2.78 us (11%)
  local copies, waits for them, and re-layouts  1.36 us (5%)
  other arithmetic  0.79 us (3%)
    ppermute x6, starting transfers between devices, from_mask(): return lax.ppermute(x, axis, pairs)  8.33 us
    pallas_call x1, Pallas kernels, on_device(): pl.pallas_call(functools.partial(local_kernel, sub_size), out_shape=out,...  3.58 us
    pallas_call x1, Pallas kernels, on_device(): pl.pallas_call(functools.partial(final_kernel, sub_size, sub_bits, leaf_b...  3.09 us
    ppermute x6, waiting for transfers between devices, from_mask(): return lax.ppermute(x, axis, pairs)  2.78 us
    pallas_call x1, Pallas kernels, on_device(): pl.pallas_call(functools.partial(send_kernel, loc_bits, sub_bits), out_sh...  2.19 us
    ppermute x1, starting transfers between devices, on_device(): from_pair = lax.ppermute(first, axes, [(i, i ^ 1) for i in range(ndev)])  1.8 us
    unnamed x16, local copies, waits for them, and re-layouts  1.36 us
    add x1, other arithmetic, on_device(): line = line + got[1:]  0.79 us
  transfers between devices with their start and end apart: 8, of which 3 were waited for; matrix products, arithmetic and copies ran while one was open for 3% of the time, Pallas kernels for 14%

profile of v8, /device:TPU:0, one launch (start us, length us, event | category | flops | bytes accessed | tf_op | source)
XLA Modules:
  0.0 24.7 jit_solution(2064914437715518773)
XLA Ops:
  0.0 2.2 %shard_map.56 = (bf16[160,512]{1,0:T(8,128)(2,1)}, bf16[160,512]{1,0:T(8,128)(2,1)}, f32[2,32,64]{2,1,0:T(8,128)}, f32[3,32,64]{2,1,0:T(8,128)}, f32[3,32,64]{2,1,0:T(8,128)}) custom-call(bf16[128,1024]{1,0:T(8,128)(2,1)} %refs_0_.1, f32[32,1024]{1,0:T(8,128)} %refs_1_.1, bf16[5,64,1024]{2,1,0:T(8,128)(2,1)} %refs_5_.1), custom_call_target="tpu_custom_call" | custom-call | tf_op jit(solution)/shard_map/pallas_call | solution.py:172
  2.2 4.0 %collective-permute-start.3 = (f32[3,32,64]{2,1,0:T(8,128)}, f32[3,32,64]{2,1,0:T(8,128)S(1)}, u32[]{:S(2)}, u32[]{:S(2)}) collective-permute-start(f32[3,32,64]{2,1,0:T(8,128)} %get-tuple-element.13), channel_id=1, source_target_pairs={{0,2},{1,3},{2,0},{3,1},{4,6},{5,7},{6,4},{7,5},{8,10},{9,11},{10,... | collective-permute-start | bytes 73736 | tf_op jit(solution)/shard_map/ppermute | solution.py:24
  6.2 1.3 %collective-permute-start.4 = (f32[3,32,64]{2,1,0:T(8,128)}, f32[3,32,64]{2,1,0:T(8,128)S(1)}, u32[]{:S(2)}, u32[]{:S(2)}) collective-permute-start(f32[3,32,64]{2,1,0:T(8,128)} %get-tuple-element.13), channel_id=1, source_target_pairs={{0,3},{1,2},{2,1},{3,0},{4,7},{5,6},{6,5},{7,4},{8,11},{9,10},{10,... | collective-permute-start | bytes 73736 | tf_op jit(solution)/shard_map/ppermute | solution.py:24
  7.6 0.2 collective-permute-start.2
  7.8 1.8 %collective-permute-start = (bf16[160,512]{1,0:T(8,128)(2,1)}, bf16[160,512]{1,0:T(8,128)(2,1)S(1)}, u32[]{:S(2)}, u32[]{:S(2)}) collective-permute-start(bf16[160,512]{1,0:T(8,128)(2,1)} %get-tuple-element.10), channel_id=1, source_target_pairs={{0,1},{1,0},{2,3},{3,2},{4,5},{5,4},{6,7},{7,6},{8,9},{9,8},{10,11... | collective-permute-start | bytes 491528 | tf_op jit(solution)/shard_map/ppermute | solution.py:180
  9.6 0.7 %collective-permute-start.1 = (bf16[160,512]{1,0:T(8,128)(2,1)}, bf16[160,512]{1,0:T(8,128)(2,1)S(1)}, u32[]{:S(2)}, u32[]{:S(2)}) collective-permute-start(bf16[160,512]{1,0:T(8,128)(2,1)} %get-tuple-element.11), channel_id=1, source_target_pairs={{1,2},{2,1},{3,4},{4,3},{5,6},{6,5},{7,8},{8,7},{9,10},{10,9},{11,... | collective-permute-start | bytes 491528 | tf_op jit(solution)/shard_map/ppermute | solution.py:181
  10.3 0.0 collective-permute-done.3.refs_9_
  10.3 0.0 copy-start.2
  10.3 2.5 %collective-permute-done.4.refs_10_ = f32[3,32,64]{2,1,0:T(8,128)S(1)} collective-permute-done((f32[3,32,64]{2,1,0:T(8,128)}, f32[3,32,64]{2,1,0:T(8,128)S(1)}, u32[]{:S(2)}, u32[]{:S(2)}) %collective-permute-start.4) | collective-permute-done | bytes 24608 | tf_op jit(solution)/shard_map/ppermute | solution.py:24
  12.8 0.0 copy-start.3
  12.8 0.2 collective-permute-done.2.refs_8_
  13.0 0.0 copy-start.4
  13.0 0.8 %slice_add_fusion = f32[2,32,64]{2,1,0:T(8,128)S(1)} fusion(f32[3,32,64]{2,1,0:T(8,128)S(1)} %collective-permute-done.4.refs_10_, f32[3,32,64]{2,1,0:T(8,128)S(1)} %collective-permute-done.3.refs_9_, f32[2,32,64]{2,1,0:T(8,128)} %get-tuple-element.14, f32[3,32,64]{2,1,0:T(8,128)S(1)} %collective-permute-done.2.refs_8_), kind=kLoop, calls=%fused_computation | loop fusion | flops 12288 | bytes 81920 | tf_op jit(solution)/shard_map/add | solution.py:185
  13.8 0.0 copy-done.2
  13.8 0.0 copy-done.3
  13.8 0.0 copy-done.4
  13.8 1.2 %collective-permute-start.5 = (f32[2,32,64]{2,1,0:T(8,128)S(1)}, f32[2,32,64]{2,1,0:T(8,128)S(1)}, u32[]{:S(2)}, u32[]{:S(2)}) collective-permute-start(f32[2,32,64]{2,1,0:T(8,128)S(1)} %slice_add_fusion), channel_id=1, source_target_pairs={{0,4},{4,0},{8,12},{12,8},{1,5},{5,1},{9,13},{13,9},{2,6},{6,2},{1... | collective-permute-start | bytes 49160 | tf_op jit(solution)/shard_map/ppermute | solution.py:24
  15.0 1.5 %collective-permute-start.6 = (f32[2,32,64]{2,1,0:T(8,128)S(1)}, f32[2,32,64]{2,1,0:T(8,128)S(1)}, u32[]{:S(2)}, u32[]{:S(2)}) collective-permute-start(f32[2,32,64]{2,1,0:T(8,128)S(1)} %slice_add_fusion), channel_id=1, source_target_pairs={{0,8},{4,12},{8,0},{12,4},{1,9},{5,13},{9,1},{13,5},{2,10},{6,14},... | collective-permute-start | bytes 49160 | tf_op jit(solution)/shard_map/ppermute | solution.py:24
  16.5 0.0 collective-permute-start.7
  16.5 3.6 %shard_map.55.refs_2_ = f32[32,1024]{1,0:T(8,128)} custom-call(bf16[128,1024]{1,0:T(8,128)(2,1)} %refs_0_.1, f32[32,1024]{1,0:T(8,128)} %refs_1_.1, bf16[5,64,1024]{2,1,0:T(8,128)(2,1)} %refs_5_.1, s32[2,8]{1,0:T(2,128)} %refs_6_.1, s32[2]{0:T(128)} %refs_7_.1), custom_call_target="tpu_custom_call" | custom-call | tf_op jit(solution)/shard_map/pallas_call | solution.py:189
  20.1 0.0 collective-permute-done.5.refs_11_
  20.1 0.0 copy-start.5
  20.1 0.0 collective-permute-done.6.refs_12_
  20.1 0.0 copy-start.6
  20.1 0.1 collective-permute-done.7.refs_13_
  20.2 0.0 copy-start.7
  20.2 0.0 collective-permute-done.refs_3_
  20.2 0.0 copy-start
  20.2 0.0 collective-permute-done.1.refs_4_
  20.2 0.5 %copy-done.5 = f32[2,32,64]{2,1,0:T(8,128)} copy-done((f32[2,32,64]{2,1,0:T(8,128)}, f32[2,32,64]{2,1,0:T(8,128)S(1)}, u32[]{:S(2)}) %copy-start.5) | copy-done | bytes 16408
  20.7 0.0 copy-done.6
  20.7 0.1 copy-done.7
  20.8 0.1 copy-done
  20.9 0.0 copy-start.1
  20.9 0.7 %copy-done.1 = bf16[160,512]{1,0:T(8,128)(2,1)} copy-done((bf16[160,512]{1,0:T(8,128)(2,1)}, bf16[160,512]{1,0:T(8,128)(2,1)S(1)}, u32[]{:S(2)}) %copy-start.1) | copy-done | bytes 163864
  21.6 3.1 %shard_map.57 = f32[32,1024]{1,0:T(8,128)} custom-call(bf16[128,1024]{1,0:T(8,128)(2,1)} %refs_0_.1, f32[32,1024]{1,0:T(8,128)} %refs_1_.1, f32[32,1024]{1,0:T(8,128)} %shard_map.55.refs_2_, bf16[160,512]{1,0:T(8,128)(2,1)} %copy-done, bf16[160,512]{1,0:T(8,128)(2,1)} %copy-done.1, bf16[5,64,1024]{2,1,0:T(8,128)(2,1)} %refs_5_.1, ...), custom_call_target="tpu_custom_call", output_to_operand_aliasing={{}: (2, {})} | custom-call | tf_op jit(solution)/shard_map/pallas_call | solution.py:197
Async XLA Ops:
  2.2 8.1 %collective-permute-start.3 = (f32[3,32,64]{2,1,0:T(8,128)}, f32[3,32,64]{2,1,0:T(8,128)S(1)}, u32[]{:S(2)}, u32[]{:S(2)}) collective-permute-start(f32[3,32,64]{2,1,0:T(8,128)} %get-tuple-element.13), channel_id=1, source_target_pairs={{0,2},{1,3},{2,0},{3,1},{4,6},{5,7},{6,4},{7,5},{8,10},{9,11},{10,... | collective-permute-start | bytes 73736 | tf_op jit(solution)/shard_map/ppermute | solution.py:24
  6.2 6.6 %collective-permute-start.4 = (f32[3,32,64]{2,1,0:T(8,128)}, f32[3,32,64]{2,1,0:T(8,128)S(1)}, u32[]{:S(2)}, u32[]{:S(2)}) collective-permute-start(f32[3,32,64]{2,1,0:T(8,128)} %get-tuple-element.13), channel_id=1, source_target_pairs={{0,3},{1,2},{2,1},{3,0},{4,7},{5,6},{6,5},{7,4},{8,11},{9,10},{10,... | collective-permute-start | bytes 73736 | tf_op jit(solution)/shard_map/ppermute | solution.py:24
  7.6 5.4 %collective-permute-start.2 = (f32[3,32,64]{2,1,0:T(8,128)}, f32[3,32,64]{2,1,0:T(8,128)S(1)}, u32[]{:S(2)}, u32[]{:S(2)}) collective-permute-start(f32[3,32,64]{2,1,0:T(8,128)} %get-tuple-element.12), channel_id=1, source_target_pairs={{0,1},{1,0},{2,3},{3,2},{4,5},{5,4},{6,7},{7,6},{8,9},{9,8},{10,11... | collective-permute-start | bytes 73736 | tf_op jit(solution)/shard_map/ppermute | solution.py:24
  7.8 12.4 %collective-permute-start = (bf16[160,512]{1,0:T(8,128)(2,1)}, bf16[160,512]{1,0:T(8,128)(2,1)S(1)}, u32[]{:S(2)}, u32[]{:S(2)}) collective-permute-start(bf16[160,512]{1,0:T(8,128)(2,1)} %get-tuple-element.10), channel_id=1, source_target_pairs={{0,1},{1,0},{2,3},{3,2},{4,5},{5,4},{6,7},{7,6},{8,9},{9,8},{10,11... | collective-permute-start | bytes 491528 | tf_op jit(solution)/shard_map/ppermute | solution.py:180
  9.6 10.6 %collective-permute-start.1 = (bf16[160,512]{1,0:T(8,128)(2,1)}, bf16[160,512]{1,0:T(8,128)(2,1)S(1)}, u32[]{:S(2)}, u32[]{:S(2)}) collective-permute-start(bf16[160,512]{1,0:T(8,128)(2,1)} %get-tuple-element.11), channel_id=1, source_target_pairs={{1,2},{2,1},{3,4},{4,3},{5,6},{6,5},{7,8},{8,7},{9,10},{10,9},{11,... | collective-permute-start | bytes 491528 | tf_op jit(solution)/shard_map/ppermute | solution.py:181
  10.3 3.5 %copy-start.2 = (f32[3,32,64]{2,1,0:T(8,128)}, f32[3,32,64]{2,1,0:T(8,128)S(1)}, u32[]{:S(2)}) copy-start(f32[3,32,64]{2,1,0:T(8,128)S(1)} %collective-permute-done.3.refs_9_) | copy-start | bytes 73732
  12.8 1.0 %copy-start.3 = (f32[3,32,64]{2,1,0:T(8,128)}, f32[3,32,64]{2,1,0:T(8,128)S(1)}, u32[]{:S(2)}) copy-start(f32[3,32,64]{2,1,0:T(8,128)S(1)} %collective-permute-done.4.refs_10_) | copy-start | bytes 73732
  13.0 0.8 %copy-start.4 = (f32[3,32,64]{2,1,0:T(8,128)}, f32[3,32,64]{2,1,0:T(8,128)S(1)}, u32[]{:S(2)}) copy-start(f32[3,32,64]{2,1,0:T(8,128)S(1)} %collective-permute-done.2.refs_8_) | copy-start | bytes 73732
  13.8 6.3 %collective-permute-start.5 = (f32[2,32,64]{2,1,0:T(8,128)S(1)}, f32[2,32,64]{2,1,0:T(8,128)S(1)}, u32[]{:S(2)}, u32[]{:S(2)}) collective-permute-start(f32[2,32,64]{2,1,0:T(8,128)S(1)} %slice_add_fusion), channel_id=1, source_target_pairs={{0,4},{4,0},{8,12},{12,8},{1,5},{5,1},{9,13},{13,9},{2,6},{6,2},{1... | collective-permute-start | bytes 49160 | tf_op jit(solution)/shard_map/ppermute | solution.py:24
  15.0 5.1 %collective-permute-start.6 = (f32[2,32,64]{2,1,0:T(8,128)S(1)}, f32[2,32,64]{2,1,0:T(8,128)S(1)}, u32[]{:S(2)}, u32[]{:S(2)}) collective-permute-start(f32[2,32,64]{2,1,0:T(8,128)S(1)} %slice_add_fusion), channel_id=1, source_target_pairs={{0,8},{4,12},{8,0},{12,4},{1,9},{5,13},{9,1},{13,5},{2,10},{6,14},... | collective-permute-start | bytes 49160 | tf_op jit(solution)/shard_map/ppermute | solution.py:24
  16.5 3.7 %collective-permute-start.7 = (f32[2,32,64]{2,1,0:T(8,128)S(1)}, f32[2,32,64]{2,1,0:T(8,128)S(1)}, u32[]{:S(2)}, u32[]{:S(2)}) collective-permute-start(f32[2,32,64]{2,1,0:T(8,128)S(1)} %slice_add_fusion), channel_id=1, source_target_pairs={{0,12},{4,8},{8,4},{12,0},{1,13},{5,9},{9,5},{13,1},{2,14},{6,10},... | collective-permute-start | bytes 49160 | tf_op jit(solution)/shard_map/ppermute | solution.py:24
  20.1 0.6 %copy-start.5 = (f32[2,32,64]{2,1,0:T(8,128)}, f32[2,32,64]{2,1,0:T(8,128)S(1)}, u32[]{:S(2)}) copy-start(f32[2,32,64]{2,1,0:T(8,128)S(1)} %collective-permute-done.5.refs_11_) | copy-start | bytes 49156
  20.1 0.6 %copy-start.6 = (f32[2,32,64]{2,1,0:T(8,128)}, f32[2,32,64]{2,1,0:T(8,128)S(1)}, u32[]{:S(2)}) copy-start(f32[2,32,64]{2,1,0:T(8,128)S(1)} %collective-permute-done.6.refs_12_) | copy-start | bytes 49156
  20.2 0.6 %copy-start.7 = (f32[2,32,64]{2,1,0:T(8,128)}, f32[2,32,64]{2,1,0:T(8,128)S(1)}, u32[]{:S(2)}) copy-start(f32[2,32,64]{2,1,0:T(8,128)S(1)} %collective-permute-done.7.refs_13_) | copy-start | bytes 49156
  20.2 0.7 %copy-start = (bf16[160,512]{1,0:T(8,128)(2,1)}, bf16[160,512]{1,0:T(8,128)(2,1)S(1)}, u32[]{:S(2)}) copy-start(bf16[160,512]{1,0:T(8,128)(2,1)S(1)} %collective-permute-done.refs_3_) | copy-start | bytes 491524
  20.9 0.7 %copy-start.1 = (bf16[160,512]{1,0:T(8,128)(2,1)}, bf16[160,512]{1,0:T(8,128)(2,1)S(1)}, u32[]{:S(2)}) copy-start(bf16[160,512]{1,0:T(8,128)(2,1)S(1)} %collective-permute-done.1.refs_4_) | copy-start | bytes 491524

commit v9 on v8

--- a/solution.py
+++ b/solution.py
@@ -19,11 +19,6 @@
 SMEM = pl.BlockSpec(memory_space=pltpu.SMEM)
 
 
-def from_mask(x, axis, mask):
-    pairs = [(i, i ^ mask) for i in range(lax.axis_size(axis))]
-    return lax.ppermute(x, axis, pairs)
-
-
 def nt_dot(a, b):
     return lax.dot_general(a, b, (((1,), (1,)), ((), ())), preferred_element_type=jnp.float32)
 
@@ -32,24 +27,47 @@
     return lax.dot_general(a, b, (((1,), (0,)), ((), ())), preferred_element_type=jnp.float32)
 
 
-def send_kernel(loc_bits, sub_bits, emb_ref, dirs_ref, basis_ref, first_ref, last_ref, upper_ref, *payload_refs):
+def send_kernel(loc_bits, sub_bits, emb_ref, dirs_ref, basis_ref, first_ref, last_ref, chunks_ref):
     width_e = emb_ref.shape[0]
     local_points = emb_ref.shape[1]
     values = dirs_ref[...].astype(jnp.bfloat16)
-    even = lax.axis_index("sub") % 2 == 0
+    me = lax.axis_index("sub")
+    even = me % 2 == 0
     head_points, tail_points = emb_ref[:, :LEAF], emb_ref[:, local_points - LEAF :]
     head_values, tail_values = values[:, :LEAF], values[:, local_points - LEAF :]
     first_ref[:width_e, :] = jnp.where(even, tail_points, head_points)
     first_ref[width_e:, :] = jnp.where(even, tail_values, head_values)
     last_ref[:width_e, :] = jnp.where(even, head_points, tail_points)
     last_ref[width_e:, :] = jnp.where(even, head_values, tail_values)
-    for level in range(upper_ref.shape[0]):
+    for level in range(chunks_ref.shape[1] - 1):
         part = nt_dot(values, basis_ref[loc_bits + sub_bits + level])
-        upper_ref[level] = part
-        for payload_ref in payload_refs:
-            payload_ref[1 + level] = part
-    for level, payload_ref in enumerate(payload_refs):
-        payload_ref[0] = nt_dot(values, basis_ref[loc_bits + level])
+        for target in range(chunks_ref.shape[0]):
+            chunks_ref[target, 1 + level] = part
+    lower = [nt_dot(values, basis_ref[loc_bits + level]) for level in range(sub_bits)]
+    for target in range(chunks_ref.shape[0]):
+        other = jnp.bitwise_xor(me, target)
+        picked = lower[0]
+        for level in range(1, sub_bits):
+            picked = jnp.where(other >= 2**level, lower[level], picked)
+        chunks_ref[target, 0] = picked
+
+
+def top_level(other, bits):
+    level = jnp.int32(0)
+    for bit in range(1, bits):
+        level = level + (other >= 2**bit).astype(jnp.int32)
+    return level
+
+
+def sibling_sums(got_ref, index, me, bits):
+    sums = [None] * bits
+    for source in range(got_ref.shape[0]):
+        other = jnp.bitwise_xor(me, source)
+        level = top_level(other, bits)
+        for bit in range(bits):
+            term = jnp.where((other > 0) & (level == bit), got_ref[source, index(bit)], 0.0)
+            sums[bit] = term if sums[bit] is None else sums[bit] + term
+    return sums
 
 
 class Leaves:
@@ -107,26 +125,13 @@
 
 
 def final_kernel(sub_size, sub_bits, leaf_bits, loc_bits, *refs):
-    sub_masks = 2**sub_bits - 1
-    leaf_masks = 2**leaf_bits - 1
-    emb_ref, dirs_ref, local_ref, pair_ref, cross_ref, basis_ref, neighbours_ref, counts_ref = refs[:8]
-    round_one = refs[8 : 8 + sub_masks]
-    round_two = refs[8 + sub_masks : 8 + sub_masks + leaf_masks]
-    out_ref = refs[8 + sub_masks + leaf_masks]
+    emb_ref, dirs_ref, local_ref, pair_ref, cross_ref, basis_ref, neighbours_ref, counts_ref, one_ref, two_ref, out_ref = refs
     lv = Leaves(emb_ref, dirs_ref, neighbours_ref, counts_ref, sub_size)
     rank = basis_ref.shape[1]
     local_points = lv.local_points
 
-    sibling = [None] * (sub_bits + leaf_bits)
-    line = None
-    for mask, got_ref in enumerate(round_one, start=1):
-        level = mask.bit_length() - 1
-        got = got_ref[0]
-        sibling[level] = got if sibling[level] is None else sibling[level] + got
-    for mask, got_ref in enumerate(round_two, start=1):
-        level = sub_bits + mask.bit_length() - 1
-        got = got_ref[level - sub_bits]
-        sibling[level] = got if sibling[level] is None else sibling[level] + got
+    sibling = sibling_sums(one_ref, lambda bit: 0, lax.axis_index("sub"), sub_bits)
+    sibling += sibling_sums(two_ref, lambda bit: bit, lax.axis_index("leaf"), leaf_bits)
 
     far = None
     for bit in range(sub_bits + leaf_bits):
@@ -167,23 +172,20 @@
     loc_bits = level_basis.shape[0] - dev_bits
 
     halo = jax.ShapeDtypeStruct((width_e + nrhs, LEAF), jnp.bfloat16)
-    upper = jax.ShapeDtypeStruct((leaf_bits, nrhs, rank), jnp.float32)
-    payload = jax.ShapeDtypeStruct((1 + leaf_bits, nrhs, rank), jnp.float32)
-    first, last, upper_own, *payloads = pl.pallas_call(
+    chunks = jax.ShapeDtypeStruct((sub_size, 1 + leaf_bits, nrhs, rank), jnp.float32)
+    first, last, outgoing = pl.pallas_call(
         functools.partial(send_kernel, loc_bits, sub_bits),
-        out_shape=(halo, halo, upper) + (payload,) * sub_bits,
+        out_shape=(halo, halo, chunks),
         in_specs=[VMEM, VMEM, VMEM],
-        out_specs=(VMEM,) * (3 + sub_bits),
+        out_specs=(VMEM, VMEM, VMEM),
     )(embeddings, directions, level_basis)
 
     ndev = sub_size * leaf_size
     from_pair = lax.ppermute(first, axes, [(i, i ^ 1) for i in range(ndev)])
     from_cross = lax.ppermute(last, axes, [(i, i - 1 + 2 * (i % 2)) for i in range(1, ndev - 1)])
-    round_one = [from_mask(payloads[mask.bit_length() - 1], "sub", mask) for mask in range(1, sub_size)]
-    line = upper_own
-    for got in round_one:
-        line = line + got[1:]
-    round_two = [from_mask(line, "leaf", mask) for mask in range(1, leaf_size)]
+    round_one = lax.all_to_all(outgoing, "sub", 0, 0, tiled=True)
+    line = jnp.sum(round_one[:, 1:], axis=0)
+    round_two = lax.all_to_all(jnp.broadcast_to(line[None], (leaf_size,) + line.shape), "leaf", 0, 0, tiled=True)
 
     out = jax.ShapeDtypeStruct((nrhs, local_points), jnp.float32)
     local = pl.pallas_call(
@@ -193,14 +195,13 @@
         out_specs=VMEM,
     )(embeddings, directions, level_basis, neighbours, counts)
 
-    remote = round_one + round_two
     return pl.pallas_call(
         functools.partial(final_kernel, sub_size, sub_bits, leaf_bits, loc_bits),
         out_shape=out,
-        in_specs=[VMEM] * 6 + [SMEM, SMEM] + [VMEM] * len(remote),
+        in_specs=[VMEM] * 6 + [SMEM, SMEM] + [VMEM] * 2,
         out_specs=VMEM,
         input_output_aliases={2: 0},
-    )(embeddings, directions, local, from_pair, from_cross, level_basis, neighbours, counts, *remote)
+    )(embeddings, directions, local, from_pair, from_cross, level_basis, neighbours, counts, round_one, round_two)
 
 
 def solution(mesh):

time: 25.1 us -> 33 us (1.31)
  local copies, waits for them, and re-layouts: 1.36 us -> 5.35 us
  starting transfers between devices: 10.8 us -> 12.4 us
  waiting for transfers between devices: 2.78 us -> 3.97 us
  other arithmetic: 0.79 us -> 1.81 us
    all_to_all x0 -> x2, starting transfers between devices: none -> 9.73 us  [the longest x1 6.45 us: on_device(): round_one = lax.all_to_all(outgoing, 'sub', 0, 0, tiled=True)]
    ppermute x6 -> x0, starting transfers between devices: 8.33 us -> none  [from_mask(): return lax.ppermute(x, axis, pairs)]
    all_to_all x0 -> x2, waiting for transfers between devices: none -> 3.96 us  [the longest x1 3.46 us: on_device(): round_one = lax.all_to_all(outgoing, 'sub', 0, 0, tiled=True)]
    unnamed x16 -> x14, local copies, waits for them, and re-layouts: 1.36 us -> 4.75 us
    ppermute x6 -> x0, waiting for transfers between devices: 2.78 us -> none  [from_mask(): return lax.ppermute(x, axis, pairs)]
    all_to_all x0 -> x2, other arithmetic: none -> 1.8 us  [the longest x1 0.94 us: on_device(): round_one = lax.all_to_all(outgoing, 'sub', 0, 0, tiled=True)]
    add x1 -> x0, other arithmetic: 0.79 us -> none  [on_device(): line = line + got[1:]]
    all_to_all x0 -> x1, local copies, waits for them, and re-layouts: none -> 0.59 us  [on_device(): round_one = lax.all_to_all(outgoing, 'sub', 0, 0, tiled=True)]
  transfers between devices with their start and end apart: 8 -> 4, of which waited for: 3 -> 2; matrix products, arithmetic and copies ran while one was open for 3% -> 12% of each run, Pallas kernels for 14% -> 11%
where the time goes in v9:
time: 33 us; the launch traced here: 32.6 us
  starting transfers between devices  12.4 us (38%)
  Pallas kernels  8.98 us (27%)
  local copies, waits for them, and re-layouts  5.35 us (16%)
  waiting for transfers between devices  3.97 us (12%)
  other arithmetic  1.81 us (5%)
    all_to_all x1, starting transfers between devices, on_device(): round_one = lax.all_to_all(outgoing, 'sub', 0, 0, tiled=True)  6.45 us
    unnamed x14, local copies, waits for them, and re-layouts  4.75 us
    pallas_call x1, Pallas kernels, on_device(): pl.pallas_call(functools.partial(local_kernel, sub_size), out_shape=out,...  3.58 us
    all_to_all x1, waiting for transfers between devices, on_device(): round_one = lax.all_to_all(outgoing, 'sub', 0, 0, tiled=True)  3.46 us
    all_to_all x1, starting transfers between devices, on_device(): lax.all_to_all(jnp.broadcast_to(line[None], (leaf_size,) + line.shape), '...  3.28 us
    pallas_call x1, Pallas kernels, on_device(): pl.pallas_call(functools.partial(final_kernel, sub_size, sub_bits, leaf_b...  3.16 us
    pallas_call x1, Pallas kernels, on_device(): pl.pallas_call(functools.partial(send_kernel, loc_bits, sub_bits), out_sh...  2.24 us
    ppermute x1, starting transfers between devices, on_device(): from_pair = lax.ppermute(first, axes, [(i, i ^ 1) for i in range(ndev)])  2.02 us
  transfers between devices with their start and end apart: 4, of which 2 were waited for; matrix products, arithmetic and copies ran while one was open for 12% of the time, Pallas kernels for 11%

profile of v9, /device:TPU:0, one launch (start us, length us, event | category | flops | bytes accessed | tf_op | source)
XLA Modules:
  0.0 32.6 jit_solution(14748140615177608788)
XLA Ops:
  0.0 2.2 %shard_map.56 = (bf16[160,512]{1,0:T(8,128)(2,1)}, bf16[160,512]{1,0:T(8,128)(2,1)}, f32[4,3,32,64]{3,2,1,0:T(8,128)}) custom-call(bf16[128,1024]{1,0:T(8,128)(2,1)} %refs_0_.1, f32[32,1024]{1,0:T(8,128)} %refs_1_.1, bf16[5,64,1024]{2,1,0:T(8,128)(2,1)} %refs_5_.1), custom_call_target="tpu_custom_call" | custom-call | tf_op jit(solution)/shard_map/pallas_call | solution.py:176
  2.2 0.0 copy-start.4
  2.2 1.8 %reshape.1 = f32[4,1,6144]{2,1,0:T(1,128)} reshape(f32[4,3,32,64]{3,2,1,0:T(8,128)} %get-tuple-element.10) | data formatting | bytes 196608
  4.0 0.0 copy-start.3
  4.0 6.5 %all-to-all-start = ((f32[4,1,6144]{2,1,0:T(1,128)}), f32[4,1,6144]{2,1,0:T(1,128)S(1)}, u32[]{:S(2)}, u32[]{:S(2)}) async-start(f32[4,1,6144]{2,1,0:T(1,128)} %reshape.1), calls=%async_computation | async-start | bytes 196608 | tf_op jit(solution)/shard_map/all_to_all | solution.py:186
  10.5 0.0 copy-done.4
  10.5 2.0 %collective-permute-start = (bf16[160,512]{1,0:T(8,128)(2,1)S(1)}, bf16[160,512]{1,0:T(8,128)(2,1)S(1)}, u32[]{:S(2)}, u32[]{:S(2)}) collective-permute-start(bf16[160,512]{1,0:T(8,128)(2,1)S(1)} %copy-done.4), channel_id=1, source_target_pairs={{0,1},{1,0},{2,3},{3,2},{4,5},{5,4},{6,7},{7,6},{8,9},{9,8},{10,11... | collective-permute-start | bytes 491528 | tf_op jit(solution)/shard_map/ppermute | solution.py:184
  12.5 0.0 copy-done.3
  12.5 0.7 %collective-permute-start.1 = (bf16[160,512]{1,0:T(8,128)(2,1)S(1)}, bf16[160,512]{1,0:T(8,128)(2,1)S(1)}, u32[]{:S(2)}, u32[]{:S(2)}) collective-permute-start(bf16[160,512]{1,0:T(8,128)(2,1)S(1)} %copy-done.3), channel_id=1, source_target_pairs={{1,2},{2,1},{3,4},{4,3},{5,6},{6,5},{7,8},{8,7},{9,10},{10,9},{11,... | collective-permute-start | bytes 491528 | tf_op jit(solution)/shard_map/ppermute | solution.py:185
  13.2 3.5 %all-to-all-done = f32[4,1,6144]{2,1,0:T(1,128)S(1)} async-done(((f32[4,1,6144]{2,1,0:T(1,128)}), f32[4,1,6144]{2,1,0:T(1,128)S(1)}, u32[]{:S(2)}, u32[]{:S(2)}) %all-to-all-start) | async-done | bytes 98336 | tf_op jit(solution)/shard_map/all_to_all | solution.py:186
  16.6 0.6 %broadcast.1 = f32[]{:T(128)} broadcast(f32[]{:T(128)} %constant.4), dimensions={} | broadcast | bytes 8 | tf_op jit(solution)/shard_map/all_to_all | solution.py:186
  17.2 0.9 %reduce = f32[4,6144]{1,0:T(4,128)S(1)} reduce(f32[4,1,6144]{2,1,0:T(1,128)S(1)} %all-to-all-done, f32[]{:T(128)} %broadcast.1), dimensions={1}, to_apply=%all_to_all.6.reduce_sub_computation | reduce | bytes 196612 | tf_op jit(solution)/shard_map/all_to_all | solution.py:186
  18.1 0.2 reshape.2.refs_8_
  18.3 0.0 copy-start
  18.3 0.7 %reshape.3 = f32[4,1,4096]{2,1,0:T(1,128)} reshape(f32[4,2,32,64]{3,2,1,0:T(8,128)S(1)} %broadcast_in_dim.2) | data formatting | bytes 131072
  19.1 0.0 copy-done
  19.1 3.3 %all-to-all-start.1 = ((f32[4,1,4096]{2,1,0:T(1,128)}), f32[4,1,4096]{2,1,0:T(1,128)S(1)}, u32[]{:S(2)}, u32[]{:S(2)}) async-start(f32[4,1,4096]{2,1,0:T(1,128)} %reshape.3), calls=%async_computation.1 | async-start | bytes 131072 | tf_op jit(solution)/shard_map/all_to_all | solution.py:188
  22.4 3.6 %shard_map.55.refs_2_ = f32[32,1024]{1,0:T(8,128)} custom-call(bf16[128,1024]{1,0:T(8,128)(2,1)} %refs_0_.1, f32[32,1024]{1,0:T(8,128)} %refs_1_.1, bf16[5,64,1024]{2,1,0:T(8,128)(2,1)} %refs_5_.1, s32[2,8]{1,0:T(2,128)} %refs_6_.1, s32[2]{0:T(128)} %refs_7_.1), custom_call_target="tpu_custom_call" | custom-call | tf_op jit(solution)/shard_map/pallas_call | solution.py:191
  26.0 0.5 %all-to-all-done.1 = f32[4,1,4096]{2,1,0:T(1,128)S(1)} async-done(((f32[4,1,4096]{2,1,0:T(1,128)}), f32[4,1,4096]{2,1,0:T(1,128)S(1)}, u32[]{:S(2)}, u32[]{:S(2)}) %all-to-all-start.1) | async-done | bytes 65568 | tf_op jit(solution)/shard_map/all_to_all | solution.py:188
  26.5 0.9 %reduce.1 = f32[4,4096]{1,0:T(4,128)S(1)} reduce(f32[4,1,4096]{2,1,0:T(1,128)S(1)} %all-to-all-done.1, f32[]{:T(128)} %broadcast.1), dimensions={1}, to_apply=%all_to_all.7.reduce_sub_computation | reduce | bytes 131076 | tf_op jit(solution)/shard_map/all_to_all | solution.py:188
  27.3 0.8 %reshape.4.refs_9_ = f32[4,2,32,64]{3,2,1,0:T(8,128)} reshape(f32[4,4096]{1,0:T(4,128)S(1)} %reduce.1) | data formatting | bytes 131072
  28.1 0.0 collective-permute-done.refs_3_
  28.1 0.0 copy-start.1
  28.1 0.0 collective-permute-done.1.refs_4_
  28.1 0.7 %copy-done.1 = bf16[160,512]{1,0:T(8,128)(2,1)} copy-done((bf16[160,512]{1,0:T(8,128)(2,1)}, bf16[160,512]{1,0:T(8,128)(2,1)S(1)}, u32[]{:S(2)}) %copy-start.1) | copy-done | bytes 163864
  28.8 0.0 copy-start.2
  28.8 0.7 %copy-done.2 = bf16[160,512]{1,0:T(8,128)(2,1)} copy-done((bf16[160,512]{1,0:T(8,128)(2,1)}, bf16[160,512]{1,0:T(8,128)(2,1)S(1)}, u32[]{:S(2)}) %copy-start.2) | copy-done | bytes 163864
  29.4 3.2 %shard_map.57 = f32[32,1024]{1,0:T(8,128)} custom-call(bf16[128,1024]{1,0:T(8,128)(2,1)} %refs_0_.1, f32[32,1024]{1,0:T(8,128)} %refs_1_.1, f32[32,1024]{1,0:T(8,128)} %shard_map.55.refs_2_, bf16[160,512]{1,0:T(8,128)(2,1)} %copy-done.1, bf16[160,512]{1,0:T(8,128)(2,1)} %copy-done.2, bf16[5,64,1024]{2,1,0:T(8,128)(2,1)} %refs_5_.1, ...), custom_call_target="tpu_custom_call", output_to_operand_aliasing={{}: (2, {})} | custom-call | tf_op jit(solution)/shard_map/pallas_call | solution.py:198
  (2 shorter events, 0.0 us)
Async XLA Ops:
  2.2 8.2 %copy-start.4 = (bf16[160,512]{1,0:T(8,128)(2,1)S(1)}, bf16[160,512]{1,0:T(8,128)(2,1)}, u32[]{:S(2)}) copy-start(bf16[160,512]{1,0:T(8,128)(2,1)} %get-tuple-element.8) | copy-start | bytes 491524
  4.0 8.5 %copy-start.3 = (bf16[160,512]{1,0:T(8,128)(2,1)S(1)}, bf16[160,512]{1,0:T(8,128)(2,1)}, u32[]{:S(2)}) copy-start(bf16[160,512]{1,0:T(8,128)(2,1)} %get-tuple-element.9) | copy-start | bytes 491524
  4.0 12.6 %all-to-all-start = ((f32[4,1,6144]{2,1,0:T(1,128)}), f32[4,1,6144]{2,1,0:T(1,128)S(1)}, u32[]{:S(2)}, u32[]{:S(2)}) async-start(f32[4,1,6144]{2,1,0:T(1,128)} %reshape.1), calls=%async_computation | async-start | bytes 196608 | tf_op jit(solution)/shard_map/all_to_all | solution.py:186
  10.5 17.6 %collective-permute-start = (bf16[160,512]{1,0:T(8,128)(2,1)S(1)}, bf16[160,512]{1,0:T(8,128)(2,1)S(1)}, u32[]{:S(2)}, u32[]{:S(2)}) collective-permute-start(bf16[160,512]{1,0:T(8,128)(2,1)S(1)} %copy-done.4), channel_id=1, source_target_pairs={{0,1},{1,0},{2,3},{3,2},{4,5},{5,4},{6,7},{7,6},{8,9},{9,8},{10,11... | collective-permute-start | bytes 491528 | tf_op jit(solution)/shard_map/ppermute | solution.py:184
  12.5 15.6 %collective-permute-start.1 = (bf16[160,512]{1,0:T(8,128)(2,1)S(1)}, bf16[160,512]{1,0:T(8,128)(2,1)S(1)}, u32[]{:S(2)}, u32[]{:S(2)}) collective-permute-start(bf16[160,512]{1,0:T(8,128)(2,1)S(1)} %copy-done.3), channel_id=1, source_target_pairs={{1,2},{2,1},{3,4},{4,3},{5,6},{6,5},{7,8},{8,7},{9,10},{10,9},{11,... | collective-permute-start | bytes 491528 | tf_op jit(solution)/shard_map/ppermute | solution.py:185
  18.3 0.8 %copy-start = (f32[4,3,32,64]{3,2,1,0:T(8,128)}, f32[4,3,32,64]{3,2,1,0:T(8,128)S(1)}, u32[]{:S(2)}) copy-start(f32[4,3,32,64]{3,2,1,0:T(8,128)S(1)} %reshape.2.refs_8_) | copy-start | bytes 294916
  19.1 7.4 %all-to-all-start.1 = ((f32[4,1,4096]{2,1,0:T(1,128)}), f32[4,1,4096]{2,1,0:T(1,128)S(1)}, u32[]{:S(2)}, u32[]{:S(2)}) async-start(f32[4,1,4096]{2,1,0:T(1,128)} %reshape.3), calls=%async_computation.1 | async-start | bytes 131072 | tf_op jit(solution)/shard_map/all_to_all | solution.py:188
  28.1 0.7 %copy-start.1 = (bf16[160,512]{1,0:T(8,128)(2,1)}, bf16[160,512]{1,0:T(8,128)(2,1)S(1)}, u32[]{:S(2)}) copy-start(bf16[160,512]{1,0:T(8,128)(2,1)S(1)} %collective-permute-done.refs_3_) | copy-start | bytes 491524
  28.8 0.7 %copy-start.2 = (bf16[160,512]{1,0:T(8,128)(2,1)}, bf16[160,512]{1,0:T(8,128)(2,1)S(1)}, u32[]{:S(2)}) copy-start(bf16[160,512]{1,0:T(8,128)(2,1)S(1)} %collective-permute-done.1.refs_4_) | copy-start | bytes 491524

commit v10 on v8

--- a/solution.py
+++ b/solution.py
@@ -32,7 +32,7 @@
     return lax.dot_general(a, b, (((1,), (0,)), ((), ())), preferred_element_type=jnp.float32)
 
 
-def send_kernel(loc_bits, sub_bits, emb_ref, dirs_ref, basis_ref, first_ref, last_ref, upper_ref, *payload_refs):
+def send_kernel(loc_bits, emb_ref, dirs_ref, basis_ref, first_ref, last_ref, lower_ref, upper_ref):
     width_e = emb_ref.shape[0]
     local_points = emb_ref.shape[1]
     values = dirs_ref[...].astype(jnp.bfloat16)
@@ -43,13 +43,10 @@
     first_ref[width_e:, :] = jnp.where(even, tail_values, head_values)
     last_ref[:width_e, :] = jnp.where(even, head_points, tail_points)
     last_ref[width_e:, :] = jnp.where(even, head_values, tail_values)
+    for level in range(lower_ref.shape[0]):
+        lower_ref[level] = nt_dot(values, basis_ref[loc_bits + level])
     for level in range(upper_ref.shape[0]):
-        part = nt_dot(values, basis_ref[loc_bits + sub_bits + level])
-        upper_ref[level] = part
-        for payload_ref in payload_refs:
-            payload_ref[1 + level] = part
-    for level, payload_ref in enumerate(payload_refs):
-        payload_ref[0] = nt_dot(values, basis_ref[loc_bits + level])
+        upper_ref[level] = nt_dot(values, basis_ref[loc_bits + lower_ref.shape[0] + level])
 
 
 class Leaves:
@@ -108,25 +105,20 @@
 
 def final_kernel(sub_size, sub_bits, leaf_bits, loc_bits, *refs):
     sub_masks = 2**sub_bits - 1
-    leaf_masks = 2**leaf_bits - 1
-    emb_ref, dirs_ref, local_ref, pair_ref, cross_ref, basis_ref, neighbours_ref, counts_ref = refs[:8]
-    round_one = refs[8 : 8 + sub_masks]
-    round_two = refs[8 + sub_masks : 8 + sub_masks + leaf_masks]
-    out_ref = refs[8 + sub_masks + leaf_masks]
+    emb_ref, dirs_ref, local_ref, pair_ref, cross_ref, basis_ref, neighbours_ref, counts_ref, own_ref = refs[:9]
+    round_two = refs[9 : 9 + sub_masks]
+    out_ref = refs[9 + sub_masks]
     lv = Leaves(emb_ref, dirs_ref, neighbours_ref, counts_ref, sub_size)
     rank = basis_ref.shape[1]
     local_points = lv.local_points
 
-    sibling = [None] * (sub_bits + leaf_bits)
-    line = None
-    for mask, got_ref in enumerate(round_one, start=1):
+    sibling = [None] * sub_bits + [own_ref[sub_bits + bit] for bit in range(leaf_bits)]
+    for mask, got_ref in enumerate(round_two, start=1):
         level = mask.bit_length() - 1
-        got = got_ref[0]
+        got = got_ref[level]
         sibling[level] = got if sibling[level] is None else sibling[level] + got
-    for mask, got_ref in enumerate(round_two, start=1):
-        level = sub_bits + mask.bit_length() - 1
-        got = got_ref[level - sub_bits]
-        sibling[level] = got if sibling[level] is None else sibling[level] + got
+        for bit in range(leaf_bits):
+            sibling[sub_bits + bit] = sibling[sub_bits + bit] + got_ref[sub_bits + bit]
 
     far = None
     for bit in range(sub_bits + leaf_bits):
@@ -167,23 +159,28 @@
     loc_bits = level_basis.shape[0] - dev_bits
 
     halo = jax.ShapeDtypeStruct((width_e + nrhs, LEAF), jnp.bfloat16)
-    upper = jax.ShapeDtypeStruct((leaf_bits, nrhs, rank), jnp.float32)
-    payload = jax.ShapeDtypeStruct((1 + leaf_bits, nrhs, rank), jnp.float32)
-    first, last, upper_own, *payloads = pl.pallas_call(
-        functools.partial(send_kernel, loc_bits, sub_bits),
-        out_shape=(halo, halo, upper) + (payload,) * sub_bits,
+    first, last, lower, upper = pl.pallas_call(
+        functools.partial(send_kernel, loc_bits),
+        out_shape=(
+            halo,
+            halo,
+            jax.ShapeDtypeStruct((sub_bits, nrhs, rank), jnp.float32),
+            jax.ShapeDtypeStruct((leaf_bits, nrhs, rank), jnp.float32),
+        ),
         in_specs=[VMEM, VMEM, VMEM],
-        out_specs=(VMEM,) * (3 + sub_bits),
+        out_specs=(VMEM,) * 4,
     )(embeddings, directions, level_basis)
 
     ndev = sub_size * leaf_size
+    round_one = [from_mask(upper, "leaf", mask) for mask in range(1, leaf_size)]
     from_pair = lax.ppermute(first, axes, [(i, i ^ 1) for i in range(ndev)])
     from_cross = lax.ppermute(last, axes, [(i, i - 1 + 2 * (i % 2)) for i in range(1, ndev - 1)])
-    round_one = [from_mask(payloads[mask.bit_length() - 1], "sub", mask) for mask in range(1, sub_size)]
-    line = upper_own
-    for got in round_one:
-        line = line + got[1:]
-    round_two = [from_mask(line, "leaf", mask) for mask in range(1, leaf_size)]
+    blocks = [None] * leaf_bits
+    for mask, got in enumerate(round_one, start=1):
+        level = mask.bit_length() - 1
+        blocks[level] = got[level] if blocks[level] is None else blocks[level] + got[level]
+    own = jnp.concatenate([lower, jnp.stack(blocks)], axis=0)
+    round_two = [from_mask(own, "sub", mask) for mask in range(1, sub_size)]
 
     out = jax.ShapeDtypeStruct((nrhs, local_points), jnp.float32)
     local = pl.pallas_call(
@@ -193,14 +190,13 @@
         out_specs=VMEM,
     )(embeddings, directions, level_basis, neighbours, counts)
 
-    remote = round_one + round_two
     return pl.pallas_call(
         functools.partial(final_kernel, sub_size, sub_bits, leaf_bits, loc_bits),
         out_shape=out,
-        in_specs=[VMEM] * 6 + [SMEM, SMEM] + [VMEM] * len(remote),
+        in_specs=[VMEM] * 6 + [SMEM, SMEM] + [VMEM] * (1 + len(round_two)),
         out_specs=VMEM,
         input_output_aliases={2: 0},
-    )(embeddings, directions, local, from_pair, from_cross, level_basis, neighbours, counts, *remote)
+    )(embeddings, directions, local, from_pair, from_cross, level_basis, neighbours, counts, own, *round_two)
 
 
 def solution(mesh):

time: 25.1 us -> 29.4 us (1.17)
  waiting for transfers between devices: 2.78 us -> 6.57 us
  starting transfers between devices: 10.8 us -> 12.3 us
  other arithmetic: 0.79 us -> 0.01 us
    ppermute x6, waiting for transfers between devices: 2.78 us -> 6.57 us  [from_mask(): return lax.ppermute(x, axis, pairs)]
    ppermute x6, starting transfers between devices: 8.33 us -> 9.41 us  [from_mask(): return lax.ppermute(x, axis, pairs)]
    add x1, other arithmetic: 0.79 us -> 0.01 us  [on_device(): blocks[level] + got[level]]
    unnamed x16 -> x14, local copies, waits for them, and re-layouts: 1.36 us -> 1.34 us
  transfers between devices with their start and end apart: 8 -> 8, of which waited for: 3 -> 3; matrix products, arithmetic and copies ran while one was open for 3% -> 0% of each run, Pallas kernels for 14% -> 12%
where the time goes in v10:
time: 29.4 us; the launch traced here: 29.1 us
  starting transfers between devices  12.3 us (42%)
  Pallas kernels  8.82 us (30%)
  waiting for transfers between devices  6.57 us (22%)
  local copies, waits for them, and re-layouts  1.34 us (5%)
    ppermute x6, starting transfers between devices, from_mask(): return lax.ppermute(x, axis, pairs)  9.41 us
    ppermute x6, waiting for transfers between devices, from_mask(): return lax.ppermute(x, axis, pairs)  6.57 us
    pallas_call x1, Pallas kernels, on_device(): pl.pallas_call(functools.partial(local_kernel, sub_size), out_shape=out,...  3.57 us
    pallas_call x1, Pallas kernels, on_device(): pl.pallas_call(functools.partial(final_kernel, sub_size, sub_bits, leaf_b...  3.07 us
    pallas_call x1, Pallas kernels, on_device(): pl.pallas_call(functools.partial(send_kernel, loc_bits), out_shape=(halo,...  2.17 us
    ppermute x1, starting transfers between devices, on_device(): from_pair = lax.ppermute(first, axes, [(i, i ^ 1) for i in range(ndev)])  2.08 us
    unnamed x14, local copies, waits for them, and re-layouts  1.34 us
    ppermute x1, starting transfers between devices, on_device(): lax.ppermute(last, axes, [(i, i - 1 + 2 * (i % 2)) for i in range(1, ndev...  0.79 us
  transfers between devices with their start and end apart: 8, of which 3 were waited for; matrix products, arithmetic and copies ran while one was open for 0% of the time, Pallas kernels for 12%

profile of v10, /device:TPU:0, one launch (start us, length us, event | category | flops | bytes accessed | tf_op | source)
XLA Modules:
  0.0 29.1 jit_solution(10902131073786268001)
XLA Ops:
  0.0 2.2 %shard_map.56 = (bf16[160,512]{1,0:T(8,128)(2,1)}, bf16[160,512]{1,0:T(8,128)(2,1)}, f32[2,32,64]{2,1,0:T(8,128)}, f32[2,32,64]{2,1,0:T(8,128)}) custom-call(bf16[128,1024]{1,0:T(8,128)(2,1)} %refs_0_.1, f32[32,1024]{1,0:T(8,128)} %refs_1_.1, bf16[5,64,1024]{2,1,0:T(8,128)(2,1)} %refs_5_.1), custom_call_target="tpu_custom_call" | custom-call | tf_op jit(solution)/shard_map/pallas_call | solution.py:162
  2.2 2.9 %collective-permute-start.3 = (f32[2,32,64]{2,1,0:T(8,128)}, f32[2,32,64]{2,1,0:T(8,128)S(1)}, u32[]{:S(2)}, u32[]{:S(2)}) collective-permute-start(f32[2,32,64]{2,1,0:T(8,128)} %get-tuple-element.12), channel_id=1, source_target_pairs={{0,8},{4,12},{8,0},{12,4},{1,9},{5,13},{9,1},{13,5},{2,10},{6,14},... | collective-permute-start | bytes 49160 | tf_op jit(solution)/shard_map/ppermute | solution.py:24
  5.1 0.0 collective-permute-start.4
  5.1 0.1 collective-permute-start.2
  5.3 2.1 %collective-permute-start = (bf16[160,512]{1,0:T(8,128)(2,1)}, bf16[160,512]{1,0:T(8,128)(2,1)S(1)}, u32[]{:S(2)}, u32[]{:S(2)}) collective-permute-start(bf16[160,512]{1,0:T(8,128)(2,1)} %get-tuple-element.9), channel_id=1, source_target_pairs={{0,1},{1,0},{2,3},{3,2},{4,5},{5,4},{6,7},{7,6},{8,9},{9,8},{10,11... | collective-permute-start | bytes 491528 | tf_op jit(solution)/shard_map/ppermute | solution.py:176
  7.3 0.0 copy-start.6
  7.3 0.8 %collective-permute-start.1 = (bf16[160,512]{1,0:T(8,128)(2,1)}, bf16[160,512]{1,0:T(8,128)(2,1)S(1)}, u32[]{:S(2)}, u32[]{:S(2)}) collective-permute-start(bf16[160,512]{1,0:T(8,128)(2,1)} %get-tuple-element.10), channel_id=1, source_target_pairs={{1,2},{2,1},{3,4},{4,3},{5,6},{6,5},{7,8},{8,7},{9,10},{10,9},{11,... | collective-permute-start | bytes 491528 | tf_op jit(solution)/shard_map/ppermute | solution.py:177
  8.1 0.0 collective-permute-done.3
  8.2 0.6 %collective-permute-done.4 = f32[2,32,64]{2,1,0:T(8,128)S(1)} collective-permute-done((f32[2,32,64]{2,1,0:T(8,128)}, f32[2,32,64]{2,1,0:T(8,128)S(1)}, u32[]{:S(2)}, u32[]{:S(2)}) %collective-permute-start.4) | collective-permute-done | bytes 16416 | tf_op jit(solution)/shard_map/ppermute | solution.py:24
  8.8 0.0 collective-permute-done.2
  8.8 0.0 copy-done.6
  8.8 0.0 copy-start
  8.8 3.9 %collective-permute-start.5 = (f32[4,32,64]{2,1,0:T(8,128)S(1)}, f32[4,32,64]{2,1,0:T(8,128)S(1)}, u32[]{:S(2)}, u32[]{:S(2)}) collective-permute-start(f32[4,32,64]{2,1,0:T(8,128)S(1)} %pad_maximum_fusion.refs_8_), channel_id=1, source_target_pairs={{0,1},{1,0},{2,3},{3,2},{4,5},{5,4},{6,7},{7,6},{8,9},{9,8},{10,11... | collective-permute-start | bytes 98312 | tf_op jit(solution)/shard_map/ppermute | solution.py:24
  12.7 0.6 %collective-permute-start.6 = (f32[4,32,64]{2,1,0:T(8,128)S(1)}, f32[4,32,64]{2,1,0:T(8,128)S(1)}, u32[]{:S(2)}, u32[]{:S(2)}) collective-permute-start(f32[4,32,64]{2,1,0:T(8,128)S(1)} %pad_maximum_fusion.refs_8_), channel_id=1, source_target_pairs={{0,2},{1,3},{2,0},{3,1},{4,6},{5,7},{6,4},{7,5},{8,10},{9,11},{10,... | collective-permute-start | bytes 98312 | tf_op jit(solution)/shard_map/ppermute | solution.py:24
  13.3 1.9 %collective-permute-start.7 = (f32[4,32,64]{2,1,0:T(8,128)S(1)}, f32[4,32,64]{2,1,0:T(8,128)S(1)}, u32[]{:S(2)}, u32[]{:S(2)}) collective-permute-start(f32[4,32,64]{2,1,0:T(8,128)S(1)} %pad_maximum_fusion.refs_8_), channel_id=1, source_target_pairs={{0,3},{1,2},{2,1},{3,0},{4,7},{5,6},{6,5},{7,4},{8,11},{9,10},{10,... | collective-permute-start | bytes 98312 | tf_op jit(solution)/shard_map/ppermute | solution.py:24
  15.1 3.6 %shard_map.55.refs_2_ = f32[32,1024]{1,0:T(8,128)} custom-call(bf16[128,1024]{1,0:T(8,128)(2,1)} %refs_0_.1, f32[32,1024]{1,0:T(8,128)} %refs_1_.1, bf16[5,64,1024]{2,1,0:T(8,128)(2,1)} %refs_5_.1, s32[2,8]{1,0:T(2,128)} %refs_6_.1, s32[2]{0:T(128)} %refs_7_.1), custom_call_target="tpu_custom_call" | custom-call | tf_op jit(solution)/shard_map/pallas_call | solution.py:186
  18.7 0.0 copy-done
  18.7 0.3 collective-permute-done.5.refs_9_
  19.0 0.0 copy-start.3
  19.0 5.7 %collective-permute-done.6.refs_10_ = f32[4,32,64]{2,1,0:T(8,128)S(1)} collective-permute-done((f32[4,32,64]{2,1,0:T(8,128)S(1)}, f32[4,32,64]{2,1,0:T(8,128)S(1)}, u32[]{:S(2)}, u32[]{:S(2)}) %collective-permute-start.6) | collective-permute-done | bytes 32800 | tf_op jit(solution)/shard_map/ppermute | solution.py:24
  24.7 0.0 copy-start.4
  24.7 0.0 collective-permute-done.7.refs_11_
  24.7 0.0 copy-start.5
  24.7 0.0 collective-permute-done.refs_3_
  24.7 0.0 copy-start.1
  24.7 0.0 collective-permute-done.1.refs_4_
  24.7 0.0 copy-done.3
  24.7 0.6 %copy-done.4 = f32[4,32,64]{2,1,0:T(8,128)} copy-done((f32[4,32,64]{2,1,0:T(8,128)}, f32[4,32,64]{2,1,0:T(8,128)S(1)}, u32[]{:S(2)}) %copy-start.4) | copy-done | bytes 32792
  25.3 0.0 copy-done.5
  25.3 0.1 copy-done.1
  25.4 0.0 copy-start.2
  25.4 0.7 %copy-done.2 = bf16[160,512]{1,0:T(8,128)(2,1)} copy-done((bf16[160,512]{1,0:T(8,128)(2,1)}, bf16[160,512]{1,0:T(8,128)(2,1)S(1)}, u32[]{:S(2)}) %copy-start.2) | copy-done | bytes 163864
  26.0 3.1 %shard_map.57 = f32[32,1024]{1,0:T(8,128)} custom-call(bf16[128,1024]{1,0:T(8,128)(2,1)} %refs_0_.1, f32[32,1024]{1,0:T(8,128)} %refs_1_.1, f32[32,1024]{1,0:T(8,128)} %shard_map.55.refs_2_, bf16[160,512]{1,0:T(8,128)(2,1)} %copy-done.1, bf16[160,512]{1,0:T(8,128)(2,1)} %copy-done.2, bf16[5,64,1024]{2,1,0:T(8,128)(2,1)} %refs_5_.1, ...), custom_call_target="tpu_custom_call", output_to_operand_aliasing={{}: (2, {})} | custom-call | tf_op jit(solution)/shard_map/pallas_call | solution.py:193
  (3 shorter events, 0.0 us)
Async XLA Ops:
  2.2 6.0 %collective-permute-start.3 = (f32[2,32,64]{2,1,0:T(8,128)}, f32[2,32,64]{2,1,0:T(8,128)S(1)}, u32[]{:S(2)}, u32[]{:S(2)}) collective-permute-start(f32[2,32,64]{2,1,0:T(8,128)} %get-tuple-element.12), channel_id=1, source_target_pairs={{0,8},{4,12},{8,0},{12,4},{1,9},{5,13},{9,1},{13,5},{2,10},{6,14},... | collective-permute-start | bytes 49160 | tf_op jit(solution)/shard_map/ppermute | solution.py:24
  5.1 3.6 %collective-permute-start.4 = (f32[2,32,64]{2,1,0:T(8,128)}, f32[2,32,64]{2,1,0:T(8,128)S(1)}, u32[]{:S(2)}, u32[]{:S(2)}) collective-permute-start(f32[2,32,64]{2,1,0:T(8,128)} %get-tuple-element.12), channel_id=1, source_target_pairs={{0,12},{4,8},{8,4},{12,0},{1,13},{5,9},{9,5},{13,1},{2,14},{6,10},... | collective-permute-start | bytes 49160 | tf_op jit(solution)/shard_map/ppermute | solution.py:24
  5.1 3.6 %collective-permute-start.2 = (f32[2,32,64]{2,1,0:T(8,128)}, f32[2,32,64]{2,1,0:T(8,128)S(1)}, u32[]{:S(2)}, u32[]{:S(2)}) collective-permute-start(f32[2,32,64]{2,1,0:T(8,128)} %get-tuple-element.12), channel_id=1, source_target_pairs={{0,4},{4,0},{8,12},{12,8},{1,5},{5,1},{9,13},{13,9},{2,6},{6,2},{1... | collective-permute-start | bytes 49160 | tf_op jit(solution)/shard_map/ppermute | solution.py:24
  5.3 19.4 %collective-permute-start = (bf16[160,512]{1,0:T(8,128)(2,1)}, bf16[160,512]{1,0:T(8,128)(2,1)S(1)}, u32[]{:S(2)}, u32[]{:S(2)}) collective-permute-start(bf16[160,512]{1,0:T(8,128)(2,1)} %get-tuple-element.9), channel_id=1, source_target_pairs={{0,1},{1,0},{2,3},{3,2},{4,5},{5,4},{6,7},{7,6},{8,9},{9,8},{10,11... | collective-permute-start | bytes 491528 | tf_op jit(solution)/shard_map/ppermute | solution.py:176
  7.3 1.4 %copy-start.6 = (f32[2,32,64]{2,1,0:T(8,128)S(1)}, f32[2,32,64]{2,1,0:T(8,128)}, u32[]{:S(2)}) copy-start(f32[2,32,64]{2,1,0:T(8,128)} %get-tuple-element.11) | copy-start | bytes 49156
  7.3 17.4 %collective-permute-start.1 = (bf16[160,512]{1,0:T(8,128)(2,1)}, bf16[160,512]{1,0:T(8,128)(2,1)S(1)}, u32[]{:S(2)}, u32[]{:S(2)}) collective-permute-start(bf16[160,512]{1,0:T(8,128)(2,1)} %get-tuple-element.10), channel_id=1, source_target_pairs={{1,2},{2,1},{3,4},{4,3},{5,6},{6,5},{7,8},{8,7},{9,10},{10,9},{11,... | collective-permute-start | bytes 491528 | tf_op jit(solution)/shard_map/ppermute | solution.py:177
  8.8 9.9 %copy-start = (f32[4,32,64]{2,1,0:T(8,128)}, f32[4,32,64]{2,1,0:T(8,128)S(1)}, u32[]{:S(2)}) copy-start(f32[4,32,64]{2,1,0:T(8,128)S(1)} %pad_maximum_fusion.refs_8_) | copy-start | bytes 98308
  8.8 10.2 %collective-permute-start.5 = (f32[4,32,64]{2,1,0:T(8,128)S(1)}, f32[4,32,64]{2,1,0:T(8,128)S(1)}, u32[]{:S(2)}, u32[]{:S(2)}) collective-permute-start(f32[4,32,64]{2,1,0:T(8,128)S(1)} %pad_maximum_fusion.refs_8_), channel_id=1, source_target_pairs={{0,1},{1,0},{2,3},{3,2},{4,5},{5,4},{6,7},{7,6},{8,9},{9,8},{10,11... | collective-permute-start | bytes 98312 | tf_op jit(solution)/shard_map/ppermute | solution.py:24
  12.7 12.0 %collective-permute-start.6 = (f32[4,32,64]{2,1,0:T(8,128)S(1)}, f32[4,32,64]{2,1,0:T(8,128)S(1)}, u32[]{:S(2)}, u32[]{:S(2)}) collective-permute-start(f32[4,32,64]{2,1,0:T(8,128)S(1)} %pad_maximum_fusion.refs_8_), channel_id=1, source_target_pairs={{0,2},{1,3},{2,0},{3,1},{4,6},{5,7},{6,4},{7,5},{8,10},{9,11},{10,... | collective-permute-start | bytes 98312 | tf_op jit(solution)/shard_map/ppermute | solution.py:24
  13.3 11.4 %collective-permute-start.7 = (f32[4,32,64]{2,1,0:T(8,128)S(1)}, f32[4,32,64]{2,1,0:T(8,128)S(1)}, u32[]{:S(2)}, u32[]{:S(2)}) collective-permute-start(f32[4,32,64]{2,1,0:T(8,128)S(1)} %pad_maximum_fusion.refs_8_), channel_id=1, source_target_pairs={{0,3},{1,2},{2,1},{3,0},{4,7},{5,6},{6,5},{7,4},{8,11},{9,10},{10,... | collective-permute-start | bytes 98312 | tf_op jit(solution)/shard_map/ppermute | solution.py:24
  19.0 5.7 %copy-start.3 = (f32[4,32,64]{2,1,0:T(8,128)}, f32[4,32,64]{2,1,0:T(8,128)S(1)}, u32[]{:S(2)}) copy-start(f32[4,32,64]{2,1,0:T(8,128)S(1)} %collective-permute-done.5.refs_9_) | copy-start | bytes 98308
  24.7 0.6 %copy-start.4 = (f32[4,32,64]{2,1,0:T(8,128)}, f32[4,32,64]{2,1,0:T(8,128)S(1)}, u32[]{:S(2)}) copy-start(f32[4,32,64]{2,1,0:T(8,128)S(1)} %collective-permute-done.6.refs_10_) | copy-start | bytes 98308
  24.7 0.6 %copy-start.5 = (f32[4,32,64]{2,1,0:T(8,128)}, f32[4,32,64]{2,1,0:T(8,128)S(1)}, u32[]{:S(2)}) copy-start(f32[4,32,64]{2,1,0:T(8,128)S(1)} %collective-permute-done.7.refs_11_) | copy-start | bytes 98308
  24.7 0.7 %copy-start.1 = (bf16[160,512]{1,0:T(8,128)(2,1)}, bf16[160,512]{1,0:T(8,128)(2,1)S(1)}, u32[]{:S(2)}) copy-start(bf16[160,512]{1,0:T(8,128)(2,1)S(1)} %collective-permute-done.refs_3_) | copy-start | bytes 491524
  25.4 0.7 %copy-start.2 = (bf16[160,512]{1,0:T(8,128)(2,1)}, bf16[160,512]{1,0:T(8,128)(2,1)S(1)}, u32[]{:S(2)}) copy-start(bf16[160,512]{1,0:T(8,128)(2,1)S(1)} %collective-permute-done.1.refs_4_) | copy-start | bytes 491524

commit v11 on v8

--- a/solution.py
+++ b/solution.py
@@ -180,11 +180,6 @@
     from_pair = lax.ppermute(first, axes, [(i, i ^ 1) for i in range(ndev)])
     from_cross = lax.ppermute(last, axes, [(i, i - 1 + 2 * (i % 2)) for i in range(1, ndev - 1)])
     round_one = [from_mask(payloads[mask.bit_length() - 1], "sub", mask) for mask in range(1, sub_size)]
-    line = upper_own
-    for got in round_one:
-        line = line + got[1:]
-    round_two = [from_mask(line, "leaf", mask) for mask in range(1, leaf_size)]
-
     out = jax.ShapeDtypeStruct((nrhs, local_points), jnp.float32)
     local = pl.pallas_call(
         functools.partial(local_kernel, sub_size),
@@ -192,6 +187,11 @@
         in_specs=[VMEM, VMEM, VMEM, SMEM, SMEM],
         out_specs=VMEM,
     )(embeddings, directions, level_basis, neighbours, counts)
+    local, *round_one = lax.optimization_barrier((local, *round_one))
+    line = upper_own
+    for got in round_one:
+        line = line + got[1:]
+    round_two = [from_mask(line, "leaf", mask) for mask in range(1, leaf_size)]
 
     remote = round_one + round_two
     return pl.pallas_call(

time: 25.1 us -> 27.9 us (1.11)
  waiting for transfers between devices: 2.78 us -> 5.01 us
  starting transfers between devices: 10.8 us -> 11.7 us
  other arithmetic: 0.79 us -> 0.01 us
  local copies, waits for them, and re-layouts: 1.36 us -> 1.94 us
    ppermute x6, waiting for transfers between devices: 2.78 us -> 5.01 us  [from_mask(): return lax.ppermute(x, axis, pairs)]
    ppermute x6, starting transfers between devices: 8.33 us -> 10 us  [from_mask(): return lax.ppermute(x, axis, pairs)]
    ppermute x1, starting transfers between devices: 1.8 us -> 0.9 us  [on_device(): from_pair = lax.ppermute(first, axes, [(i, i ^ 1) for i in range(ndev)])]
    add x1, other arithmetic: 0.79 us -> 0.01 us  [on_device(): line = line + got[1:]]
    unnamed x16 -> x18, local copies, waits for them, and re-layouts: 1.36 us -> 1.94 us
  transfers between devices with their start and end apart: 8 -> 8, of which waited for: 3 -> 3; matrix products, arithmetic and copies ran while one was open for 3% -> 0% of each run, Pallas kernels for 14% -> 13%
where the time goes in v11:
time: 27.9 us; the launch traced here: 27.7 us
  starting transfers between devices  11.7 us (42%)
  Pallas kernels  8.91 us (32%)
  waiting for transfers between devices  5.01 us (18%)
  local copies, waits for them, and re-layouts  1.94 us (7%)
    ppermute x6, starting transfers between devices, from_mask(): return lax.ppermute(x, axis, pairs)  10 us
    ppermute x6, waiting for transfers between devices, from_mask(): return lax.ppermute(x, axis, pairs)  5.01 us
    pallas_call x1, Pallas kernels, on_device(): pl.pallas_call(functools.partial(local_kernel, sub_size), out_shape=out,...  3.58 us
    pallas_call x1, Pallas kernels, on_device(): pl.pallas_call(functools.partial(final_kernel, sub_size, sub_bits, leaf_b...  3.09 us
    pallas_call x1, Pallas kernels, on_device(): pl.pallas_call(functools.partial(send_kernel, loc_bits, sub_bits), out_sh...  2.24 us
    unnamed x18, local copies, waits for them, and re-layouts  1.94 us
    ppermute x1, starting transfers between devices, on_device(): from_pair = lax.ppermute(first, axes, [(i, i ^ 1) for i in range(ndev)])  0.9 us
    ppermute x1, starting transfers between devices, on_device(): lax.ppermute(last, axes, [(i, i - 1 + 2 * (i % 2)) for i in range(1, ndev...  0.79 us
  transfers between devices with their start and end apart: 8, of which 3 were waited for; matrix products, arithmetic and copies ran while one was open for 0% of the time, Pallas kernels for 13%

profile of v11, /device:TPU:0, one launch (start us, length us, event | category | flops | bytes accessed | tf_op | source)
XLA Modules:
  0.0 27.7 jit_solution(11520948246307349785)
XLA Ops:
  0.0 2.2 %shard_map.56 = (bf16[160,512]{1,0:T(8,128)(2,1)}, bf16[160,512]{1,0:T(8,128)(2,1)}, f32[2,32,64]{2,1,0:T(8,128)}, f32[3,32,64]{2,1,0:T(8,128)}, f32[3,32,64]{2,1,0:T(8,128)}) custom-call(bf16[128,1024]{1,0:T(8,128)(2,1)} %refs_0_.1, f32[32,1024]{1,0:T(8,128)} %refs_1_.1, bf16[5,64,1024]{2,1,0:T(8,128)(2,1)} %refs_5_.1), custom_call_target="tpu_custom_call" | custom-call | tf_op jit(solution)/shard_map/pallas_call | solution.py:172
  2.2 3.0 %collective-permute-start = (f32[3,32,64]{2,1,0:T(8,128)}, f32[3,32,64]{2,1,0:T(8,128)S(1)}, u32[]{:S(2)}, u32[]{:S(2)}) collective-permute-start(f32[3,32,64]{2,1,0:T(8,128)} %get-tuple-element.14), channel_id=1, source_target_pairs={{0,1},{1,0},{2,3},{3,2},{4,5},{5,4},{6,7},{7,6},{8,9},{9,8},{10,11... | collective-permute-start | bytes 73736 | tf_op jit(solution)/shard_map/ppermute | solution.py:24
  5.3 2.6 %collective-permute-start.1 = (f32[3,32,64]{2,1,0:T(8,128)}, f32[3,32,64]{2,1,0:T(8,128)S(1)}, u32[]{:S(2)}, u32[]{:S(2)}) collective-permute-start(f32[3,32,64]{2,1,0:T(8,128)} %get-tuple-element.15), channel_id=1, source_target_pairs={{0,2},{1,3},{2,0},{3,1},{4,6},{5,7},{6,4},{7,5},{8,10},{9,11},{10,... | collective-permute-start | bytes 73736 | tf_op jit(solution)/shard_map/ppermute | solution.py:24
  7.9 0.0 collective-permute-start.2
  7.9 0.9 %collective-permute-start.3 = (bf16[160,512]{1,0:T(8,128)(2,1)}, bf16[160,512]{1,0:T(8,128)(2,1)S(1)}, u32[]{:S(2)}, u32[]{:S(2)}) collective-permute-start(bf16[160,512]{1,0:T(8,128)(2,1)} %get-tuple-element.17), channel_id=1, source_target_pairs={{0,1},{1,0},{2,3},{3,2},{4,5},{5,4},{6,7},{7,6},{8,9},{9,8},{10,11... | collective-permute-start | bytes 491528 | tf_op jit(solution)/shard_map/ppermute | solution.py:180
  8.8 0.0 copy-start.8
  8.8 0.8 %collective-permute-start.4 = (bf16[160,512]{1,0:T(8,128)(2,1)}, bf16[160,512]{1,0:T(8,128)(2,1)S(1)}, u32[]{:S(2)}, u32[]{:S(2)}) collective-permute-start(bf16[160,512]{1,0:T(8,128)(2,1)} %get-tuple-element.18), channel_id=1, source_target_pairs={{1,2},{2,1},{3,4},{4,3},{5,6},{6,5},{7,8},{8,7},{9,10},{10,9},{11,... | collective-permute-start | bytes 491528 | tf_op jit(solution)/shard_map/ppermute | solution.py:181
  9.6 3.6 %shard_map.55.refs_2_ = f32[32,1024]{1,0:T(8,128)} custom-call(bf16[128,1024]{1,0:T(8,128)(2,1)} %refs_0_.1, f32[32,1024]{1,0:T(8,128)} %refs_1_.1, bf16[5,64,1024]{2,1,0:T(8,128)(2,1)} %refs_5_.1, s32[2,8]{1,0:T(2,128)} %refs_6_.1, s32[2]{0:T(128)} %refs_7_.1), custom_call_target="tpu_custom_call" | custom-call | tf_op jit(solution)/shard_map/pallas_call | solution.py:184
  13.1 0.0 collective-permute-done.refs_8_
  13.1 0.0 copy-start.2
  13.1 0.0 collective-permute-done.1.refs_9_
  13.1 0.0 copy-start.3
  13.2 1.4 %collective-permute-done.2.refs_10_ = f32[3,32,64]{2,1,0:T(8,128)S(1)} collective-permute-done((f32[3,32,64]{2,1,0:T(8,128)}, f32[3,32,64]{2,1,0:T(8,128)S(1)}, u32[]{:S(2)}, u32[]{:S(2)}) %collective-permute-start.2) | collective-permute-done | bytes 24608 | tf_op jit(solution)/shard_map/ppermute | solution.py:24
  14.5 0.0 copy-start.4
  14.5 0.0 copy-done.8
  14.6 0.0 copy-done.2
  14.6 0.0 copy-done.3
  14.6 0.6 %copy-done.4 = f32[3,32,64]{2,1,0:T(8,128)} copy-done((f32[3,32,64]{2,1,0:T(8,128)}, f32[3,32,64]{2,1,0:T(8,128)S(1)}, u32[]{:S(2)}) %copy-start.4) | copy-done | bytes 24600
  15.2 2.9 %collective-permute-start.5 = (f32[2,32,64]{2,1,0:T(8,128)S(1)}, f32[2,32,64]{2,1,0:T(8,128)S(1)}, u32[]{:S(2)}, u32[]{:S(2)}) collective-permute-start(f32[2,32,64]{2,1,0:T(8,128)S(1)} %slice_add_fusion), channel_id=1, source_target_pairs={{0,4},{4,0},{8,12},{12,8},{1,5},{5,1},{9,13},{13,9},{2,6},{6,2},{1... | collective-permute-start | bytes 49160 | tf_op jit(solution)/shard_map/ppermute | solution.py:24
  18.1 1.5 %collective-permute-start.6 = (f32[2,32,64]{2,1,0:T(8,128)S(1)}, f32[2,32,64]{2,1,0:T(8,128)S(1)}, u32[]{:S(2)}, u32[]{:S(2)}) collective-permute-start(f32[2,32,64]{2,1,0:T(8,128)S(1)} %slice_add_fusion), channel_id=1, source_target_pairs={{0,8},{4,12},{8,0},{12,4},{1,9},{5,13},{9,1},{13,5},{2,10},{6,14},... | collective-permute-start | bytes 49160 | tf_op jit(solution)/shard_map/ppermute | solution.py:24
  19.6 0.0 collective-permute-start.7
  19.6 0.0 collective-permute-done.5.refs_11_
  19.6 0.0 copy-start.5
  19.6 2.4 %collective-permute-done.6.refs_12_ = f32[2,32,64]{2,1,0:T(8,128)S(1)} collective-permute-done((f32[2,32,64]{2,1,0:T(8,128)S(1)}, f32[2,32,64]{2,1,0:T(8,128)S(1)}, u32[]{:S(2)}, u32[]{:S(2)}) %collective-permute-start.6) | collective-permute-done | bytes 16416 | tf_op jit(solution)/shard_map/ppermute | solution.py:24
  22.0 0.0 copy-start.6
  22.0 1.2 %collective-permute-done.7.refs_13_ = f32[2,32,64]{2,1,0:T(8,128)S(1)} collective-permute-done((f32[2,32,64]{2,1,0:T(8,128)S(1)}, f32[2,32,64]{2,1,0:T(8,128)S(1)}, u32[]{:S(2)}, u32[]{:S(2)}) %collective-permute-start.7) | collective-permute-done | bytes 16416 | tf_op jit(solution)/shard_map/ppermute | solution.py:24
  23.2 0.0 copy-start.7
  23.2 0.0 collective-permute-done.3.refs_3_
  23.2 0.0 copy-start
  23.2 0.0 collective-permute-done.4.refs_4_
  23.2 0.0 copy-done.5
  23.2 0.0 copy-done.6
  23.2 0.6 %copy-done.7 = f32[2,32,64]{2,1,0:T(8,128)} copy-done((f32[2,32,64]{2,1,0:T(8,128)}, f32[2,32,64]{2,1,0:T(8,128)S(1)}, u32[]{:S(2)}) %copy-start.7) | copy-done | bytes 16408
  23.8 0.1 copy-done
  23.9 0.0 copy-start.1
  23.9 0.7 %copy-done.1 = bf16[160,512]{1,0:T(8,128)(2,1)} copy-done((bf16[160,512]{1,0:T(8,128)(2,1)}, bf16[160,512]{1,0:T(8,128)(2,1)S(1)}, u32[]{:S(2)}) %copy-start.1) | copy-done | bytes 163864
  24.6 3.1 %shard_map.57 = f32[32,1024]{1,0:T(8,128)} custom-call(bf16[128,1024]{1,0:T(8,128)(2,1)} %refs_0_.1, f32[32,1024]{1,0:T(8,128)} %refs_1_.1, f32[32,1024]{1,0:T(8,128)} %shard_map.55.refs_2_, bf16[160,512]{1,0:T(8,128)(2,1)} %copy-done, bf16[160,512]{1,0:T(8,128)(2,1)} %copy-done.1, bf16[5,64,1024]{2,1,0:T(8,128)(2,1)} %refs_5_.1, ...), custom_call_target="tpu_custom_call", output_to_operand_aliasing={{}: (2, {})} | custom-call | tf_op jit(solution)/shard_map/pallas_call | solution.py:197
  (1 shorter events, 0.0 us)
Async XLA Ops:
  2.2 10.9 %collective-permute-start = (f32[3,32,64]{2,1,0:T(8,128)}, f32[3,32,64]{2,1,0:T(8,128)S(1)}, u32[]{:S(2)}, u32[]{:S(2)}) collective-permute-start(f32[3,32,64]{2,1,0:T(8,128)} %get-tuple-element.14), channel_id=1, source_target_pairs={{0,1},{1,0},{2,3},{3,2},{4,5},{5,4},{6,7},{7,6},{8,9},{9,8},{10,11... | collective-permute-start | bytes 73736 | tf_op jit(solution)/shard_map/ppermute | solution.py:24
  5.3 7.9 %collective-permute-start.1 = (f32[3,32,64]{2,1,0:T(8,128)}, f32[3,32,64]{2,1,0:T(8,128)S(1)}, u32[]{:S(2)}, u32[]{:S(2)}) collective-permute-start(f32[3,32,64]{2,1,0:T(8,128)} %get-tuple-element.15), channel_id=1, source_target_pairs={{0,2},{1,3},{2,0},{3,1},{4,6},{5,7},{6,4},{7,5},{8,10},{9,11},{10,... | collective-permute-start | bytes 73736 | tf_op jit(solution)/shard_map/ppermute | solution.py:24
  7.9 6.7 %collective-permute-start.2 = (f32[3,32,64]{2,1,0:T(8,128)}, f32[3,32,64]{2,1,0:T(8,128)S(1)}, u32[]{:S(2)}, u32[]{:S(2)}) collective-permute-start(f32[3,32,64]{2,1,0:T(8,128)} %get-tuple-element.15), channel_id=1, source_target_pairs={{0,3},{1,2},{2,1},{3,0},{4,7},{5,6},{6,5},{7,4},{8,11},{9,10},{10,... | collective-permute-start | bytes 73736 | tf_op jit(solution)/shard_map/ppermute | solution.py:24
  7.9 15.3 %collective-permute-start.3 = (bf16[160,512]{1,0:T(8,128)(2,1)}, bf16[160,512]{1,0:T(8,128)(2,1)S(1)}, u32[]{:S(2)}, u32[]{:S(2)}) collective-permute-start(bf16[160,512]{1,0:T(8,128)(2,1)} %get-tuple-element.17), channel_id=1, source_target_pairs={{0,1},{1,0},{2,3},{3,2},{4,5},{5,4},{6,7},{7,6},{8,9},{9,8},{10,11... | collective-permute-start | bytes 491528 | tf_op jit(solution)/shard_map/ppermute | solution.py:180
  8.8 5.8 %copy-start.8 = (f32[2,32,64]{2,1,0:T(8,128)S(1)}, f32[2,32,64]{2,1,0:T(8,128)}, u32[]{:S(2)}) copy-start(f32[2,32,64]{2,1,0:T(8,128)} %get-tuple-element.22) | copy-start | bytes 49156
  8.8 14.4 %collective-permute-start.4 = (bf16[160,512]{1,0:T(8,128)(2,1)}, bf16[160,512]{1,0:T(8,128)(2,1)S(1)}, u32[]{:S(2)}, u32[]{:S(2)}) collective-permute-start(bf16[160,512]{1,0:T(8,128)(2,1)} %get-tuple-element.18), channel_id=1, source_target_pairs={{1,2},{2,1},{3,4},{4,3},{5,6},{6,5},{7,8},{8,7},{9,10},{10,9},{11,... | collective-permute-start | bytes 491528 | tf_op jit(solution)/shard_map/ppermute | solution.py:181
  13.1 1.4 %copy-start.2 = (f32[3,32,64]{2,1,0:T(8,128)}, f32[3,32,64]{2,1,0:T(8,128)S(1)}, u32[]{:S(2)}) copy-start(f32[3,32,64]{2,1,0:T(8,128)S(1)} %collective-permute-done.refs_8_) | copy-start | bytes 73732
  13.1 1.4 %copy-start.3 = (f32[3,32,64]{2,1,0:T(8,128)}, f32[3,32,64]{2,1,0:T(8,128)S(1)}, u32[]{:S(2)}) copy-start(f32[3,32,64]{2,1,0:T(8,128)S(1)} %collective-permute-done.1.refs_9_) | copy-start | bytes 73732
  14.5 0.6 %copy-start.4 = (f32[3,32,64]{2,1,0:T(8,128)}, f32[3,32,64]{2,1,0:T(8,128)S(1)}, u32[]{:S(2)}) copy-start(f32[3,32,64]{2,1,0:T(8,128)S(1)} %collective-permute-done.2.refs_10_) | copy-start | bytes 73732
  15.2 4.4 %collective-permute-start.5 = (f32[2,32,64]{2,1,0:T(8,128)S(1)}, f32[2,32,64]{2,1,0:T(8,128)S(1)}, u32[]{:S(2)}, u32[]{:S(2)}) collective-permute-start(f32[2,32,64]{2,1,0:T(8,128)S(1)} %slice_add_fusion), channel_id=1, source_target_pairs={{0,4},{4,0},{8,12},{12,8},{1,5},{5,1},{9,13},{13,9},{2,6},{6,2},{1... | collective-permute-start | bytes 49160 | tf_op jit(solution)/shard_map/ppermute | solution.py:24
  18.1 3.9 %collective-permute-start.6 = (f32[2,32,64]{2,1,0:T(8,128)S(1)}, f32[2,32,64]{2,1,0:T(8,128)S(1)}, u32[]{:S(2)}, u32[]{:S(2)}) collective-permute-start(f32[2,32,64]{2,1,0:T(8,128)S(1)} %slice_add_fusion), channel_id=1, source_target_pairs={{0,8},{4,12},{8,0},{12,4},{1,9},{5,13},{9,1},{13,5},{2,10},{6,14},... | collective-permute-start | bytes 49160 | tf_op jit(solution)/shard_map/ppermute | solution.py:24
  19.6 3.6 %collective-permute-start.7 = (f32[2,32,64]{2,1,0:T(8,128)S(1)}, f32[2,32,64]{2,1,0:T(8,128)S(1)}, u32[]{:S(2)}, u32[]{:S(2)}) collective-permute-start(f32[2,32,64]{2,1,0:T(8,128)S(1)} %slice_add_fusion), channel_id=1, source_target_pairs={{0,12},{4,8},{8,4},{12,0},{1,13},{5,9},{9,5},{13,1},{2,14},{6,10},... | collective-permute-start | bytes 49160 | tf_op jit(solution)/shard_map/ppermute | solution.py:24
  19.6 3.6 %copy-start.5 = (f32[2,32,64]{2,1,0:T(8,128)}, f32[2,32,64]{2,1,0:T(8,128)S(1)}, u32[]{:S(2)}) copy-start(f32[2,32,64]{2,1,0:T(8,128)S(1)} %collective-permute-done.5.refs_11_) | copy-start | bytes 49156
  22.0 1.2 %copy-start.6 = (f32[2,32,64]{2,1,0:T(8,128)}, f32[2,32,64]{2,1,0:T(8,128)S(1)}, u32[]{:S(2)}) copy-start(f32[2,32,64]{2,1,0:T(8,128)S(1)} %collective-permute-done.6.refs_12_) | copy-start | bytes 49156
  23.2 0.6 %copy-start.7 = (f32[2,32,64]{2,1,0:T(8,128)}, f32[2,32,64]{2,1,0:T(8,128)S(1)}, u32[]{:S(2)}) copy-start(f32[2,32,64]{2,1,0:T(8,128)S(1)} %collective-permute-done.7.refs_13_) | copy-start | bytes 49156
  23.2 0.7 %copy-start = (bf16[160,512]{1,0:T(8,128)(2,1)}, bf16[160,512]{1,0:T(8,128)(2,1)S(1)}, u32[]{:S(2)}) copy-start(bf16[160,512]{1,0:T(8,128)(2,1)S(1)} %collective-permute-done.3.refs_3_) | copy-start | bytes 491524
  23.9 0.7 %copy-start.1 = (bf16[160,512]{1,0:T(8,128)(2,1)}, bf16[160,512]{1,0:T(8,128)(2,1)S(1)}, u32[]{:S(2)}) copy-start(bf16[160,512]{1,0:T(8,128)(2,1)S(1)} %collective-permute-done.4.refs_4_) | copy-start | bytes 491524

commit v12 on v8

--- a/solution.py
+++ b/solution.py
@@ -32,24 +32,49 @@
     return lax.dot_general(a, b, (((1,), (0,)), ((), ())), preferred_element_type=jnp.float32)
 
 
-def send_kernel(loc_bits, sub_bits, emb_ref, dirs_ref, basis_ref, first_ref, last_ref, upper_ref, *payload_refs):
+def split_rows(x, width):
+    groups = width // x.shape[1]
+    step = x.shape[0] // groups
+    return jnp.concatenate([x[g * step : (g + 1) * step] for g in range(groups)], axis=1)
+
+
+def join_rows(x, columns):
+    groups = x.shape[1] // columns
+    return jnp.concatenate([x[:, g * columns : (g + 1) * columns] for g in range(groups)], axis=0)
+
+
+def send_kernel(loc_bits, emb_ref, dirs_ref, basis_ref, pair_ref, cross_ref, parts_ref):
     width_e = emb_ref.shape[0]
     local_points = emb_ref.shape[1]
+    nrhs = dirs_ref.shape[0]
     values = dirs_ref[...].astype(jnp.bfloat16)
     even = lax.axis_index("sub") % 2 == 0
     head_points, tail_points = emb_ref[:, :LEAF], emb_ref[:, local_points - LEAF :]
     head_values, tail_values = values[:, :LEAF], values[:, local_points - LEAF :]
-    first_ref[:width_e, :] = jnp.where(even, tail_points, head_points)
-    first_ref[width_e:, :] = jnp.where(even, tail_values, head_values)
-    last_ref[:width_e, :] = jnp.where(even, head_points, tail_points)
-    last_ref[width_e:, :] = jnp.where(even, head_values, tail_values)
-    for level in range(upper_ref.shape[0]):
-        part = nt_dot(values, basis_ref[loc_bits + sub_bits + level])
-        upper_ref[level] = part
-        for payload_ref in payload_refs:
-            payload_ref[1 + level] = part
-    for level, payload_ref in enumerate(payload_refs):
-        payload_ref[0] = nt_dot(values, basis_ref[loc_bits + level])
+    pair_ref[:width_e, :] = jnp.where(even, tail_points, head_points)
+    pair_ref[width_e : width_e + nrhs, :] = jnp.where(even, tail_values, head_values)
+    cross_ref[:width_e, :] = jnp.where(even, head_points, tail_points)
+    cross_ref[width_e:, :] = jnp.where(even, head_values, tail_values)
+    levels, rank = parts_ref.shape[1] // basis_ref.shape[1], basis_ref.shape[1]
+    stacked = basis_ref[loc_bits : loc_bits + levels].reshape(levels * rank, local_points)
+    parts = nt_dot(values, stacked)
+    parts_ref[...] = parts
+    rows = split_rows(parts, LEAF)
+    high = rows.astype(jnp.bfloat16)
+    rest = rows - high.astype(jnp.float32)
+    middle = rest.astype(jnp.bfloat16)
+    low = (rest - middle.astype(jnp.float32)).astype(jnp.bfloat16)
+    start = width_e + nrhs
+    step = rows.shape[0]
+    pair_ref[start : start + step, :] = high
+    pair_ref[start + step : start + 2 * step, :] = middle
+    pair_ref[start + 2 * step : start + 3 * step, :] = low
+
+
+def unpack_parts(pair, start, step, columns):
+    pieces = pair[start : start + 3 * step].astype(jnp.float32)
+    rows = (pieces[:step] + pieces[step : 2 * step]) + pieces[2 * step :]
+    return join_rows(rows, columns)
 
 
 class Leaves:
@@ -110,34 +135,40 @@
     sub_masks = 2**sub_bits - 1
     leaf_masks = 2**leaf_bits - 1
     emb_ref, dirs_ref, local_ref, pair_ref, cross_ref, basis_ref, neighbours_ref, counts_ref = refs[:8]
-    round_one = refs[8 : 8 + sub_masks]
-    round_two = refs[8 + sub_masks : 8 + sub_masks + leaf_masks]
-    out_ref = refs[8 + sub_masks + leaf_masks]
+    round_one = refs[8 : 8 + sub_masks - 1]
+    round_two = refs[8 + sub_masks - 1 : 8 + sub_masks - 1 + leaf_masks]
+    out_ref = refs[8 + sub_masks - 1 + leaf_masks]
     lv = Leaves(emb_ref, dirs_ref, neighbours_ref, counts_ref, sub_size)
     rank = basis_ref.shape[1]
+    nrhs = dirs_ref.shape[0]
     local_points = lv.local_points
-
-    sibling = [None] * (sub_bits + leaf_bits)
-    line = None
-    for mask, got_ref in enumerate(round_one, start=1):
-        level = mask.bit_length() - 1
-        got = got_ref[0]
-        sibling[level] = got if sibling[level] is None else sibling[level] + got
+    levels = sub_bits + leaf_bits
+    lower_width = rank * sub_bits
+
+    pair, cross = pair_ref[...], cross_ref[...]
+    step = nrhs * rank * levels // LEAF
+    from_pair = unpack_parts(pair, lv.width_e + nrhs, step, rank * levels)
+    column_level = lax.broadcasted_iota(jnp.int32, (1, rank * levels), 1) // rank
+    lower_level = column_level[:, :lower_width]
+    upper_level = column_level[:, : rank * leaf_bits]
+    lower = jnp.where(lower_level == 0, from_pair[:, :lower_width], 0.0)
+    for mask, got_ref in enumerate(round_one, start=2):
+        lower = lower + jnp.where(lower_level == mask.bit_length() - 1, got_ref[:, :lower_width], 0.0)
+    upper = None
     for mask, got_ref in enumerate(round_two, start=1):
-        level = sub_bits + mask.bit_length() - 1
-        got = got_ref[level - sub_bits]
-        sibling[level] = got if sibling[level] is None else sibling[level] + got
-
-    far = None
-    for bit in range(sub_bits + leaf_bits):
-        factor = 1.0 / math.sqrt(rank * local_points * 2**bit)
-        scaled = (sibling[bit] * factor).astype(jnp.bfloat16)
-        term = nn_dot(scaled, basis_ref[loc_bits + bit])
-        far = term if far is None else far + term
+        term = jnp.where(upper_level == mask.bit_length() - 1, got_ref[...], 0.0)
+        upper = term if upper is None else upper + term
+    sibling = jnp.concatenate([lower, upper], axis=1)
+    factor = jnp.zeros((1, rank * levels), jnp.float32)
+    for bit in range(levels):
+        factor = jnp.where(column_level == bit, 1.0 / math.sqrt(rank * local_points * 2**bit), factor)
+    scaled = (sibling * factor).astype(jnp.bfloat16)
+    stacked = basis_ref[loc_bits : loc_bits + levels].reshape(levels * rank, local_points)
+    far = nn_dot(scaled, stacked)
 
     even = lax.axis_index("sub") % 2 == 0
-    pair, cross = pair_ref[...], cross_ref[...]
-    left, right = jnp.where(even, cross, pair), jnp.where(even, pair, cross)
+    halo_pair = pair[: lv.width_e + nrhs]
+    left, right = jnp.where(even, cross, halo_pair), jnp.where(even, halo_pair, cross)
     halo = {}
     for j, received, offset in ((0, left, -1), (lv.count - 1, right, 1)):
         halo_points = received[: lv.width_e, :]
@@ -166,23 +197,25 @@
     dev_bits = sub_bits + leaf_bits
     loc_bits = level_basis.shape[0] - dev_bits
 
-    halo = jax.ShapeDtypeStruct((width_e + nrhs, LEAF), jnp.bfloat16)
-    upper = jax.ShapeDtypeStruct((leaf_bits, nrhs, rank), jnp.float32)
-    payload = jax.ShapeDtypeStruct((1 + leaf_bits, nrhs, rank), jnp.float32)
-    first, last, upper_own, *payloads = pl.pallas_call(
-        functools.partial(send_kernel, loc_bits, sub_bits),
-        out_shape=(halo, halo, upper) + (payload,) * sub_bits,
+    step = nrhs * rank * dev_bits // LEAF
+    pair_shape = jax.ShapeDtypeStruct((width_e + nrhs + 3 * step, LEAF), jnp.bfloat16)
+    cross_shape = jax.ShapeDtypeStruct((width_e + nrhs, LEAF), jnp.bfloat16)
+    parts_shape = jax.ShapeDtypeStruct((nrhs, rank * dev_bits), jnp.float32)
+    pair, cross, parts = pl.pallas_call(
+        functools.partial(send_kernel, loc_bits),
+        out_shape=(pair_shape, cross_shape, parts_shape),
         in_specs=[VMEM, VMEM, VMEM],
-        out_specs=(VMEM,) * (3 + sub_bits),
+        out_specs=(VMEM, VMEM, VMEM),
     )(embeddings, directions, level_basis)
 
     ndev = sub_size * leaf_size
-    from_pair = lax.ppermute(first, axes, [(i, i ^ 1) for i in range(ndev)])
-    from_cross = lax.ppermute(last, axes, [(i, i - 1 + 2 * (i % 2)) for i in range(1, ndev - 1)])
-    round_one = [from_mask(payloads[mask.bit_length() - 1], "sub", mask) for mask in range(1, sub_size)]
-    line = upper_own
+    from_pair = lax.ppermute(pair, axes, [(i, i ^ 1) for i in range(ndev)])
+    round_one = [from_mask(parts, "sub", mask) for mask in range(2, sub_size)]
+    from_cross = lax.ppermute(cross, axes, [(i, i - 1 + 2 * (i % 2)) for i in range(1, ndev - 1)])
+    upper = slice(rank * sub_bits, rank * dev_bits)
+    line = parts[:, upper] + unpack_parts(from_pair, width_e + nrhs, step, rank * dev_bits)[:, upper]
     for got in round_one:
-        line = line + got[1:]
+        line = line + got[:, upper]
     round_two = [from_mask(line, "leaf", mask) for mask in range(1, leaf_size)]
 
     out = jax.ShapeDtypeStruct((nrhs, local_points), jnp.float32)

time: 25.1 us -> 25.1 us (level)
  waiting for transfers between devices: 2.78 us -> 5.84 us
  starting transfers between devices: 10.8 us -> 8.14 us
  other arithmetic: 0.79 us -> 0.03 us
  local copies, waits for them, and re-layouts: 1.36 us -> 1.83 us
    ppermute x6 -> x5, starting transfers between devices: 8.33 us -> 4.45 us  [from_mask(): return lax.ppermute(x, axis, pairs)]
    ppermute x2, waiting for transfers between devices: 0.01 us -> 2.9 us  [the longest x1 2.9 us: on_device(): from_pair = lax.ppermute(pair, axes, [(i, i ^ 1) for i in range(ndev)])]
    ppermute x2, starting transfers between devices: 2.45 us -> 3.68 us  [the longest x1 3.02 us: on_device(): from_pair = lax.ppermute(pair, axes, [(i, i ^ 1) for i in range(ndev)])]
    add x1 -> x2, other arithmetic: 0.79 us -> 0.02 us  [the longest x1 0.01 us: unpack_parts(): rows = pieces[:step] + pieces[step:2 * step] + pieces[2 * step:]]
    unnamed x16, local copies, waits for them, and re-layouts: 1.36 us -> 1.82 us
    ppermute x6 -> x5, waiting for transfers between devices: 2.78 us -> 2.93 us  [from_mask(): return lax.ppermute(x, axis, pairs)]
  transfers between devices with their start and end apart: 8 -> 7, of which waited for: 3 -> 2; matrix products, arithmetic and copies ran while one was open for 3% -> 0% of each run, Pallas kernels for 14% -> 14%
where the time goes in v12:
time: 25.1 us; the launch traced here: 24.8 us
  Pallas kernels  8.9 us (35%)
  starting transfers between devices  8.14 us (32%)
  waiting for transfers between devices  5.84 us (23%)
  local copies, waits for them, and re-layouts  1.83 us (7%)
    ppermute x5, starting transfers between devices, from_mask(): return lax.ppermute(x, axis, pairs)  4.45 us
    pallas_call x1, Pallas kernels, on_device(): pl.pallas_call(functools.partial(local_kernel, sub_size), out_shape=out,...  3.59 us
    pallas_call x1, Pallas kernels, on_device(): pl.pallas_call(functools.partial(final_kernel, sub_size, sub_bits, leaf_b...  3.12 us
    ppermute x1, starting transfers between devices, on_device(): from_pair = lax.ppermute(pair, axes, [(i, i ^ 1) for i in range(ndev)])  3.02 us
    ppermute x5, waiting for transfers between devices, from_mask(): return lax.ppermute(x, axis, pairs)  2.93 us
    ppermute x1, waiting for transfers between devices, on_device(): from_pair = lax.ppermute(pair, axes, [(i, i ^ 1) for i in range(ndev)])  2.9 us
    pallas_call x1, Pallas kernels, on_device(): pl.pallas_call(functools.partial(send_kernel, loc_bits), out_shape=(pair_...  2.19 us
    unnamed x16, local copies, waits for them, and re-layouts  1.82 us
  transfers between devices with their start and end apart: 7, of which 2 were waited for; matrix products, arithmetic and copies ran while one was open for 0% of the time, Pallas kernels for 14%

profile of v12, /device:TPU:0, one launch (start us, length us, event | category | flops | bytes accessed | tf_op | source)
XLA Modules:
  0.0 24.8 jit_solution(12615094491780877337)
XLA Ops:
  0.0 2.2 %shard_map.56 = (bf16[208,512]{1,0:T(8,128)(2,1)}, bf16[160,512]{1,0:T(8,128)(2,1)}, f32[32,256]{1,0:T(8,128)}) custom-call(bf16[128,1024]{1,0:T(8,128)(2,1)} %refs_0_.1, f32[32,1024]{1,0:T(8,128)} %refs_1_.1, bf16[5,64,1024]{2,1,0:T(8,128)(2,1)} %refs_5_.1), custom_call_target="tpu_custom_call" | custom-call | tf_op jit(solution)/shard_map/pallas_call | solution.py:204
  2.2 3.0 %collective-permute-start = (bf16[208,512]{1,0:T(8,128)(2,1)}, bf16[208,512]{1,0:T(8,128)(2,1)S(1)}, u32[]{:S(2)}, u32[]{:S(2)}) collective-permute-start(bf16[208,512]{1,0:T(8,128)(2,1)} %get-tuple-element.8), channel_id=1, source_target_pairs={{0,1},{1,0},{2,3},{3,2},{4,5},{5,4},{6,7},{7,6},{8,9},{9,8},{10,11... | collective-permute-start | bytes 638984 | tf_op jit(solution)/shard_map/ppermute | solution.py:212
  5.2 2.6 %collective-permute-start.2 = (f32[32,256]{1,0:T(8,128)}, f32[32,256]{1,0:T(8,128)S(1)}, u32[]{:S(2)}, u32[]{:S(2)}) collective-permute-start(f32[32,256]{1,0:T(8,128)} %get-tuple-element.10), channel_id=1, source_target_pairs={{0,2},{1,3},{2,0},{3,1},{4,6},{5,7},{6,4},{7,5},{8,10},{9,11},{10,... | collective-permute-start | bytes 98312 | tf_op jit(solution)/shard_map/ppermute | solution.py:24
  7.8 0.0 collective-permute-start.3
  7.8 0.7 %collective-permute-start.1 = (bf16[160,512]{1,0:T(8,128)(2,1)}, bf16[160,512]{1,0:T(8,128)(2,1)S(1)}, u32[]{:S(2)}, u32[]{:S(2)}) collective-permute-start(bf16[160,512]{1,0:T(8,128)(2,1)} %get-tuple-element.9), channel_id=1, source_target_pairs={{1,2},{2,1},{3,4},{4,3},{5,6},{6,5},{7,8},{8,7},{9,10},{10,9},{11,... | collective-permute-start | bytes 491528 | tf_op jit(solution)/shard_map/ppermute | solution.py:214
  8.5 2.9 %collective-permute-done.refs_3_ = bf16[208,512]{1,0:T(8,128)(2,1)S(1)} collective-permute-done((bf16[208,512]{1,0:T(8,128)(2,1)}, bf16[208,512]{1,0:T(8,128)(2,1)S(1)}, u32[]{:S(2)}, u32[]{:S(2)}) %collective-permute-start) | collective-permute-done | bytes 213024 | tf_op jit(solution)/shard_map/ppermute | solution.py:212
  11.4 0.0 copy-start
  11.4 0.0 copy-start.7
  11.4 0.0 collective-permute-done.2.refs_8_
  11.4 0.0 copy-start.2
  11.5 2.9 %collective-permute-done.3.refs_9_ = f32[32,256]{1,0:T(8,128)S(1)} collective-permute-done((f32[32,256]{1,0:T(8,128)}, f32[32,256]{1,0:T(8,128)S(1)}, u32[]{:S(2)}, u32[]{:S(2)}) %collective-permute-start.3) | collective-permute-done | bytes 32800 | tf_op jit(solution)/shard_map/ppermute | solution.py:24
  14.4 0.0 copy-start.3
  14.4 0.0 copy-done.7
  14.4 0.0 copy-done
  14.4 0.0 copy-done.2
  14.4 0.6 %copy-done.3 = f32[32,256]{1,0:T(8,128)} copy-done((f32[32,256]{1,0:T(8,128)}, f32[32,256]{1,0:T(8,128)S(1)}, u32[]{:S(2)}) %copy-start.3) | copy-done | bytes 32792
  15.0 0.0 collective-permute-start.4
  15.0 1.5 %collective-permute-start.5 = (f32[32,128]{1,0:T(8,128)S(1)}, f32[32,128]{1,0:T(8,128)S(1)}, u32[]{:S(2)}, u32[]{:S(2)}) collective-permute-start(f32[32,128]{1,0:T(8,128)S(1)} %slice_add_fusion.2), channel_id=1, source_target_pairs={{0,8},{4,12},{8,0},{12,4},{1,9},{5,13},{9,1},{13,5},{2,10},{6,14},... | collective-permute-start | bytes 49160 | tf_op jit(solution)/shard_map/ppermute | solution.py:24
  16.5 0.4 %collective-permute-start.6 = (f32[32,128]{1,0:T(8,128)S(1)}, f32[32,128]{1,0:T(8,128)S(1)}, u32[]{:S(2)}, u32[]{:S(2)}) collective-permute-start(f32[32,128]{1,0:T(8,128)S(1)} %slice_add_fusion.2), channel_id=1, source_target_pairs={{0,12},{4,8},{8,4},{12,0},{1,13},{5,9},{9,5},{13,1},{2,14},{6,10},... | collective-permute-start | bytes 49160 | tf_op jit(solution)/shard_map/ppermute | solution.py:24
  16.9 3.6 %shard_map.55.refs_2_ = f32[32,1024]{1,0:T(8,128)} custom-call(bf16[128,1024]{1,0:T(8,128)(2,1)} %refs_0_.1, f32[32,1024]{1,0:T(8,128)} %refs_1_.1, bf16[5,64,1024]{2,1,0:T(8,128)(2,1)} %refs_5_.1, s32[2,8]{1,0:T(2,128)} %refs_6_.1, s32[2]{0:T(128)} %refs_7_.1), custom_call_target="tpu_custom_call" | custom-call | tf_op jit(solution)/shard_map/pallas_call | solution.py:222
  20.4 0.0 collective-permute-done.1.refs_4_
  20.4 0.0 copy-start.1
  20.4 0.0 collective-permute-done.4.refs_10_
  20.5 0.0 copy-start.4
  20.5 0.0 collective-permute-done.5.refs_11_
  20.5 0.0 copy-start.5
  20.5 0.0 collective-permute-done.6.refs_12_
  20.5 0.6 %copy-done.1 = bf16[160,512]{1,0:T(8,128)(2,1)} copy-done((bf16[160,512]{1,0:T(8,128)(2,1)}, bf16[160,512]{1,0:T(8,128)(2,1)S(1)}, u32[]{:S(2)}) %copy-start.1) | copy-done | bytes 163864
  21.1 0.0 copy-done.4
  21.1 0.0 copy-done.5
  21.1 0.0 copy-start.6
  21.1 0.6 %copy-done.6 = f32[32,128]{1,0:T(8,128)} copy-done((f32[32,128]{1,0:T(8,128)}, f32[32,128]{1,0:T(8,128)S(1)}, u32[]{:S(2)}) %copy-start.6) | copy-done | bytes 16408
  21.7 3.1 %shard_map.57 = f32[32,1024]{1,0:T(8,128)} custom-call(bf16[128,1024]{1,0:T(8,128)(2,1)} %refs_0_.1, f32[32,1024]{1,0:T(8,128)} %refs_1_.1, f32[32,1024]{1,0:T(8,128)} %shard_map.55.refs_2_, bf16[208,512]{1,0:T(8,128)(2,1)} %copy-done, bf16[160,512]{1,0:T(8,128)(2,1)} %copy-done.1, bf16[5,64,1024]{2,1,0:T(8,128)(2,1)} %refs_5_.1, ...), custom_call_target="tpu_custom_call", output_to_operand_aliasing={{}: (2, {})} | custom-call | tf_op jit(solution)/shard_map/pallas_call | solution.py:230
  (4 shorter events, 0.0 us)
Async XLA Ops:
  2.2 9.2 %collective-permute-start = (bf16[208,512]{1,0:T(8,128)(2,1)}, bf16[208,512]{1,0:T(8,128)(2,1)S(1)}, u32[]{:S(2)}, u32[]{:S(2)}) collective-permute-start(bf16[208,512]{1,0:T(8,128)(2,1)} %get-tuple-element.8), channel_id=1, source_target_pairs={{0,1},{1,0},{2,3},{3,2},{4,5},{5,4},{6,7},{7,6},{8,9},{9,8},{10,11... | collective-permute-start | bytes 638984 | tf_op jit(solution)/shard_map/ppermute | solution.py:212
  5.2 6.2 %collective-permute-start.2 = (f32[32,256]{1,0:T(8,128)}, f32[32,256]{1,0:T(8,128)S(1)}, u32[]{:S(2)}, u32[]{:S(2)}) collective-permute-start(f32[32,256]{1,0:T(8,128)} %get-tuple-element.10), channel_id=1, source_target_pairs={{0,2},{1,3},{2,0},{3,1},{4,6},{5,7},{6,4},{7,5},{8,10},{9,11},{10,... | collective-permute-start | bytes 98312 | tf_op jit(solution)/shard_map/ppermute | solution.py:24
  7.8 6.6 %collective-permute-start.3 = (f32[32,256]{1,0:T(8,128)}, f32[32,256]{1,0:T(8,128)S(1)}, u32[]{:S(2)}, u32[]{:S(2)}) collective-permute-start(f32[32,256]{1,0:T(8,128)} %get-tuple-element.10), channel_id=1, source_target_pairs={{0,3},{1,2},{2,1},{3,0},{4,7},{5,6},{6,5},{7,4},{8,11},{9,10},{10,... | collective-permute-start | bytes 98312 | tf_op jit(solution)/shard_map/ppermute | solution.py:24
  7.8 12.6 %collective-permute-start.1 = (bf16[160,512]{1,0:T(8,128)(2,1)}, bf16[160,512]{1,0:T(8,128)(2,1)S(1)}, u32[]{:S(2)}, u32[]{:S(2)}) collective-permute-start(bf16[160,512]{1,0:T(8,128)(2,1)} %get-tuple-element.9), channel_id=1, source_target_pairs={{1,2},{2,1},{3,4},{4,3},{5,6},{6,5},{7,8},{8,7},{9,10},{10,9},{11,... | collective-permute-start | bytes 491528 | tf_op jit(solution)/shard_map/ppermute | solution.py:214
  11.4 3.0 %copy-start = (bf16[208,512]{1,0:T(8,128)(2,1)}, bf16[208,512]{1,0:T(8,128)(2,1)S(1)}, u32[]{:S(2)}) copy-start(bf16[208,512]{1,0:T(8,128)(2,1)S(1)} %collective-permute-done.refs_3_) | copy-start | bytes 638980
  11.4 3.0 %copy-start.7 = (f32[32,256]{1,0:T(8,128)S(1)}, f32[32,256]{1,0:T(8,128)}, u32[]{:S(2)}) copy-start(f32[32,256]{1,0:T(8,128)} %get-tuple-element.10) | copy-start | bytes 98308
  11.4 3.0 %copy-start.2 = (f32[32,256]{1,0:T(8,128)}, f32[32,256]{1,0:T(8,128)S(1)}, u32[]{:S(2)}) copy-start(f32[32,256]{1,0:T(8,128)S(1)} %collective-permute-done.2.refs_8_) | copy-start | bytes 98308
  14.4 0.6 %copy-start.3 = (f32[32,256]{1,0:T(8,128)}, f32[32,256]{1,0:T(8,128)S(1)}, u32[]{:S(2)}) copy-start(f32[32,256]{1,0:T(8,128)S(1)} %collective-permute-done.3.refs_9_) | copy-start | bytes 98308
  15.0 5.5 %collective-permute-start.4 = (f32[32,128]{1,0:T(8,128)S(1)}, f32[32,128]{1,0:T(8,128)S(1)}, u32[]{:S(2)}, u32[]{:S(2)}) collective-permute-start(f32[32,128]{1,0:T(8,128)S(1)} %slice_add_fusion.2), channel_id=1, source_target_pairs={{0,4},{4,0},{8,12},{12,8},{1,5},{5,1},{9,13},{13,9},{2,6},{6,2},{1... | collective-permute-start | bytes 49160 | tf_op jit(solution)/shard_map/ppermute | solution.py:24
  15.0 5.5 %collective-permute-start.5 = (f32[32,128]{1,0:T(8,128)S(1)}, f32[32,128]{1,0:T(8,128)S(1)}, u32[]{:S(2)}, u32[]{:S(2)}) collective-permute-start(f32[32,128]{1,0:T(8,128)S(1)} %slice_add_fusion.2), channel_id=1, source_target_pairs={{0,8},{4,12},{8,0},{12,4},{1,9},{5,13},{9,1},{13,5},{2,10},{6,14},... | collective-permute-start | bytes 49160 | tf_op jit(solution)/shard_map/ppermute | solution.py:24
  16.5 4.0 %collective-permute-start.6 = (f32[32,128]{1,0:T(8,128)S(1)}, f32[32,128]{1,0:T(8,128)S(1)}, u32[]{:S(2)}, u32[]{:S(2)}) collective-permute-start(f32[32,128]{1,0:T(8,128)S(1)} %slice_add_fusion.2), channel_id=1, source_target_pairs={{0,12},{4,8},{8,4},{12,0},{1,13},{5,9},{9,5},{13,1},{2,14},{6,10},... | collective-permute-start | bytes 49160 | tf_op jit(solution)/shard_map/ppermute | solution.py:24
  20.4 0.7 %copy-start.1 = (bf16[160,512]{1,0:T(8,128)(2,1)}, bf16[160,512]{1,0:T(8,128)(2,1)S(1)}, u32[]{:S(2)}) copy-start(bf16[160,512]{1,0:T(8,128)(2,1)S(1)} %collective-permute-done.1.refs_4_) | copy-start | bytes 491524
  20.5 0.7 %copy-start.4 = (f32[32,128]{1,0:T(8,128)}, f32[32,128]{1,0:T(8,128)S(1)}, u32[]{:S(2)}) copy-start(f32[32,128]{1,0:T(8,128)S(1)} %collective-permute-done.4.refs_10_) | copy-start | bytes 49156
  20.5 0.7 %copy-start.5 = (f32[32,128]{1,0:T(8,128)}, f32[32,128]{1,0:T(8,128)S(1)}, u32[]{:S(2)}) copy-start(f32[32,128]{1,0:T(8,128)S(1)} %collective-permute-done.5.refs_11_) | copy-start | bytes 49156
  21.1 0.6 %copy-start.6 = (f32[32,128]{1,0:T(8,128)}, f32[32,128]{1,0:T(8,128)S(1)}, u32[]{:S(2)}) copy-start(f32[32,128]{1,0:T(8,128)S(1)} %collective-permute-done.6.refs_12_) | copy-start | bytes 49156

commit v13 on v12

--- a/solution.py
+++ b/solution.py
@@ -131,23 +131,43 @@
         )
 
 
-def final_kernel(sub_size, sub_bits, leaf_bits, loc_bits, *refs):
+def halo_kernel(sub_size, emb_ref, dirs_ref, local_ref, pair_ref, cross_ref, neighbours_ref, counts_ref, out_ref):
+    lv = Leaves(emb_ref, dirs_ref, neighbours_ref, counts_ref, sub_size)
+    nrhs = dirs_ref.shape[0]
+    even = lax.axis_index("sub") % 2 == 0
+    halo_pair = pair_ref[: lv.width_e + nrhs, :]
+    cross = cross_ref[...]
+    left, right = jnp.where(even, cross, halo_pair), jnp.where(even, halo_pair, cross)
+    halo = {}
+    for j, received, offset in ((0, left, -1), (lv.count - 1, right, 1)):
+        halo_points = received[: lv.width_e, :]
+        halo_float = halo_points.astype(jnp.float32)
+        halo_norms = -DISTANCE_SCALE * jnp.sum(halo_float * halo_float, axis=0, keepdims=True)
+        weights = lv.block(j, halo_points, halo_norms)
+        term = lv.weight(j, offset) * nt_dot(received[lv.width_e :, :], weights)
+        halo[j] = term if j not in halo else halo[j] + term
+    for j in range(lv.count):
+        total = local_ref[:, j * LEAF : (j + 1) * LEAF]
+        if j in halo:
+            total = total + halo[j]
+        out_ref[:, j * LEAF : (j + 1) * LEAF] = total
+
+
+def far_kernel(sub_bits, leaf_bits, loc_bits, *refs):
     sub_masks = 2**sub_bits - 1
     leaf_masks = 2**leaf_bits - 1
-    emb_ref, dirs_ref, local_ref, pair_ref, cross_ref, basis_ref, neighbours_ref, counts_ref = refs[:8]
-    round_one = refs[8 : 8 + sub_masks - 1]
-    round_two = refs[8 + sub_masks - 1 : 8 + sub_masks - 1 + leaf_masks]
-    out_ref = refs[8 + sub_masks - 1 + leaf_masks]
-    lv = Leaves(emb_ref, dirs_ref, neighbours_ref, counts_ref, sub_size)
+    near_ref, pair_ref, basis_ref = refs[:3]
+    round_one = refs[3 : 3 + sub_masks - 1]
+    round_two = refs[3 + sub_masks - 1 : 3 + sub_masks - 1 + leaf_masks]
+    out_ref = refs[3 + sub_masks - 1 + leaf_masks]
     rank = basis_ref.shape[1]
-    nrhs = dirs_ref.shape[0]
-    local_points = lv.local_points
+    nrhs, local_points = near_ref.shape
+    width_e = pair_ref.shape[0] - nrhs - 3 * (nrhs * rank * (sub_bits + leaf_bits) // LEAF)
     levels = sub_bits + leaf_bits
     lower_width = rank * sub_bits
 
-    pair, cross = pair_ref[...], cross_ref[...]
     step = nrhs * rank * levels // LEAF
-    from_pair = unpack_parts(pair, lv.width_e + nrhs, step, rank * levels)
+    from_pair = unpack_parts(pair_ref[...], width_e + nrhs, step, rank * levels)
     column_level = lax.broadcasted_iota(jnp.int32, (1, rank * levels), 1) // rank
     lower_level = column_level[:, :lower_width]
     upper_level = column_level[:, : rank * leaf_bits]
@@ -164,24 +184,7 @@
         factor = jnp.where(column_level == bit, 1.0 / math.sqrt(rank * local_points * 2**bit), factor)
     scaled = (sibling * factor).astype(jnp.bfloat16)
     stacked = basis_ref[loc_bits : loc_bits + levels].reshape(levels * rank, local_points)
-    far = nn_dot(scaled, stacked)
-
-    even = lax.axis_index("sub") % 2 == 0
-    halo_pair = pair[: lv.width_e + nrhs]
-    left, right = jnp.where(even, cross, halo_pair), jnp.where(even, halo_pair, cross)
-    halo = {}
-    for j, received, offset in ((0, left, -1), (lv.count - 1, right, 1)):
-        halo_points = received[: lv.width_e, :]
-        halo_float = halo_points.astype(jnp.float32)
-        halo_norms = -DISTANCE_SCALE * jnp.sum(halo_float * halo_float, axis=0, keepdims=True)
-        weights = lv.block(j, halo_points, halo_norms)
-        term = lv.weight(j, offset) * nt_dot(received[lv.width_e :, :], weights)
-        halo[j] = term if j not in halo else halo[j] + term
-    for j in range(lv.count):
-        total = local_ref[:, j * LEAF : (j + 1) * LEAF] + far[:, j * LEAF : (j + 1) * LEAF]
-        if j in halo:
-            total = total + halo[j]
-        out_ref[:, j * LEAF : (j + 1) * LEAF] = total
+    out_ref[...] = near_ref[...] + nn_dot(scaled, stacked)
 
 
 def on_device(embeddings, directions, level_basis, neighbours, counts):
@@ -212,12 +215,6 @@
     from_pair = lax.ppermute(pair, axes, [(i, i ^ 1) for i in range(ndev)])
     round_one = [from_mask(parts, "sub", mask) for mask in range(2, sub_size)]
     from_cross = lax.ppermute(cross, axes, [(i, i - 1 + 2 * (i % 2)) for i in range(1, ndev - 1)])
-    upper = slice(rank * sub_bits, rank * dev_bits)
-    line = parts[:, upper] + unpack_parts(from_pair, width_e + nrhs, step, rank * dev_bits)[:, upper]
-    for got in round_one:
-        line = line + got[:, upper]
-    round_two = [from_mask(line, "leaf", mask) for mask in range(1, leaf_size)]
-
     out = jax.ShapeDtypeStruct((nrhs, local_points), jnp.float32)
     local = pl.pallas_call(
         functools.partial(local_kernel, sub_size),
@@ -225,15 +222,28 @@
         in_specs=[VMEM, VMEM, VMEM, SMEM, SMEM],
         out_specs=VMEM,
     )(embeddings, directions, level_basis, neighbours, counts)
-
+    local, from_pair, *round_one = lax.optimization_barrier((local, from_pair, *round_one))
+    upper = slice(rank * sub_bits, rank * dev_bits)
+    line = parts[:, upper] + unpack_parts(from_pair, width_e + nrhs, step, rank * dev_bits)[:, upper]
+    for got in round_one:
+        line = line + got[:, upper]
+    round_two = [from_mask(line, "leaf", mask) for mask in range(1, leaf_size)]
+
+    near = pl.pallas_call(
+        functools.partial(halo_kernel, sub_size),
+        out_shape=out,
+        in_specs=[VMEM] * 5 + [SMEM, SMEM],
+        out_specs=VMEM,
+        input_output_aliases={2: 0},
+    )(embeddings, directions, local, from_pair, from_cross, neighbours, counts)
     remote = round_one + round_two
     return pl.pallas_call(
-        functools.partial(final_kernel, sub_size, sub_bits, leaf_bits, loc_bits),
+        functools.partial(far_kernel, sub_bits, leaf_bits, loc_bits),
         out_shape=out,
-        in_specs=[VMEM] * 6 + [SMEM, SMEM] + [VMEM] * len(remote),
+        in_specs=[VMEM] * (3 + len(remote)),
         out_specs=VMEM,
-        input_output_aliases={2: 0},
-    )(embeddings, directions, local, from_pair, from_cross, level_basis, neighbours, counts, *remote)
+        input_output_aliases={0: 0},
+    )(near, from_pair, level_basis, *remote)
 
 
 def solution(mesh):

time: 25.1 us -> 27.1 us (1.080)
  waiting for transfers between devices: 5.84 us -> 2.33 us
  starting transfers between devices: 8.14 us -> 10.7 us
  Pallas kernels: 8.9 us -> 10.8 us
  local copies, waits for them, and re-layouts: 1.83 us -> 2.61 us
    ppermute x1, waiting for transfers between devices: 2.9 us -> 0.01 us  [on_device(): from_pair = lax.ppermute(pair, axes, [(i, i ^ 1) for i in range(ndev)])]
    ppermute x5, starting transfers between devices: 4.45 us -> 7.06 us  [from_mask(): return lax.ppermute(x, axis, pairs)]
    pallas_call x1 -> x2, Pallas kernels: 3.12 us -> 5.03 us  [the longest x1 2.86 us: on_device(): pl.pallas_call(functools.partial(halo_kernel, sub_size), out_shape=out, i...]
    unnamed x16, local copies, waits for them, and re-layouts: 1.82 us -> 2.61 us
    ppermute x5, waiting for transfers between devices: 2.93 us -> 2.32 us  [from_mask(): return lax.ppermute(x, axis, pairs)]
  transfers between devices with their start and end apart: 7 -> 7, of which waited for: 2 -> 1; matrix products, arithmetic and copies ran while one was open for 0% -> 0% of each run, Pallas kernels for 14% -> 24%
where the time goes in v13:
time: 27.1 us; the launch traced here: 26.6 us
  Pallas kernels  10.8 us (40%)
  starting transfers between devices  10.7 us (39%)
  local copies, waits for them, and re-layouts  2.61 us (10%)
  waiting for transfers between devices  2.33 us (9%)
    ppermute x5, starting transfers between devices, from_mask(): return lax.ppermute(x, axis, pairs)  7.06 us
    pallas_call x1, Pallas kernels, on_device(): pl.pallas_call(functools.partial(local_kernel, sub_size), out_shape=out,...  3.59 us
    ppermute x1, starting transfers between devices, on_device(): from_pair = lax.ppermute(pair, axes, [(i, i ^ 1) for i in range(ndev)])  3.02 us
    pallas_call x1, Pallas kernels, on_device(): pl.pallas_call(functools.partial(halo_kernel, sub_size), out_shape=out, i...  2.86 us
    unnamed x16, local copies, waits for them, and re-layouts  2.61 us
    ppermute x5, waiting for transfers between devices, from_mask(): return lax.ppermute(x, axis, pairs)  2.32 us
    pallas_call x1, Pallas kernels, on_device(): pl.pallas_call(functools.partial(send_kernel, loc_bits), out_shape=(pair_...  2.2 us
    pallas_call x1, Pallas kernels, on_device(): pl.pallas_call(functools.partial(far_kernel, sub_bits, leaf_bits, loc_bit...  2.17 us
  transfers between devices with their start and end apart: 7, of which 1 were waited for; matrix products, arithmetic and copies ran while one was open for 0% of the time, Pallas kernels for 24%

profile of v13, /device:TPU:0, one launch (start us, length us, event | category | flops | bytes accessed | tf_op | source)
XLA Modules:
  0.0 26.6 jit_solution(17917508203561786496)
XLA Ops:
  0.0 2.2 %shard_map.56 = (bf16[208,512]{1,0:T(8,128)(2,1)}, bf16[160,512]{1,0:T(8,128)(2,1)}, f32[32,256]{1,0:T(8,128)}) custom-call(bf16[128,1024]{1,0:T(8,128)(2,1)} %emb_ref.5, f32[32,1024]{1,0:T(8,128)} %dirs_ref.5, bf16[5,64,1024]{2,1,0:T(8,128)(2,1)} %refs_2_.1), custom_call_target="tpu_custom_call" | custom-call | tf_op jit(solution)/shard_map/pallas_call | solution.py:207
  2.2 3.0 %collective-permute-start = (bf16[208,512]{1,0:T(8,128)(2,1)}, bf16[208,512]{1,0:T(8,128)(2,1)S(1)}, u32[]{:S(2)}, u32[]{:S(2)}) collective-permute-start(bf16[208,512]{1,0:T(8,128)(2,1)} %get-tuple-element.12), channel_id=1, source_target_pairs={{0,1},{1,0},{2,3},{3,2},{4,5},{5,4},{6,7},{7,6},{8,9},{9,8},{10,11... | collective-permute-start | bytes 638984 | tf_op jit(solution)/shard_map/ppermute | solution.py:215
  5.2 2.6 %collective-permute-start.1 = (f32[32,256]{1,0:T(8,128)}, f32[32,256]{1,0:T(8,128)S(1)}, u32[]{:S(2)}, u32[]{:S(2)}) collective-permute-start(f32[32,256]{1,0:T(8,128)} %get-tuple-element.13), channel_id=1, source_target_pairs={{0,2},{1,3},{2,0},{3,1},{4,6},{5,7},{6,4},{7,5},{8,10},{9,11},{10,... | collective-permute-start | bytes 98312 | tf_op jit(solution)/shard_map/ppermute | solution.py:24
  7.8 0.0 collective-permute-start.2
  7.8 0.7 %collective-permute-start.3 = (bf16[160,512]{1,0:T(8,128)(2,1)}, bf16[160,512]{1,0:T(8,128)(2,1)S(1)}, u32[]{:S(2)}, u32[]{:S(2)}) collective-permute-start(bf16[160,512]{1,0:T(8,128)(2,1)} %get-tuple-element.16), channel_id=1, source_target_pairs={{1,2},{2,1},{3,4},{4,3},{5,6},{6,5},{7,8},{8,7},{9,10},{10,9},{11,... | collective-permute-start | bytes 491528 | tf_op jit(solution)/shard_map/ppermute | solution.py:217
  8.5 3.6 %shard_map.55.local_ref = f32[32,1024]{1,0:T(8,128)} custom-call(bf16[128,1024]{1,0:T(8,128)(2,1)} %emb_ref.5, f32[32,1024]{1,0:T(8,128)} %dirs_ref.5, bf16[5,64,1024]{2,1,0:T(8,128)(2,1)} %refs_2_.1, s32[2,8]{1,0:T(2,128)} %neighbours_ref.3, s32[2]{0:T(128)} %counts_ref.3), custom_call_target="tpu_custom_call" | custom-call | tf_op jit(solution)/shard_map/pallas_call | solution.py:219
  12.1 0.0 collective-permute-done.1.refs_3_
  12.1 0.0 copy-start.2
  12.1 2.3 %collective-permute-done.2.refs_4_ = f32[32,256]{1,0:T(8,128)S(1)} collective-permute-done((f32[32,256]{1,0:T(8,128)}, f32[32,256]{1,0:T(8,128)S(1)}, u32[]{:S(2)}, u32[]{:S(2)}) %collective-permute-start.2) | collective-permute-done | bytes 32800 | tf_op jit(solution)/shard_map/ppermute | solution.py:24
  14.4 0.0 copy-start.3
  14.4 0.0 collective-permute-done.pair_ref.refs_1_
  14.4 0.0 copy-start
  14.4 0.0 copy-start.7
  14.4 0.0 copy-done.2
  14.5 0.5 %copy-done.3 = f32[32,256]{1,0:T(8,128)} copy-done((f32[32,256]{1,0:T(8,128)}, f32[32,256]{1,0:T(8,128)S(1)}, u32[]{:S(2)}) %copy-start.3) | copy-done | bytes 32792
  15.0 0.2 copy-done.7
  15.2 0.0 copy-done
  15.2 3.0 %collective-permute-start.4 = (f32[32,128]{1,0:T(8,128)S(1)}, f32[32,128]{1,0:T(8,128)S(1)}, u32[]{:S(2)}, u32[]{:S(2)}) collective-permute-start(f32[32,128]{1,0:T(8,128)S(1)} %fusion.2), channel_id=1, source_target_pairs={{0,4},{4,0},{8,12},{12,8},{1,5},{5,1},{9,13},{13,9},{2,6},{6,2},{1... | collective-permute-start | bytes 49160 | tf_op jit(solution)/shard_map/ppermute | solution.py:24
  18.2 1.5 %collective-permute-start.5 = (f32[32,128]{1,0:T(8,128)S(1)}, f32[32,128]{1,0:T(8,128)S(1)}, u32[]{:S(2)}, u32[]{:S(2)}) collective-permute-start(f32[32,128]{1,0:T(8,128)S(1)} %fusion.2), channel_id=1, source_target_pairs={{0,8},{4,12},{8,0},{12,4},{1,9},{5,13},{9,1},{13,5},{2,10},{6,14},... | collective-permute-start | bytes 49160 | tf_op jit(solution)/shard_map/ppermute | solution.py:24
  19.7 0.0 collective-permute-start.6
  19.7 0.0 collective-permute-done.3.cross_ref
  19.7 0.0 copy-start.1
  19.7 0.7 %copy-done.1 = bf16[160,512]{1,0:T(8,128)(2,1)} copy-done((bf16[160,512]{1,0:T(8,128)(2,1)}, bf16[160,512]{1,0:T(8,128)(2,1)S(1)}, u32[]{:S(2)}) %copy-start.1) | copy-done | bytes 163864
  20.4 2.9 %shard_map.57.refs_0_ = f32[32,1024]{1,0:T(8,128)} custom-call(bf16[128,1024]{1,0:T(8,128)(2,1)} %emb_ref.5, f32[32,1024]{1,0:T(8,128)} %dirs_ref.5, f32[32,1024]{1,0:T(8,128)} %shard_map.55.local_ref, bf16[208,512]{1,0:T(8,128)(2,1)} %copy-done, bf16[160,512]{1,0:T(8,128)(2,1)} %copy-done.1, s32[2,8]{1,0:T(2,128)} %neighbours_ref.3, ...), custom_call_target="tpu_custom_call", output_to_operand_aliasing={{}: (2, {})} | custom-call | tf_op jit(solution)/shard_map/pallas_call | solution.py:232
  23.2 0.0 collective-permute-done.4.refs_5_
  23.2 0.0 copy-start.4
  23.2 0.0 collective-permute-done.5.refs_6_
  23.2 0.0 copy-start.5
  23.2 0.0 collective-permute-done.6.refs_7_
  23.3 0.6 %copy-done.4 = f32[32,128]{1,0:T(8,128)} copy-done((f32[32,128]{1,0:T(8,128)}, f32[32,128]{1,0:T(8,128)S(1)}, u32[]{:S(2)}) %copy-start.4) | copy-done | bytes 16408
  23.8 0.0 copy-done.5
  23.8 0.0 copy-start.6
  23.8 0.6 %copy-done.6 = f32[32,128]{1,0:T(8,128)} copy-done((f32[32,128]{1,0:T(8,128)}, f32[32,128]{1,0:T(8,128)S(1)}, u32[]{:S(2)}) %copy-start.6) | copy-done | bytes 16408
  24.4 2.2 %shard_map.58 = f32[32,1024]{1,0:T(8,128)} custom-call(f32[32,1024]{1,0:T(8,128)} %shard_map.57.refs_0_, bf16[208,512]{1,0:T(8,128)(2,1)} %copy-done, bf16[5,64,1024]{2,1,0:T(8,128)(2,1)} %refs_2_.1, f32[32,256]{1,0:T(8,128)} %copy-done.2, f32[32,256]{1,0:T(8,128)} %copy-done.3, f32[32,128]{1,0:T(8,128)} %copy-done.4, ...), custom_call_target="tpu_custom_call", output_to_operand_aliasing={{}: (0, {})} | custom-call | tf_op jit(solution)/shard_map/pallas_call | solution.py:240
  (4 shorter events, 0.0 us)
Async XLA Ops:
  2.2 12.2 %collective-permute-start = (bf16[208,512]{1,0:T(8,128)(2,1)}, bf16[208,512]{1,0:T(8,128)(2,1)S(1)}, u32[]{:S(2)}, u32[]{:S(2)}) collective-permute-start(bf16[208,512]{1,0:T(8,128)(2,1)} %get-tuple-element.12), channel_id=1, source_target_pairs={{0,1},{1,0},{2,3},{3,2},{4,5},{5,4},{6,7},{7,6},{8,9},{9,8},{10,11... | collective-permute-start | bytes 638984 | tf_op jit(solution)/shard_map/ppermute | solution.py:215
  5.2 6.8 %collective-permute-start.1 = (f32[32,256]{1,0:T(8,128)}, f32[32,256]{1,0:T(8,128)S(1)}, u32[]{:S(2)}, u32[]{:S(2)}) collective-permute-start(f32[32,256]{1,0:T(8,128)} %get-tuple-element.13), channel_id=1, source_target_pairs={{0,2},{1,3},{2,0},{3,1},{4,6},{5,7},{6,4},{7,5},{8,10},{9,11},{10,... | collective-permute-start | bytes 98312 | tf_op jit(solution)/shard_map/ppermute | solution.py:24
  7.8 6.6 %collective-permute-start.2 = (f32[32,256]{1,0:T(8,128)}, f32[32,256]{1,0:T(8,128)S(1)}, u32[]{:S(2)}, u32[]{:S(2)}) collective-permute-start(f32[32,256]{1,0:T(8,128)} %get-tuple-element.13), channel_id=1, source_target_pairs={{0,3},{1,2},{2,1},{3,0},{4,7},{5,6},{6,5},{7,4},{8,11},{9,10},{10,... | collective-permute-start | bytes 98312 | tf_op jit(solution)/shard_map/ppermute | solution.py:24
  7.8 11.9 %collective-permute-start.3 = (bf16[160,512]{1,0:T(8,128)(2,1)}, bf16[160,512]{1,0:T(8,128)(2,1)S(1)}, u32[]{:S(2)}, u32[]{:S(2)}) collective-permute-start(bf16[160,512]{1,0:T(8,128)(2,1)} %get-tuple-element.16), channel_id=1, source_target_pairs={{1,2},{2,1},{3,4},{4,3},{5,6},{6,5},{7,8},{8,7},{9,10},{10,9},{11,... | collective-permute-start | bytes 491528 | tf_op jit(solution)/shard_map/ppermute | solution.py:217
  12.1 2.4 %copy-start.2 = (f32[32,256]{1,0:T(8,128)}, f32[32,256]{1,0:T(8,128)S(1)}, u32[]{:S(2)}) copy-start(f32[32,256]{1,0:T(8,128)S(1)} %collective-permute-done.1.refs_3_) | copy-start | bytes 98308
  14.4 0.6 %copy-start.3 = (f32[32,256]{1,0:T(8,128)}, f32[32,256]{1,0:T(8,128)S(1)}, u32[]{:S(2)}) copy-start(f32[32,256]{1,0:T(8,128)S(1)} %collective-permute-done.2.refs_4_) | copy-start | bytes 98308
  14.4 0.8 %copy-start = (bf16[208,512]{1,0:T(8,128)(2,1)}, bf16[208,512]{1,0:T(8,128)(2,1)S(1)}, u32[]{:S(2)}) copy-start(bf16[208,512]{1,0:T(8,128)(2,1)S(1)} %collective-permute-done.pair_ref.refs_1_) | copy-start | bytes 638980
  14.4 0.8 %copy-start.7 = (f32[32,256]{1,0:T(8,128)S(1)}, f32[32,256]{1,0:T(8,128)}, u32[]{:S(2)}) copy-start(f32[32,256]{1,0:T(8,128)} %get-tuple-element.13) | copy-start | bytes 98308
  15.2 8.0 %collective-permute-start.4 = (f32[32,128]{1,0:T(8,128)S(1)}, f32[32,128]{1,0:T(8,128)S(1)}, u32[]{:S(2)}, u32[]{:S(2)}) collective-permute-start(f32[32,128]{1,0:T(8,128)S(1)} %fusion.2), channel_id=1, source_target_pairs={{0,4},{4,0},{8,12},{12,8},{1,5},{5,1},{9,13},{13,9},{2,6},{6,2},{1... | collective-permute-start | bytes 49160 | tf_op jit(solution)/shard_map/ppermute | solution.py:24
  18.2 5.0 %collective-permute-start.5 = (f32[32,128]{1,0:T(8,128)S(1)}, f32[32,128]{1,0:T(8,128)S(1)}, u32[]{:S(2)}, u32[]{:S(2)}) collective-permute-start(f32[32,128]{1,0:T(8,128)S(1)} %fusion.2), channel_id=1, source_target_pairs={{0,8},{4,12},{8,0},{12,4},{1,9},{5,13},{9,1},{13,5},{2,10},{6,14},... | collective-permute-start | bytes 49160 | tf_op jit(solution)/shard_map/ppermute | solution.py:24
  19.7 3.6 %collective-permute-start.6 = (f32[32,128]{1,0:T(8,128)S(1)}, f32[32,128]{1,0:T(8,128)S(1)}, u32[]{:S(2)}, u32[]{:S(2)}) collective-permute-start(f32[32,128]{1,0:T(8,128)S(1)} %fusion.2), channel_id=1, source_target_pairs={{0,12},{4,8},{8,4},{12,0},{1,13},{5,9},{9,5},{13,1},{2,14},{6,10},... | collective-permute-start | bytes 49160 | tf_op jit(solution)/shard_map/ppermute | solution.py:24
  19.7 0.7 %copy-start.1 = (bf16[160,512]{1,0:T(8,128)(2,1)}, bf16[160,512]{1,0:T(8,128)(2,1)S(1)}, u32[]{:S(2)}) copy-start(bf16[160,512]{1,0:T(8,128)(2,1)S(1)} %collective-permute-done.3.cross_ref) | copy-start | bytes 491524
  23.2 0.6 %copy-start.4 = (f32[32,128]{1,0:T(8,128)}, f32[32,128]{1,0:T(8,128)S(1)}, u32[]{:S(2)}) copy-start(f32[32,128]{1,0:T(8,128)S(1)} %collective-permute-done.4.refs_5_) | copy-start | bytes 49156
  23.2 0.6 %copy-start.5 = (f32[32,128]{1,0:T(8,128)}, f32[32,128]{1,0:T(8,128)S(1)}, u32[]{:S(2)}) copy-start(f32[32,128]{1,0:T(8,128)S(1)} %collective-permute-done.5.refs_6_) | copy-start | bytes 49156
  23.8 0.6 %copy-start.6 = (f32[32,128]{1,0:T(8,128)}, f32[32,128]{1,0:T(8,128)S(1)}, u32[]{:S(2)}) copy-start(f32[32,128]{1,0:T(8,128)S(1)} %collective-permute-done.6.refs_7_) | copy-start | bytes 49156

commit v14 on v12

--- a/solution.py
+++ b/solution.py
@@ -22,6 +22,10 @@
 def from_mask(x, axis, mask):
     pairs = [(i, i ^ mask) for i in range(lax.axis_size(axis))]
     return lax.ppermute(x, axis, pairs)
+
+
+def in_vmem(*arrays):
+    return [pltpu.with_memory_space_constraint(a, pltpu.VMEM) for a in arrays]
 
 
 def nt_dot(a, b):
@@ -233,7 +237,16 @@
         in_specs=[VMEM] * 6 + [SMEM, SMEM] + [VMEM] * len(remote),
         out_specs=VMEM,
         input_output_aliases={2: 0},
-    )(embeddings, directions, local, from_pair, from_cross, level_basis, neighbours, counts, *remote)
+    )(
+        embeddings,
+        directions,
+        local,
+        *in_vmem(from_pair, from_cross),
+        level_basis,
+        neighbours,
+        counts,
+        *in_vmem(*remote),
+    )
 
 
 def solution(mesh):

time: 25.1 us -> 23.2 us (0.924)
  local copies, waits for them, and re-layouts: 1.83 us -> 0.01 us
    unnamed x16 -> x2, local copies, waits for them, and re-layouts: 1.82 us -> 0.01 us
  transfers between devices with their start and end apart: 7 -> 7, of which waited for: 2 -> 2; matrix products, arithmetic and copies ran while one was open for 0% -> 0% of each run, Pallas kernels for 14% -> 16%
where the time goes in v14:
time: 23.2 us; the launch traced here: 22.9 us
  Pallas kernels  8.76 us (38%)
  starting transfers between devices  8.21 us (35%)
  waiting for transfers between devices  5.85 us (25%)
    ppermute x5, starting transfers between devices, from_mask(): return lax.ppermute(x, axis, pairs)  4.53 us
    pallas_call x1, Pallas kernels, on_device(): pl.pallas_call(functools.partial(local_kernel, sub_size), out_shape=out,...  3.58 us
    ppermute x1, starting transfers between devices, on_device(): from_pair = lax.ppermute(pair, axes, [(i, i ^ 1) for i in range(ndev)])  3.02 us
    pallas_call x1, Pallas kernels, on_device(): pl.pallas_call(functools.partial(final_kernel, sub_size, sub_bits, leaf_b...  2.99 us
    ppermute x5, waiting for transfers between devices, from_mask(): return lax.ppermute(x, axis, pairs)  2.95 us
    ppermute x1, waiting for transfers between devices, on_device(): from_pair = lax.ppermute(pair, axes, [(i, i ^ 1) for i in range(ndev)])  2.9 us
    pallas_call x1, Pallas kernels, on_device(): pl.pallas_call(functools.partial(send_kernel, loc_bits), out_shape=(pair_...  2.2 us
    ppermute x1, starting transfers between devices, on_device(): lax.ppermute(cross, axes, [(i, i - 1 + 2 * (i % 2)) for i in range(1, nde...  0.66 us
  transfers between devices with their start and end apart: 7, of which 2 were waited for; matrix products, arithmetic and copies ran while one was open for 0% of the time, Pallas kernels for 16%

profile of v14, /device:TPU:0, one launch (start us, length us, event | category | flops | bytes accessed | tf_op | source)
XLA Modules:
  0.0 22.9 jit_solution(17243520211206064820)
XLA Ops:
  0.0 2.2 %shard_map.56 = (bf16[208,512]{1,0:T(8,128)(2,1)}, bf16[160,512]{1,0:T(8,128)(2,1)}, f32[32,256]{1,0:T(8,128)}) custom-call(bf16[128,1024]{1,0:T(8,128)(2,1)} %refs_0_.1, f32[32,1024]{1,0:T(8,128)} %refs_1_.1, bf16[5,64,1024]{2,1,0:T(8,128)(2,1)} %refs_5_.1), custom_call_target="tpu_custom_call" | custom-call | tf_op jit(solution)/shard_map/pallas_call | solution.py:208
  2.2 3.0 %collective-permute-start = (bf16[208,512]{1,0:T(8,128)(2,1)}, bf16[208,512]{1,0:T(8,128)(2,1)S(1)}, u32[]{:S(2)}, u32[]{:S(2)}) collective-permute-start(bf16[208,512]{1,0:T(8,128)(2,1)} %get-tuple-element.8), channel_id=1, source_target_pairs={{0,1},{1,0},{2,3},{3,2},{4,5},{5,4},{6,7},{7,6},{8,9},{9,8},{10,11... | collective-permute-start | bytes 638984 | tf_op jit(solution)/shard_map/ppermute | solution.py:216
  5.2 2.6 %collective-permute-start.2 = (f32[32,256]{1,0:T(8,128)}, f32[32,256]{1,0:T(8,128)S(1)}, u32[]{:S(2)}, u32[]{:S(2)}) collective-permute-start(f32[32,256]{1,0:T(8,128)} %get-tuple-element.10), channel_id=1, source_target_pairs={{0,2},{1,3},{2,0},{3,1},{4,6},{5,7},{6,4},{7,5},{8,10},{9,11},{10,... | collective-permute-start | bytes 98312 | tf_op jit(solution)/shard_map/ppermute | solution.py:24
  7.8 0.0 collective-permute-start.3
  7.8 0.7 %collective-permute-start.1 = (bf16[160,512]{1,0:T(8,128)(2,1)}, bf16[160,512]{1,0:T(8,128)(2,1)S(1)}, u32[]{:S(2)}, u32[]{:S(2)}) collective-permute-start(bf16[160,512]{1,0:T(8,128)(2,1)} %get-tuple-element.9), channel_id=1, source_target_pairs={{1,2},{2,1},{3,4},{4,3},{5,6},{6,5},{7,8},{8,7},{9,10},{10,9},{11,... | collective-permute-start | bytes 491528 | tf_op jit(solution)/shard_map/ppermute | solution.py:218
  8.5 2.9 %collective-permute-done.refs_3_ = bf16[208,512]{1,0:T(8,128)(2,1)S(1)} collective-permute-done((bf16[208,512]{1,0:T(8,128)(2,1)}, bf16[208,512]{1,0:T(8,128)(2,1)S(1)}, u32[]{:S(2)}, u32[]{:S(2)}) %collective-permute-start) | collective-permute-done | bytes 213024 | tf_op jit(solution)/shard_map/ppermute | solution.py:216
  11.4 0.0 copy-start
  11.4 0.0 collective-permute-done.2.refs_8_
  11.5 2.9 %collective-permute-done.3.refs_9_ = f32[32,256]{1,0:T(8,128)S(1)} collective-permute-done((f32[32,256]{1,0:T(8,128)}, f32[32,256]{1,0:T(8,128)S(1)}, u32[]{:S(2)}, u32[]{:S(2)}) %collective-permute-start.3) | collective-permute-done | bytes 32800 | tf_op jit(solution)/shard_map/ppermute | solution.py:24
  14.4 0.0 copy-done
  14.4 0.1 collective-permute-start.4
  14.5 1.6 %collective-permute-start.5 = (f32[32,128]{1,0:T(8,128)S(1)}, f32[32,128]{1,0:T(8,128)S(1)}, u32[]{:S(2)}, u32[]{:S(2)}) collective-permute-start(f32[32,128]{1,0:T(8,128)S(1)} %slice_add_fusion.2), channel_id=1, source_target_pairs={{0,8},{4,12},{8,0},{12,4},{1,9},{5,13},{9,1},{13,5},{2,10},{6,14},... | collective-permute-start | bytes 49160 | tf_op jit(solution)/shard_map/ppermute | solution.py:24
  16.0 0.3 %collective-permute-start.6 = (f32[32,128]{1,0:T(8,128)S(1)}, f32[32,128]{1,0:T(8,128)S(1)}, u32[]{:S(2)}, u32[]{:S(2)}) collective-permute-start(f32[32,128]{1,0:T(8,128)S(1)} %slice_add_fusion.2), channel_id=1, source_target_pairs={{0,12},{4,8},{8,4},{12,0},{1,13},{5,9},{9,5},{13,1},{2,14},{6,10},... | collective-permute-start | bytes 49160 | tf_op jit(solution)/shard_map/ppermute | solution.py:24
  16.3 3.6 %shard_map.55.refs_2_ = f32[32,1024]{1,0:T(8,128)} custom-call(bf16[128,1024]{1,0:T(8,128)(2,1)} %refs_0_.1, f32[32,1024]{1,0:T(8,128)} %refs_1_.1, bf16[5,64,1024]{2,1,0:T(8,128)(2,1)} %refs_5_.1, s32[2,8]{1,0:T(2,128)} %refs_6_.1, s32[2]{0:T(128)} %refs_7_.1), custom_call_target="tpu_custom_call" | custom-call | tf_op jit(solution)/shard_map/pallas_call | solution.py:226
  19.9 0.0 collective-permute-done.1.refs_4_
  19.9 0.0 collective-permute-done.4.refs_10_
  19.9 0.0 collective-permute-done.5.refs_11_
  19.9 0.0 collective-permute-done.6.refs_12_
  19.9 3.0 %shard_map.57 = f32[32,1024]{1,0:T(8,128)} custom-call(bf16[128,1024]{1,0:T(8,128)(2,1)} %refs_0_.1, f32[32,1024]{1,0:T(8,128)} %refs_1_.1, f32[32,1024]{1,0:T(8,128)} %shard_map.55.refs_2_, bf16[208,512]{1,0:T(8,128)(2,1)S(1)} %collective-permute-done.refs_3_, bf16[160,512]{1,0:T(8,128)(2,1)S(1)} %collective-permute-done.1.refs_4_, ...), custom_call_target="tpu_custom_call", output_to_operand_aliasing={{}: (2, {})} | custom-call | tf_op jit(solution)/shard_map/pallas_call | solution.py:234
  (4 shorter events, 0.0 us)
Async XLA Ops:
  2.2 9.2 %collective-permute-start = (bf16[208,512]{1,0:T(8,128)(2,1)}, bf16[208,512]{1,0:T(8,128)(2,1)S(1)}, u32[]{:S(2)}, u32[]{:S(2)}) collective-permute-start(bf16[208,512]{1,0:T(8,128)(2,1)} %get-tuple-element.8), channel_id=1, source_target_pairs={{0,1},{1,0},{2,3},{3,2},{4,5},{5,4},{6,7},{7,6},{8,9},{9,8},{10,11... | collective-permute-start | bytes 638984 | tf_op jit(solution)/shard_map/ppermute | solution.py:216
  5.2 6.2 %collective-permute-start.2 = (f32[32,256]{1,0:T(8,128)}, f32[32,256]{1,0:T(8,128)S(1)}, u32[]{:S(2)}, u32[]{:S(2)}) collective-permute-start(f32[32,256]{1,0:T(8,128)} %get-tuple-element.10), channel_id=1, source_target_pairs={{0,2},{1,3},{2,0},{3,1},{4,6},{5,7},{6,4},{7,5},{8,10},{9,11},{10,... | collective-permute-start | bytes 98312 | tf_op jit(solution)/shard_map/ppermute | solution.py:24
  7.8 6.6 %collective-permute-start.3 = (f32[32,256]{1,0:T(8,128)}, f32[32,256]{1,0:T(8,128)S(1)}, u32[]{:S(2)}, u32[]{:S(2)}) collective-permute-start(f32[32,256]{1,0:T(8,128)} %get-tuple-element.10), channel_id=1, source_target_pairs={{0,3},{1,2},{2,1},{3,0},{4,7},{5,6},{6,5},{7,4},{8,11},{9,10},{10,... | collective-permute-start | bytes 98312 | tf_op jit(solution)/shard_map/ppermute | solution.py:24
  7.8 12.1 %collective-permute-start.1 = (bf16[160,512]{1,0:T(8,128)(2,1)}, bf16[160,512]{1,0:T(8,128)(2,1)S(1)}, u32[]{:S(2)}, u32[]{:S(2)}) collective-permute-start(bf16[160,512]{1,0:T(8,128)(2,1)} %get-tuple-element.9), channel_id=1, source_target_pairs={{1,2},{2,1},{3,4},{4,3},{5,6},{6,5},{7,8},{8,7},{9,10},{10,9},{11,... | collective-permute-start | bytes 491528 | tf_op jit(solution)/shard_map/ppermute | solution.py:218
  11.4 3.0 %copy-start = (f32[32,256]{1,0:T(8,128)S(1)}, f32[32,256]{1,0:T(8,128)}, u32[]{:S(2)}) copy-start(f32[32,256]{1,0:T(8,128)} %get-tuple-element.10) | copy-start | bytes 98308
  14.4 5.5 %collective-permute-start.4 = (f32[32,128]{1,0:T(8,128)S(1)}, f32[32,128]{1,0:T(8,128)S(1)}, u32[]{:S(2)}, u32[]{:S(2)}) collective-permute-start(f32[32,128]{1,0:T(8,128)S(1)} %slice_add_fusion.2), channel_id=1, source_target_pairs={{0,4},{4,0},{8,12},{12,8},{1,5},{5,1},{9,13},{13,9},{2,6},{6,2},{1... | collective-permute-start | bytes 49160 | tf_op jit(solution)/shard_map/ppermute | solution.py:24
  14.5 5.5 %collective-permute-start.5 = (f32[32,128]{1,0:T(8,128)S(1)}, f32[32,128]{1,0:T(8,128)S(1)}, u32[]{:S(2)}, u32[]{:S(2)}) collective-permute-start(f32[32,128]{1,0:T(8,128)S(1)} %slice_add_fusion.2), channel_id=1, source_target_pairs={{0,8},{4,12},{8,0},{12,4},{1,9},{5,13},{9,1},{13,5},{2,10},{6,14},... | collective-permute-start | bytes 49160 | tf_op jit(solution)/shard_map/ppermute | solution.py:24
  16.0 3.9 %collective-permute-start.6 = (f32[32,128]{1,0:T(8,128)S(1)}, f32[32,128]{1,0:T(8,128)S(1)}, u32[]{:S(2)}, u32[]{:S(2)}) collective-permute-start(f32[32,128]{1,0:T(8,128)S(1)} %slice_add_fusion.2), channel_id=1, source_target_pairs={{0,12},{4,8},{8,4},{12,0},{1,13},{5,9},{9,5},{13,1},{2,14},{6,10},... | collective-permute-start | bytes 49160 | tf_op jit(solution)/shard_map/ppermute | solution.py:24

commit v15 on v14

--- a/solution.py
+++ b/solution.py
@@ -228,7 +228,7 @@
         out_shape=out,
         in_specs=[VMEM, VMEM, VMEM, SMEM, SMEM],
         out_specs=VMEM,
-    )(embeddings, directions, level_basis, neighbours, counts)
+    )(*in_vmem(embeddings, directions, level_basis), neighbours, counts)
 
     remote = round_one + round_two
     return pl.pallas_call(
@@ -238,11 +238,7 @@
         out_specs=VMEM,
         input_output_aliases={2: 0},
     )(
-        embeddings,
-        directions,
-        local,
-        *in_vmem(from_pair, from_cross),
-        level_basis,
+        *in_vmem(embeddings, directions, local, from_pair, from_cross, level_basis),
         neighbours,
         counts,
         *in_vmem(*remote),

time: 23.2 us -> 21.8 us (0.940)
  Pallas kernels: 8.76 us -> 6.33 us
  local copies, waits for them, and re-layouts: 0.01 us -> 0.68 us
  waiting for transfers between devices: 5.85 us -> 6.3 us
    pallas_call x1, Pallas kernels: 2.99 us -> 1.71 us  [on_device(): pl.pallas_call(functools.partial(final_kernel, sub_size, sub_bits, leaf_b...]
    pallas_call x1, Pallas kernels: 3.58 us -> 2.37 us  [on_device(): pl.pallas_call(functools.partial(local_kernel, sub_size), out_shape=out,...]
    unnamed x2 -> x9, local copies, waits for them, and re-layouts: 0.01 us -> 0.68 us
    ppermute x5, waiting for transfers between devices: 2.95 us -> 3.39 us  [from_mask(): return lax.ppermute(x, axis, pairs)]
  transfers between devices with their start and end apart: 7 -> 7, of which waited for: 2 -> 3; matrix products, arithmetic and copies ran while one was open for 0% -> 0% of each run, Pallas kernels for 16% -> 11%
where the time goes in v15:
time: 21.8 us; the launch traced here: 21.6 us
  starting transfers between devices  8.21 us (38%)
  Pallas kernels  6.33 us (29%)
  waiting for transfers between devices  6.3 us (29%)
  local copies, waits for them, and re-layouts  0.68 us (3%)
    ppermute x5, starting transfers between devices, from_mask(): return lax.ppermute(x, axis, pairs)  4.52 us
    ppermute x5, waiting for transfers between devices, from_mask(): return lax.ppermute(x, axis, pairs)  3.39 us
    ppermute x1, starting transfers between devices, on_device(): from_pair = lax.ppermute(pair, axes, [(i, i ^ 1) for i in range(ndev)])  3.02 us
    ppermute x1, waiting for transfers between devices, on_device(): from_pair = lax.ppermute(pair, axes, [(i, i ^ 1) for i in range(ndev)])  2.9 us
    pallas_call x1, Pallas kernels, on_device(): pl.pallas_call(functools.partial(local_kernel, sub_size), out_shape=out,...  2.37 us
    pallas_call x1, Pallas kernels, on_device(): pl.pallas_call(functools.partial(send_kernel, loc_bits), out_shape=(pair_...  2.26 us
    pallas_call x1, Pallas kernels, on_device(): pl.pallas_call(functools.partial(final_kernel, sub_size, sub_bits, leaf_b...  1.71 us
    unnamed x9, local copies, waits for them, and re-layouts  0.68 us
  transfers between devices with their start and end apart: 7, of which 3 were waited for; matrix products, arithmetic and copies ran while one was open for 0% of the time, Pallas kernels for 11%

profile of v15, /device:TPU:0, one launch (start us, length us, event | category | flops | bytes accessed | tf_op | source)
XLA Modules:
  0.0 21.6 jit_solution(10811462726769121592)
XLA Ops:
  0.0 0.0 copy-start
  0.0 2.3 %shard_map.56 = (bf16[208,512]{1,0:T(8,128)(2,1)}, bf16[160,512]{1,0:T(8,128)(2,1)}, f32[32,256]{1,0:T(8,128)}) custom-call(bf16[128,1024]{1,0:T(8,128)(2,1)} %refs_0_.1, f32[32,1024]{1,0:T(8,128)} %refs_1_.1, bf16[5,64,1024]{2,1,0:T(8,128)(2,1)} %refs_5_.1), custom_call_target="tpu_custom_call" | custom-call | tf_op jit(solution)/shard_map/pallas_call | solution.py:208
  2.3 0.0 copy-start.1
  2.3 3.0 %collective-permute-start = (bf16[208,512]{1,0:T(8,128)(2,1)}, bf16[208,512]{1,0:T(8,128)(2,1)S(1)}, u32[]{:S(2)}, u32[]{:S(2)}) collective-permute-start(bf16[208,512]{1,0:T(8,128)(2,1)} %get-tuple-element.8), channel_id=1, source_target_pairs={{0,1},{1,0},{2,3},{3,2},{4,5},{5,4},{6,7},{7,6},{8,9},{9,8},{10,11... | collective-permute-start | bytes 638984 | tf_op jit(solution)/shard_map/ppermute | solution.py:216
  5.3 2.6 %collective-permute-start.2 = (f32[32,256]{1,0:T(8,128)}, f32[32,256]{1,0:T(8,128)S(1)}, u32[]{:S(2)}, u32[]{:S(2)}) collective-permute-start(f32[32,256]{1,0:T(8,128)} %get-tuple-element.10), channel_id=1, source_target_pairs={{0,2},{1,3},{2,0},{3,1},{4,6},{5,7},{6,4},{7,5},{8,10},{9,11},{10,... | collective-permute-start | bytes 98312 | tf_op jit(solution)/shard_map/ppermute | solution.py:24
  7.9 0.0 collective-permute-start.3
  7.9 0.7 %collective-permute-start.1 = (bf16[160,512]{1,0:T(8,128)(2,1)}, bf16[160,512]{1,0:T(8,128)(2,1)S(1)}, u32[]{:S(2)}, u32[]{:S(2)}) collective-permute-start(bf16[160,512]{1,0:T(8,128)(2,1)} %get-tuple-element.9), channel_id=1, source_target_pairs={{1,2},{2,1},{3,4},{4,3},{5,6},{6,5},{7,8},{8,7},{9,10},{10,9},{11,... | collective-permute-start | bytes 491528 | tf_op jit(solution)/shard_map/ppermute | solution.py:218
  8.5 2.9 %collective-permute-done.refs_3_ = bf16[208,512]{1,0:T(8,128)(2,1)S(1)} collective-permute-done((bf16[208,512]{1,0:T(8,128)(2,1)}, bf16[208,512]{1,0:T(8,128)(2,1)S(1)}, u32[]{:S(2)}, u32[]{:S(2)}) %collective-permute-start) | collective-permute-done | bytes 213024 | tf_op jit(solution)/shard_map/ppermute | solution.py:216
  11.4 0.0 copy-start.3
  11.5 0.0 copy-start.2
  11.5 0.0 collective-permute-done.2.refs_8_
  11.5 2.9 %collective-permute-done.3.refs_9_ = f32[32,256]{1,0:T(8,128)S(1)} collective-permute-done((f32[32,256]{1,0:T(8,128)}, f32[32,256]{1,0:T(8,128)S(1)}, u32[]{:S(2)}, u32[]{:S(2)}) %collective-permute-start.3) | collective-permute-done | bytes 32800 | tf_op jit(solution)/shard_map/ppermute | solution.py:24
  14.4 0.0 copy-done.3
  14.5 0.1 collective-permute-start.4
  14.5 1.6 %collective-permute-start.5 = (f32[32,128]{1,0:T(8,128)S(1)}, f32[32,128]{1,0:T(8,128)S(1)}, u32[]{:S(2)}, u32[]{:S(2)}) collective-permute-start(f32[32,128]{1,0:T(8,128)S(1)} %slice_add_fusion.2), channel_id=1, source_target_pairs={{0,8},{4,12},{8,0},{12,4},{1,9},{5,13},{9,1},{13,5},{2,10},{6,14},... | collective-permute-start | bytes 49160 | tf_op jit(solution)/shard_map/ppermute | solution.py:24
  16.1 0.3 %collective-permute-start.6 = (f32[32,128]{1,0:T(8,128)S(1)}, f32[32,128]{1,0:T(8,128)S(1)}, u32[]{:S(2)}, u32[]{:S(2)}) collective-permute-start(f32[32,128]{1,0:T(8,128)S(1)} %slice_add_fusion.2), channel_id=1, source_target_pairs={{0,12},{4,8},{8,4},{12,0},{1,13},{5,9},{9,5},{13,1},{2,14},{6,10},... | collective-permute-start | bytes 49160 | tf_op jit(solution)/shard_map/ppermute | solution.py:24
  16.4 0.0 copy-done
  16.4 0.0 copy-done.1
  16.4 0.0 copy-done.2
  16.4 2.4 %shard_map.55.refs_2_ = f32[32,1024]{1,0:T(8,128)S(1)} custom-call(bf16[128,1024]{1,0:T(8,128)(2,1)S(1)} %copy-done.1, f32[32,1024]{1,0:T(8,128)S(1)} %copy-done.2, bf16[5,64,1024]{2,1,0:T(8,128)(2,1)S(1)} %copy-done, s32[2,8]{1,0:T(2,128)} %refs_6_.1, s32[2]{0:T(128)} %refs_7_.1), custom_call_target="tpu_custom_call" | custom-call | tf_op jit(solution)/shard_map/pallas_call | solution.py:226
  18.8 0.0 collective-permute-done.1.refs_4_
  18.8 0.0 collective-permute-done.4.refs_10_
  18.8 0.0 collective-permute-done.5.refs_11_
  18.8 0.5 %collective-permute-done.6.refs_12_ = f32[32,128]{1,0:T(8,128)S(1)} collective-permute-done((f32[32,128]{1,0:T(8,128)S(1)}, f32[32,128]{1,0:T(8,128)S(1)}, u32[]{:S(2)}, u32[]{:S(2)}) %collective-permute-start.6) | collective-permute-done | bytes 16416 | tf_op jit(solution)/shard_map/ppermute | solution.py:24
  19.3 1.7 %shard_map.57 = f32[32,1024]{1,0:T(8,128)S(1)} custom-call(bf16[128,1024]{1,0:T(8,128)(2,1)S(1)} %copy-done.1, f32[32,1024]{1,0:T(8,128)S(1)} %copy-done.2, f32[32,1024]{1,0:T(8,128)S(1)} %shard_map.55.refs_2_, bf16[208,512]{1,0:T(8,128)(2,1)S(1)} %collective-permute-done.refs_3_, ...), custom_call_target="tpu_custom_call", output_to_operand_aliasing={{}: (2, {})} | custom-call | tf_op jit(solution)/shard_map/pallas_call | solution.py:234
  21.0 0.7 %copy.8 = f32[32,1024]{1,0:T(8,128)} copy(f32[32,1024]{1,0:T(8,128)S(1)} %shard_map.57) | data formatting | bytes 262144
  (4 shorter events, 0.0 us)
Async XLA Ops:
  0.0 16.4 %copy-start = (bf16[5,64,1024]{2,1,0:T(8,128)(2,1)S(1)}, bf16[5,64,1024]{2,1,0:T(8,128)(2,1)}, u32[]{:S(2)}) copy-start(bf16[5,64,1024]{2,1,0:T(8,128)(2,1)} %refs_5_.1) | copy-start | bytes 1966084
  2.3 14.1 %copy-start.1 = (bf16[128,1024]{1,0:T(8,128)(2,1)S(1)}, bf16[128,1024]{1,0:T(8,128)(2,1)}, u32[]{:S(2)}) copy-start(bf16[128,1024]{1,0:T(8,128)(2,1)} %refs_0_.1) | copy-start | bytes 786436
  2.3 9.2 %collective-permute-start = (bf16[208,512]{1,0:T(8,128)(2,1)}, bf16[208,512]{1,0:T(8,128)(2,1)S(1)}, u32[]{:S(2)}, u32[]{:S(2)}) collective-permute-start(bf16[208,512]{1,0:T(8,128)(2,1)} %get-tuple-element.8), channel_id=1, source_target_pairs={{0,1},{1,0},{2,3},{3,2},{4,5},{5,4},{6,7},{7,6},{8,9},{9,8},{10,11... | collective-permute-start | bytes 638984 | tf_op jit(solution)/shard_map/ppermute | solution.py:216
  5.3 6.2 %collective-permute-start.2 = (f32[32,256]{1,0:T(8,128)}, f32[32,256]{1,0:T(8,128)S(1)}, u32[]{:S(2)}, u32[]{:S(2)}) collective-permute-start(f32[32,256]{1,0:T(8,128)} %get-tuple-element.10), channel_id=1, source_target_pairs={{0,2},{1,3},{2,0},{3,1},{4,6},{5,7},{6,4},{7,5},{8,10},{9,11},{10,... | collective-permute-start | bytes 98312 | tf_op jit(solution)/shard_map/ppermute | solution.py:24
  7.9 6.6 %collective-permute-start.3 = (f32[32,256]{1,0:T(8,128)}, f32[32,256]{1,0:T(8,128)S(1)}, u32[]{:S(2)}, u32[]{:S(2)}) collective-permute-start(f32[32,256]{1,0:T(8,128)} %get-tuple-element.10), channel_id=1, source_target_pairs={{0,3},{1,2},{2,1},{3,0},{4,7},{5,6},{6,5},{7,4},{8,11},{9,10},{10,... | collective-permute-start | bytes 98312 | tf_op jit(solution)/shard_map/ppermute | solution.py:24
  7.9 10.9 %collective-permute-start.1 = (bf16[160,512]{1,0:T(8,128)(2,1)}, bf16[160,512]{1,0:T(8,128)(2,1)S(1)}, u32[]{:S(2)}, u32[]{:S(2)}) collective-permute-start(bf16[160,512]{1,0:T(8,128)(2,1)} %get-tuple-element.9), channel_id=1, source_target_pairs={{1,2},{2,1},{3,4},{4,3},{5,6},{6,5},{7,8},{8,7},{9,10},{10,9},{11,... | collective-permute-start | bytes 491528 | tf_op jit(solution)/shard_map/ppermute | solution.py:218
  11.4 3.0 %copy-start.3 = (f32[32,256]{1,0:T(8,128)S(1)}, f32[32,256]{1,0:T(8,128)}, u32[]{:S(2)}) copy-start(f32[32,256]{1,0:T(8,128)} %get-tuple-element.10) | copy-start | bytes 98308
  11.5 4.9 %copy-start.2 = (f32[32,1024]{1,0:T(8,128)S(1)}, f32[32,1024]{1,0:T(8,128)}, u32[]{:S(2)}) copy-start(f32[32,1024]{1,0:T(8,128)} %refs_1_.1) | copy-start | bytes 393220
  14.5 4.3 %collective-permute-start.4 = (f32[32,128]{1,0:T(8,128)S(1)}, f32[32,128]{1,0:T(8,128)S(1)}, u32[]{:S(2)}, u32[]{:S(2)}) collective-permute-start(f32[32,128]{1,0:T(8,128)S(1)} %slice_add_fusion.2), channel_id=1, source_target_pairs={{0,4},{4,0},{8,12},{12,8},{1,5},{5,1},{9,13},{13,9},{2,6},{6,2},{1... | collective-permute-start | bytes 49160 | tf_op jit(solution)/shard_map/ppermute | solution.py:24
  14.5 4.3 %collective-permute-start.5 = (f32[32,128]{1,0:T(8,128)S(1)}, f32[32,128]{1,0:T(8,128)S(1)}, u32[]{:S(2)}, u32[]{:S(2)}) collective-permute-start(f32[32,128]{1,0:T(8,128)S(1)} %slice_add_fusion.2), channel_id=1, source_target_pairs={{0,8},{4,12},{8,0},{12,4},{1,9},{5,13},{9,1},{13,5},{2,10},{6,14},... | collective-permute-start | bytes 49160 | tf_op jit(solution)/shard_map/ppermute | solution.py:24
  16.1 3.2 %collective-permute-start.6 = (f32[32,128]{1,0:T(8,128)S(1)}, f32[32,128]{1,0:T(8,128)S(1)}, u32[]{:S(2)}, u32[]{:S(2)}) collective-permute-start(f32[32,128]{1,0:T(8,128)S(1)} %slice_add_fusion.2), channel_id=1, source_target_pairs={{0,12},{4,8},{8,4},{12,0},{1,13},{5,9},{9,5},{13,1},{2,14},{6,10},... | collective-permute-start | bytes 49160 | tf_op jit(solution)/shard_map/ppermute | solution.py:24

commit v16 on v15

--- a/solution.py
+++ b/solution.py
@@ -238,7 +238,9 @@
         out_specs=VMEM,
         input_output_aliases={2: 0},
     )(
-        *in_vmem(embeddings, directions, local, from_pair, from_cross, level_basis),
+        *in_vmem(embeddings, directions),
+        local,
+        *in_vmem(from_pair, from_cross, level_basis),
         neighbours,
         counts,
         *in_vmem(*remote),

time: 21.8 us -> 22.2 us (1.018)
  Pallas kernels: 6.33 us -> 7.87 us
  local copies, waits for them, and re-layouts: 0.68 us -> 0.02 us
  waiting for transfers between devices: 6.3 us -> 5.85 us
    pallas_call x1, Pallas kernels: 1.71 us -> 2.59 us  [on_device(): pl.pallas_call(functools.partial(final_kernel, sub_size, sub_bits, leaf_b...]
    pallas_call x1, Pallas kernels: 2.37 us -> 3.02 us  [on_device(): pl.pallas_call(functools.partial(local_kernel, sub_size), out_shape=out,...]
    unnamed x9 -> x8, local copies, waits for them, and re-layouts: 0.68 us -> 0.02 us
    ppermute x5, waiting for transfers between devices: 3.39 us -> 2.94 us  [from_mask(): return lax.ppermute(x, axis, pairs)]
  transfers between devices with their start and end apart: 7 -> 7, of which waited for: 3 -> 2; matrix products, arithmetic and copies ran while one was open for 0% -> 0% of each run, Pallas kernels for 11% -> 14%
where the time goes in v16:
time: 22.2 us; the launch traced here: 22 us
  starting transfers between devices  8.21 us (37%)
  Pallas kernels  7.87 us (35%)
  waiting for transfers between devices  5.85 us (26%)
    ppermute x5, starting transfers between devices, from_mask(): return lax.ppermute(x, axis, pairs)  4.52 us
    ppermute x1, starting transfers between devices, on_device(): from_pair = lax.ppermute(pair, axes, [(i, i ^ 1) for i in range(ndev)])  3.02 us
    pallas_call x1, Pallas kernels, on_device(): pl.pallas_call(functools.partial(local_kernel, sub_size), out_shape=out,...  3.02 us
    ppermute x5, waiting for transfers between devices, from_mask(): return lax.ppermute(x, axis, pairs)  2.94 us
    ppermute x1, waiting for transfers between devices, on_device(): from_pair = lax.ppermute(pair, axes, [(i, i ^ 1) for i in range(ndev)])  2.9 us
    pallas_call x1, Pallas kernels, on_device(): pl.pallas_call(functools.partial(final_kernel, sub_size, sub_bits, leaf_b...  2.59 us
    pallas_call x1, Pallas kernels, on_device(): pl.pallas_call(functools.partial(send_kernel, loc_bits), out_shape=(pair_...  2.26 us
    ppermute x1, starting transfers between devices, on_device(): lax.ppermute(cross, axes, [(i, i - 1 + 2 * (i % 2)) for i in range(1, nde...  0.66 us
  transfers between devices with their start and end apart: 7, of which 2 were waited for; matrix products, arithmetic and copies ran while one was open for 0% of the time, Pallas kernels for 14%

profile of v16, /device:TPU:0, one launch (start us, length us, event | category | flops | bytes accessed | tf_op | source)
XLA Modules:
  0.0 22.0 jit_solution(10574033075872046640)
XLA Ops:
  0.0 0.0 copy-start
  0.0 2.3 %shard_map.56 = (bf16[208,512]{1,0:T(8,128)(2,1)}, bf16[160,512]{1,0:T(8,128)(2,1)}, f32[32,256]{1,0:T(8,128)}) custom-call(bf16[128,1024]{1,0:T(8,128)(2,1)} %refs_0_.1, f32[32,1024]{1,0:T(8,128)} %refs_1_.1, bf16[5,64,1024]{2,1,0:T(8,128)(2,1)} %refs_5_.1), custom_call_target="tpu_custom_call" | custom-call | tf_op jit(solution)/shard_map/pallas_call | solution.py:208
  2.3 0.0 copy-start.1
  2.3 3.0 %collective-permute-start = (bf16[208,512]{1,0:T(8,128)(2,1)}, bf16[208,512]{1,0:T(8,128)(2,1)S(1)}, u32[]{:S(2)}, u32[]{:S(2)}) collective-permute-start(bf16[208,512]{1,0:T(8,128)(2,1)} %get-tuple-element.8), channel_id=1, source_target_pairs={{0,1},{1,0},{2,3},{3,2},{4,5},{5,4},{6,7},{7,6},{8,9},{9,8},{10,11... | collective-permute-start | bytes 638984 | tf_op jit(solution)/shard_map/ppermute | solution.py:216
  5.3 2.6 %collective-permute-start.2 = (f32[32,256]{1,0:T(8,128)}, f32[32,256]{1,0:T(8,128)S(1)}, u32[]{:S(2)}, u32[]{:S(2)}) collective-permute-start(f32[32,256]{1,0:T(8,128)} %get-tuple-element.10), channel_id=1, source_target_pairs={{0,2},{1,3},{2,0},{3,1},{4,6},{5,7},{6,4},{7,5},{8,10},{9,11},{10,... | collective-permute-start | bytes 98312 | tf_op jit(solution)/shard_map/ppermute | solution.py:24
  7.9 0.0 collective-permute-start.3
  7.9 0.7 %collective-permute-start.1 = (bf16[160,512]{1,0:T(8,128)(2,1)}, bf16[160,512]{1,0:T(8,128)(2,1)S(1)}, u32[]{:S(2)}, u32[]{:S(2)}) collective-permute-start(bf16[160,512]{1,0:T(8,128)(2,1)} %get-tuple-element.9), channel_id=1, source_target_pairs={{1,2},{2,1},{3,4},{4,3},{5,6},{6,5},{7,8},{8,7},{9,10},{10,9},{11,... | collective-permute-start | bytes 491528 | tf_op jit(solution)/shard_map/ppermute | solution.py:218
  8.5 2.9 %collective-permute-done.refs_3_ = bf16[208,512]{1,0:T(8,128)(2,1)S(1)} collective-permute-done((bf16[208,512]{1,0:T(8,128)(2,1)}, bf16[208,512]{1,0:T(8,128)(2,1)S(1)}, u32[]{:S(2)}, u32[]{:S(2)}) %collective-permute-start) | collective-permute-done | bytes 213024 | tf_op jit(solution)/shard_map/ppermute | solution.py:216
  11.4 0.0 copy-start.3
  11.5 0.0 copy-start.2
  11.5 0.0 collective-permute-done.2.refs_8_
  11.5 2.9 %collective-permute-done.3.refs_9_ = f32[32,256]{1,0:T(8,128)S(1)} collective-permute-done((f32[32,256]{1,0:T(8,128)}, f32[32,256]{1,0:T(8,128)S(1)}, u32[]{:S(2)}, u32[]{:S(2)}) %collective-permute-start.3) | collective-permute-done | bytes 32800 | tf_op jit(solution)/shard_map/ppermute | solution.py:24
  14.4 0.0 copy-done.3
  14.5 0.1 collective-permute-start.4
  14.5 1.6 %collective-permute-start.5 = (f32[32,128]{1,0:T(8,128)S(1)}, f32[32,128]{1,0:T(8,128)S(1)}, u32[]{:S(2)}, u32[]{:S(2)}) collective-permute-start(f32[32,128]{1,0:T(8,128)S(1)} %slice_add_fusion.2), channel_id=1, source_target_pairs={{0,8},{4,12},{8,0},{12,4},{1,9},{5,13},{9,1},{13,5},{2,10},{6,14},... | collective-permute-start | bytes 49160 | tf_op jit(solution)/shard_map/ppermute | solution.py:24
  16.1 0.3 %collective-permute-start.6 = (f32[32,128]{1,0:T(8,128)S(1)}, f32[32,128]{1,0:T(8,128)S(1)}, u32[]{:S(2)}, u32[]{:S(2)}) collective-permute-start(f32[32,128]{1,0:T(8,128)S(1)} %slice_add_fusion.2), channel_id=1, source_target_pairs={{0,12},{4,8},{8,4},{12,0},{1,13},{5,9},{9,5},{13,1},{2,14},{6,10},... | collective-permute-start | bytes 49160 | tf_op jit(solution)/shard_map/ppermute | solution.py:24
  16.4 0.0 copy-done
  16.4 0.0 copy-done.1
  16.4 0.0 copy-done.2
  16.4 3.0 %shard_map.55.refs_2_ = f32[32,1024]{1,0:T(8,128)} custom-call(bf16[128,1024]{1,0:T(8,128)(2,1)S(1)} %copy-done.1, f32[32,1024]{1,0:T(8,128)S(1)} %copy-done.2, bf16[5,64,1024]{2,1,0:T(8,128)(2,1)S(1)} %copy-done, s32[2,8]{1,0:T(2,128)} %refs_6_.1, s32[2]{0:T(128)} %refs_7_.1), custom_call_target="tpu_custom_call" | custom-call | tf_op jit(solution)/shard_map/pallas_call | solution.py:226
  19.4 0.0 collective-permute-done.1.refs_4_
  19.4 0.0 collective-permute-done.4.refs_10_
  19.4 0.0 collective-permute-done.5.refs_11_
  19.4 0.0 collective-permute-done.6.refs_12_
  19.5 2.6 %shard_map.57 = f32[32,1024]{1,0:T(8,128)} custom-call(bf16[128,1024]{1,0:T(8,128)(2,1)S(1)} %copy-done.1, f32[32,1024]{1,0:T(8,128)S(1)} %copy-done.2, f32[32,1024]{1,0:T(8,128)} %shard_map.55.refs_2_, bf16[208,512]{1,0:T(8,128)(2,1)S(1)} %collective-permute-done.refs_3_, ...), custom_call_target="tpu_custom_call", output_to_operand_aliasing={{}: (2, {})} | custom-call | tf_op jit(solution)/shard_map/pallas_call | solution.py:234
  (4 shorter events, 0.0 us)
Async XLA Ops:
  0.0 16.4 %copy-start = (bf16[5,64,1024]{2,1,0:T(8,128)(2,1)S(1)}, bf16[5,64,1024]{2,1,0:T(8,128)(2,1)}, u32[]{:S(2)}) copy-start(bf16[5,64,1024]{2,1,0:T(8,128)(2,1)} %refs_5_.1) | copy-start | bytes 1966084
  2.3 14.1 %copy-start.1 = (bf16[128,1024]{1,0:T(8,128)(2,1)S(1)}, bf16[128,1024]{1,0:T(8,128)(2,1)}, u32[]{:S(2)}) copy-start(bf16[128,1024]{1,0:T(8,128)(2,1)} %refs_0_.1) | copy-start | bytes 786436
  2.3 9.2 %collective-permute-start = (bf16[208,512]{1,0:T(8,128)(2,1)}, bf16[208,512]{1,0:T(8,128)(2,1)S(1)}, u32[]{:S(2)}, u32[]{:S(2)}) collective-permute-start(bf16[208,512]{1,0:T(8,128)(2,1)} %get-tuple-element.8), channel_id=1, source_target_pairs={{0,1},{1,0},{2,3},{3,2},{4,5},{5,4},{6,7},{7,6},{8,9},{9,8},{10,11... | collective-permute-start | bytes 638984 | tf_op jit(solution)/shard_map/ppermute | solution.py:216
  5.3 6.2 %collective-permute-start.2 = (f32[32,256]{1,0:T(8,128)}, f32[32,256]{1,0:T(8,128)S(1)}, u32[]{:S(2)}, u32[]{:S(2)}) collective-permute-start(f32[32,256]{1,0:T(8,128)} %get-tuple-element.10), channel_id=1, source_target_pairs={{0,2},{1,3},{2,0},{3,1},{4,6},{5,7},{6,4},{7,5},{8,10},{9,11},{10,... | collective-permute-start | bytes 98312 | tf_op jit(solution)/shard_map/ppermute | solution.py:24
  7.9 6.6 %collective-permute-start.3 = (f32[32,256]{1,0:T(8,128)}, f32[32,256]{1,0:T(8,128)S(1)}, u32[]{:S(2)}, u32[]{:S(2)}) collective-permute-start(f32[32,256]{1,0:T(8,128)} %get-tuple-element.10), channel_id=1, source_target_pairs={{0,3},{1,2},{2,1},{3,0},{4,7},{5,6},{6,5},{7,4},{8,11},{9,10},{10,... | collective-permute-start | bytes 98312 | tf_op jit(solution)/shard_map/ppermute | solution.py:24
  7.9 11.6 %collective-permute-start.1 = (bf16[160,512]{1,0:T(8,128)(2,1)}, bf16[160,512]{1,0:T(8,128)(2,1)S(1)}, u32[]{:S(2)}, u32[]{:S(2)}) collective-permute-start(bf16[160,512]{1,0:T(8,128)(2,1)} %get-tuple-element.9), channel_id=1, source_target_pairs={{1,2},{2,1},{3,4},{4,3},{5,6},{6,5},{7,8},{8,7},{9,10},{10,9},{11,... | collective-permute-start | bytes 491528 | tf_op jit(solution)/shard_map/ppermute | solution.py:218
  11.4 3.0 %copy-start.3 = (f32[32,256]{1,0:T(8,128)S(1)}, f32[32,256]{1,0:T(8,128)}, u32[]{:S(2)}) copy-start(f32[32,256]{1,0:T(8,128)} %get-tuple-element.10) | copy-start | bytes 98308
  11.5 4.9 %copy-start.2 = (f32[32,1024]{1,0:T(8,128)S(1)}, f32[32,1024]{1,0:T(8,128)}, u32[]{:S(2)}) copy-start(f32[32,1024]{1,0:T(8,128)} %refs_1_.1) | copy-start | bytes 393220
  14.5 5.0 %collective-permute-start.4 = (f32[32,128]{1,0:T(8,128)S(1)}, f32[32,128]{1,0:T(8,128)S(1)}, u32[]{:S(2)}, u32[]{:S(2)}) collective-permute-start(f32[32,128]{1,0:T(8,128)S(1)} %slice_add_fusion.2), channel_id=1, source_target_pairs={{0,4},{4,0},{8,12},{12,8},{1,5},{5,1},{9,13},{13,9},{2,6},{6,2},{1... | collective-permute-start | bytes 49160 | tf_op jit(solution)/shard_map/ppermute | solution.py:24
  14.5 4.9 %collective-permute-start.5 = (f32[32,128]{1,0:T(8,128)S(1)}, f32[32,128]{1,0:T(8,128)S(1)}, u32[]{:S(2)}, u32[]{:S(2)}) collective-permute-start(f32[32,128]{1,0:T(8,128)S(1)} %slice_add_fusion.2), channel_id=1, source_target_pairs={{0,8},{4,12},{8,0},{12,4},{1,9},{5,13},{9,1},{13,5},{2,10},{6,14},... | collective-permute-start | bytes 49160 | tf_op jit(solution)/shard_map/ppermute | solution.py:24
  16.1 3.4 %collective-permute-start.6 = (f32[32,128]{1,0:T(8,128)S(1)}, f32[32,128]{1,0:T(8,128)S(1)}, u32[]{:S(2)}, u32[]{:S(2)}) collective-permute-start(f32[32,128]{1,0:T(8,128)S(1)} %slice_add_fusion.2), channel_id=1, source_target_pairs={{0,12},{4,8},{8,4},{12,0},{1,13},{5,9},{9,5},{13,1},{2,14},{6,10},... | collective-permute-start | bytes 49160 | tf_op jit(solution)/shard_map/ppermute | solution.py:24

commit v17 on v15

--- a/solution.py
+++ b/solution.py
@@ -236,7 +236,6 @@
         out_shape=out,
         in_specs=[VMEM] * 6 + [SMEM, SMEM] + [VMEM] * len(remote),
         out_specs=VMEM,
-        input_output_aliases={2: 0},
     )(
         *in_vmem(embeddings, directions, local, from_pair, from_cross, level_basis),
         neighbours,

time: 21.8 us -> 22.9 us (1.050)
  Pallas kernels: 6.33 us -> 7.64 us
  waiting for transfers between devices: 6.3 us -> 5.85 us
  local copies, waits for them, and re-layouts: 0.68 us -> 0.92 us
    pallas_call x1, Pallas kernels: 2.37 us -> 3.02 us  [on_device(): pl.pallas_call(functools.partial(local_kernel, sub_size), out_shape=out,...]
    pallas_call x1, Pallas kernels: 1.71 us -> 2.35 us  [on_device(): pl.pallas_call(functools.partial(final_kernel, sub_size, sub_bits, leaf_b...]
    ppermute x5, waiting for transfers between devices: 3.39 us -> 2.94 us  [from_mask(): return lax.ppermute(x, axis, pairs)]
    unnamed x9 -> x10, local copies, waits for them, and re-layouts: 0.68 us -> 0.92 us
  transfers between devices with their start and end apart: 7 -> 7, of which waited for: 3 -> 2; matrix products, arithmetic and copies ran while one was open for 0% -> 0% of each run, Pallas kernels for 11% -> 13%
where the time goes in v17:
time: 22.9 us; the launch traced here: 22.7 us
  starting transfers between devices  8.21 us (36%)
  Pallas kernels  7.64 us (33%)
  waiting for transfers between devices  5.85 us (26%)
  local copies, waits for them, and re-layouts  0.92 us (4%)
    ppermute x5, starting transfers between devices, from_mask(): return lax.ppermute(x, axis, pairs)  4.52 us
    ppermute x1, starting transfers between devices, on_device(): from_pair = lax.ppermute(pair, axes, [(i, i ^ 1) for i in range(ndev)])  3.02 us
    pallas_call x1, Pallas kernels, on_device(): pl.pallas_call(functools.partial(local_kernel, sub_size), out_shape=out,...  3.02 us
    ppermute x5, waiting for transfers between devices, from_mask(): return lax.ppermute(x, axis, pairs)  2.94 us
    ppermute x1, waiting for transfers between devices, on_device(): from_pair = lax.ppermute(pair, axes, [(i, i ^ 1) for i in range(ndev)])  2.9 us
    pallas_call x1, Pallas kernels, on_device(): pl.pallas_call(functools.partial(final_kernel, sub_size, sub_bits, leaf_b...  2.35 us
    pallas_call x1, Pallas kernels, on_device(): pl.pallas_call(functools.partial(send_kernel, loc_bits), out_shape=(pair_...  2.27 us
    unnamed x10, local copies, waits for them, and re-layouts  0.92 us
  transfers between devices with their start and end apart: 7, of which 2 were waited for; matrix products, arithmetic and copies ran while one was open for 0% of the time, Pallas kernels for 13%

profile of v17, /device:TPU:0, one launch (start us, length us, event | category | flops | bytes accessed | tf_op | source)
XLA Modules:
  0.0 22.7 jit_solution(10014417841133382799)
XLA Ops:
  0.0 0.0 copy-start
  0.0 2.3 %shard_map.56 = (bf16[208,512]{1,0:T(8,128)(2,1)}, bf16[160,512]{1,0:T(8,128)(2,1)}, f32[32,256]{1,0:T(8,128)}) custom-call(bf16[128,1024]{1,0:T(8,128)(2,1)} %refs_0_.1, f32[32,1024]{1,0:T(8,128)} %refs_1_.1, bf16[5,64,1024]{2,1,0:T(8,128)(2,1)} %refs_5_.1), custom_call_target="tpu_custom_call" | custom-call | tf_op jit(solution)/shard_map/pallas_call | solution.py:208
  2.3 0.0 copy-start.1
  2.3 3.0 %collective-permute-start = (bf16[208,512]{1,0:T(8,128)(2,1)}, bf16[208,512]{1,0:T(8,128)(2,1)S(1)}, u32[]{:S(2)}, u32[]{:S(2)}) collective-permute-start(bf16[208,512]{1,0:T(8,128)(2,1)} %get-tuple-element.8), channel_id=1, source_target_pairs={{0,1},{1,0},{2,3},{3,2},{4,5},{5,4},{6,7},{7,6},{8,9},{9,8},{10,11... | collective-permute-start | bytes 638984 | tf_op jit(solution)/shard_map/ppermute | solution.py:216
  5.3 2.6 %collective-permute-start.2 = (f32[32,256]{1,0:T(8,128)}, f32[32,256]{1,0:T(8,128)S(1)}, u32[]{:S(2)}, u32[]{:S(2)}) collective-permute-start(f32[32,256]{1,0:T(8,128)} %get-tuple-element.10), channel_id=1, source_target_pairs={{0,2},{1,3},{2,0},{3,1},{4,6},{5,7},{6,4},{7,5},{8,10},{9,11},{10,... | collective-permute-start | bytes 98312 | tf_op jit(solution)/shard_map/ppermute | solution.py:24
  7.9 0.0 collective-permute-start.3
  7.9 0.7 %collective-permute-start.1 = (bf16[160,512]{1,0:T(8,128)(2,1)}, bf16[160,512]{1,0:T(8,128)(2,1)S(1)}, u32[]{:S(2)}, u32[]{:S(2)}) collective-permute-start(bf16[160,512]{1,0:T(8,128)(2,1)} %get-tuple-element.9), channel_id=1, source_target_pairs={{1,2},{2,1},{3,4},{4,3},{5,6},{6,5},{7,8},{8,7},{9,10},{10,9},{11,... | collective-permute-start | bytes 491528 | tf_op jit(solution)/shard_map/ppermute | solution.py:218
  8.6 2.9 %collective-permute-done.refs_3_ = bf16[208,512]{1,0:T(8,128)(2,1)S(1)} collective-permute-done((bf16[208,512]{1,0:T(8,128)(2,1)}, bf16[208,512]{1,0:T(8,128)(2,1)S(1)}, u32[]{:S(2)}, u32[]{:S(2)}) %collective-permute-start) | collective-permute-done | bytes 213024 | tf_op jit(solution)/shard_map/ppermute | solution.py:216
  11.5 0.0 copy-start.4
  11.5 0.0 copy-start.2
  11.5 0.0 collective-permute-done.2.refs_8_
  11.5 2.9 %collective-permute-done.3.refs_9_ = f32[32,256]{1,0:T(8,128)S(1)} collective-permute-done((f32[32,256]{1,0:T(8,128)}, f32[32,256]{1,0:T(8,128)S(1)}, u32[]{:S(2)}, u32[]{:S(2)}) %collective-permute-start.3) | collective-permute-done | bytes 32800 | tf_op jit(solution)/shard_map/ppermute | solution.py:24
  14.5 0.0 copy-done.4
  14.5 0.1 collective-permute-start.4
  14.6 1.6 %collective-permute-start.5 = (f32[32,128]{1,0:T(8,128)S(1)}, f32[32,128]{1,0:T(8,128)S(1)}, u32[]{:S(2)}, u32[]{:S(2)}) collective-permute-start(f32[32,128]{1,0:T(8,128)S(1)} %slice_add_fusion.2), channel_id=1, source_target_pairs={{0,8},{4,12},{8,0},{12,4},{1,9},{5,13},{9,1},{13,5},{2,10},{6,14},... | collective-permute-start | bytes 49160 | tf_op jit(solution)/shard_map/ppermute | solution.py:24
  16.1 0.3 %collective-permute-start.6 = (f32[32,128]{1,0:T(8,128)S(1)}, f32[32,128]{1,0:T(8,128)S(1)}, u32[]{:S(2)}, u32[]{:S(2)}) collective-permute-start(f32[32,128]{1,0:T(8,128)S(1)} %slice_add_fusion.2), channel_id=1, source_target_pairs={{0,12},{4,8},{8,4},{12,0},{1,13},{5,9},{9,5},{13,1},{2,14},{6,10},... | collective-permute-start | bytes 49160 | tf_op jit(solution)/shard_map/ppermute | solution.py:24
  16.4 0.0 copy-done
  16.4 0.0 copy-done.1
  16.4 0.0 copy-done.2
  16.4 3.0 %shard_map.55.refs_2_ = f32[32,1024]{1,0:T(8,128)} custom-call(bf16[128,1024]{1,0:T(8,128)(2,1)S(1)} %copy-done.1, f32[32,1024]{1,0:T(8,128)S(1)} %copy-done.2, bf16[5,64,1024]{2,1,0:T(8,128)(2,1)S(1)} %copy-done, s32[2,8]{1,0:T(2,128)} %refs_6_.1, s32[2]{0:T(128)} %refs_7_.1), custom_call_target="tpu_custom_call" | custom-call | tf_op jit(solution)/shard_map/pallas_call | solution.py:226
  19.4 0.0 collective-permute-done.1.refs_4_
  19.4 0.0 collective-permute-done.4.refs_10_
  19.5 0.0 collective-permute-done.5.refs_11_
  19.5 0.0 collective-permute-done.6.refs_12_
  19.5 0.0 copy-start.3
  19.5 0.9 %copy-done.3 = f32[32,1024]{1,0:T(8,128)S(1)} copy-done((f32[32,1024]{1,0:T(8,128)S(1)}, f32[32,1024]{1,0:T(8,128)}, u32[]{:S(2)}) %copy-start.3) | copy-done | bytes 131096
  20.4 2.4 %shard_map.57 = f32[32,1024]{1,0:T(8,128)} custom-call(bf16[128,1024]{1,0:T(8,128)(2,1)S(1)} %copy-done.1, f32[32,1024]{1,0:T(8,128)S(1)} %copy-done.2, f32[32,1024]{1,0:T(8,128)S(1)} %copy-done.3, bf16[208,512]{1,0:T(8,128)(2,1)S(1)} %collective-permute-done.refs_3_, bf16[160,512]{1,0:T(8,128)(2,1)S(1)} %collective-permute-done.1.refs_4_, ...), custom_call_target="tpu_custom_call" | custom-call | tf_op jit(solution)/shard_map/pallas_call | solution.py:234
  (4 shorter events, 0.0 us)
Async XLA Ops:
  0.0 16.4 %copy-start = (bf16[5,64,1024]{2,1,0:T(8,128)(2,1)S(1)}, bf16[5,64,1024]{2,1,0:T(8,128)(2,1)}, u32[]{:S(2)}) copy-start(bf16[5,64,1024]{2,1,0:T(8,128)(2,1)} %refs_5_.1) | copy-start | bytes 1966084
  2.3 14.1 %copy-start.1 = (bf16[128,1024]{1,0:T(8,128)(2,1)S(1)}, bf16[128,1024]{1,0:T(8,128)(2,1)}, u32[]{:S(2)}) copy-start(bf16[128,1024]{1,0:T(8,128)(2,1)} %refs_0_.1) | copy-start | bytes 786436
  2.3 9.2 %collective-permute-start = (bf16[208,512]{1,0:T(8,128)(2,1)}, bf16[208,512]{1,0:T(8,128)(2,1)S(1)}, u32[]{:S(2)}, u32[]{:S(2)}) collective-permute-start(bf16[208,512]{1,0:T(8,128)(2,1)} %get-tuple-element.8), channel_id=1, source_target_pairs={{0,1},{1,0},{2,3},{3,2},{4,5},{5,4},{6,7},{7,6},{8,9},{9,8},{10,11... | collective-permute-start | bytes 638984 | tf_op jit(solution)/shard_map/ppermute | solution.py:216
  5.3 6.2 %collective-permute-start.2 = (f32[32,256]{1,0:T(8,128)}, f32[32,256]{1,0:T(8,128)S(1)}, u32[]{:S(2)}, u32[]{:S(2)}) collective-permute-start(f32[32,256]{1,0:T(8,128)} %get-tuple-element.10), channel_id=1, source_target_pairs={{0,2},{1,3},{2,0},{3,1},{4,6},{5,7},{6,4},{7,5},{8,10},{9,11},{10,... | collective-permute-start | bytes 98312 | tf_op jit(solution)/shard_map/ppermute | solution.py:24
  7.9 6.6 %collective-permute-start.3 = (f32[32,256]{1,0:T(8,128)}, f32[32,256]{1,0:T(8,128)S(1)}, u32[]{:S(2)}, u32[]{:S(2)}) collective-permute-start(f32[32,256]{1,0:T(8,128)} %get-tuple-element.10), channel_id=1, source_target_pairs={{0,3},{1,2},{2,1},{3,0},{4,7},{5,6},{6,5},{7,4},{8,11},{9,10},{10,... | collective-permute-start | bytes 98312 | tf_op jit(solution)/shard_map/ppermute | solution.py:24
  7.9 11.6 %collective-permute-start.1 = (bf16[160,512]{1,0:T(8,128)(2,1)}, bf16[160,512]{1,0:T(8,128)(2,1)S(1)}, u32[]{:S(2)}, u32[]{:S(2)}) collective-permute-start(bf16[160,512]{1,0:T(8,128)(2,1)} %get-tuple-element.9), channel_id=1, source_target_pairs={{1,2},{2,1},{3,4},{4,3},{5,6},{6,5},{7,8},{8,7},{9,10},{10,9},{11,... | collective-permute-start | bytes 491528 | tf_op jit(solution)/shard_map/ppermute | solution.py:218
  11.5 3.0 %copy-start.4 = (f32[32,256]{1,0:T(8,128)S(1)}, f32[32,256]{1,0:T(8,128)}, u32[]{:S(2)}) copy-start(f32[32,256]{1,0:T(8,128)} %get-tuple-element.10) | copy-start | bytes 98308
  11.5 4.9 %copy-start.2 = (f32[32,1024]{1,0:T(8,128)S(1)}, f32[32,1024]{1,0:T(8,128)}, u32[]{:S(2)}) copy-start(f32[32,1024]{1,0:T(8,128)} %refs_1_.1) | copy-start | bytes 393220
  14.5 5.0 %collective-permute-start.4 = (f32[32,128]{1,0:T(8,128)S(1)}, f32[32,128]{1,0:T(8,128)S(1)}, u32[]{:S(2)}, u32[]{:S(2)}) collective-permute-start(f32[32,128]{1,0:T(8,128)S(1)} %slice_add_fusion.2), channel_id=1, source_target_pairs={{0,4},{4,0},{8,12},{12,8},{1,5},{5,1},{9,13},{13,9},{2,6},{6,2},{1... | collective-permute-start | bytes 49160 | tf_op jit(solution)/shard_map/ppermute | solution.py:24
  14.6 4.9 %collective-permute-start.5 = (f32[32,128]{1,0:T(8,128)S(1)}, f32[32,128]{1,0:T(8,128)S(1)}, u32[]{:S(2)}, u32[]{:S(2)}) collective-permute-start(f32[32,128]{1,0:T(8,128)S(1)} %slice_add_fusion.2), channel_id=1, source_target_pairs={{0,8},{4,12},{8,0},{12,4},{1,9},{5,13},{9,1},{13,5},{2,10},{6,14},... | collective-permute-start | bytes 49160 | tf_op jit(solution)/shard_map/ppermute | solution.py:24
  16.1 3.4 %collective-permute-start.6 = (f32[32,128]{1,0:T(8,128)S(1)}, f32[32,128]{1,0:T(8,128)S(1)}, u32[]{:S(2)}, u32[]{:S(2)}) collective-permute-start(f32[32,128]{1,0:T(8,128)S(1)} %slice_add_fusion.2), channel_id=1, source_target_pairs={{0,12},{4,8},{8,4},{12,0},{1,13},{5,9},{9,5},{13,1},{2,14},{6,10},... | collective-permute-start | bytes 49160 | tf_op jit(solution)/shard_map/ppermute | solution.py:24
  19.5 0.9 %copy-start.3 = (f32[32,1024]{1,0:T(8,128)S(1)}, f32[32,1024]{1,0:T(8,128)}, u32[]{:S(2)}) copy-start(f32[32,1024]{1,0:T(8,128)} %shard_map.55.refs_2_) | copy-start | bytes 393220

commit v18 on v15

--- a/solution.py
+++ b/solution.py
@@ -210,7 +210,7 @@
         out_shape=(pair_shape, cross_shape, parts_shape),
         in_specs=[VMEM, VMEM, VMEM],
         out_specs=(VMEM, VMEM, VMEM),
-    )(embeddings, directions, level_basis)
+    )(*in_vmem(embeddings, directions, level_basis))
 
     ndev = sub_size * leaf_size
     from_pair = lax.ppermute(pair, axes, [(i, i ^ 1) for i in range(ndev)])

time: 21.8 us -> 23.6 us (1.083)
  local copies, waits for them, and re-layouts: 0.68 us -> 3.61 us
  Pallas kernels: 6.33 us -> 5.03 us
    unnamed x9, local copies, waits for them, and re-layouts: 0.68 us -> 3.6 us
    pallas_call x1, Pallas kernels: 2.26 us -> 0.96 us  [on_device(): pl.pallas_call(functools.partial(send_kernel, loc_bits), out_shape=(pair_...]
  transfers between devices with their start and end apart: 7 -> 7, of which waited for: 3 -> 3; matrix products, arithmetic and copies ran while one was open for 0% -> 0% of each run, Pallas kernels for 11% -> 10%
where the time goes in v18:
time: 23.6 us; the launch traced here: 23.3 us
  starting transfers between devices  8.21 us (35%)
  waiting for transfers between devices  6.31 us (27%)
  Pallas kernels  5.03 us (21%)
  local copies, waits for them, and re-layouts  3.61 us (15%)
    ppermute x5, starting transfers between devices, from_mask(): return lax.ppermute(x, axis, pairs)  4.53 us
    unnamed x9, local copies, waits for them, and re-layouts  3.6 us
    ppermute x5, waiting for transfers between devices, from_mask(): return lax.ppermute(x, axis, pairs)  3.41 us
    ppermute x1, starting transfers between devices, on_device(): from_pair = lax.ppermute(pair, axes, [(i, i ^ 1) for i in range(ndev)])  3.02 us
    ppermute x1, waiting for transfers between devices, on_device(): from_pair = lax.ppermute(pair, axes, [(i, i ^ 1) for i in range(ndev)])  2.9 us
    pallas_call x1, Pallas kernels, on_device(): pl.pallas_call(functools.partial(local_kernel, sub_size), out_shape=out,...  2.36 us
    pallas_call x1, Pallas kernels, on_device(): pl.pallas_call(functools.partial(final_kernel, sub_size, sub_bits, leaf_b...  1.71 us
    pallas_call x1, Pallas kernels, on_device(): pl.pallas_call(functools.partial(send_kernel, loc_bits), out_shape=(pair_...  0.96 us
  transfers between devices with their start and end apart: 7, of which 3 were waited for; matrix products, arithmetic and copies ran while one was open for 0% of the time, Pallas kernels for 10%

profile of v18, /device:TPU:0, one launch (start us, length us, event | category | flops | bytes accessed | tf_op | source)
XLA Modules:
  0.0 23.3 jit_solution(17913166490785442538)
XLA Ops:
  0.0 0.0 copy-start
  0.0 1.1 %copy-done = bf16[5,64,1024]{2,1,0:T(8,128)(2,1)S(1)} copy-done((bf16[5,64,1024]{2,1,0:T(8,128)(2,1)S(1)}, bf16[5,64,1024]{2,1,0:T(8,128)(2,1)}, u32[]{:S(2)}) %copy-start) | copy-done | bytes 655384
  1.1 0.0 copy-start.1
  1.1 0.9 %copy-done.1 = bf16[128,1024]{1,0:T(8,128)(2,1)S(1)} copy-done((bf16[128,1024]{1,0:T(8,128)(2,1)S(1)}, bf16[128,1024]{1,0:T(8,128)(2,1)}, u32[]{:S(2)}) %copy-start.1) | copy-done | bytes 262168
  2.0 0.0 copy-start.2
  2.0 0.9 %copy-done.2 = f32[32,1024]{1,0:T(8,128)S(1)} copy-done((f32[32,1024]{1,0:T(8,128)S(1)}, f32[32,1024]{1,0:T(8,128)}, u32[]{:S(2)}) %copy-start.2) | copy-done | bytes 131096
  2.9 1.0 %shard_map.56 = (bf16[208,512]{1,0:T(8,128)(2,1)}, bf16[160,512]{1,0:T(8,128)(2,1)}, f32[32,256]{1,0:T(8,128)}) custom-call(bf16[128,1024]{1,0:T(8,128)(2,1)S(1)} %copy-done.1, f32[32,1024]{1,0:T(8,128)S(1)} %copy-done.2, bf16[5,64,1024]{2,1,0:T(8,128)(2,1)S(1)} %copy-done), custom_call_target="tpu_custom_call" | custom-call | tf_op jit(solution)/shard_map/pallas_call | solution.py:208
  3.9 3.0 %collective-permute-start = (bf16[208,512]{1,0:T(8,128)(2,1)}, bf16[208,512]{1,0:T(8,128)(2,1)S(1)}, u32[]{:S(2)}, u32[]{:S(2)}) collective-permute-start(bf16[208,512]{1,0:T(8,128)(2,1)} %get-tuple-element.8), channel_id=1, source_target_pairs={{0,1},{1,0},{2,3},{3,2},{4,5},{5,4},{6,7},{7,6},{8,9},{9,8},{10,11... | collective-permute-start | bytes 638984 | tf_op jit(solution)/shard_map/ppermute | solution.py:216
  6.9 2.6 %collective-permute-start.2 = (f32[32,256]{1,0:T(8,128)}, f32[32,256]{1,0:T(8,128)S(1)}, u32[]{:S(2)}, u32[]{:S(2)}) collective-permute-start(f32[32,256]{1,0:T(8,128)} %get-tuple-element.10), channel_id=1, source_target_pairs={{0,2},{1,3},{2,0},{3,1},{4,6},{5,7},{6,4},{7,5},{8,10},{9,11},{10,... | collective-permute-start | bytes 98312 | tf_op jit(solution)/shard_map/ppermute | solution.py:24
  9.5 0.0 collective-permute-start.3
  9.5 0.7 %collective-permute-start.1 = (bf16[160,512]{1,0:T(8,128)(2,1)}, bf16[160,512]{1,0:T(8,128)(2,1)S(1)}, u32[]{:S(2)}, u32[]{:S(2)}) collective-permute-start(bf16[160,512]{1,0:T(8,128)(2,1)} %get-tuple-element.9), channel_id=1, source_target_pairs={{1,2},{2,1},{3,4},{4,3},{5,6},{6,5},{7,8},{8,7},{9,10},{10,9},{11,... | collective-permute-start | bytes 491528 | tf_op jit(solution)/shard_map/ppermute | solution.py:218
  10.2 2.9 %collective-permute-done.refs_3_ = bf16[208,512]{1,0:T(8,128)(2,1)S(1)} collective-permute-done((bf16[208,512]{1,0:T(8,128)(2,1)}, bf16[208,512]{1,0:T(8,128)(2,1)S(1)}, u32[]{:S(2)}, u32[]{:S(2)}) %collective-permute-start) | collective-permute-done | bytes 213024 | tf_op jit(solution)/shard_map/ppermute | solution.py:216
  13.1 0.0 copy-start.3
  13.1 0.0 collective-permute-done.2.refs_8_
  13.2 2.9 %collective-permute-done.3.refs_9_ = f32[32,256]{1,0:T(8,128)S(1)} collective-permute-done((f32[32,256]{1,0:T(8,128)}, f32[32,256]{1,0:T(8,128)S(1)}, u32[]{:S(2)}, u32[]{:S(2)}) %collective-permute-start.3) | collective-permute-done | bytes 32800 | tf_op jit(solution)/shard_map/ppermute | solution.py:24
  16.1 0.0 copy-done.3
  16.1 0.1 collective-permute-start.4
  16.2 1.6 %collective-permute-start.5 = (f32[32,128]{1,0:T(8,128)S(1)}, f32[32,128]{1,0:T(8,128)S(1)}, u32[]{:S(2)}, u32[]{:S(2)}) collective-permute-start(f32[32,128]{1,0:T(8,128)S(1)} %slice_add_fusion.2), channel_id=1, source_target_pairs={{0,8},{4,12},{8,0},{12,4},{1,9},{5,13},{9,1},{13,5},{2,10},{6,14},... | collective-permute-start | bytes 49160 | tf_op jit(solution)/shard_map/ppermute | solution.py:24
  17.7 0.3 %collective-permute-start.6 = (f32[32,128]{1,0:T(8,128)S(1)}, f32[32,128]{1,0:T(8,128)S(1)}, u32[]{:S(2)}, u32[]{:S(2)}) collective-permute-start(f32[32,128]{1,0:T(8,128)S(1)} %slice_add_fusion.2), channel_id=1, source_target_pairs={{0,12},{4,8},{8,4},{12,0},{1,13},{5,9},{9,5},{13,1},{2,14},{6,10},... | collective-permute-start | bytes 49160 | tf_op jit(solution)/shard_map/ppermute | solution.py:24
  18.0 2.4 %shard_map.55.refs_2_ = f32[32,1024]{1,0:T(8,128)S(1)} custom-call(bf16[128,1024]{1,0:T(8,128)(2,1)S(1)} %copy-done.1, f32[32,1024]{1,0:T(8,128)S(1)} %copy-done.2, bf16[5,64,1024]{2,1,0:T(8,128)(2,1)S(1)} %copy-done, s32[2,8]{1,0:T(2,128)} %refs_6_.1, s32[2]{0:T(128)} %refs_7_.1), custom_call_target="tpu_custom_call" | custom-call | tf_op jit(solution)/shard_map/pallas_call | solution.py:226
  20.4 0.0 collective-permute-done.1.refs_4_
  20.4 0.0 collective-permute-done.4.refs_10_
  20.4 0.0 collective-permute-done.5.refs_11_
  20.4 0.5 %collective-permute-done.6.refs_12_ = f32[32,128]{1,0:T(8,128)S(1)} collective-permute-done((f32[32,128]{1,0:T(8,128)S(1)}, f32[32,128]{1,0:T(8,128)S(1)}, u32[]{:S(2)}, u32[]{:S(2)}) %collective-permute-start.6) | collective-permute-done | bytes 16416 | tf_op jit(solution)/shard_map/ppermute | solution.py:24
  20.9 1.7 %shard_map.57 = f32[32,1024]{1,0:T(8,128)S(1)} custom-call(bf16[128,1024]{1,0:T(8,128)(2,1)S(1)} %copy-done.1, f32[32,1024]{1,0:T(8,128)S(1)} %copy-done.2, f32[32,1024]{1,0:T(8,128)S(1)} %shard_map.55.refs_2_, bf16[208,512]{1,0:T(8,128)(2,1)S(1)} %collective-permute-done.refs_3_, ...), custom_call_target="tpu_custom_call", output_to_operand_aliasing={{}: (2, {})} | custom-call | tf_op jit(solution)/shard_map/pallas_call | solution.py:234
  22.6 0.7 %copy.8 = f32[32,1024]{1,0:T(8,128)} copy(f32[32,1024]{1,0:T(8,128)S(1)} %shard_map.57) | data formatting | bytes 262144
  (4 shorter events, 0.0 us)
Async XLA Ops:
  0.0 1.1 %copy-start = (bf16[5,64,1024]{2,1,0:T(8,128)(2,1)S(1)}, bf16[5,64,1024]{2,1,0:T(8,128)(2,1)}, u32[]{:S(2)}) copy-start(bf16[5,64,1024]{2,1,0:T(8,128)(2,1)} %refs_5_.1) | copy-start | bytes 1966084
  1.1 0.9 %copy-start.1 = (bf16[128,1024]{1,0:T(8,128)(2,1)S(1)}, bf16[128,1024]{1,0:T(8,128)(2,1)}, u32[]{:S(2)}) copy-start(bf16[128,1024]{1,0:T(8,128)(2,1)} %refs_0_.1) | copy-start | bytes 786436
  2.0 0.9 %copy-start.2 = (f32[32,1024]{1,0:T(8,128)S(1)}, f32[32,1024]{1,0:T(8,128)}, u32[]{:S(2)}) copy-start(f32[32,1024]{1,0:T(8,128)} %refs_1_.1) | copy-start | bytes 393220
  3.9 9.2 %collective-permute-start = (bf16[208,512]{1,0:T(8,128)(2,1)}, bf16[208,512]{1,0:T(8,128)(2,1)S(1)}, u32[]{:S(2)}, u32[]{:S(2)}) collective-permute-start(bf16[208,512]{1,0:T(8,128)(2,1)} %get-tuple-element.8), channel_id=1, source_target_pairs={{0,1},{1,0},{2,3},{3,2},{4,5},{5,4},{6,7},{7,6},{8,9},{9,8},{10,11... | collective-permute-start | bytes 638984 | tf_op jit(solution)/shard_map/ppermute | solution.py:216
  6.9 6.2 %collective-permute-start.2 = (f32[32,256]{1,0:T(8,128)}, f32[32,256]{1,0:T(8,128)S(1)}, u32[]{:S(2)}, u32[]{:S(2)}) collective-permute-start(f32[32,256]{1,0:T(8,128)} %get-tuple-element.10), channel_id=1, source_target_pairs={{0,2},{1,3},{2,0},{3,1},{4,6},{5,7},{6,4},{7,5},{8,10},{9,11},{10,... | collective-permute-start | bytes 98312 | tf_op jit(solution)/shard_map/ppermute | solution.py:24
  9.5 6.6 %collective-permute-start.3 = (f32[32,256]{1,0:T(8,128)}, f32[32,256]{1,0:T(8,128)S(1)}, u32[]{:S(2)}, u32[]{:S(2)}) collective-permute-start(f32[32,256]{1,0:T(8,128)} %get-tuple-element.10), channel_id=1, source_target_pairs={{0,3},{1,2},{2,1},{3,0},{4,7},{5,6},{6,5},{7,4},{8,11},{9,10},{10,... | collective-permute-start | bytes 98312 | tf_op jit(solution)/shard_map/ppermute | solution.py:24
  9.5 10.9 %collective-permute-start.1 = (bf16[160,512]{1,0:T(8,128)(2,1)}, bf16[160,512]{1,0:T(8,128)(2,1)S(1)}, u32[]{:S(2)}, u32[]{:S(2)}) collective-permute-start(bf16[160,512]{1,0:T(8,128)(2,1)} %get-tuple-element.9), channel_id=1, source_target_pairs={{1,2},{2,1},{3,4},{4,3},{5,6},{6,5},{7,8},{8,7},{9,10},{10,9},{11,... | collective-permute-start | bytes 491528 | tf_op jit(solution)/shard_map/ppermute | solution.py:218
  13.1 3.0 %copy-start.3 = (f32[32,256]{1,0:T(8,128)S(1)}, f32[32,256]{1,0:T(8,128)}, u32[]{:S(2)}) copy-start(f32[32,256]{1,0:T(8,128)} %get-tuple-element.10) | copy-start | bytes 98308
  16.1 4.3 %collective-permute-start.4 = (f32[32,128]{1,0:T(8,128)S(1)}, f32[32,128]{1,0:T(8,128)S(1)}, u32[]{:S(2)}, u32[]{:S(2)}) collective-permute-start(f32[32,128]{1,0:T(8,128)S(1)} %slice_add_fusion.2), channel_id=1, source_target_pairs={{0,4},{4,0},{8,12},{12,8},{1,5},{5,1},{9,13},{13,9},{2,6},{6,2},{1... | collective-permute-start | bytes 49160 | tf_op jit(solution)/shard_map/ppermute | solution.py:24
  16.2 4.3 %collective-permute-start.5 = (f32[32,128]{1,0:T(8,128)S(1)}, f32[32,128]{1,0:T(8,128)S(1)}, u32[]{:S(2)}, u32[]{:S(2)}) collective-permute-start(f32[32,128]{1,0:T(8,128)S(1)} %slice_add_fusion.2), channel_id=1, source_target_pairs={{0,8},{4,12},{8,0},{12,4},{1,9},{5,13},{9,1},{13,5},{2,10},{6,14},... | collective-permute-start | bytes 49160 | tf_op jit(solution)/shard_map/ppermute | solution.py:24
  17.7 3.2 %collective-permute-start.6 = (f32[32,128]{1,0:T(8,128)S(1)}, f32[32,128]{1,0:T(8,128)S(1)}, u32[]{:S(2)}, u32[]{:S(2)}) collective-permute-start(f32[32,128]{1,0:T(8,128)S(1)} %slice_add_fusion.2), channel_id=1, source_target_pairs={{0,12},{4,8},{8,4},{12,0},{1,13},{5,9},{9,5},{13,1},{2,14},{6,10},... | collective-permute-start | bytes 49160 | tf_op jit(solution)/shard_map/ppermute | solution.py:24

commit v19 on v15

--- a/solution.py
+++ b/solution.py
@@ -47,7 +47,10 @@
     return jnp.concatenate([x[:, g * columns : (g + 1) * columns] for g in range(groups)], axis=0)
 
 
-def send_kernel(loc_bits, emb_ref, dirs_ref, basis_ref, pair_ref, cross_ref, parts_ref):
+def send_kernel(loc_bits, emb_ref, dirs_ref, basis_ref, pair_ref, cross_ref, parts_ref, upper_ref, sem):
+    levels = upper_ref.shape[0]
+    fetch = pltpu.make_async_copy(basis_ref.at[pl.ds(loc_bits, levels)], upper_ref, sem)
+    fetch.start()
     width_e = emb_ref.shape[0]
     local_points = emb_ref.shape[1]
     nrhs = dirs_ref.shape[0]
@@ -59,8 +62,9 @@
     pair_ref[width_e : width_e + nrhs, :] = jnp.where(even, tail_values, head_values)
     cross_ref[:width_e, :] = jnp.where(even, head_points, tail_points)
     cross_ref[width_e:, :] = jnp.where(even, head_values, tail_values)
-    levels, rank = parts_ref.shape[1] // basis_ref.shape[1], basis_ref.shape[1]
-    stacked = basis_ref[loc_bits : loc_bits + levels].reshape(levels * rank, local_points)
+    rank = upper_ref.shape[1]
+    fetch.wait()
+    stacked = upper_ref[...].reshape(levels * rank, local_points)
     parts = nt_dot(values, stacked)
     parts_ref[...] = parts
     rows = split_rows(parts, LEAF)
@@ -208,8 +212,12 @@
     pair, cross, parts = pl.pallas_call(
         functools.partial(send_kernel, loc_bits),
         out_shape=(pair_shape, cross_shape, parts_shape),
-        in_specs=[VMEM, VMEM, VMEM],
+        in_specs=[VMEM, VMEM, pl.BlockSpec(memory_space=pl.ANY)],
         out_specs=(VMEM, VMEM, VMEM),
+        scratch_shapes=[
+            pltpu.VMEM((dev_bits, rank, local_points), level_basis.dtype),
+            pltpu.SemaphoreType.DMA(()),
+        ],
     )(embeddings, directions, level_basis)
 
     ndev = sub_size * leaf_size

time: 21.8 us -> 22.7 us (1.041)
  Pallas kernels: 6.33 us -> 7.12 us
    pallas_call x1, Pallas kernels: 2.26 us -> 3.06 us  [on_device(): pl.pallas_call(functools.partial(send_kernel, loc_bits), out_shape=(pair_...]
  transfers between devices with their start and end apart: 7 -> 7, of which waited for: 3 -> 3; matrix products, arithmetic and copies ran while one was open for 0% -> 0% of each run, Pallas kernels for 11% -> 10%
where the time goes in v19:
time: 22.7 us; the launch traced here: 22.5 us
  starting transfers between devices  8.27 us (36%)
  Pallas kernels  7.12 us (31%)
  waiting for transfers between devices  6.3 us (28%)
  local copies, waits for them, and re-layouts  0.68 us (3%)
    ppermute x5, starting transfers between devices, from_mask(): return lax.ppermute(x, axis, pairs)  4.52 us
    ppermute x5, waiting for transfers between devices, from_mask(): return lax.ppermute(x, axis, pairs)  3.4 us
    ppermute x1, starting transfers between devices, on_device(): from_pair = lax.ppermute(pair, axes, [(i, i ^ 1) for i in range(ndev)])  3.09 us
    pallas_call x1, Pallas kernels, on_device(): pl.pallas_call(functools.partial(send_kernel, loc_bits), out_shape=(pair_...  3.06 us
    ppermute x1, waiting for transfers between devices, on_device(): from_pair = lax.ppermute(pair, axes, [(i, i ^ 1) for i in range(ndev)])  2.9 us
    pallas_call x1, Pallas kernels, on_device(): pl.pallas_call(functools.partial(local_kernel, sub_size), out_shape=out,...  2.35 us
    pallas_call x1, Pallas kernels, on_device(): pl.pallas_call(functools.partial(final_kernel, sub_size, sub_bits, leaf_b...  1.71 us
    unnamed x9, local copies, waits for them, and re-layouts  0.68 us
  transfers between devices with their start and end apart: 7, of which 3 were waited for; matrix products, arithmetic and copies ran while one was open for 0% of the time, Pallas kernels for 10%

profile of v19, /device:TPU:0, one launch (start us, length us, event | category | flops | bytes accessed | tf_op | source)
XLA Modules:
  0.0 22.5 jit_solution(3756462648952972207)
XLA Ops:
  0.0 0.0 copy-start
  0.0 3.1 %shard_map.56 = (bf16[208,512]{1,0:T(8,128)(2,1)}, bf16[160,512]{1,0:T(8,128)(2,1)}, f32[32,256]{1,0:T(8,128)}) custom-call(bf16[128,1024]{1,0:T(8,128)(2,1)} %refs_0_.1, f32[32,1024]{1,0:T(8,128)} %refs_1_.1, bf16[5,64,1024]{2,1,0:T(8,128)(2,1)} %refs_5_.1), custom_call_target="tpu_custom_call" | custom-call | tf_op jit(solution)/shard_map/pallas_call | solution.py:212
  3.1 0.0 copy-start.1
  3.1 3.1 %collective-permute-start = (bf16[208,512]{1,0:T(8,128)(2,1)}, bf16[208,512]{1,0:T(8,128)(2,1)S(1)}, u32[]{:S(2)}, u32[]{:S(2)}) collective-permute-start(bf16[208,512]{1,0:T(8,128)(2,1)} %get-tuple-element.8), channel_id=1, source_target_pairs={{0,1},{1,0},{2,3},{3,2},{4,5},{5,4},{6,7},{7,6},{8,9},{9,8},{10,11... | collective-permute-start | bytes 638984 | tf_op jit(solution)/shard_map/ppermute | solution.py:224
  6.2 2.6 %collective-permute-start.2 = (f32[32,256]{1,0:T(8,128)}, f32[32,256]{1,0:T(8,128)S(1)}, u32[]{:S(2)}, u32[]{:S(2)}) collective-permute-start(f32[32,256]{1,0:T(8,128)} %get-tuple-element.10), channel_id=1, source_target_pairs={{0,2},{1,3},{2,0},{3,1},{4,6},{5,7},{6,4},{7,5},{8,10},{9,11},{10,... | collective-permute-start | bytes 98312 | tf_op jit(solution)/shard_map/ppermute | solution.py:24
  8.8 0.0 collective-permute-start.3
  8.8 0.7 %collective-permute-start.1 = (bf16[160,512]{1,0:T(8,128)(2,1)}, bf16[160,512]{1,0:T(8,128)(2,1)S(1)}, u32[]{:S(2)}, u32[]{:S(2)}) collective-permute-start(bf16[160,512]{1,0:T(8,128)(2,1)} %get-tuple-element.9), channel_id=1, source_target_pairs={{1,2},{2,1},{3,4},{4,3},{5,6},{6,5},{7,8},{8,7},{9,10},{10,9},{11,... | collective-permute-start | bytes 491528 | tf_op jit(solution)/shard_map/ppermute | solution.py:226
  9.4 2.9 %collective-permute-done.refs_3_ = bf16[208,512]{1,0:T(8,128)(2,1)S(1)} collective-permute-done((bf16[208,512]{1,0:T(8,128)(2,1)}, bf16[208,512]{1,0:T(8,128)(2,1)S(1)}, u32[]{:S(2)}, u32[]{:S(2)}) %collective-permute-start) | collective-permute-done | bytes 213024 | tf_op jit(solution)/shard_map/ppermute | solution.py:224
  12.3 0.0 copy-start.3
  12.4 0.0 copy-start.2
  12.4 0.0 collective-permute-done.2.refs_8_
  12.4 2.9 %collective-permute-done.3.refs_9_ = f32[32,256]{1,0:T(8,128)S(1)} collective-permute-done((f32[32,256]{1,0:T(8,128)}, f32[32,256]{1,0:T(8,128)S(1)}, u32[]{:S(2)}, u32[]{:S(2)}) %collective-permute-start.3) | collective-permute-done | bytes 32800 | tf_op jit(solution)/shard_map/ppermute | solution.py:24
  15.3 0.0 copy-done.3
  15.3 0.1 collective-permute-start.4
  15.4 1.6 %collective-permute-start.5 = (f32[32,128]{1,0:T(8,128)S(1)}, f32[32,128]{1,0:T(8,128)S(1)}, u32[]{:S(2)}, u32[]{:S(2)}) collective-permute-start(f32[32,128]{1,0:T(8,128)S(1)} %slice_add_fusion.2), channel_id=1, source_target_pairs={{0,8},{4,12},{8,0},{12,4},{1,9},{5,13},{9,1},{13,5},{2,10},{6,14},... | collective-permute-start | bytes 49160 | tf_op jit(solution)/shard_map/ppermute | solution.py:24
  17.0 0.3 %collective-permute-start.6 = (f32[32,128]{1,0:T(8,128)S(1)}, f32[32,128]{1,0:T(8,128)S(1)}, u32[]{:S(2)}, u32[]{:S(2)}) collective-permute-start(f32[32,128]{1,0:T(8,128)S(1)} %slice_add_fusion.2), channel_id=1, source_target_pairs={{0,12},{4,8},{8,4},{12,0},{1,13},{5,9},{9,5},{13,1},{2,14},{6,10},... | collective-permute-start | bytes 49160 | tf_op jit(solution)/shard_map/ppermute | solution.py:24
  17.3 0.0 copy-done
  17.3 0.0 copy-done.1
  17.3 0.0 copy-done.2
  17.3 2.4 %shard_map.55.refs_2_ = f32[32,1024]{1,0:T(8,128)S(1)} custom-call(bf16[128,1024]{1,0:T(8,128)(2,1)S(1)} %copy-done.1, f32[32,1024]{1,0:T(8,128)S(1)} %copy-done.2, bf16[5,64,1024]{2,1,0:T(8,128)(2,1)S(1)} %copy-done, s32[2,8]{1,0:T(2,128)} %refs_6_.1, s32[2]{0:T(128)} %refs_7_.1), custom_call_target="tpu_custom_call" | custom-call | tf_op jit(solution)/shard_map/pallas_call | solution.py:234
  19.7 0.0 collective-permute-done.1.refs_4_
  19.7 0.0 collective-permute-done.4.refs_10_
  19.7 0.0 collective-permute-done.5.refs_11_
  19.7 0.5 %collective-permute-done.6.refs_12_ = f32[32,128]{1,0:T(8,128)S(1)} collective-permute-done((f32[32,128]{1,0:T(8,128)S(1)}, f32[32,128]{1,0:T(8,128)S(1)}, u32[]{:S(2)}, u32[]{:S(2)}) %collective-permute-start.6) | collective-permute-done | bytes 16416 | tf_op jit(solution)/shard_map/ppermute | solution.py:24
  20.1 1.7 %shard_map.57 = f32[32,1024]{1,0:T(8,128)S(1)} custom-call(bf16[128,1024]{1,0:T(8,128)(2,1)S(1)} %copy-done.1, f32[32,1024]{1,0:T(8,128)S(1)} %copy-done.2, f32[32,1024]{1,0:T(8,128)S(1)} %shard_map.55.refs_2_, bf16[208,512]{1,0:T(8,128)(2,1)S(1)} %collective-permute-done.refs_3_, ...), custom_call_target="tpu_custom_call", output_to_operand_aliasing={{}: (2, {})} | custom-call | tf_op jit(solution)/shard_map/pallas_call | solution.py:242
  21.9 0.7 %copy.8 = f32[32,1024]{1,0:T(8,128)} copy(f32[32,1024]{1,0:T(8,128)S(1)} %shard_map.57) | data formatting | bytes 262144
  (4 shorter events, 0.0 us)
Async XLA Ops:
  0.0 17.3 %copy-start = (bf16[5,64,1024]{2,1,0:T(8,128)(2,1)S(1)}, bf16[5,64,1024]{2,1,0:T(8,128)(2,1)}, u32[]{:S(2)}) copy-start(bf16[5,64,1024]{2,1,0:T(8,128)(2,1)} %refs_5_.1) | copy-start | bytes 1966084
  3.1 14.2 %copy-start.1 = (bf16[128,1024]{1,0:T(8,128)(2,1)S(1)}, bf16[128,1024]{1,0:T(8,128)(2,1)}, u32[]{:S(2)}) copy-start(bf16[128,1024]{1,0:T(8,128)(2,1)} %refs_0_.1) | copy-start | bytes 786436
  3.1 9.3 %collective-permute-start = (bf16[208,512]{1,0:T(8,128)(2,1)}, bf16[208,512]{1,0:T(8,128)(2,1)S(1)}, u32[]{:S(2)}, u32[]{:S(2)}) collective-permute-start(bf16[208,512]{1,0:T(8,128)(2,1)} %get-tuple-element.8), channel_id=1, source_target_pairs={{0,1},{1,0},{2,3},{3,2},{4,5},{5,4},{6,7},{7,6},{8,9},{9,8},{10,11... | collective-permute-start | bytes 638984 | tf_op jit(solution)/shard_map/ppermute | solution.py:224
  6.2 6.2 %collective-permute-start.2 = (f32[32,256]{1,0:T(8,128)}, f32[32,256]{1,0:T(8,128)S(1)}, u32[]{:S(2)}, u32[]{:S(2)}) collective-permute-start(f32[32,256]{1,0:T(8,128)} %get-tuple-element.10), channel_id=1, source_target_pairs={{0,2},{1,3},{2,0},{3,1},{4,6},{5,7},{6,4},{7,5},{8,10},{9,11},{10,... | collective-permute-start | bytes 98312 | tf_op jit(solution)/shard_map/ppermute | solution.py:24
  8.8 6.6 %collective-permute-start.3 = (f32[32,256]{1,0:T(8,128)}, f32[32,256]{1,0:T(8,128)S(1)}, u32[]{:S(2)}, u32[]{:S(2)}) collective-permute-start(f32[32,256]{1,0:T(8,128)} %get-tuple-element.10), channel_id=1, source_target_pairs={{0,3},{1,2},{2,1},{3,0},{4,7},{5,6},{6,5},{7,4},{8,11},{9,10},{10,... | collective-permute-start | bytes 98312 | tf_op jit(solution)/shard_map/ppermute | solution.py:24
  8.8 10.9 %collective-permute-start.1 = (bf16[160,512]{1,0:T(8,128)(2,1)}, bf16[160,512]{1,0:T(8,128)(2,1)S(1)}, u32[]{:S(2)}, u32[]{:S(2)}) collective-permute-start(bf16[160,512]{1,0:T(8,128)(2,1)} %get-tuple-element.9), channel_id=1, source_target_pairs={{1,2},{2,1},{3,4},{4,3},{5,6},{6,5},{7,8},{8,7},{9,10},{10,9},{11,... | collective-permute-start | bytes 491528 | tf_op jit(solution)/shard_map/ppermute | solution.py:226
  12.3 3.0 %copy-start.3 = (f32[32,256]{1,0:T(8,128)S(1)}, f32[32,256]{1,0:T(8,128)}, u32[]{:S(2)}) copy-start(f32[32,256]{1,0:T(8,128)} %get-tuple-element.10) | copy-start | bytes 98308
  12.4 4.9 %copy-start.2 = (f32[32,1024]{1,0:T(8,128)S(1)}, f32[32,1024]{1,0:T(8,128)}, u32[]{:S(2)}) copy-start(f32[32,1024]{1,0:T(8,128)} %refs_1_.1) | copy-start | bytes 393220
  15.3 4.3 %collective-permute-start.4 = (f32[32,128]{1,0:T(8,128)S(1)}, f32[32,128]{1,0:T(8,128)S(1)}, u32[]{:S(2)}, u32[]{:S(2)}) collective-permute-start(f32[32,128]{1,0:T(8,128)S(1)} %slice_add_fusion.2), channel_id=1, source_target_pairs={{0,4},{4,0},{8,12},{12,8},{1,5},{5,1},{9,13},{13,9},{2,6},{6,2},{1... | collective-permute-start | bytes 49160 | tf_op jit(solution)/shard_map/ppermute | solution.py:24
  15.4 4.3 %collective-permute-start.5 = (f32[32,128]{1,0:T(8,128)S(1)}, f32[32,128]{1,0:T(8,128)S(1)}, u32[]{:S(2)}, u32[]{:S(2)}) collective-permute-start(f32[32,128]{1,0:T(8,128)S(1)} %slice_add_fusion.2), channel_id=1, source_target_pairs={{0,8},{4,12},{8,0},{12,4},{1,9},{5,13},{9,1},{13,5},{2,10},{6,14},... | collective-permute-start | bytes 49160 | tf_op jit(solution)/shard_map/ppermute | solution.py:24
  17.0 3.2 %collective-permute-start.6 = (f32[32,128]{1,0:T(8,128)S(1)}, f32[32,128]{1,0:T(8,128)S(1)}, u32[]{:S(2)}, u32[]{:S(2)}) collective-permute-start(f32[32,128]{1,0:T(8,128)S(1)} %slice_add_fusion.2), channel_id=1, source_target_pairs={{0,12},{4,8},{8,4},{12,0},{1,13},{5,9},{9,5},{13,1},{2,14},{6,10},... | collective-permute-start | bytes 49160 | tf_op jit(solution)/shard_map/ppermute | solution.py:24

commit v20 on v15

--- a/solution.py
+++ b/solution.py
@@ -114,9 +114,10 @@
         return total.astype(jnp.float32)
 
 
-def local_kernel(sub_size, emb_ref, dirs_ref, basis_ref, neighbours_ref, counts_ref, out_ref):
+def local_kernel(sub_size, emb_ref, dirs_ref, basis_ref, pair_ref, cross_ref, neighbours_ref, counts_ref, out_ref):
     lv = Leaves(emb_ref, dirs_ref, neighbours_ref, counts_ref, sub_size)
     rank = basis_ref.shape[1]
+    nrhs = dirs_ref.shape[0]
     near = [nt_dot(lv.leaf_values[j], lv.block(j, lv.points[j], lv.norms[j])) for j in range(lv.count)]
     for j in range(lv.count - 1):
         pair = lv.block(j, lv.points[j + 1], lv.norms[j + 1])
@@ -128,6 +129,16 @@
         (nt_dot(lv.leaf_values[q], basis0[:, q * LEAF : (q + 1) * LEAF]) * factor0).astype(jnp.bfloat16)
         for q in range(lv.count)
     ]
+    even = lax.axis_index("sub") % 2 == 0
+    halo_pair = pair_ref[: lv.width_e + nrhs, :]
+    cross = cross_ref[...]
+    left, right = jnp.where(even, cross, halo_pair), jnp.where(even, halo_pair, cross)
+    for j, received, offset in ((0, left, -1), (lv.count - 1, right, 1)):
+        halo_points = received[: lv.width_e, :]
+        halo_float = halo_points.astype(jnp.float32)
+        halo_norms = -DISTANCE_SCALE * jnp.sum(halo_float * halo_float, axis=0, keepdims=True)
+        weights = lv.block(j, halo_points, halo_norms)
+        near[j] = near[j] + lv.weight(j, offset) * nt_dot(received[lv.width_e :, :], weights)
     for q in range(lv.count):
         far0 = nn_dot(scaled0[q ^ 1], basis0[:, q * LEAF : (q + 1) * LEAF])
         out_ref[:, q * LEAF : (q + 1) * LEAF] = (
@@ -142,16 +153,14 @@
     round_one = refs[8 : 8 + sub_masks - 1]
     round_two = refs[8 + sub_masks - 1 : 8 + sub_masks - 1 + leaf_masks]
     out_ref = refs[8 + sub_masks - 1 + leaf_masks]
-    lv = Leaves(emb_ref, dirs_ref, neighbours_ref, counts_ref, sub_size)
     rank = basis_ref.shape[1]
-    nrhs = dirs_ref.shape[0]
-    local_points = lv.local_points
+    nrhs, local_points = local_ref.shape
+    width_e = emb_ref.shape[0]
     levels = sub_bits + leaf_bits
     lower_width = rank * sub_bits
 
-    pair, cross = pair_ref[...], cross_ref[...]
     step = nrhs * rank * levels // LEAF
-    from_pair = unpack_parts(pair, lv.width_e + nrhs, step, rank * levels)
+    from_pair = unpack_parts(pair_ref[...], width_e + nrhs, step, rank * levels)
     column_level = lax.broadcasted_iota(jnp.int32, (1, rank * levels), 1) // rank
     lower_level = column_level[:, :lower_width]
     upper_level = column_level[:, : rank * leaf_bits]
@@ -170,22 +179,7 @@
     stacked = basis_ref[loc_bits : loc_bits + levels].reshape(levels * rank, local_points)
     far = nn_dot(scaled, stacked)
 
-    even = lax.axis_index("sub") % 2 == 0
-    halo_pair = pair[: lv.width_e + nrhs]
-    left, right = jnp.where(even, cross, halo_pair), jnp.where(even, halo_pair, cross)
-    halo = {}
-    for j, received, offset in ((0, left, -1), (lv.count - 1, right, 1)):
-        halo_points = received[: lv.width_e, :]
-        halo_float = halo_points.astype(jnp.float32)
-        halo_norms = -DISTANCE_SCALE * jnp.sum(halo_float * halo_float, axis=0, keepdims=True)
-        weights = lv.block(j, halo_points, halo_norms)
-        term = lv.weight(j, offset) * nt_dot(received[lv.width_e :, :], weights)
-        halo[j] = term if j not in halo else halo[j] + term
-    for j in range(lv.count):
-        total = local_ref[:, j * LEAF : (j + 1) * LEAF] + far[:, j * LEAF : (j + 1) * LEAF]
-        if j in halo:
-            total = total + halo[j]
-        out_ref[:, j * LEAF : (j + 1) * LEAF] = total
+    out_ref[...] = local_ref[...] + far
 
 
 def on_device(embeddings, directions, level_basis, neighbours, counts):
@@ -226,9 +220,9 @@
     local = pl.pallas_call(
         functools.partial(local_kernel, sub_size),
         out_shape=out,
-        in_specs=[VMEM, VMEM, VMEM, SMEM, SMEM],
+        in_specs=[VMEM] * 5 + [SMEM, SMEM],
         out_specs=VMEM,
-    )(*in_vmem(embeddings, directions, level_basis), neighbours, counts)
+    )(*in_vmem(embeddings, directions, level_basis, from_pair, from_cross), neighbours, counts)
 
     remote = round_one + round_two
     return pl.pallas_call(

time: 21.8 us -> 23.1 us (1.060)
  the two profiles are of different devices: /device:TPU:0 before, /device:TPU:12 now
where the time goes in v20:
time: 23.1 us; the launch traced here: 23 us
  starting transfers between devices  9.78 us (42%)
  waiting for transfers between devices  6.3 us (27%)
  Pallas kernels  6.08 us (26%)
  local copies, waits for them, and re-layouts  0.68 us (3%)
    ppermute x5, starting transfers between devices, from_mask(): return lax.ppermute(x, axis, pairs)  5.86 us
    ppermute x1, waiting for transfers between devices, on_device(): lax.ppermute(cross, axes, [(i, i - 1 + 2 * (i % 2)) for i in range(1, nde...  4.5 us
    ppermute x1, starting transfers between devices, on_device(): lax.ppermute(cross, axes, [(i, i - 1 + 2 * (i % 2)) for i in range(1, nde...  3.47 us
    pallas_call x1, Pallas kernels, on_device(): pl.pallas_call(functools.partial(local_kernel, sub_size), out_shape=out,...  2.93 us
    pallas_call x1, Pallas kernels, on_device(): pl.pallas_call(functools.partial(send_kernel, loc_bits), out_shape=(pair_...  2.26 us
    ppermute x5, waiting for transfers between devices, from_mask(): return lax.ppermute(x, axis, pairs)  1.76 us
    pallas_call x1, Pallas kernels, on_device(): pl.pallas_call(functools.partial(final_kernel, sub_size, sub_bits, leaf_b...  0.89 us
    unnamed x9, local copies, waits for them, and re-layouts  0.68 us
  transfers between devices with their start and end apart: 7, of which 2 were waited for; matrix products, arithmetic and copies ran while one was open for 0% of the time, Pallas kernels for 13%

profile of v20, /device:TPU:12, one launch (start us, length us, event | category | flops | bytes accessed | tf_op | source)
XLA Modules:
  0.0 23.0 jit_solution(2548857658698956437)
XLA Ops:
  0.0 0.0 copy-start
  0.0 2.3 %shard_map.55 = (bf16[208,512]{1,0:T(8,128)(2,1)}, bf16[160,512]{1,0:T(8,128)(2,1)}, f32[32,256]{1,0:T(8,128)}) custom-call(bf16[128,1024]{1,0:T(8,128)(2,1)} %refs_0_.1, f32[32,1024]{1,0:T(8,128)} %refs_1_.1, bf16[5,64,1024]{2,1,0:T(8,128)(2,1)} %refs_5_.1), custom_call_target="tpu_custom_call" | custom-call | tf_op jit(solution)/shard_map/pallas_call | solution.py:202
  2.3 0.0 copy-start.1
  2.3 0.4 %collective-permute-start = (bf16[208,512]{1,0:T(8,128)(2,1)}, bf16[208,512]{1,0:T(8,128)(2,1)S(1)}, u32[]{:S(2)}, u32[]{:S(2)}) collective-permute-start(bf16[208,512]{1,0:T(8,128)(2,1)} %get-tuple-element.8), channel_id=1, source_target_pairs={{0,1},{1,0},{2,3},{3,2},{4,5},{5,4},{6,7},{7,6},{8,9},{9,8},{10,11... | collective-permute-start | bytes 638984 | tf_op jit(solution)/shard_map/ppermute | solution.py:210
  2.7 2.7 %collective-permute-start.3 = (f32[32,256]{1,0:T(8,128)}, f32[32,256]{1,0:T(8,128)S(1)}, u32[]{:S(2)}, u32[]{:S(2)}) collective-permute-start(f32[32,256]{1,0:T(8,128)} %get-tuple-element.10), channel_id=1, source_target_pairs={{0,3},{1,2},{2,1},{3,0},{4,7},{5,6},{6,5},{7,4},{8,11},{9,10},{10,... | collective-permute-start | bytes 98312 | tf_op jit(solution)/shard_map/ppermute | solution.py:24
  5.4 1.2 %collective-permute-start.2 = (f32[32,256]{1,0:T(8,128)}, f32[32,256]{1,0:T(8,128)S(1)}, u32[]{:S(2)}, u32[]{:S(2)}) collective-permute-start(f32[32,256]{1,0:T(8,128)} %get-tuple-element.10), channel_id=1, source_target_pairs={{0,2},{1,3},{2,0},{3,1},{4,6},{5,7},{6,4},{7,5},{8,10},{9,11},{10,... | collective-permute-start | bytes 98312 | tf_op jit(solution)/shard_map/ppermute | solution.py:24
  6.7 3.5 %collective-permute-start.1 = (bf16[160,512]{1,0:T(8,128)(2,1)}, bf16[160,512]{1,0:T(8,128)(2,1)S(1)}, u32[]{:S(2)}, u32[]{:S(2)}) collective-permute-start(bf16[160,512]{1,0:T(8,128)(2,1)} %get-tuple-element.9), channel_id=1, source_target_pairs={{1,2},{2,1},{3,4},{4,3},{5,6},{6,5},{7,8},{8,7},{9,10},{10,9},{11,... | collective-permute-start | bytes 491528 | tf_op jit(solution)/shard_map/ppermute | solution.py:212
  10.1 0.0 collective-permute-done.pair_ref.refs_3_
  10.2 0.0 copy-start.3
  10.2 0.0 copy-start.2
  10.2 0.0 collective-permute-done.3.refs_9_
  10.2 1.8 %collective-permute-done.2.refs_8_ = f32[32,256]{1,0:T(8,128)S(1)} collective-permute-done((f32[32,256]{1,0:T(8,128)}, f32[32,256]{1,0:T(8,128)S(1)}, u32[]{:S(2)}, u32[]{:S(2)}) %collective-permute-start.2) | collective-permute-done | bytes 32800 | tf_op jit(solution)/shard_map/ppermute | solution.py:24
  12.0 0.0 copy-done.3
  12.0 0.1 collective-permute-start.6
  12.1 1.6 %collective-permute-start.5 = (f32[32,128]{1,0:T(8,128)S(1)}, f32[32,128]{1,0:T(8,128)S(1)}, u32[]{:S(2)}, u32[]{:S(2)}) collective-permute-start(f32[32,128]{1,0:T(8,128)S(1)} %slice_add_fusion.2), channel_id=1, source_target_pairs={{0,8},{4,12},{8,0},{12,4},{1,9},{5,13},{9,1},{13,5},{2,10},{6,14},... | collective-permute-start | bytes 49160 | tf_op jit(solution)/shard_map/ppermute | solution.py:24
  13.6 0.3 %collective-permute-start.4 = (f32[32,128]{1,0:T(8,128)S(1)}, f32[32,128]{1,0:T(8,128)S(1)}, u32[]{:S(2)}, u32[]{:S(2)}) collective-permute-start(f32[32,128]{1,0:T(8,128)S(1)} %slice_add_fusion.2), channel_id=1, source_target_pairs={{0,4},{4,0},{8,12},{12,8},{1,5},{5,1},{9,13},{13,9},{2,6},{6,2},{1... | collective-permute-start | bytes 49160 | tf_op jit(solution)/shard_map/ppermute | solution.py:24
  13.9 4.5 %collective-permute-done.1.cross_ref.refs_4_ = bf16[160,512]{1,0:T(8,128)(2,1)S(1)} collective-permute-done((bf16[160,512]{1,0:T(8,128)(2,1)}, bf16[160,512]{1,0:T(8,128)(2,1)S(1)}, u32[]{:S(2)}, u32[]{:S(2)}) %collective-permute-start.1) | collective-permute-done | bytes 163872 | tf_op jit(solution)/shard_map/ppermute | solution.py:212
  18.4 0.0 copy-done
  18.4 0.0 copy-done.1
  18.4 0.0 copy-done.2
  18.4 2.9 %shard_map.56.refs_2_ = f32[32,1024]{1,0:T(8,128)S(1)} custom-call(bf16[128,1024]{1,0:T(8,128)(2,1)S(1)} %copy-done.1, f32[32,1024]{1,0:T(8,128)S(1)} %copy-done.2, bf16[5,64,1024]{2,1,0:T(8,128)(2,1)S(1)} %copy-done, bf16[208,512]{1,0:T(8,128)(2,1)S(1)} %collective-permute-done.pair_ref.refs_3_, ...), custom_call_target="tpu_custom_call" | custom-call | tf_op jit(solution)/shard_map/pallas_call | solution.py:220
  21.4 0.0 collective-permute-done.6.refs_12_
  21.4 0.0 collective-permute-done.5.refs_11_
  21.4 0.0 collective-permute-done.4.refs_10_
  21.4 0.9 %shard_map.57 = f32[32,1024]{1,0:T(8,128)S(1)} custom-call(bf16[128,1024]{1,0:T(8,128)(2,1)S(1)} %copy-done.1, f32[32,1024]{1,0:T(8,128)S(1)} %copy-done.2, f32[32,1024]{1,0:T(8,128)S(1)} %shard_map.56.refs_2_, bf16[208,512]{1,0:T(8,128)(2,1)S(1)} %collective-permute-done.pair_ref.refs_3_, ...), custom_call_target="tpu_custom_call", output_to_operand_aliasing={{}: (2, {})} | custom-call | tf_op jit(solution)/shard_map/pallas_call | solution.py:228
  22.3 0.7 %copy.8 = f32[32,1024]{1,0:T(8,128)} copy(f32[32,1024]{1,0:T(8,128)S(1)} %shard_map.57) | data formatting | bytes 262144
  (4 shorter events, 0.0 us)
Async XLA Ops:
  0.0 18.4 %copy-start = (bf16[5,64,1024]{2,1,0:T(8,128)(2,1)S(1)}, bf16[5,64,1024]{2,1,0:T(8,128)(2,1)}, u32[]{:S(2)}) copy-start(bf16[5,64,1024]{2,1,0:T(8,128)(2,1)} %refs_5_.1) | copy-start | bytes 1966084
  2.3 16.2 %copy-start.1 = (bf16[128,1024]{1,0:T(8,128)(2,1)S(1)}, bf16[128,1024]{1,0:T(8,128)(2,1)}, u32[]{:S(2)}) copy-start(bf16[128,1024]{1,0:T(8,128)(2,1)} %refs_0_.1) | copy-start | bytes 786436
  2.3 7.9 %collective-permute-start = (bf16[208,512]{1,0:T(8,128)(2,1)}, bf16[208,512]{1,0:T(8,128)(2,1)S(1)}, u32[]{:S(2)}, u32[]{:S(2)}) collective-permute-start(bf16[208,512]{1,0:T(8,128)(2,1)} %get-tuple-element.8), channel_id=1, source_target_pairs={{0,1},{1,0},{2,3},{3,2},{4,5},{5,4},{6,7},{7,6},{8,9},{9,8},{10,11... | collective-permute-start | bytes 638984 | tf_op jit(solution)/shard_map/ppermute | solution.py:210
  2.7 7.5 %collective-permute-start.3 = (f32[32,256]{1,0:T(8,128)}, f32[32,256]{1,0:T(8,128)S(1)}, u32[]{:S(2)}, u32[]{:S(2)}) collective-permute-start(f32[32,256]{1,0:T(8,128)} %get-tuple-element.10), channel_id=1, source_target_pairs={{0,3},{1,2},{2,1},{3,0},{4,7},{5,6},{6,5},{7,4},{8,11},{9,10},{10,... | collective-permute-start | bytes 98312 | tf_op jit(solution)/shard_map/ppermute | solution.py:24
  5.4 6.6 %collective-permute-start.2 = (f32[32,256]{1,0:T(8,128)}, f32[32,256]{1,0:T(8,128)S(1)}, u32[]{:S(2)}, u32[]{:S(2)}) collective-permute-start(f32[32,256]{1,0:T(8,128)} %get-tuple-element.10), channel_id=1, source_target_pairs={{0,2},{1,3},{2,0},{3,1},{4,6},{5,7},{6,4},{7,5},{8,10},{9,11},{10,... | collective-permute-start | bytes 98312 | tf_op jit(solution)/shard_map/ppermute | solution.py:24
  6.7 11.8 %collective-permute-start.1 = (bf16[160,512]{1,0:T(8,128)(2,1)}, bf16[160,512]{1,0:T(8,128)(2,1)S(1)}, u32[]{:S(2)}, u32[]{:S(2)}) collective-permute-start(bf16[160,512]{1,0:T(8,128)(2,1)} %get-tuple-element.9), channel_id=1, source_target_pairs={{1,2},{2,1},{3,4},{4,3},{5,6},{6,5},{7,8},{8,7},{9,10},{10,9},{11,... | collective-permute-start | bytes 491528 | tf_op jit(solution)/shard_map/ppermute | solution.py:212
  10.2 1.8 %copy-start.3 = (f32[32,256]{1,0:T(8,128)S(1)}, f32[32,256]{1,0:T(8,128)}, u32[]{:S(2)}) copy-start(f32[32,256]{1,0:T(8,128)} %get-tuple-element.10) | copy-start | bytes 98308
  10.2 8.3 %copy-start.2 = (f32[32,1024]{1,0:T(8,128)S(1)}, f32[32,1024]{1,0:T(8,128)}, u32[]{:S(2)}) copy-start(f32[32,1024]{1,0:T(8,128)} %refs_1_.1) | copy-start | bytes 393220
  12.0 9.4 %collective-permute-start.6 = (f32[32,128]{1,0:T(8,128)S(1)}, f32[32,128]{1,0:T(8,128)S(1)}, u32[]{:S(2)}, u32[]{:S(2)}) collective-permute-start(f32[32,128]{1,0:T(8,128)S(1)} %slice_add_fusion.2), channel_id=1, source_target_pairs={{0,12},{4,8},{8,4},{12,0},{1,13},{5,9},{9,5},{13,1},{2,14},{6,10},... | collective-permute-start | bytes 49160 | tf_op jit(solution)/shard_map/ppermute | solution.py:24
  12.1 9.3 %collective-permute-start.5 = (f32[32,128]{1,0:T(8,128)S(1)}, f32[32,128]{1,0:T(8,128)S(1)}, u32[]{:S(2)}, u32[]{:S(2)}) collective-permute-start(f32[32,128]{1,0:T(8,128)S(1)} %slice_add_fusion.2), channel_id=1, source_target_pairs={{0,8},{4,12},{8,0},{12,4},{1,9},{5,13},{9,1},{13,5},{2,10},{6,14},... | collective-permute-start | bytes 49160 | tf_op jit(solution)/shard_map/ppermute | solution.py:24
  13.6 7.8 %collective-permute-start.4 = (f32[32,128]{1,0:T(8,128)S(1)}, f32[32,128]{1,0:T(8,128)S(1)}, u32[]{:S(2)}, u32[]{:S(2)}) collective-permute-start(f32[32,128]{1,0:T(8,128)S(1)} %slice_add_fusion.2), channel_id=1, source_target_pairs={{0,4},{4,0},{8,12},{12,8},{1,5},{5,1},{9,13},{13,9},{2,6},{6,2},{1... | collective-permute-start | bytes 49160 | tf_op jit(solution)/shard_map/ppermute | solution.py:24

commit v21 on v17

--- a/solution.py
+++ b/solution.py
@@ -228,6 +228,7 @@
         out_shape=out,
         in_specs=[VMEM, VMEM, VMEM, SMEM, SMEM],
         out_specs=VMEM,
+        input_output_aliases={1: 0},
     )(*in_vmem(embeddings, directions, level_basis), neighbours, counts)
 
     remote = round_one + round_two
@@ -237,7 +238,7 @@
         in_specs=[VMEM] * 6 + [SMEM, SMEM] + [VMEM] * len(remote),
         out_specs=VMEM,
     )(
-        *in_vmem(embeddings, directions, local, from_pair, from_cross, level_basis),
+        *in_vmem(embeddings, local, local, from_pair, from_cross, level_basis),
         neighbours,
         counts,
         *in_vmem(*remote),

time: 22.9 us -> 23.4 us (1.022)
  local copies, waits for them, and re-layouts: 0.92 us -> 1.59 us
  Pallas kernels: 7.64 us -> 6.98 us
  waiting for transfers between devices: 5.85 us -> 6.28 us
    unnamed x10 -> x9, local copies, waits for them, and re-layouts: 0.92 us -> 1.58 us
    pallas_call x1, Pallas kernels: 3.02 us -> 2.37 us  [on_device(): pl.pallas_call(functools.partial(local_kernel, sub_size), out_shape=out,...]
    ppermute x5, waiting for transfers between devices: 2.94 us -> 3.38 us  [from_mask(): return lax.ppermute(x, axis, pairs)]
  transfers between devices with their start and end apart: 7 -> 7, of which waited for: 2 -> 3; matrix products, arithmetic and copies ran while one was open for 0% -> 0% of each run, Pallas kernels for 13% -> 10%
where the time goes in v21:
time: 23.4 us; the launch traced here: 23.2 us
  starting transfers between devices  8.21 us (35%)
  Pallas kernels  6.98 us (30%)
  waiting for transfers between devices  6.28 us (27%)
  local copies, waits for them, and re-layouts  1.59 us (7%)
    ppermute x5, starting transfers between devices, from_mask(): return lax.ppermute(x, axis, pairs)  4.52 us
    ppermute x5, waiting for transfers between devices, from_mask(): return lax.ppermute(x, axis, pairs)  3.38 us
    ppermute x1, starting transfers between devices, on_device(): from_pair = lax.ppermute(pair, axes, [(i, i ^ 1) for i in range(ndev)])  3.02 us
    ppermute x1, waiting for transfers between devices, on_device(): from_pair = lax.ppermute(pair, axes, [(i, i ^ 1) for i in range(ndev)])  2.9 us
    pallas_call x1, Pallas kernels, on_device(): pl.pallas_call(functools.partial(local_kernel, sub_size), out_shape=out,...  2.37 us
    pallas_call x1, Pallas kernels, on_device(): pl.pallas_call(functools.partial(final_kernel, sub_size, sub_bits, leaf_b...  2.35 us
    pallas_call x1, Pallas kernels, on_device(): pl.pallas_call(functools.partial(send_kernel, loc_bits), out_shape=(pair_...  2.26 us
    unnamed x9, local copies, waits for them, and re-layouts  1.58 us
  transfers between devices with their start and end apart: 7, of which 3 were waited for; matrix products, arithmetic and copies ran while one was open for 0% of the time, Pallas kernels for 10%

profile of v21, /device:TPU:0, one launch (start us, length us, event | category | flops | bytes accessed | tf_op | source)
XLA Modules:
  0.0 23.2 jit_solution(5120140200714395241)
XLA Ops:
  0.0 1.6 %copy.9.dirs_ref = f32[32,1024]{1,0:T(8,128)} copy(f32[32,1024]{1,0:T(8,128)} %param.6) | data formatting | bytes 262144
  1.6 0.0 copy-start
  1.6 2.3 %shard_map.56 = (bf16[208,512]{1,0:T(8,128)(2,1)}, bf16[160,512]{1,0:T(8,128)(2,1)}, f32[32,256]{1,0:T(8,128)}) custom-call(bf16[128,1024]{1,0:T(8,128)(2,1)} %refs_0_.1, f32[32,1024]{1,0:T(8,128)} %copy.9.dirs_ref, bf16[5,64,1024]{2,1,0:T(8,128)(2,1)} %refs_5_.1), custom_call_target="tpu_custom_call" | custom-call | tf_op jit(solution)/shard_map/pallas_call | solution.py:208
  3.8 0.0 copy-start.2
  3.8 3.0 %collective-permute-start = (bf16[208,512]{1,0:T(8,128)(2,1)}, bf16[208,512]{1,0:T(8,128)(2,1)S(1)}, u32[]{:S(2)}, u32[]{:S(2)}) collective-permute-start(bf16[208,512]{1,0:T(8,128)(2,1)} %get-tuple-element.8), channel_id=1, source_target_pairs={{0,1},{1,0},{2,3},{3,2},{4,5},{5,4},{6,7},{7,6},{8,9},{9,8},{10,11... | collective-permute-start | bytes 638984 | tf_op jit(solution)/shard_map/ppermute | solution.py:216
  6.9 2.6 %collective-permute-start.2 = (f32[32,256]{1,0:T(8,128)}, f32[32,256]{1,0:T(8,128)S(1)}, u32[]{:S(2)}, u32[]{:S(2)}) collective-permute-start(f32[32,256]{1,0:T(8,128)} %get-tuple-element.10), channel_id=1, source_target_pairs={{0,2},{1,3},{2,0},{3,1},{4,6},{5,7},{6,4},{7,5},{8,10},{9,11},{10,... | collective-permute-start | bytes 98312 | tf_op jit(solution)/shard_map/ppermute | solution.py:24
  9.4 0.0 collective-permute-start.3
  9.4 0.7 %collective-permute-start.1 = (bf16[160,512]{1,0:T(8,128)(2,1)}, bf16[160,512]{1,0:T(8,128)(2,1)S(1)}, u32[]{:S(2)}, u32[]{:S(2)}) collective-permute-start(bf16[160,512]{1,0:T(8,128)(2,1)} %get-tuple-element.9), channel_id=1, source_target_pairs={{1,2},{2,1},{3,4},{4,3},{5,6},{6,5},{7,8},{8,7},{9,10},{10,9},{11,... | collective-permute-start | bytes 491528 | tf_op jit(solution)/shard_map/ppermute | solution.py:218
  10.1 2.9 %collective-permute-done.refs_3_ = bf16[208,512]{1,0:T(8,128)(2,1)S(1)} collective-permute-done((bf16[208,512]{1,0:T(8,128)(2,1)}, bf16[208,512]{1,0:T(8,128)(2,1)S(1)}, u32[]{:S(2)}, u32[]{:S(2)}) %collective-permute-start) | collective-permute-done | bytes 213024 | tf_op jit(solution)/shard_map/ppermute | solution.py:216
  13.0 0.0 copy-start.3
  13.0 0.0 copy-start.1
  13.1 0.0 collective-permute-done.2.refs_8_
  13.1 2.9 %collective-permute-done.3.refs_9_ = f32[32,256]{1,0:T(8,128)S(1)} collective-permute-done((f32[32,256]{1,0:T(8,128)}, f32[32,256]{1,0:T(8,128)S(1)}, u32[]{:S(2)}, u32[]{:S(2)}) %collective-permute-start.3) | collective-permute-done | bytes 32800 | tf_op jit(solution)/shard_map/ppermute | solution.py:24
  16.0 0.0 copy-done.3
  16.0 0.1 collective-permute-start.4
  16.1 1.6 %collective-permute-start.5 = (f32[32,128]{1,0:T(8,128)S(1)}, f32[32,128]{1,0:T(8,128)S(1)}, u32[]{:S(2)}, u32[]{:S(2)}) collective-permute-start(f32[32,128]{1,0:T(8,128)S(1)} %slice_add_fusion.2), channel_id=1, source_target_pairs={{0,8},{4,12},{8,0},{12,4},{1,9},{5,13},{9,1},{13,5},{2,10},{6,14},... | collective-permute-start | bytes 49160 | tf_op jit(solution)/shard_map/ppermute | solution.py:24
  17.7 0.3 %collective-permute-start.6 = (f32[32,128]{1,0:T(8,128)S(1)}, f32[32,128]{1,0:T(8,128)S(1)}, u32[]{:S(2)}, u32[]{:S(2)}) collective-permute-start(f32[32,128]{1,0:T(8,128)S(1)} %slice_add_fusion.2), channel_id=1, source_target_pairs={{0,12},{4,8},{8,4},{12,0},{1,13},{5,9},{9,5},{13,1},{2,14},{6,10},... | collective-permute-start | bytes 49160 | tf_op jit(solution)/shard_map/ppermute | solution.py:24
  18.0 0.0 copy-done
  18.0 0.0 copy-done.2
  18.0 0.0 copy-done.1
  18.0 2.4 %shard_map.55.refs_1_.refs_2_ = f32[32,1024]{1,0:T(8,128)S(1)} custom-call(bf16[128,1024]{1,0:T(8,128)(2,1)S(1)} %copy-done.2, f32[32,1024]{1,0:T(8,128)S(1)} %copy-done.1, bf16[5,64,1024]{2,1,0:T(8,128)(2,1)S(1)} %copy-done, s32[2,8]{1,0:T(2,128)} %refs_6_.1, s32[2]{0:T(128)} %refs_7_.1), custom_call_target="tpu_custom_call", output_to_operand_aliasing={{}: (1, {})} | custom-call | tf_op jit(solution)/shard_map/pallas_call | solution.py:226
  20.4 0.0 collective-permute-done.1.refs_4_
  20.4 0.0 collective-permute-done.4.refs_10_
  20.4 0.0 collective-permute-done.5.refs_11_
  20.4 0.4 %collective-permute-done.6.refs_12_ = f32[32,128]{1,0:T(8,128)S(1)} collective-permute-done((f32[32,128]{1,0:T(8,128)S(1)}, f32[32,128]{1,0:T(8,128)S(1)}, u32[]{:S(2)}, u32[]{:S(2)}) %collective-permute-start.6) | collective-permute-done | bytes 16416 | tf_op jit(solution)/shard_map/ppermute | solution.py:24
  20.8 2.4 %shard_map.57 = f32[32,1024]{1,0:T(8,128)} custom-call(bf16[128,1024]{1,0:T(8,128)(2,1)S(1)} %copy-done.2, f32[32,1024]{1,0:T(8,128)S(1)} %shard_map.55.refs_1_.refs_2_, f32[32,1024]{1,0:T(8,128)S(1)} %shard_map.55.refs_1_.refs_2_, bf16[208,512]{1,0:T(8,128)(2,1)S(1)} %collective-permute-done.refs_3_, bf16[160,512]{1,0:T(8,128)(2,1)S(1)} %collective-permute-done.1.refs_4_, ...), custom_call_target="tpu_custom_call" | custom-call | tf_op jit(solution)/shard_map/pallas_call | solution.py:235
  (4 shorter events, 0.0 us)
Async XLA Ops:
  1.6 16.4 %copy-start = (bf16[5,64,1024]{2,1,0:T(8,128)(2,1)S(1)}, bf16[5,64,1024]{2,1,0:T(8,128)(2,1)}, u32[]{:S(2)}) copy-start(bf16[5,64,1024]{2,1,0:T(8,128)(2,1)} %refs_5_.1) | copy-start | bytes 1966084
  3.8 14.1 %copy-start.2 = (bf16[128,1024]{1,0:T(8,128)(2,1)S(1)}, bf16[128,1024]{1,0:T(8,128)(2,1)}, u32[]{:S(2)}) copy-start(bf16[128,1024]{1,0:T(8,128)(2,1)} %refs_0_.1) | copy-start | bytes 786436
  3.8 9.2 %collective-permute-start = (bf16[208,512]{1,0:T(8,128)(2,1)}, bf16[208,512]{1,0:T(8,128)(2,1)S(1)}, u32[]{:S(2)}, u32[]{:S(2)}) collective-permute-start(bf16[208,512]{1,0:T(8,128)(2,1)} %get-tuple-element.8), channel_id=1, source_target_pairs={{0,1},{1,0},{2,3},{3,2},{4,5},{5,4},{6,7},{7,6},{8,9},{9,8},{10,11... | collective-permute-start | bytes 638984 | tf_op jit(solution)/shard_map/ppermute | solution.py:216
  6.9 6.2 %collective-permute-start.2 = (f32[32,256]{1,0:T(8,128)}, f32[32,256]{1,0:T(8,128)S(1)}, u32[]{:S(2)}, u32[]{:S(2)}) collective-permute-start(f32[32,256]{1,0:T(8,128)} %get-tuple-element.10), channel_id=1, source_target_pairs={{0,2},{1,3},{2,0},{3,1},{4,6},{5,7},{6,4},{7,5},{8,10},{9,11},{10,... | collective-permute-start | bytes 98312 | tf_op jit(solution)/shard_map/ppermute | solution.py:24
  9.4 6.6 %collective-permute-start.3 = (f32[32,256]{1,0:T(8,128)}, f32[32,256]{1,0:T(8,128)S(1)}, u32[]{:S(2)}, u32[]{:S(2)}) collective-permute-start(f32[32,256]{1,0:T(8,128)} %get-tuple-element.10), channel_id=1, source_target_pairs={{0,3},{1,2},{2,1},{3,0},{4,7},{5,6},{6,5},{7,4},{8,11},{9,10},{10,... | collective-permute-start | bytes 98312 | tf_op jit(solution)/shard_map/ppermute | solution.py:24
  9.4 10.9 %collective-permute-start.1 = (bf16[160,512]{1,0:T(8,128)(2,1)}, bf16[160,512]{1,0:T(8,128)(2,1)S(1)}, u32[]{:S(2)}, u32[]{:S(2)}) collective-permute-start(bf16[160,512]{1,0:T(8,128)(2,1)} %get-tuple-element.9), channel_id=1, source_target_pairs={{1,2},{2,1},{3,4},{4,3},{5,6},{6,5},{7,8},{8,7},{9,10},{10,9},{11,... | collective-permute-start | bytes 491528 | tf_op jit(solution)/shard_map/ppermute | solution.py:218
  13.0 3.0 %copy-start.3 = (f32[32,256]{1,0:T(8,128)S(1)}, f32[32,256]{1,0:T(8,128)}, u32[]{:S(2)}) copy-start(f32[32,256]{1,0:T(8,128)} %get-tuple-element.10) | copy-start | bytes 98308
  13.0 4.9 %copy-start.1 = (f32[32,1024]{1,0:T(8,128)S(1)}, f32[32,1024]{1,0:T(8,128)}, u32[]{:S(2)}) copy-start(f32[32,1024]{1,0:T(8,128)} %copy.9.dirs_ref) | copy-start | bytes 393220
  16.0 4.3 %collective-permute-start.4 = (f32[32,128]{1,0:T(8,128)S(1)}, f32[32,128]{1,0:T(8,128)S(1)}, u32[]{:S(2)}, u32[]{:S(2)}) collective-permute-start(f32[32,128]{1,0:T(8,128)S(1)} %slice_add_fusion.2), channel_id=1, source_target_pairs={{0,4},{4,0},{8,12},{12,8},{1,5},{5,1},{9,13},{13,9},{2,6},{6,2},{1... | collective-permute-start | bytes 49160 | tf_op jit(solution)/shard_map/ppermute | solution.py:24
  16.1 4.3 %collective-permute-start.5 = (f32[32,128]{1,0:T(8,128)S(1)}, f32[32,128]{1,0:T(8,128)S(1)}, u32[]{:S(2)}, u32[]{:S(2)}) collective-permute-start(f32[32,128]{1,0:T(8,128)S(1)} %slice_add_fusion.2), channel_id=1, source_target_pairs={{0,8},{4,12},{8,0},{12,4},{1,9},{5,13},{9,1},{13,5},{2,10},{6,14},... | collective-permute-start | bytes 49160 | tf_op jit(solution)/shard_map/ppermute | solution.py:24
  17.7 3.2 %collective-permute-start.6 = (f32[32,128]{1,0:T(8,128)S(1)}, f32[32,128]{1,0:T(8,128)S(1)}, u32[]{:S(2)}, u32[]{:S(2)}) collective-permute-start(f32[32,128]{1,0:T(8,128)S(1)} %slice_add_fusion.2), channel_id=1, source_target_pairs={{0,12},{4,8},{8,4},{12,0},{1,13},{5,9},{9,5},{13,1},{2,14},{6,10},... | collective-permute-start | bytes 49160 | tf_op jit(solution)/shard_map/ppermute | solution.py:24

commit v22 on v17

--- a/solution.py
+++ b/solution.py
@@ -114,7 +114,7 @@
         return total.astype(jnp.float32)
 
 
-def local_kernel(sub_size, emb_ref, dirs_ref, basis_ref, neighbours_ref, counts_ref, out_ref):
+def local_kernel(sub_size, emb_ref, dirs_ref, basis_ref, neighbours_ref, counts_ref, place_ref, out_ref):
     lv = Leaves(emb_ref, dirs_ref, neighbours_ref, counts_ref, sub_size)
     rank = basis_ref.shape[1]
     near = [nt_dot(lv.leaf_values[j], lv.block(j, lv.points[j], lv.norms[j])) for j in range(lv.count)]
@@ -226,9 +226,10 @@
     local = pl.pallas_call(
         functools.partial(local_kernel, sub_size),
         out_shape=out,
-        in_specs=[VMEM, VMEM, VMEM, SMEM, SMEM],
+        in_specs=[VMEM, VMEM, VMEM, SMEM, SMEM, VMEM],
         out_specs=VMEM,
-    )(*in_vmem(embeddings, directions, level_basis), neighbours, counts)
+        input_output_aliases={5: 0},
+    )(*in_vmem(embeddings, directions, level_basis), neighbours, counts, *in_vmem(jnp.zeros(out.shape, out.dtype)))
 
     remote = round_one + round_two
     return pl.pallas_call(

time: 22.9 us -> 21.9 us (0.956)
  local copies, waits for them, and re-layouts: 0.92 us -> 0.03 us
  Pallas kernels: 7.64 us -> 6.98 us
  waiting for transfers between devices: 5.85 us -> 6.2 us
    unnamed x10 -> x8, local copies, waits for them, and re-layouts: 0.92 us -> 0.02 us
    pallas_call x1, Pallas kernels: 3.02 us -> 2.37 us  [on_device(): pl.pallas_call(functools.partial(local_kernel, sub_size), out_shape=out,...]
    ppermute x5, waiting for transfers between devices: 2.94 us -> 3.43 us  [from_mask(): return lax.ppermute(x, axis, pairs)]
  transfers between devices with their start and end apart: 7 -> 7, of which waited for: 2 -> 3; matrix products, arithmetic and copies ran while one was open for 0% -> 0% of each run, Pallas kernels for 13% -> 11%
where the time goes in v22:
time: 21.9 us; the launch traced here: 21.7 us
  starting transfers between devices  8.33 us (38%)
  Pallas kernels  6.98 us (32%)
  waiting for transfers between devices  6.2 us (28%)
    ppermute x5, starting transfers between devices, from_mask(): return lax.ppermute(x, axis, pairs)  4.52 us
    ppermute x5, waiting for transfers between devices, from_mask(): return lax.ppermute(x, axis, pairs)  3.43 us
    ppermute x1, starting transfers between devices, on_device(): from_pair = lax.ppermute(pair, axes, [(i, i ^ 1) for i in range(ndev)])  3.02 us
    ppermute x1, waiting for transfers between devices, on_device(): from_pair = lax.ppermute(pair, axes, [(i, i ^ 1) for i in range(ndev)])  2.77 us
    pallas_call x1, Pallas kernels, on_device(): pl.pallas_call(functools.partial(local_kernel, sub_size), out_shape=out,...  2.37 us
    pallas_call x1, Pallas kernels, on_device(): pl.pallas_call(functools.partial(final_kernel, sub_size, sub_bits, leaf_b...  2.35 us
    pallas_call x1, Pallas kernels, on_device(): pl.pallas_call(functools.partial(send_kernel, loc_bits), out_shape=(pair_...  2.26 us
    ppermute x1, starting transfers between devices, on_device(): lax.ppermute(cross, axes, [(i, i - 1 + 2 * (i % 2)) for i in range(1, nde...  0.79 us
  transfers between devices with their start and end apart: 7, of which 3 were waited for; matrix products, arithmetic and copies ran while one was open for 0% of the time, Pallas kernels for 11%

profile of v22, /device:TPU:0, one launch (start us, length us, event | category | flops | bytes accessed | tf_op | source)
XLA Modules:
  0.0 21.7 jit_solution(4794751957569921417)
XLA Ops:
  0.0 0.0 copy-start
  0.0 2.3 %shard_map.56 = (bf16[208,512]{1,0:T(8,128)(2,1)}, bf16[160,512]{1,0:T(8,128)(2,1)}, f32[32,256]{1,0:T(8,128)}) custom-call(bf16[128,1024]{1,0:T(8,128)(2,1)} %refs_0_.1, f32[32,1024]{1,0:T(8,128)} %refs_1_.1, bf16[5,64,1024]{2,1,0:T(8,128)(2,1)} %refs_5_.1), custom_call_target="tpu_custom_call" | custom-call | tf_op jit(solution)/shard_map/pallas_call | solution.py:208
  2.3 3.0 %collective-permute-start = (bf16[208,512]{1,0:T(8,128)(2,1)}, bf16[208,512]{1,0:T(8,128)(2,1)S(1)}, u32[]{:S(2)}, u32[]{:S(2)}) collective-permute-start(bf16[208,512]{1,0:T(8,128)(2,1)} %get-tuple-element.8), channel_id=1, source_target_pairs={{0,1},{1,0},{2,3},{3,2},{4,5},{5,4},{6,7},{7,6},{8,9},{9,8},{10,11... | collective-permute-start | bytes 638984 | tf_op jit(solution)/shard_map/ppermute | solution.py:216
  5.3 2.6 %collective-permute-start.2 = (f32[32,256]{1,0:T(8,128)}, f32[32,256]{1,0:T(8,128)S(1)}, u32[]{:S(2)}, u32[]{:S(2)}) collective-permute-start(f32[32,256]{1,0:T(8,128)} %get-tuple-element.10), channel_id=1, source_target_pairs={{0,2},{1,3},{2,0},{3,1},{4,6},{5,7},{6,4},{7,5},{8,10},{9,11},{10,... | collective-permute-start | bytes 98312 | tf_op jit(solution)/shard_map/ppermute | solution.py:24
  7.9 0.0 collective-permute-start.3
  7.9 0.0 copy-start.1
  7.9 0.8 %collective-permute-start.1 = (bf16[160,512]{1,0:T(8,128)(2,1)}, bf16[160,512]{1,0:T(8,128)(2,1)S(1)}, u32[]{:S(2)}, u32[]{:S(2)}) collective-permute-start(bf16[160,512]{1,0:T(8,128)(2,1)} %get-tuple-element.9), channel_id=1, source_target_pairs={{1,2},{2,1},{3,4},{4,3},{5,6},{6,5},{7,8},{8,7},{9,10},{10,9},{11,... | collective-permute-start | bytes 491528 | tf_op jit(solution)/shard_map/ppermute | solution.py:218
  8.7 2.8 %collective-permute-done.refs_3_ = bf16[208,512]{1,0:T(8,128)(2,1)S(1)} collective-permute-done((bf16[208,512]{1,0:T(8,128)(2,1)}, bf16[208,512]{1,0:T(8,128)(2,1)S(1)}, u32[]{:S(2)}, u32[]{:S(2)}) %collective-permute-start) | collective-permute-done | bytes 213024 | tf_op jit(solution)/shard_map/ppermute | solution.py:216
  11.5 0.0 copy-start.3
  11.5 0.0 copy-start.2
  11.5 0.0 collective-permute-done.2.refs_8_
  11.5 2.9 %collective-permute-done.3.refs_9_ = f32[32,256]{1,0:T(8,128)S(1)} collective-permute-done((f32[32,256]{1,0:T(8,128)}, f32[32,256]{1,0:T(8,128)S(1)}, u32[]{:S(2)}, u32[]{:S(2)}) %collective-permute-start.3) | collective-permute-done | bytes 32800 | tf_op jit(solution)/shard_map/ppermute | solution.py:24
  14.4 0.0 copy-done.3
  14.5 0.2 collective-permute-start.4
  14.7 1.5 %collective-permute-start.5 = (f32[32,128]{1,0:T(8,128)S(1)}, f32[32,128]{1,0:T(8,128)S(1)}, u32[]{:S(2)}, u32[]{:S(2)}) collective-permute-start(f32[32,128]{1,0:T(8,128)S(1)} %slice_add_fusion.2), channel_id=1, source_target_pairs={{0,8},{4,12},{8,0},{12,4},{1,9},{5,13},{9,1},{13,5},{2,10},{6,14},... | collective-permute-start | bytes 49160 | tf_op jit(solution)/shard_map/ppermute | solution.py:24
  16.2 0.2 collective-permute-start.6
  16.4 0.0 copy-done
  16.4 0.0 copy-done.1
  16.4 0.0 copy-done.2
  16.4 2.4 %shard_map.55.refs_2_ = f32[32,1024]{1,0:T(8,128)S(1)} custom-call(bf16[128,1024]{1,0:T(8,128)(2,1)S(1)} %copy-done.1, f32[32,1024]{1,0:T(8,128)S(1)} %copy-done.2, bf16[5,64,1024]{2,1,0:T(8,128)(2,1)S(1)} %copy-done, s32[2,8]{1,0:T(2,128)} %refs_6_.1, s32[2]{0:T(128)} %refs_7_.1, ...), custom_call_target="tpu_custom_call", output_to_operand_aliasing={{}: (5, {})} | custom-call | tf_op jit(solution)/shard_map/pallas_call | solution.py:226
  18.8 0.0 collective-permute-done.1.refs_4_
  18.8 0.0 collective-permute-done.4.refs_10_
  18.8 0.0 collective-permute-done.5.refs_11_
  18.8 0.5 %collective-permute-done.6.refs_12_ = f32[32,128]{1,0:T(8,128)S(1)} collective-permute-done((f32[32,128]{1,0:T(8,128)S(1)}, f32[32,128]{1,0:T(8,128)S(1)}, u32[]{:S(2)}, u32[]{:S(2)}) %collective-permute-start.6) | collective-permute-done | bytes 16416 | tf_op jit(solution)/shard_map/ppermute | solution.py:24
  19.3 2.4 %shard_map.57 = f32[32,1024]{1,0:T(8,128)} custom-call(bf16[128,1024]{1,0:T(8,128)(2,1)S(1)} %copy-done.1, f32[32,1024]{1,0:T(8,128)S(1)} %copy-done.2, f32[32,1024]{1,0:T(8,128)S(1)} %shard_map.55.refs_2_, bf16[208,512]{1,0:T(8,128)(2,1)S(1)} %collective-permute-done.refs_3_, bf16[160,512]{1,0:T(8,128)(2,1)S(1)} %collective-permute-done.1.refs_4_, ...), custom_call_target="tpu_custom_call" | custom-call | tf_op jit(solution)/shard_map/pallas_call | solution.py:235
  (5 shorter events, 0.0 us)
Async XLA Ops:
  0.0 16.4 %copy-start = (bf16[5,64,1024]{2,1,0:T(8,128)(2,1)S(1)}, bf16[5,64,1024]{2,1,0:T(8,128)(2,1)}, u32[]{:S(2)}) copy-start(bf16[5,64,1024]{2,1,0:T(8,128)(2,1)} %refs_5_.1) | copy-start | bytes 1966084
  2.3 9.2 %collective-permute-start = (bf16[208,512]{1,0:T(8,128)(2,1)}, bf16[208,512]{1,0:T(8,128)(2,1)S(1)}, u32[]{:S(2)}, u32[]{:S(2)}) collective-permute-start(bf16[208,512]{1,0:T(8,128)(2,1)} %get-tuple-element.8), channel_id=1, source_target_pairs={{0,1},{1,0},{2,3},{3,2},{4,5},{5,4},{6,7},{7,6},{8,9},{9,8},{10,11... | collective-permute-start | bytes 638984 | tf_op jit(solution)/shard_map/ppermute | solution.py:216
  5.3 6.2 %collective-permute-start.2 = (f32[32,256]{1,0:T(8,128)}, f32[32,256]{1,0:T(8,128)S(1)}, u32[]{:S(2)}, u32[]{:S(2)}) collective-permute-start(f32[32,256]{1,0:T(8,128)} %get-tuple-element.10), channel_id=1, source_target_pairs={{0,2},{1,3},{2,0},{3,1},{4,6},{5,7},{6,4},{7,5},{8,10},{9,11},{10,... | collective-permute-start | bytes 98312 | tf_op jit(solution)/shard_map/ppermute | solution.py:24
  7.9 6.6 %collective-permute-start.3 = (f32[32,256]{1,0:T(8,128)}, f32[32,256]{1,0:T(8,128)S(1)}, u32[]{:S(2)}, u32[]{:S(2)}) collective-permute-start(f32[32,256]{1,0:T(8,128)} %get-tuple-element.10), channel_id=1, source_target_pairs={{0,3},{1,2},{2,1},{3,0},{4,7},{5,6},{6,5},{7,4},{8,11},{9,10},{10,... | collective-permute-start | bytes 98312 | tf_op jit(solution)/shard_map/ppermute | solution.py:24
  7.9 8.5 %copy-start.1 = (bf16[128,1024]{1,0:T(8,128)(2,1)S(1)}, bf16[128,1024]{1,0:T(8,128)(2,1)}, u32[]{:S(2)}) copy-start(bf16[128,1024]{1,0:T(8,128)(2,1)} %refs_0_.1) | copy-start | bytes 786436
  7.9 10.9 %collective-permute-start.1 = (bf16[160,512]{1,0:T(8,128)(2,1)}, bf16[160,512]{1,0:T(8,128)(2,1)S(1)}, u32[]{:S(2)}, u32[]{:S(2)}) collective-permute-start(bf16[160,512]{1,0:T(8,128)(2,1)} %get-tuple-element.9), channel_id=1, source_target_pairs={{1,2},{2,1},{3,4},{4,3},{5,6},{6,5},{7,8},{8,7},{9,10},{10,9},{11,... | collective-permute-start | bytes 491528 | tf_op jit(solution)/shard_map/ppermute | solution.py:218
  11.5 3.0 %copy-start.3 = (f32[32,256]{1,0:T(8,128)S(1)}, f32[32,256]{1,0:T(8,128)}, u32[]{:S(2)}) copy-start(f32[32,256]{1,0:T(8,128)} %get-tuple-element.10) | copy-start | bytes 98308
  11.5 4.9 %copy-start.2 = (f32[32,1024]{1,0:T(8,128)S(1)}, f32[32,1024]{1,0:T(8,128)}, u32[]{:S(2)}) copy-start(f32[32,1024]{1,0:T(8,128)} %refs_1_.1) | copy-start | bytes 393220
  14.5 4.4 %collective-permute-start.4 = (f32[32,128]{1,0:T(8,128)S(1)}, f32[32,128]{1,0:T(8,128)S(1)}, u32[]{:S(2)}, u32[]{:S(2)}) collective-permute-start(f32[32,128]{1,0:T(8,128)S(1)} %slice_add_fusion.2), channel_id=1, source_target_pairs={{0,4},{4,0},{8,12},{12,8},{1,5},{5,1},{9,13},{13,9},{2,6},{6,2},{1... | collective-permute-start | bytes 49160 | tf_op jit(solution)/shard_map/ppermute | solution.py:24
  14.7 4.2 %collective-permute-start.5 = (f32[32,128]{1,0:T(8,128)S(1)}, f32[32,128]{1,0:T(8,128)S(1)}, u32[]{:S(2)}, u32[]{:S(2)}) collective-permute-start(f32[32,128]{1,0:T(8,128)S(1)} %slice_add_fusion.2), channel_id=1, source_target_pairs={{0,8},{4,12},{8,0},{12,4},{1,9},{5,13},{9,1},{13,5},{2,10},{6,14},... | collective-permute-start | bytes 49160 | tf_op jit(solution)/shard_map/ppermute | solution.py:24
  16.2 3.2 %collective-permute-start.6 = (f32[32,128]{1,0:T(8,128)S(1)}, f32[32,128]{1,0:T(8,128)S(1)}, u32[]{:S(2)}, u32[]{:S(2)}) collective-permute-start(f32[32,128]{1,0:T(8,128)S(1)} %slice_add_fusion.2), channel_id=1, source_target_pairs={{0,12},{4,8},{8,4},{12,0},{1,13},{5,9},{9,5},{13,1},{2,14},{6,10},... | collective-permute-start | bytes 49160 | tf_op jit(solution)/shard_map/ppermute | solution.py:24

commit v23 on v15

--- a/solution.py
+++ b/solution.py
@@ -215,12 +215,13 @@
     ndev = sub_size * leaf_size
     from_pair = lax.ppermute(pair, axes, [(i, i ^ 1) for i in range(ndev)])
     round_one = [from_mask(parts, "sub", mask) for mask in range(2, sub_size)]
-    from_cross = lax.ppermute(cross, axes, [(i, i - 1 + 2 * (i % 2)) for i in range(1, ndev - 1)])
     upper = slice(rank * sub_bits, rank * dev_bits)
     line = parts[:, upper] + unpack_parts(from_pair, width_e + nrhs, step, rank * dev_bits)[:, upper]
     for got in round_one:
         line = line + got[:, upper]
+    cross, line = lax.optimization_barrier((cross, line))
     round_two = [from_mask(line, "leaf", mask) for mask in range(1, leaf_size)]
+    from_cross = lax.ppermute(cross, axes, [(i, i - 1 + 2 * (i % 2)) for i in range(1, ndev - 1)])
 
     out = jax.ShapeDtypeStruct((nrhs, local_points), jnp.float32)
     local = pl.pallas_call(

time: 21.8 us -> 26.1 us (1.20)
  starting transfers between devices: 8.21 us -> 11.5 us
  waiting for transfers between devices: 6.3 us -> 7.32 us
    ppermute x5, starting transfers between devices: 4.52 us -> 7.82 us  [from_mask(): return lax.ppermute(x, axis, pairs)]
    ppermute x1, waiting for transfers between devices: 2.9 us -> 3.57 us  [on_device(): from_pair = lax.ppermute(pair, axes, [(i, i ^ 1) for i in range(ndev)])]
    ppermute x5, waiting for transfers between devices: 3.39 us -> 3.75 us  [from_mask(): return lax.ppermute(x, axis, pairs)]
  transfers between devices with their start and end apart: 7 -> 7, of which waited for: 3 -> 4; matrix products, arithmetic and copies ran while one was open for 0% -> 0% of each run, Pallas kernels for 11% -> 9%
where the time goes in v23:
time: 26.1 us; the launch traced here: 26 us
  starting transfers between devices  11.5 us (44%)
  waiting for transfers between devices  7.32 us (28%)
  Pallas kernels  6.33 us (24%)
  local copies, waits for them, and re-layouts  0.68 us (3%)
    ppermute x5, starting transfers between devices, from_mask(): return lax.ppermute(x, axis, pairs)  7.82 us
    ppermute x5, waiting for transfers between devices, from_mask(): return lax.ppermute(x, axis, pairs)  3.75 us
    ppermute x1, waiting for transfers between devices, on_device(): from_pair = lax.ppermute(pair, axes, [(i, i ^ 1) for i in range(ndev)])  3.57 us
    ppermute x1, starting transfers between devices, on_device(): from_pair = lax.ppermute(pair, axes, [(i, i ^ 1) for i in range(ndev)])  3.02 us
    pallas_call x1, Pallas kernels, on_device(): pl.pallas_call(functools.partial(local_kernel, sub_size), out_shape=out,...  2.37 us
    pallas_call x1, Pallas kernels, on_device(): pl.pallas_call(functools.partial(send_kernel, loc_bits), out_shape=(pair_...  2.26 us
    pallas_call x1, Pallas kernels, on_device(): pl.pallas_call(functools.partial(final_kernel, sub_size, sub_bits, leaf_b...  1.71 us
    unnamed x9, local copies, waits for them, and re-layouts  0.68 us
  transfers between devices with their start and end apart: 7, of which 4 were waited for; matrix products, arithmetic and copies ran while one was open for 0% of the time, Pallas kernels for 9%

profile of v23, /device:TPU:0, one launch (start us, length us, event | category | flops | bytes accessed | tf_op | source)
XLA Modules:
  0.0 26.0 jit_solution(11718422612088715065)
XLA Ops:
  0.0 0.0 copy-start
  0.0 2.3 %shard_map.56 = (bf16[208,512]{1,0:T(8,128)(2,1)}, bf16[160,512]{1,0:T(8,128)(2,1)}, f32[32,256]{1,0:T(8,128)}) custom-call(bf16[128,1024]{1,0:T(8,128)(2,1)} %refs_0_.1, f32[32,1024]{1,0:T(8,128)} %refs_1_.1, bf16[5,64,1024]{2,1,0:T(8,128)(2,1)} %refs_5_.1), custom_call_target="tpu_custom_call" | custom-call | tf_op jit(solution)/shard_map/pallas_call | solution.py:208
  2.3 0.0 copy-start.1
  2.3 3.0 %collective-permute-start = (bf16[208,512]{1,0:T(8,128)(2,1)}, bf16[208,512]{1,0:T(8,128)(2,1)S(1)}, u32[]{:S(2)}, u32[]{:S(2)}) collective-permute-start(bf16[208,512]{1,0:T(8,128)(2,1)} %get-tuple-element.10), channel_id=1, source_target_pairs={{0,1},{1,0},{2,3},{3,2},{4,5},{5,4},{6,7},{7,6},{8,9},{9,8},{10,11... | collective-permute-start | bytes 638984 | tf_op jit(solution)/shard_map/ppermute | solution.py:216
  5.3 2.6 %collective-permute-start.1 = (f32[32,256]{1,0:T(8,128)}, f32[32,256]{1,0:T(8,128)S(1)}, u32[]{:S(2)}, u32[]{:S(2)}) collective-permute-start(f32[32,256]{1,0:T(8,128)} %get-tuple-element.12), channel_id=1, source_target_pairs={{0,2},{1,3},{2,0},{3,1},{4,6},{5,7},{6,4},{7,5},{8,10},{9,11},{10,... | collective-permute-start | bytes 98312 | tf_op jit(solution)/shard_map/ppermute | solution.py:24
  7.9 0.0 collective-permute-start.2
  7.9 3.6 %collective-permute-done.refs_3_ = bf16[208,512]{1,0:T(8,128)(2,1)S(1)} collective-permute-done((bf16[208,512]{1,0:T(8,128)(2,1)}, bf16[208,512]{1,0:T(8,128)(2,1)S(1)}, u32[]{:S(2)}, u32[]{:S(2)}) %collective-permute-start) | collective-permute-done | bytes 213024 | tf_op jit(solution)/shard_map/ppermute | solution.py:216
  11.4 0.0 copy-start.3
  11.5 0.0 copy-start.2
  11.5 0.0 collective-permute-done.1.refs_8_
  11.5 2.8 %collective-permute-done.2.refs_9_ = f32[32,256]{1,0:T(8,128)S(1)} collective-permute-done((f32[32,256]{1,0:T(8,128)}, f32[32,256]{1,0:T(8,128)S(1)}, u32[]{:S(2)}, u32[]{:S(2)}) %collective-permute-start.2) | collective-permute-done | bytes 32800 | tf_op jit(solution)/shard_map/ppermute | solution.py:24
  14.3 0.0 copy-done.3
  14.4 0.7 %collective-permute-start.3 = (bf16[160,512]{1,0:T(8,128)(2,1)}, bf16[160,512]{1,0:T(8,128)(2,1)S(1)}, u32[]{:S(2)}, u32[]{:S(2)}) collective-permute-start(bf16[160,512]{1,0:T(8,128)(2,1)} %get-tuple-element.13), channel_id=1, source_target_pairs={{1,2},{2,1},{3,4},{4,3},{5,6},{6,5},{7,8},{8,7},{9,10},{10,9},{11,... | collective-permute-start | bytes 491528 | tf_op jit(solution)/shard_map/ppermute | solution.py:224
  15.0 3.7 %collective-permute-start.4 = (f32[32,128]{1,0:T(8,128)S(1)}, f32[32,128]{1,0:T(8,128)S(1)}, u32[]{:S(2)}, u32[]{:S(2)}) collective-permute-start(f32[32,128]{1,0:T(8,128)S(1)} %slice_add_fusion.2), channel_id=1, source_target_pairs={{0,4},{4,0},{8,12},{12,8},{1,5},{5,1},{9,13},{13,9},{2,6},{6,2},{1... | collective-permute-start | bytes 49160 | tf_op jit(solution)/shard_map/ppermute | solution.py:24
  18.8 1.5 %collective-permute-start.5 = (f32[32,128]{1,0:T(8,128)S(1)}, f32[32,128]{1,0:T(8,128)S(1)}, u32[]{:S(2)}, u32[]{:S(2)}) collective-permute-start(f32[32,128]{1,0:T(8,128)S(1)} %slice_add_fusion.2), channel_id=1, source_target_pairs={{0,8},{4,12},{8,0},{12,4},{1,9},{5,13},{9,1},{13,5},{2,10},{6,14},... | collective-permute-start | bytes 49160 | tf_op jit(solution)/shard_map/ppermute | solution.py:24
  20.3 0.0 collective-permute-start.6
  20.3 0.0 copy-done
  20.3 0.0 copy-done.1
  20.3 0.0 copy-done.2
  20.3 2.4 %shard_map.55.refs_2_ = f32[32,1024]{1,0:T(8,128)S(1)} custom-call(bf16[128,1024]{1,0:T(8,128)(2,1)S(1)} %copy-done.1, f32[32,1024]{1,0:T(8,128)S(1)} %copy-done.2, bf16[5,64,1024]{2,1,0:T(8,128)(2,1)S(1)} %copy-done, s32[2,8]{1,0:T(2,128)} %refs_6_.1, s32[2]{0:T(128)} %refs_7_.1), custom_call_target="tpu_custom_call" | custom-call | tf_op jit(solution)/shard_map/pallas_call | solution.py:227
  22.7 0.0 collective-permute-done.4.refs_10_
  22.7 0.7 %collective-permute-done.5.refs_11_ = f32[32,128]{1,0:T(8,128)S(1)} collective-permute-done((f32[32,128]{1,0:T(8,128)S(1)}, f32[32,128]{1,0:T(8,128)S(1)}, u32[]{:S(2)}, u32[]{:S(2)}) %collective-permute-start.5) | collective-permute-done | bytes 16416 | tf_op jit(solution)/shard_map/ppermute | solution.py:24
  23.3 0.3 %collective-permute-done.6.refs_12_ = f32[32,128]{1,0:T(8,128)S(1)} collective-permute-done((f32[32,128]{1,0:T(8,128)S(1)}, f32[32,128]{1,0:T(8,128)S(1)}, u32[]{:S(2)}, u32[]{:S(2)}) %collective-permute-start.6) | collective-permute-done | bytes 16416 | tf_op jit(solution)/shard_map/ppermute | solution.py:24
  23.6 0.0 collective-permute-done.3.refs_4_
  23.6 1.7 %shard_map.57 = f32[32,1024]{1,0:T(8,128)S(1)} custom-call(bf16[128,1024]{1,0:T(8,128)(2,1)S(1)} %copy-done.1, f32[32,1024]{1,0:T(8,128)S(1)} %copy-done.2, f32[32,1024]{1,0:T(8,128)S(1)} %shard_map.55.refs_2_, bf16[208,512]{1,0:T(8,128)(2,1)S(1)} %collective-permute-done.refs_3_, ...), custom_call_target="tpu_custom_call", output_to_operand_aliasing={{}: (2, {})} | custom-call | tf_op jit(solution)/shard_map/pallas_call | solution.py:235
  25.3 0.7 %copy.8 = f32[32,1024]{1,0:T(8,128)} copy(f32[32,1024]{1,0:T(8,128)S(1)} %shard_map.57) | data formatting | bytes 262144
  (4 shorter events, 0.0 us)
Async XLA Ops:
  0.0 20.3 %copy-start = (bf16[5,64,1024]{2,1,0:T(8,128)(2,1)S(1)}, bf16[5,64,1024]{2,1,0:T(8,128)(2,1)}, u32[]{:S(2)}) copy-start(bf16[5,64,1024]{2,1,0:T(8,128)(2,1)} %refs_5_.1) | copy-start | bytes 1966084
  2.3 18.0 %copy-start.1 = (bf16[128,1024]{1,0:T(8,128)(2,1)S(1)}, bf16[128,1024]{1,0:T(8,128)(2,1)}, u32[]{:S(2)}) copy-start(bf16[128,1024]{1,0:T(8,128)(2,1)} %refs_0_.1) | copy-start | bytes 786436
  2.3 9.2 %collective-permute-start = (bf16[208,512]{1,0:T(8,128)(2,1)}, bf16[208,512]{1,0:T(8,128)(2,1)S(1)}, u32[]{:S(2)}, u32[]{:S(2)}) collective-permute-start(bf16[208,512]{1,0:T(8,128)(2,1)} %get-tuple-element.10), channel_id=1, source_target_pairs={{0,1},{1,0},{2,3},{3,2},{4,5},{5,4},{6,7},{7,6},{8,9},{9,8},{10,11... | collective-permute-start | bytes 638984 | tf_op jit(solution)/shard_map/ppermute | solution.py:216
  5.3 6.2 %collective-permute-start.1 = (f32[32,256]{1,0:T(8,128)}, f32[32,256]{1,0:T(8,128)S(1)}, u32[]{:S(2)}, u32[]{:S(2)}) collective-permute-start(f32[32,256]{1,0:T(8,128)} %get-tuple-element.12), channel_id=1, source_target_pairs={{0,2},{1,3},{2,0},{3,1},{4,6},{5,7},{6,4},{7,5},{8,10},{9,11},{10,... | collective-permute-start | bytes 98312 | tf_op jit(solution)/shard_map/ppermute | solution.py:24
  7.9 6.5 %collective-permute-start.2 = (f32[32,256]{1,0:T(8,128)}, f32[32,256]{1,0:T(8,128)S(1)}, u32[]{:S(2)}, u32[]{:S(2)}) collective-permute-start(f32[32,256]{1,0:T(8,128)} %get-tuple-element.12), channel_id=1, source_target_pairs={{0,3},{1,2},{2,1},{3,0},{4,7},{5,6},{6,5},{7,4},{8,11},{9,10},{10,... | collective-permute-start | bytes 98312 | tf_op jit(solution)/shard_map/ppermute | solution.py:24
  11.4 2.9 %copy-start.3 = (f32[32,256]{1,0:T(8,128)S(1)}, f32[32,256]{1,0:T(8,128)}, u32[]{:S(2)}) copy-start(f32[32,256]{1,0:T(8,128)} %get-tuple-element.12) | copy-start | bytes 98308
  11.5 8.8 %copy-start.2 = (f32[32,1024]{1,0:T(8,128)S(1)}, f32[32,1024]{1,0:T(8,128)}, u32[]{:S(2)}) copy-start(f32[32,1024]{1,0:T(8,128)} %refs_1_.1) | copy-start | bytes 393220
  14.4 9.2 %collective-permute-start.3 = (bf16[160,512]{1,0:T(8,128)(2,1)}, bf16[160,512]{1,0:T(8,128)(2,1)S(1)}, u32[]{:S(2)}, u32[]{:S(2)}) collective-permute-start(bf16[160,512]{1,0:T(8,128)(2,1)} %get-tuple-element.13), channel_id=1, source_target_pairs={{1,2},{2,1},{3,4},{4,3},{5,6},{6,5},{7,8},{8,7},{9,10},{10,9},{11,... | collective-permute-start | bytes 491528 | tf_op jit(solution)/shard_map/ppermute | solution.py:224
  15.0 7.6 %collective-permute-start.4 = (f32[32,128]{1,0:T(8,128)S(1)}, f32[32,128]{1,0:T(8,128)S(1)}, u32[]{:S(2)}, u32[]{:S(2)}) collective-permute-start(f32[32,128]{1,0:T(8,128)S(1)} %slice_add_fusion.2), channel_id=1, source_target_pairs={{0,4},{4,0},{8,12},{12,8},{1,5},{5,1},{9,13},{13,9},{2,6},{6,2},{1... | collective-permute-start | bytes 49160 | tf_op jit(solution)/shard_map/ppermute | solution.py:24
  18.8 4.5 %collective-permute-start.5 = (f32[32,128]{1,0:T(8,128)S(1)}, f32[32,128]{1,0:T(8,128)S(1)}, u32[]{:S(2)}, u32[]{:S(2)}) collective-permute-start(f32[32,128]{1,0:T(8,128)S(1)} %slice_add_fusion.2), channel_id=1, source_target_pairs={{0,8},{4,12},{8,0},{12,4},{1,9},{5,13},{9,1},{13,5},{2,10},{6,14},... | collective-permute-start | bytes 49160 | tf_op jit(solution)/shard_map/ppermute | solution.py:24
  20.3 3.3 %collective-permute-start.6 = (f32[32,128]{1,0:T(8,128)S(1)}, f32[32,128]{1,0:T(8,128)S(1)}, u32[]{:S(2)}, u32[]{:S(2)}) collective-permute-start(f32[32,128]{1,0:T(8,128)S(1)} %slice_add_fusion.2), channel_id=1, source_target_pairs={{0,12},{4,8},{8,4},{12,0},{1,13},{5,9},{9,5},{13,1},{2,14},{6,10},... | collective-permute-start | bytes 49160 | tf_op jit(solution)/shard_map/ppermute | solution.py:24

commit v24 on v18

--- a/solution.py
+++ b/solution.py
@@ -47,7 +47,16 @@
     return jnp.concatenate([x[:, g * columns : (g + 1) * columns] for g in range(groups)], axis=0)
 
 
-def send_kernel(loc_bits, emb_ref, dirs_ref, basis_ref, pair_ref, cross_ref, parts_ref):
+def cross_kernel(emb_ref, dirs_ref, cross_ref):
+    width_e = emb_ref.shape[0]
+    local_points = emb_ref.shape[1]
+    values = dirs_ref[...].astype(jnp.bfloat16)
+    even = lax.axis_index("sub") % 2 == 0
+    cross_ref[:width_e, :] = jnp.where(even, emb_ref[:, :LEAF], emb_ref[:, local_points - LEAF :])
+    cross_ref[width_e:, :] = jnp.where(even, values[:, :LEAF], values[:, local_points - LEAF :])
+
+
+def send_kernel(loc_bits, emb_ref, dirs_ref, basis_ref, pair_ref, parts_ref):
     width_e = emb_ref.shape[0]
     local_points = emb_ref.shape[1]
     nrhs = dirs_ref.shape[0]
@@ -57,8 +66,6 @@
     head_values, tail_values = values[:, :LEAF], values[:, local_points - LEAF :]
     pair_ref[:width_e, :] = jnp.where(even, tail_points, head_points)
     pair_ref[width_e : width_e + nrhs, :] = jnp.where(even, tail_values, head_values)
-    cross_ref[:width_e, :] = jnp.where(even, head_points, tail_points)
-    cross_ref[width_e:, :] = jnp.where(even, head_values, tail_values)
     levels, rank = parts_ref.shape[1] // basis_ref.shape[1], basis_ref.shape[1]
     stacked = basis_ref[loc_bits : loc_bits + levels].reshape(levels * rank, local_points)
     parts = nt_dot(values, stacked)
@@ -205,17 +212,21 @@
     pair_shape = jax.ShapeDtypeStruct((width_e + nrhs + 3 * step, LEAF), jnp.bfloat16)
     cross_shape = jax.ShapeDtypeStruct((width_e + nrhs, LEAF), jnp.bfloat16)
     parts_shape = jax.ShapeDtypeStruct((nrhs, rank * dev_bits), jnp.float32)
-    pair, cross, parts = pl.pallas_call(
+    cross = pl.pallas_call(
+        cross_kernel, out_shape=cross_shape, in_specs=[VMEM, VMEM], out_specs=VMEM
+    )(embeddings, directions)
+    ndev = sub_size * leaf_size
+    from_cross = lax.ppermute(cross, axes, [(i, i - 1 + 2 * (i % 2)) for i in range(1, ndev - 1)])
+    pair, parts = pl.pallas_call(
         functools.partial(send_kernel, loc_bits),
-        out_shape=(pair_shape, cross_shape, parts_shape),
+        out_shape=(pair_shape, parts_shape),
         in_specs=[VMEM, VMEM, VMEM],
-        out_specs=(VMEM, VMEM, VMEM),
-    )(*in_vmem(embeddings, directions, level_basis))
+        out_specs=(VMEM, VMEM),
+    )(embeddings, directions, *in_vmem(level_basis))
 
     ndev = sub_size * leaf_size
     from_pair = lax.ppermute(pair, axes, [(i, i ^ 1) for i in range(ndev)])
     round_one = [from_mask(parts, "sub", mask) for mask in range(2, sub_size)]
-    from_cross = lax.ppermute(cross, axes, [(i, i - 1 + 2 * (i % 2)) for i in range(1, ndev - 1)])
     upper = slice(rank * sub_bits, rank * dev_bits)
     line = parts[:, upper] + unpack_parts(from_pair, width_e + nrhs, step, rank * dev_bits)[:, upper]
     for got in round_one:

time: 23.6 us -> 24 us (1.017)
  Pallas kernels: 5.03 us -> 7.74 us
  local copies, waits for them, and re-layouts: 3.61 us -> 1.76 us
  waiting for transfers between devices: 6.31 us -> 4.9 us
  starting transfers between devices: 8.21 us -> 9.19 us
    unnamed x9 -> x11, local copies, waits for them, and re-layouts: 3.6 us -> 1.76 us
    ppermute x1, waiting for transfers between devices: 2.9 us -> 1.08 us  [on_device(): from_pair = lax.ppermute(pair, axes, [(i, i ^ 1) for i in range(ndev)])]
    pallas_call x0 -> x1, Pallas kernels: none -> 1.68 us  [on_device(): pl.pallas_call(cross_kernel, out_shape=cross_shape, in_specs=[VMEM, VMEM]...]
    pallas_call x1, Pallas kernels: 0.96 us -> 1.99 us  [on_device(): pl.pallas_call(functools.partial(send_kernel, loc_bits), out_shape=(pair_...]
    ppermute x5, starting transfers between devices: 4.53 us -> 5.37 us  [from_mask(): return lax.ppermute(x, axis, pairs)]
    ppermute x5, waiting for transfers between devices: 3.41 us -> 3.82 us  [from_mask(): return lax.ppermute(x, axis, pairs)]
  transfers between devices with their start and end apart: 7 -> 7, of which waited for: 3 -> 3; matrix products, arithmetic and copies ran while one was open for 0% -> 0% of each run, Pallas kernels for 10% -> 17%
where the time goes in v24:
time: 24 us; the launch traced here: 23.7 us
  starting transfers between devices  9.19 us (38%)
  Pallas kernels  7.74 us (32%)
  waiting for transfers between devices  4.9 us (20%)
  local copies, waits for them, and re-layouts  1.76 us (7%)
    ppermute x5, starting transfers between devices, from_mask(): return lax.ppermute(x, axis, pairs)  5.37 us
    ppermute x5, waiting for transfers between devices, from_mask(): return lax.ppermute(x, axis, pairs)  3.82 us
    ppermute x1, starting transfers between devices, on_device(): from_pair = lax.ppermute(pair, axes, [(i, i ^ 1) for i in range(ndev)])  3.02 us
    pallas_call x1, Pallas kernels, on_device(): pl.pallas_call(functools.partial(local_kernel, sub_size), out_shape=out,...  2.36 us
    pallas_call x1, Pallas kernels, on_device(): pl.pallas_call(functools.partial(send_kernel, loc_bits), out_shape=(pair_...  1.99 us
    unnamed x11, local copies, waits for them, and re-layouts  1.76 us
    pallas_call x1, Pallas kernels, on_device(): pl.pallas_call(functools.partial(final_kernel, sub_size, sub_bits, leaf_b...  1.71 us
    pallas_call x1, Pallas kernels, on_device(): pl.pallas_call(cross_kernel, out_shape=cross_shape, in_specs=[VMEM, VMEM]...  1.68 us
  transfers between devices with their start and end apart: 7, of which 3 were waited for; matrix products, arithmetic and copies ran while one was open for 0% of the time, Pallas kernels for 17%

profile of v24, /device:TPU:0, one launch (start us, length us, event | category | flops | bytes accessed | tf_op | source)
XLA Modules:
  0.0 23.7 jit_solution(11776173325537070015)
XLA Ops:
  0.0 0.0 copy-start
  0.0 1.1 %copy-done = bf16[5,64,1024]{2,1,0:T(8,128)(2,1)S(1)} copy-done((bf16[5,64,1024]{2,1,0:T(8,128)(2,1)S(1)}, bf16[5,64,1024]{2,1,0:T(8,128)(2,1)}, u32[]{:S(2)}) %copy-start) | copy-done | bytes 655384
  1.1 0.0 copy-start.3
  1.1 2.0 %shard_map.56 = (bf16[208,512]{1,0:T(8,128)(2,1)}, f32[32,256]{1,0:T(8,128)}) custom-call(bf16[128,1024]{1,0:T(8,128)(2,1)} %refs_0_.1, f32[32,1024]{1,0:T(8,128)} %refs_1_.1, bf16[5,64,1024]{2,1,0:T(8,128)(2,1)S(1)} %copy-done), custom_call_target="tpu_custom_call" | custom-call | tf_op jit(solution)/shard_map/pallas_call | solution.py:220
  3.1 0.0 copy-start.1
  3.1 3.0 %collective-permute-start = (bf16[208,512]{1,0:T(8,128)(2,1)}, bf16[208,512]{1,0:T(8,128)(2,1)S(1)}, u32[]{:S(2)}, u32[]{:S(2)}) collective-permute-start(bf16[208,512]{1,0:T(8,128)(2,1)} %get-tuple-element.7), channel_id=1, source_target_pairs={{0,1},{1,0},{2,3},{3,2},{4,5},{5,4},{6,7},{7,6},{8,9},{9,8},{10,11... | collective-permute-start | bytes 638984 | tf_op jit(solution)/shard_map/ppermute | solution.py:228
  6.1 2.6 %collective-permute-start.2 = (f32[32,256]{1,0:T(8,128)}, f32[32,256]{1,0:T(8,128)S(1)}, u32[]{:S(2)}, u32[]{:S(2)}) collective-permute-start(f32[32,256]{1,0:T(8,128)} %get-tuple-element.8), channel_id=1, source_target_pairs={{0,2},{1,3},{2,0},{3,1},{4,6},{5,7},{6,4},{7,5},{8,10},{9,11},{10,... | collective-permute-start | bytes 98312 | tf_op jit(solution)/shard_map/ppermute | solution.py:24
  8.7 0.0 collective-permute-start.3
  8.7 0.0 copy-start.4
  8.7 1.7 %shard_map.57 = bf16[160,512]{1,0:T(8,128)(2,1)} custom-call(bf16[128,1024]{1,0:T(8,128)(2,1)} %refs_0_.1, f32[32,1024]{1,0:T(8,128)} %refs_1_.1), custom_call_target="tpu_custom_call" | custom-call | tf_op jit(solution)/shard_map/pallas_call | solution.py:215
  10.4 0.0 copy-start.2
  10.4 0.8 %collective-permute-start.1 = (bf16[160,512]{1,0:T(8,128)(2,1)}, bf16[160,512]{1,0:T(8,128)(2,1)S(1)}, u32[]{:S(2)}, u32[]{:S(2)}) collective-permute-start(bf16[160,512]{1,0:T(8,128)(2,1)} %shard_map.57), channel_id=1, source_target_pairs={{1,2},{2,1},{3,4},{4,3},{5,6},{6,5},{7,8},{8,7},{9,10},{10,9},{11,... | collective-permute-start | bytes 491528 | tf_op jit(solution)/shard_map/ppermute | solution.py:219
  11.2 1.1 %collective-permute-done.refs_3_ = bf16[208,512]{1,0:T(8,128)(2,1)S(1)} collective-permute-done((bf16[208,512]{1,0:T(8,128)(2,1)}, bf16[208,512]{1,0:T(8,128)(2,1)S(1)}, u32[]{:S(2)}, u32[]{:S(2)}) %collective-permute-start) | collective-permute-done | bytes 213024 | tf_op jit(solution)/shard_map/ppermute | solution.py:228
  12.3 0.0 collective-permute-done.2.refs_8_
  12.3 2.9 %collective-permute-done.3.refs_9_ = f32[32,256]{1,0:T(8,128)S(1)} collective-permute-done((f32[32,256]{1,0:T(8,128)}, f32[32,256]{1,0:T(8,128)S(1)}, u32[]{:S(2)}, u32[]{:S(2)}) %collective-permute-start.3) | collective-permute-done | bytes 32800 | tf_op jit(solution)/shard_map/ppermute | solution.py:24
  15.2 0.0 copy-done.4
  15.2 1.3 %collective-permute-start.4 = (f32[32,128]{1,0:T(8,128)S(1)}, f32[32,128]{1,0:T(8,128)S(1)}, u32[]{:S(2)}, u32[]{:S(2)}) collective-permute-start(f32[32,128]{1,0:T(8,128)S(1)} %slice_add_fusion.2), channel_id=1, source_target_pairs={{0,4},{4,0},{8,12},{12,8},{1,5},{5,1},{9,13},{13,9},{2,6},{6,2},{1... | collective-permute-start | bytes 49160 | tf_op jit(solution)/shard_map/ppermute | solution.py:24
  16.5 1.5 %collective-permute-start.5 = (f32[32,128]{1,0:T(8,128)S(1)}, f32[32,128]{1,0:T(8,128)S(1)}, u32[]{:S(2)}, u32[]{:S(2)}) collective-permute-start(f32[32,128]{1,0:T(8,128)S(1)} %slice_add_fusion.2), channel_id=1, source_target_pairs={{0,8},{4,12},{8,0},{12,4},{1,9},{5,13},{9,1},{13,5},{2,10},{6,14},... | collective-permute-start | bytes 49160 | tf_op jit(solution)/shard_map/ppermute | solution.py:24
  18.0 0.0 collective-permute-start.6
  18.0 0.0 copy-done.3
  18.0 0.0 copy-done.1
  18.0 0.0 copy-done.2
  18.0 2.4 %shard_map.55.refs_2_ = f32[32,1024]{1,0:T(8,128)S(1)} custom-call(bf16[128,1024]{1,0:T(8,128)(2,1)S(1)} %copy-done.2, f32[32,1024]{1,0:T(8,128)S(1)} %copy-done.3, bf16[5,64,1024]{2,1,0:T(8,128)(2,1)S(1)} %copy-done.1, s32[2,8]{1,0:T(2,128)} %refs_6_.1, s32[2]{0:T(128)} %refs_7_.1), custom_call_target="tpu_custom_call" | custom-call | tf_op jit(solution)/shard_map/pallas_call | solution.py:237
  20.4 0.0 collective-permute-done.1.refs_4_
  20.4 0.0 collective-permute-done.4.refs_10_
  20.4 0.0 collective-permute-done.5.refs_11_
  20.4 0.9 %collective-permute-done.6.refs_12_ = f32[32,128]{1,0:T(8,128)S(1)} collective-permute-done((f32[32,128]{1,0:T(8,128)S(1)}, f32[32,128]{1,0:T(8,128)S(1)}, u32[]{:S(2)}, u32[]{:S(2)}) %collective-permute-start.6) | collective-permute-done | bytes 16416 | tf_op jit(solution)/shard_map/ppermute | solution.py:24
  21.3 1.7 %shard_map.58 = f32[32,1024]{1,0:T(8,128)S(1)} custom-call(bf16[128,1024]{1,0:T(8,128)(2,1)S(1)} %copy-done.2, f32[32,1024]{1,0:T(8,128)S(1)} %copy-done.3, f32[32,1024]{1,0:T(8,128)S(1)} %shard_map.55.refs_2_, bf16[208,512]{1,0:T(8,128)(2,1)S(1)} %collective-permute-done.refs_3_, ...), custom_call_target="tpu_custom_call", output_to_operand_aliasing={{}: (2, {})} | custom-call | tf_op jit(solution)/shard_map/pallas_call | solution.py:245
  23.1 0.7 %copy.8 = f32[32,1024]{1,0:T(8,128)} copy(f32[32,1024]{1,0:T(8,128)S(1)} %shard_map.58) | data formatting | bytes 262144
  (4 shorter events, 0.0 us)
Async XLA Ops:
  0.0 1.1 %copy-start = (bf16[5,64,1024]{2,1,0:T(8,128)(2,1)S(1)}, bf16[5,64,1024]{2,1,0:T(8,128)(2,1)}, u32[]{:S(2)}) copy-start(bf16[5,64,1024]{2,1,0:T(8,128)(2,1)} %refs_5_.1) | copy-start | bytes 1966084
  1.1 16.9 %copy-start.3 = (f32[32,1024]{1,0:T(8,128)S(1)}, f32[32,1024]{1,0:T(8,128)}, u32[]{:S(2)}) copy-start(f32[32,1024]{1,0:T(8,128)} %refs_1_.1) | copy-start | bytes 393220
  3.1 14.9 %copy-start.1 = (bf16[5,64,1024]{2,1,0:T(8,128)(2,1)S(1)}, bf16[5,64,1024]{2,1,0:T(8,128)(2,1)}, u32[]{:S(2)}) copy-start(bf16[5,64,1024]{2,1,0:T(8,128)(2,1)} %refs_5_.1) | copy-start | bytes 1966084
  3.1 9.2 %collective-permute-start = (bf16[208,512]{1,0:T(8,128)(2,1)}, bf16[208,512]{1,0:T(8,128)(2,1)S(1)}, u32[]{:S(2)}, u32[]{:S(2)}) collective-permute-start(bf16[208,512]{1,0:T(8,128)(2,1)} %get-tuple-element.7), channel_id=1, source_target_pairs={{0,1},{1,0},{2,3},{3,2},{4,5},{5,4},{6,7},{7,6},{8,9},{9,8},{10,11... | collective-permute-start | bytes 638984 | tf_op jit(solution)/shard_map/ppermute | solution.py:228
  6.1 6.2 %collective-permute-start.2 = (f32[32,256]{1,0:T(8,128)}, f32[32,256]{1,0:T(8,128)S(1)}, u32[]{:S(2)}, u32[]{:S(2)}) collective-permute-start(f32[32,256]{1,0:T(8,128)} %get-tuple-element.8), channel_id=1, source_target_pairs={{0,2},{1,3},{2,0},{3,1},{4,6},{5,7},{6,4},{7,5},{8,10},{9,11},{10,... | collective-permute-start | bytes 98312 | tf_op jit(solution)/shard_map/ppermute | solution.py:24
  8.7 6.5 %collective-permute-start.3 = (f32[32,256]{1,0:T(8,128)}, f32[32,256]{1,0:T(8,128)S(1)}, u32[]{:S(2)}, u32[]{:S(2)}) collective-permute-start(f32[32,256]{1,0:T(8,128)} %get-tuple-element.8), channel_id=1, source_target_pairs={{0,3},{1,2},{2,1},{3,0},{4,7},{5,6},{6,5},{7,4},{8,11},{9,10},{10,... | collective-permute-start | bytes 98312 | tf_op jit(solution)/shard_map/ppermute | solution.py:24
  8.7 6.5 %copy-start.4 = (f32[32,256]{1,0:T(8,128)S(1)}, f32[32,256]{1,0:T(8,128)}, u32[]{:S(2)}) copy-start(f32[32,256]{1,0:T(8,128)} %get-tuple-element.8) | copy-start | bytes 98308
  10.4 7.6 %copy-start.2 = (bf16[128,1024]{1,0:T(8,128)(2,1)S(1)}, bf16[128,1024]{1,0:T(8,128)(2,1)}, u32[]{:S(2)}) copy-start(bf16[128,1024]{1,0:T(8,128)(2,1)} %refs_0_.1) | copy-start | bytes 786436
  10.4 10.0 %collective-permute-start.1 = (bf16[160,512]{1,0:T(8,128)(2,1)}, bf16[160,512]{1,0:T(8,128)(2,1)S(1)}, u32[]{:S(2)}, u32[]{:S(2)}) collective-permute-start(bf16[160,512]{1,0:T(8,128)(2,1)} %shard_map.57), channel_id=1, source_target_pairs={{1,2},{2,1},{3,4},{4,3},{5,6},{6,5},{7,8},{8,7},{9,10},{10,9},{11,... | collective-permute-start | bytes 491528 | tf_op jit(solution)/shard_map/ppermute | solution.py:219
  15.2 5.2 %collective-permute-start.4 = (f32[32,128]{1,0:T(8,128)S(1)}, f32[32,128]{1,0:T(8,128)S(1)}, u32[]{:S(2)}, u32[]{:S(2)}) collective-permute-start(f32[32,128]{1,0:T(8,128)S(1)} %slice_add_fusion.2), channel_id=1, source_target_pairs={{0,4},{4,0},{8,12},{12,8},{1,5},{5,1},{9,13},{13,9},{2,6},{6,2},{1... | collective-permute-start | bytes 49160 | tf_op jit(solution)/shard_map/ppermute | solution.py:24
  16.5 3.9 %collective-permute-start.5 = (f32[32,128]{1,0:T(8,128)S(1)}, f32[32,128]{1,0:T(8,128)S(1)}, u32[]{:S(2)}, u32[]{:S(2)}) collective-permute-start(f32[32,128]{1,0:T(8,128)S(1)} %slice_add_fusion.2), channel_id=1, source_target_pairs={{0,8},{4,12},{8,0},{12,4},{1,9},{5,13},{9,1},{13,5},{2,10},{6,14},... | collective-permute-start | bytes 49160 | tf_op jit(solution)/shard_map/ppermute | solution.py:24
  18.0 3.3 %collective-permute-start.6 = (f32[32,128]{1,0:T(8,128)S(1)}, f32[32,128]{1,0:T(8,128)S(1)}, u32[]{:S(2)}, u32[]{:S(2)}) collective-permute-start(f32[32,128]{1,0:T(8,128)S(1)} %slice_add_fusion.2), channel_id=1, source_target_pairs={{0,12},{4,8},{8,4},{12,0},{1,13},{5,9},{9,5},{13,1},{2,14},{6,10},... | collective-permute-start | bytes 49160 | tf_op jit(solution)/shard_map/ppermute | solution.py:24
